TPU v7x, 256 devices: a whole 4x4x8 slice. The times are simulated.
256 devices in a mesh: dp: 2 (over y_hi), retr: 16 (over x, y_lo, core), tensor: 8 (over z).
Axes of the slice: x: 4, y: 4 (y_hi: 2, y_lo: 2; y = y_hi * 2 + y_lo), z: 8, core: 2. Of those that a mesh axis runs over, the one named last changes fastest.
Arguments:
- hidden_in: bfloat16 [16384, 4096], P(('dp', 'retr'), 'tensor'), may hold values from -12 to 12
- norm_gain: float32 [4096], replicated, may hold values from 0.1 to 1.9
- nbr_table: int32 [256, 2], P(('dp', 'retr')), may hold values from 0 to 63, as said below
- encodings: bfloat16 [64, 128, 1024], P('retr'), may hold values from -21 to 21
- enc_mask: int32 [64, 4], P('retr'), may hold values from 0 to 1, as said below
- w_query: bfloat16 [4096, 4096], P(None, 'tensor'), may hold values from -0.02703125 to 0.02703125
- w_key: bfloat16 [1024, 4096], P(None, 'tensor'), may hold values from -0.1021875 to 0.1021875
- w_value: bfloat16 [1024, 4096], P(None, 'tensor'), may hold values from -0.1875 to 0.1875
- w_out: bfloat16 [4096, 4096], P('tensor'), may hold values from -0.125 to 0.125
Outputs:
- mixed: bfloat16 [16384, 4096], P(('dp', 'retr'), 'tensor')
Inputs may be any that keep to these rules, and one draw needn't show every extreme that they name: `nbr_table`: each aligned block of 8 table rows (the rows of one device) holds 16 distinct ids; at most 2 of them share the value id // 4, and in every block some value of id // 4 has exactly 2. `enc_mask`: in each row the ones come first; the first entry is 1.
All inputs are finite; a program needn't handle non-finite values.
Results may differ from a plain program's by a relative error of at most 0.012.
The roundings to bfloat16 on the way count: a program that leaves them out, or rounds other values in their place, can miss the bound.
Values may be sent and summed in bfloat16 or wider, within the bound.
No kernel may reach another device: no remote copies, remote signals or barrier semaphores. Data moves between devices by JAX's collectives and lax.ppermute only.
A program may use at most 128 MiB of HBM per device.

v0:
```python
import math

import jax
import jax.numpy as jnp
from jax import lax
from jax.sharding import PartitionSpec as P

HD = 128
NBRS = 2
BLOCK = 32


def attend_gathered(queries, key_value, selected_marks, segment_count, head_cols):
    tok_rows = queries.shape[0]
    head_count = head_cols // HD
    entry_keys = key_value.shape[0] // segment_count * key_value.shape[1]
    mask_cols = selected_marks.shape[1]
    key_block = key_value[:, :, :head_cols].reshape(segment_count, entry_keys, head_count, HD)
    value_block = key_value[:, :, head_cols:].reshape(segment_count, entry_keys, head_count, HD)
    key_live = (
        jnp.repeat(selected_marks.reshape(segment_count, NBRS * mask_cols), BLOCK, axis=1) > 0
    )
    query_block = queries.reshape(segment_count, tok_rows // segment_count, head_count, HD)
    factor = 1.0 / math.sqrt(HD)
    scores = (
        jnp.einsum("cqhd,ckhd->chqk", query_block, key_block, preferred_element_type=jnp.float32)
        * factor
    )
    key_open = key_live[:, None, None, :]
    scores = jnp.where(key_open, scores, -1e30)
    row_max = jnp.max(scores, axis=-1, keepdims=True)
    weights = jnp.exp(scores - row_max) * key_open.astype(jnp.float32)
    probabilities = (weights / jnp.sum(weights, axis=-1, keepdims=True)).astype(jnp.bfloat16)
    attended = jnp.einsum(
        "chqk,ckhd->cqhd", probabilities, value_block, preferred_element_type=jnp.float32
    )
    return attended.astype(jnp.bfloat16).reshape(tok_rows, head_cols)


def local(hidden_in, norm_gain, nbr_table, encodings, enc_mask, w_query, w_key, w_value, w_out):
    gathered = lax.all_gather(hidden_in, "tensor", axis=1, tiled=True)
    widened = gathered.astype(jnp.float32)
    mean_sq = jnp.mean(widened * widened, axis=-1, keepdims=True)
    normed = (widened * lax.rsqrt(mean_sq + 1e-05) * norm_gain).astype(jnp.bfloat16)
    queries = jnp.dot(normed, w_query, preferred_element_type=jnp.float32).astype(jnp.bfloat16)
    w_both = jnp.concatenate([w_key, w_value], axis=1)
    segment_count = nbr_table.shape[0]
    entry_len = encodings.shape[1]
    enc_width = encodings.shape[2]
    head_cols = w_key.shape[1]
    wanted = nbr_table.reshape(-1)
    need_count = wanted.shape[0]
    live_marks = enc_mask.astype(jnp.bfloat16)
    entry_rows = lax.all_gather(encodings, "retr", axis=0, tiled=True)
    entry_marks = lax.all_gather(live_marks, "retr", axis=0, tiled=True)
    piece_count = entry_rows.shape[0]
    one_hot = (wanted[:, None] == jnp.arange(piece_count, dtype=jnp.int32)[None, :]).astype(
        jnp.bfloat16
    )
    picked = jnp.einsum(
        "jn,nre->jre", one_hot, entry_rows, preferred_element_type=jnp.float32
    ).astype(jnp.bfloat16)
    picked_marks = jnp.dot(one_hot, entry_marks, preferred_element_type=jnp.float32).astype(
        jnp.bfloat16
    )
    key_value = jnp.dot(
        picked.reshape(need_count * entry_len, enc_width),
        w_both,
        preferred_element_type=jnp.float32,
    )
    key_value = key_value.astype(jnp.bfloat16).reshape(need_count, entry_len, 2 * head_cols)
    attended = attend_gathered(queries, key_value, picked_marks, segment_count, head_cols)
    partial_value = jnp.dot(attended, w_out, preferred_element_type=jnp.float32)
    summed = lax.psum_scatter(partial_value, "tensor", scatter_dimension=1, tiled=True)
    return (hidden_in.astype(jnp.float32) + summed).astype(jnp.bfloat16)


def solution(mesh):
    in_specs = (
        P(("dp", "retr"), "tensor"),
        P(),
        P(("dp", "retr"), None),
        P("retr", None, None),
        P("retr", None),
        P(None, "tensor"),
        P(None, "tensor"),
        P(None, "tensor"),
        P("tensor", None),
    )
    out_specs = P(("dp", "retr"), "tensor")
    return jax.shard_map(local, mesh=mesh, in_specs=in_specs, out_specs=out_specs, check_vma=False)
```

profile of v0, /device:TPU:1, one launch (start us, length us, event | category | flops | bytes accessed | tf_op | source)
XLA Modules:
  0.0 318.5 jit_solution(9526612523659051779)
XLA Ops:
  6.5 0.0 copy-start.6
  6.5 0.0 all-gather.6.cloned.1.call-start
  6.5 0.7 all-gather.6.cloned.1.call-update
  7.3 0.0 all-gather.4.cloned.1.call-start
  7.3 0.7 all-gather.4.cloned.1.call-update
  8.0 0.0 reduce-scatter.2.cloned.1.call-start
  8.1 0.8 copy.24
  8.8 0.1 eq.15
  8.9 0.7 convert_bitcast_fusion
  9.6 21.0 %all-gather = bf16[16,4,4]{2,1,0:T(4,128)(2,1)S(1)} all-gather(bf16[1,4,4]{2,1,0:T(4,128)(2,1)S(1)} %convert_bitcast_fusion), channel_id=1, replica_groups=mesh['dp'=2,'retr'=16,'tensor'=8] {'retr'}, dimensions={0}, use_global_device_ids=true | all-gather | bytes 544 | tf_op jit(solution)/shard_map/all_gather | solution.py:55
  30.6 0.2 fusion.30
  30.8 0.1 copy.28
  30.9 0.1 gt.22
  31.0 0.1 broadcast_in_dim.14
  31.0 0.1 gt.23
  31.2 36.4 %all-gather.6.cloned.1.call-done = bf16[512,4096]{1,0:T(8,128)(2,1)} async-done(((bf16[512,512]{1,0:T(8,128)(2,1)}), bf16[512,4096]{1,0:T(8,128)(2,1)}) %all-gather.6.cloned.1.call-update) | async-done | bytes 4194320 | tf_op jit(solution)/shard_map/all_gather | solution.py:41
  67.5 0.0 copy-start.1
  67.5 3.2 %fusion.3 = f32[512]{0:T(512)S(1)} fusion(bf16[512,4096]{1,0:T(8,128)(2,1)} %all-gather.6.cloned.1.call-done), kind=kLoop, calls=%fused_computation.5 | loop fusion | flops 6290944 | bytes 4196352 | tf_op jit(solution)/shard_map/reduce_sum | solution.py:43
  70.8 0.0 copy-done.6
  70.8 0.2 copy-done.1
  71.0 4.6 %fusion.24 = bf16[512,512]{1,0:T(8,128)(2,1)S(1)} fusion(bf16[4096,512]{1,0:T(8,128)(2,1)} %param.14, bf16[512,4096]{1,0:T(8,128)(2,1)S(1)} %copy-done.1, f32[4096]{0:T(1024)S(1)} %copy-done.6, f32[512]{0:T(512)S(1)} %add_rsqrt_fusion), kind=kOutput, calls=%fused_computation.25 | convolution fusion | flops 2156134400 | bytes 8931328 | tf_op jit(solution)/shard_map/dot_general | solution.py:45
  75.6 0.1 reshape.49
  75.7 87.0 %all-gather.4.cloned.1.call-done = bf16[64,128,1024]{2,1,0:T(8,128)(2,1)} async-done(((bf16[4,128,1024]{2,1,0:T(8,128)(2,1)}), bf16[64,128,1024]{2,1,0:T(8,128)(2,1)}) %all-gather.4.cloned.1.call-update) | async-done | bytes 16777232 | tf_op jit(solution)/shard_map/all_gather | solution.py:54
  162.7 23.7 %fusion.10 = bf16[16,128,1024]{2,0,1:T(8,128)(2,1)S(1)} fusion(bf16[64,128,1024]{2,1,0:T(8,128)(2,1)} %all-gather.4.cloned.1.call-done, s32[16]{0:T(128)S(1)} %eq.15), kind=kOutput, calls=%fused_computation.12 | convolution fusion | flops 270533632 | bytes 20971584 | tf_op jit(solution)/shard_map/jn,nre->jre/dot_general | solution.py:60
  186.4 0.0 copy-start.4
  186.4 0.0 copy-start.5
  186.4 2.5 copy.26
  188.9 0.0 copy-done.4
  189.0 0.0 copy-done.5
  189.0 5.0 %convolution_convert_fusion = bf16[2048,1024]{1,0:T(8,128)(2,1)S(1)} fusion(bf16[2048,1024]{1,0:T(8,128)(2,1)S(1)} %bitcast.20, bf16[1024,512]{1,0:T(8,128)(2,1)S(1)} %copy-done.4, bf16[1024,512]{1,0:T(8,128)(2,1)S(1)} %copy-done.5), kind=kOutput, calls=%fused_computation.11 | convolution fusion | flops 4301258752 | bytes 10485760 | tf_op jit(solution)/shard_map/dot_general | solution.py:66
  194.0 1.8 fusion.46
  195.8 4.0 %reshape.55 = bf16[8,256,4,128]{3,2,1,0:T(4,128)(2,1)} reshape(bf16[16,128,512]{2,1,0:T(8,128)(2,1)} %get-tuple-element.5) | data formatting | bytes 4194304 | tf_op jit(solution)/shard_map/reshape | solution.py:18
  199.8 2.0 reshape.56
  201.8 0.0 copy-start.2
  201.8 4.1 %fusion.47 = (f32[8,4,64]{2,1,0:T(4,128)S(1)}, f32[8,4,64,256]{3,2,1,0:T(8,128)}) fusion(f32[8,256]{1,0:T(8,128)S(1)} %convert_element_type.53, pred[8,256]{1,0:T(8,128)(4,1)S(1)} %gt.23, bf16[8,256,4,128]{3,2,1,0:T(4,128)(2,1)} %reshape.55, bf16[8,64,4,128]{3,2,1,0:T(4,128)(2,1)S(1)} %reshape.49), kind=kOutput, calls=%fused_computation.48 | convolution fusion | flops 136839424 | bytes 4737024 | tf_op jit(solution)/shard_map/sub | solution.py:32
  206.0 0.0 copy-done.2
  206.0 0.0 copy-start
  206.0 2.3 fusion.27
  208.3 0.4 copy.33
  208.7 0.1 copy-done
  208.8 5.6 %fusion.35 = f32[512,4096]{1,0:T(8,128)} fusion(bf16[512,4096]{1,0:T(8,128)(2,1)S(1)} %copy-done, bf16[64,8,4,128]{3,2,1,0:T(4,128)(2,1)S(1)} %bitcast.21), kind=kOutput, calls=%fused_computation.34 | convolution fusion | flops 2147483648 | bytes 13107200 | tf_op jit(solution)/shard_map/dot_general | solution.py:73
  214.4 0.0 copy-start.3
  214.4 0.0 reduce-scatter.2.cloned.1.call-update
  214.4 95.4 %reduce-scatter.2.cloned.1.call-done = f32[512,512]{1,0:T(8,128)} async-done(((f32[512,4096]{1,0:T(8,128)}), f32[512,512]{1,0:T(8,128)}) %reduce-scatter.2.cloned.1.call-update) | async-done | bytes 1048592 | tf_op jit(solution)/shard_map/reduce_scatter | solution.py:74
  309.8 0.0 copy-done.3
  309.8 2.2 add_convert_fusion
  (2 shorter events, 0.0 us)
Async XLA Ops:
  6.5 64.2 %copy-start.6 = (f32[4096]{0:T(1024)S(1)}, f32[4096]{0:T(1024)}, u32[]{:S(2)}) copy-start(f32[4096]{0:T(1024)} %param.10) | copy-start | bytes 49156
  6.5 61.0 %all-gather.6.cloned.1.call-start = ((), (), s32[]{:S(2)}) async-start(), calls=%async_computation.2 | async-start | bytes 4718592 | tf_op jit(solution)/shard_map/all_gather | solution.py:41
  7.3 155.4 %all-gather.4.cloned.1.call-start = ((), (), s32[]{:S(2)}) async-start(), calls=%async_computation.1 | async-start | bytes 17825792 | tf_op jit(solution)/shard_map/all_gather | solution.py:54
  8.0 301.8 %reduce-scatter.2.cloned.1.call-start = ((), (), s32[]{:S(2)}) async-start(), calls=%async_computation.3 | async-start | bytes 9437184 | tf_op jit(solution)/shard_map/reduce_scatter | solution.py:74
  67.5 3.4 %copy-start.1 = (bf16[512,4096]{1,0:T(8,128)(2,1)S(1)}, bf16[512,4096]{1,0:T(8,128)(2,1)}, u32[]{:S(2)}) copy-start(bf16[512,4096]{1,0:T(8,128)(2,1)} %all-gather.6.cloned.1.call-done) | copy-start | bytes 12582916
  186.4 2.6 copy-start.4
  186.4 2.6 copy-start.5
  201.8 4.2 %copy-start.2 = (bf16[8,256,4,128]{3,2,1,0:T(4,128)(2,1)S(1)}, bf16[8,256,4,128]{3,2,1,0:T(4,128)(2,1)}, u32[]{:S(2)}) copy-start(bf16[8,256,4,128]{3,2,1,0:T(4,128)(2,1)} %reshape.56) | copy-start | bytes 6291460
  206.0 2.8 copy-start
  214.4 95.4 %copy-start.3 = (bf16[512,512]{1,0:T(8,128)(2,1)S(1)}, bf16[512,512]{1,0:T(8,128)(2,1)}, u32[]{:S(2)}) copy-start(bf16[512,512]{1,0:T(8,128)(2,1)} %param.9) | copy-start | bytes 1572868
Sparse Core Ops, SparseCore 0:
  9.1 58.3 all-gather.5
  69.4 93.2 all-gather.3
  214.5 95.2 reduce-scatter.1
where the time goes:
time: 319 us
  waiting for transfers between devices  220 us (69%)
  matrix products  45.5 us (14%)
  blocking collectives  21 us (7%)
  between operations  13.2 us (4%)
  local copies, waits for them, and re-layouts  12.5 us (4%)
  other arithmetic  6.11 us (2%)
    reduce_scatter x1, waiting for transfers between devices, local(): lax.psum_scatter(partial_value, 'tensor', scatter_dimension=1, tiled=True)  95.4 us
    all_gather x1, waiting for transfers between devices, local(): entry_rows = lax.all_gather(encodings, 'retr', axis=0, tiled=True)  87 us
    all_gather x1, waiting for transfers between devices, local(): gathered = lax.all_gather(hidden_in, 'tensor', axis=1, tiled=True)  36.4 us
    dot_general x1, matrix products, local(): jnp.einsum('jn,nre->jre', one_hot, entry_rows, preferred_element_type=jnp...  23.7 us
    all_gather x1, blocking collectives, local(): entry_marks = lax.all_gather(live_marks, 'retr', axis=0, tiled=True)  21 us
  transfers between devices with their start and end apart: 3, of which 3 were waited for; matrix products, arithmetic and copies ran while one was open for 3% of the time, Pallas kernels for 0%

commit v1 on v0

--- a/solution.py
+++ b/solution.py
@@ -8,6 +8,7 @@
 HD = 128
 NBRS = 2
 BLOCK = 32
+CAP = 2
 
 
 def attend_gathered(queries, key_value, selected_marks, segment_count, head_cols):
@@ -38,41 +39,58 @@
 
 
 def local(hidden_in, norm_gain, nbr_table, encodings, enc_mask, w_query, w_key, w_value, w_out):
+    segment_count = nbr_table.shape[0]
+    nb_dev, entry_len, enc_width = encodings.shape
+    mask_cols = enc_mask.shape[1]
+    head_cols = w_key.shape[1]
+    wanted = nbr_table.reshape(-1)
+    need_count = wanted.shape[0]
+
+    info = jnp.concatenate([wanted, enc_mask.reshape(-1)])
+    all_info = lax.all_gather(info, "retr", axis=0, tiled=False)
+    retr_count = all_info.shape[0]
+    all_wanted = all_info[:, :need_count]
+    all_marks = all_info[:, need_count:].reshape(retr_count * nb_dev, mask_cols)
+
     gathered = lax.all_gather(hidden_in, "tensor", axis=1, tiled=True)
+
+    w_both = jnp.concatenate([w_key, w_value], axis=1)
+    own_kv = jnp.dot(
+        encodings.reshape(nb_dev * entry_len, enc_width), w_both, preferred_element_type=jnp.float32
+    ).astype(jnp.bfloat16).reshape(nb_dev, entry_len * 2 * head_cols)
+
+    me = lax.axis_index("retr")
+    mine = (all_wanted // nb_dev) == me
+    rank = jnp.cumsum(mine.astype(jnp.int32), axis=1) - 1
+    slot_ids = jnp.arange(CAP, dtype=jnp.int32)
+    chosen = mine[:, None, :] & (rank[:, None, :] == slot_ids[None, :, None])
+    local_idx = jnp.sum(jnp.where(chosen, all_wanted[:, None, :] % nb_dev, 0), axis=2)
+    pick = (local_idx[:, :, None] == jnp.arange(nb_dev, dtype=jnp.int32)).astype(jnp.bfloat16)
+    send = jnp.einsum(
+        "qjn,nf->qjf", pick, own_kv, preferred_element_type=jnp.float32
+    ).astype(jnp.bfloat16)
+    recv = lax.all_to_all(send, "retr", 0, 0, tiled=True)
+
+    owner = wanted // nb_dev
+    same = owner[:, None] == owner[None, :]
+    earlier = jnp.arange(need_count)[None, :] < jnp.arange(need_count)[:, None]
+    my_rank = jnp.sum((same & earlier).astype(jnp.int32), axis=1)
+    flat_idx = owner * CAP + my_rank
+    key_value = jnp.take(recv.reshape(retr_count * CAP, -1), flat_idx, axis=0)
+    key_value = key_value.reshape(need_count, entry_len, 2 * head_cols)
+    picked_marks = jnp.take(all_marks, wanted, axis=0)
+
     widened = gathered.astype(jnp.float32)
     mean_sq = jnp.mean(widened * widened, axis=-1, keepdims=True)
     normed = (widened * lax.rsqrt(mean_sq + 1e-05) * norm_gain).astype(jnp.bfloat16)
     queries = jnp.dot(normed, w_query, preferred_element_type=jnp.float32).astype(jnp.bfloat16)
-    w_both = jnp.concatenate([w_key, w_value], axis=1)
-    segment_count = nbr_table.shape[0]
-    entry_len = encodings.shape[1]
-    enc_width = encodings.shape[2]
-    head_cols = w_key.shape[1]
-    wanted = nbr_table.reshape(-1)
-    need_count = wanted.shape[0]
-    live_marks = enc_mask.astype(jnp.bfloat16)
-    entry_rows = lax.all_gather(encodings, "retr", axis=0, tiled=True)
-    entry_marks = lax.all_gather(live_marks, "retr", axis=0, tiled=True)
-    piece_count = entry_rows.shape[0]
-    one_hot = (wanted[:, None] == jnp.arange(piece_count, dtype=jnp.int32)[None, :]).astype(
-        jnp.bfloat16
-    )
-    picked = jnp.einsum(
-        "jn,nre->jre", one_hot, entry_rows, preferred_element_type=jnp.float32
-    ).astype(jnp.bfloat16)
-    picked_marks = jnp.dot(one_hot, entry_marks, preferred_element_type=jnp.float32).astype(
-        jnp.bfloat16
-    )
-    key_value = jnp.dot(
-        picked.reshape(need_count * entry_len, enc_width),
-        w_both,
-        preferred_element_type=jnp.float32,
-    )
-    key_value = key_value.astype(jnp.bfloat16).reshape(need_count, entry_len, 2 * head_cols)
+
     attended = attend_gathered(queries, key_value, picked_marks, segment_count, head_cols)
     partial_value = jnp.dot(attended, w_out, preferred_element_type=jnp.float32)
-    summed = lax.psum_scatter(partial_value, "tensor", scatter_dimension=1, tiled=True)
-    return (hidden_in.astype(jnp.float32) + summed).astype(jnp.bfloat16)
+    summed = lax.psum_scatter(
+        partial_value.astype(jnp.bfloat16), "tensor", scatter_dimension=1, tiled=True
+    )
+    return (hidden_in.astype(jnp.float32) + summed.astype(jnp.float32)).astype(jnp.bfloat16)
 
 
 def solution(mesh):

time: 319 us -> 318 us (level)
  local copies, waits for them, and re-layouts: 12.5 us -> 70 us
  waiting for transfers between devices: 220 us -> 182 us
  matrix products: 45.5 us -> 21.7 us
  blocking collectives: 21 us -> 10.8 us
  starting transfers between devices: 0.08 us -> 7.8 us
  other arithmetic: 6.11 us -> 10.5 us
    all_to_all x0 -> x1, waiting for transfers between devices: none -> 108 us  [local(): recv = lax.all_to_all(send, 'retr', 0, 0, tiled=True)]
    all_gather x1 -> x0, waiting for transfers between devices: 87 us -> none  [local(): entry_rows = lax.all_gather(encodings, 'retr', axis=0, tiled=True)]
    reduce_scatter x1, waiting for transfers between devices: 95.4 us -> 60.3 us  [local(): lax.psum_scatter(partial_value.astype(jnp.bfloat16), 'tensor', scatter_di...]
    gather x0 -> x7, local copies, waits for them, and re-layouts: none -> 27.3 us  [the longest x4 26.6 us: local(): key_value = jnp.take(recv.reshape(retr_count * CAP, -1), flat_idx, axis=0)]
    all_gather x1, waiting for transfers between devices: 36.4 us -> 12.6 us  [local(): gathered = lax.all_gather(hidden_in, 'tensor', axis=1, tiled=True)]
    dot_general x3 -> x2, matrix products: 28.9 us -> 5.81 us  [the longest x1 2.97 us: local(): jnp.einsum('qjn,nf->qjf', pick, own_kv, preferred_element_type=jnp.float32)]
    all_gather x1 -> x0, blocking collectives: 21 us -> none  [local(): entry_marks = lax.all_gather(live_marks, 'retr', axis=0, tiled=True)]
    convert_element_type x1 -> x2, local copies, waits for them, and re-layouts: 2.54 us -> 16.9 us  [the longest x1 16.4 us: local(): send = jnp.einsum('qjn,nf->qjf', pick, own_kv, preferred_element_type=jnp...]
  transfers between devices with their start and end apart: 3 -> 3, of which waited for: 3 -> 3; matrix products, arithmetic and copies ran while one was open for 3% -> 11% of each run, Pallas kernels for 0% -> 0%
where the time goes in v1:
time: 318 us; the launch traced here: 317 us
  waiting for transfers between devices  182 us (57%)
  local copies, waits for them, and re-layouts  70 us (22%)
  matrix products  21.7 us (7%)
  between operations  14.2 us (4%)
  blocking collectives  10.8 us (3%)
  other arithmetic  10.5 us (3%)
  starting transfers between devices  7.8 us (2%)
    all_to_all x1, waiting for transfers between devices, local(): recv = lax.all_to_all(send, 'retr', 0, 0, tiled=True)  108 us
    reduce_scatter x1, waiting for transfers between devices, local(): lax.psum_scatter(partial_value.astype(jnp.bfloat16), 'tensor', scatter_di...  60.3 us
    gather x4, local copies, waits for them, and re-layouts, local(): key_value = jnp.take(recv.reshape(retr_count * CAP, -1), flat_idx, axis=0)  26.6 us
    convert_element_type x1, local copies, waits for them, and re-layouts, local(): send = jnp.einsum('qjn,nf->qjf', pick, own_kv, preferred_element_type=jnp...  16.4 us
    all_gather x1, waiting for transfers between devices, local(): gathered = lax.all_gather(hidden_in, 'tensor', axis=1, tiled=True)  12.6 us
    unnamed x1, blocking collectives  10.8 us
    reshape x1, local copies, waits for them, and re-layouts, local(): key_value = jnp.take(recv.reshape(retr_count * CAP, -1), flat_idx, axis=0)  8.44 us
    all_to_all x1, starting transfers between devices, local(): recv = lax.all_to_all(send, 'retr', 0, 0, tiled=True)  7.76 us
  transfers between devices with their start and end apart: 3, of which 3 were waited for; matrix products, arithmetic and copies ran while one was open for 11% of the time, Pallas kernels for 0%

profile of v1, /device:TPU:1, one launch (start us, length us, event | category | flops | bytes accessed | tf_op | source)
XLA Modules:
  0.0 317.1 jit_solution(4664920492474158840)
XLA Ops:
  6.5 0.7 all-gather.3.cloned.1.call-update
  7.3 0.8 copy.37
  8.0 0.1 reshape.243
  8.1 0.8 reshape.244
  8.9 1.3 dynamic-slice
  10.8 0.2 add_dynamic-update-slice_fusion
  11.0 10.8 %all-reduce = s32[512]{0:T(512)S(1)} all-reduce(s32[512]{0:T(512)S(1)} %add_dynamic-update-slice_fusion), channel_id=2, replica_groups=mesh['dp'=2,'retr'=16,'tensor'=8] {'retr'}, use_global_device_ids=true, to_apply=%add | all-reduce | flops 512 | bytes 4096
  21.8 0.1 reshape.278
  21.9 2.8 fusion.20
  24.7 0.2 reduce_window_sum.11
  24.9 0.5 copy.38
  25.4 0.8 reshape.284
  26.2 0.1 fusion.54
  26.3 0.1 select_reduce_fusion
  26.4 3.0 convolution_convert_fusion
  29.4 16.4 %copy.39 = bf16[16,2,131072]{2,1,0:T(2,128)(2,1)} copy(bf16[16,2,131072]{2,0,1:T(8,128)(2,1)S(1)} %convolution_convert_fusion) | data formatting | bytes 16777216 | tf_op jit(solution)/shard_map/convert_element_type | solution.py:71
  45.7 7.8 %all-to-all-start = ((bf16[16,2,131072]{2,1,0:T(2,128)(2,1)}), bf16[16,2,131072]{2,1,0:T(2,128)(2,1)}, u32[]{:S(2)}, u32[]{:S(2)}) async-start(bf16[16,2,131072]{2,1,0:T(2,128)(2,1)} %copy.39), calls=%async_computation | async-start | bytes 16777216 | tf_op jit(solution)/shard_map/all_to_all | solution.py:72
  53.5 0.1 reshape.248
  53.7 0.2 convert_reduce_fusion
  53.9 0.6 gather_fusion
  54.5 0.1 gather.15
  54.6 0.1 copy.42
  54.7 0.1 copy.43
  54.8 0.1 broadcast_in_dim.71
  54.8 0.1 gt.19
  55.0 12.6 %all-gather.3.cloned.1.call-done = bf16[512,4096]{1,0:T(8,128)(2,1)} async-done(((bf16[512,512]{1,0:T(8,128)(2,1)}), bf16[512,4096]{1,0:T(8,128)(2,1)}) %all-gather.3.cloned.1.call-update) | async-done | bytes 4194320 | tf_op jit(solution)/shard_map/all_gather | solution.py:55
  67.5 3.2 %fusion.1 = f32[512]{0:T(512)S(1)} fusion(bf16[512,4096]{1,0:T(8,128)(2,1)} %all-gather.3.cloned.1.call-done), kind=kLoop, calls=%fused_computation.7 | loop fusion | flops 6290944 | bytes 4196352 | tf_op jit(solution)/shard_map/reduce_sum | solution.py:84
  70.8 0.2 copy-done.2
  71.0 4.6 %fusion.26 = bf16[512,512]{1,0:T(8,128)(2,1)S(1)} fusion(bf16[4096,512]{1,0:T(8,128)(2,1)} %param.14, bf16[512,4096]{1,0:T(8,128)(2,1)S(1)} %copy-done.2, f32[4096]{0:T(1024)S(1)} %copy-done.7, f32[512]{0:T(512)S(1)} %add_rsqrt_fusion), kind=kOutput, calls=%fused_computation.31 | convolution fusion | flops 2156134400 | bytes 8931328 | tf_op jit(solution)/shard_map/dot_general | solution.py:86
  75.6 0.1 reshape.251
  75.7 108.4 %all-to-all-done = bf16[16,2,131072]{2,1,0:T(2,128)(2,1)} async-done(((bf16[16,2,131072]{2,1,0:T(2,128)(2,1)}), bf16[16,2,131072]{2,1,0:T(2,128)(2,1)}, u32[]{:S(2)}, u32[]{:S(2)}) %all-to-all-start) | async-done | bytes 8388640 | tf_op jit(solution)/shard_map/all_to_all | solution.py:72
  184.0 8.4 %reshape.247 = bf16[32,131072]{1,0:T(8,128)(2,1)} reshape(bf16[16,2,131072]{2,1,0:T(2,128)(2,1)} %all-to-all-done) | data formatting | bytes 16777216 | tf_op jit(solution)/shard_map/reshape | solution.py:79
  192.5 5.7 %fusion.52 = (bf16[32,65536]{1,0:T(8,128)(2,1)}, bf16[32,65536]{1,0:T(8,128)(2,1)}) fusion(bf16[32,131072]{1,0:T(8,128)(2,1)} %reshape.247), kind=kLoop, calls=%fused_computation.86 | loop fusion | bytes 16777216 | tf_op jit(solution)/shard_map/jit(_take)/gather | solution.py:79
  198.2 6.4 %gather_fusion.1 = bf16[16,65536]{1,0:T(8,128)(2,1)S(1)} fusion(bf16[32,65536]{1,0:T(8,128)(2,1)} %get-tuple-element.8, s32[1024]{0:T(1024)S(1)} %get-tuple-element.19), kind=kCustom, calls=%fused_computation.1 | custom fusion | bytes 4194368 | tf_op jit(solution)/shard_map/jit(_take)/gather | solution.py:79
  204.5 7.7 %gather_fusion.2 = bf16[16,65536]{1,0:T(8,128)(2,1)} fusion(bf16[32,65536]{1,0:T(8,128)(2,1)} %get-tuple-element.9, s32[1024]{0:T(1024)S(1)} %get-tuple-element.19), kind=kCustom, calls=%fused_computation.2 | custom fusion | bytes 4194368 | tf_op jit(solution)/shard_map/jit(_take)/gather | solution.py:79
  212.2 1.9 pad_maximum_fusion
  214.1 4.2 %copy.48 = bf16[2,8,128,1024]{3,2,1,0:T(8,128)(2,1)} copy(bf16[2,8,128,1024]{3,1,2,0:T(8,128)(2,1)S(1)} %bitcast.31) | data formatting | bytes 8388608
  218.3 6.9 %copy.41 = bf16[16,128,1024]{1,0,2:T(8,128)(2,1)} copy(bf16[16,128,1024]{2,1,0:T(8,128)(2,1)} %bitcast.32) | data formatting | bytes 8388608 | tf_op jit(solution)/shard_map/jit(_take)/gather | solution.py:79
  225.2 2.6 broadcast_select_fusion
  227.9 2.0 fusion.53
  229.9 4.1 %reshape.252 = bf16[8,256,4,128]{1,0,3,2:T(8,128)(2,1)} reshape(bf16[16,128,512]{1,0,2:T(8,128)(2,1)} %get-tuple-element.10) | data formatting | bytes 4194304 | tf_op jit(solution)/shard_map/reshape | solution.py:19
  233.9 2.2 reshape.249
  236.1 4.4 %fusion.55 = (f32[8,4,64]{2,1,0:T(4,128)S(1)}, f32[8,4,64,256]{3,2,1,0:T(8,128)}) fusion(f32[8,256]{1,0:T(8,128)S(1)} %convert_element_type.63, pred[8,256]{1,0:T(8,128)(4,1)S(1)} %gt.19, bf16[8,256,4,128]{1,0,3,2:T(8,128)(2,1)} %reshape.252, bf16[8,64,4,128]{3,2,1,0:T(4,128)(2,1)S(1)} %reshape.251), kind=kOutput, calls=%fused_computation.89 | convolution fusion | flops 136839424 | bytes 4737024 | tf_op jit(solution)/shard_map/sub | solution.py:33
  240.5 2.6 fusion.29
  243.2 0.4 copy.47
  243.6 4.3 %convolution_convert_fusion.1 = bf16[512,4096]{1,0:T(8,128)(2,1)} fusion(bf16[512,4096]{1,0:T(8,128)(2,1)S(1)} %copy-done.6, bf16[64,8,4,128]{3,2,1,0:T(4,128)(2,1)S(1)} %bitcast.33), kind=kOutput, calls=%fused_computation.10 | convolution fusion | flops 2149580800 | bytes 8912896 | tf_op jit(solution)/shard_map/dot_general | solution.py:89
  247.9 60.3 %reduce-scatter.2.cloned.1.call-done = bf16[512,512]{1,0:T(8,128)(2,1)} async-done(((bf16[512,4096]{1,0:T(8,128)(2,1)}), bf16[512,512]{1,0:T(8,128)(2,1)}) %reduce-scatter.2.cloned.1.call-update) | async-done | bytes 524304 | tf_op jit(solution)/shard_map/reduce_scatter | solution.py:90
  308.2 2.0 add_convert_fusion
  (30 shorter events, 0.3 us)
Async XLA Ops:
  6.5 15.3 %copy-start = (bf16[4,128,1024]{2,1,0:T(8,128)(2,1)S(1)}, bf16[4,128,1024]{2,1,0:T(8,128)(2,1)}, u32[]{:S(2)}) copy-start(bf16[4,128,1024]{2,1,0:T(8,128)(2,1)} %param.12) | copy-start | bytes 3145732
  6.5 61.0 %all-gather.3.cloned.1.call-start = ((), (), s32[]{:S(2)}) async-start(), calls=%async_computation.2 | async-start | bytes 4718592 | tf_op jit(solution)/shard_map/all_gather | solution.py:55
  45.7 8.9 %copy-start.5 = (s32[8,2]{0,1:T(2,128)S(1)}, s32[8,2]{0,1:T(2,128)}, u32[]{:S(2)}) copy-start(s32[8,2]{0,1:T(2,128)} %param.11) | copy-start | bytes 196
  45.7 138.3 %all-to-all-start = ((bf16[16,2,131072]{2,1,0:T(2,128)(2,1)}), bf16[16,2,131072]{2,1,0:T(2,128)(2,1)}, u32[]{:S(2)}, u32[]{:S(2)}) async-start(bf16[16,2,131072]{2,1,0:T(2,128)(2,1)} %copy.39), calls=%async_computation | async-start | bytes 16777216 | tf_op jit(solution)/shard_map/all_to_all | solution.py:72
  53.5 17.3 %copy-start.7 = (f32[4096]{0:T(1024)S(1)}, f32[4096]{0:T(1024)}, u32[]{:S(2)}) copy-start(f32[4096]{0:T(1024)} %param.10) | copy-start | bytes 49156
  53.5 254.8 %reduce-scatter.2.cloned.1.call-start = ((), (), s32[]{:S(2)}) async-start(), calls=%async_computation.3 | async-start | bytes 4718592 | tf_op jit(solution)/shard_map/reduce_scatter | solution.py:90
  67.5 3.4 %copy-start.2 = (bf16[512,4096]{1,0:T(8,128)(2,1)S(1)}, bf16[512,4096]{1,0:T(8,128)(2,1)}, u32[]{:S(2)}) copy-start(bf16[512,4096]{1,0:T(8,128)(2,1)} %all-gather.3.cloned.1.call-done) | copy-start | bytes 12582916
  236.1 4.4 %copy-start.4 = (bf16[8,256,4,128]{1,0,3,2:T(8,128)(2,1)S(1)}, bf16[8,256,4,128]{1,0,3,2:T(8,128)(2,1)}, u32[]{:S(2)}) copy-start(bf16[8,256,4,128]{1,0,3,2:T(8,128)(2,1)} %reshape.249) | copy-start | bytes 6291460
  240.5 3.1 copy-start.6
  243.6 66.6 %copy-start.1 = (bf16[4,128,1024]{2,1,0:T(8,128)(2,1)S(1)}, bf16[4,128,1024]{2,1,0:T(8,128)(2,1)}, u32[]{:S(2)}) copy-start(bf16[4,128,1024]{2,1,0:T(8,128)(2,1)} %param.12) | copy-start | bytes 3145732
  247.9 60.4 %copy-start.3 = (bf16[512,512]{1,0:T(8,128)(2,1)S(1)}, bf16[512,512]{1,0:T(8,128)(2,1)}, u32[]{:S(2)}) copy-start(bf16[512,512]{1,0:T(8,128)(2,1)} %param.9) | copy-start | bytes 1572868
Sparse Core Ops, SparseCore 0:
  9.1 58.3 all-gather.2
  248.0 60.1 reduce-scatter.1

commit v2 on v1

v2 whole, which is shorter than its diff:
```python
import math

import jax
import jax.numpy as jnp
from jax import lax
from jax.experimental import pallas as pl
from jax.experimental.pallas import tpu as pltpu
from jax.sharding import PartitionSpec as P

HD = 128
NBRS = 2
BLOCK = 32
CAP = 2


def attend_kernel(flat_ref, marks_ref, q_ref, kv0_ref, kv1_ref, o_ref):
    seg = pl.program_id(0)
    head_cols = q_ref.shape[1]
    entry_len = kv0_ref.shape[1]
    mask_cols = marks_ref.shape[0] // flat_ref.shape[0]
    factor = 1.0 / math.sqrt(HD)
    block_of = lax.broadcasted_iota(jnp.int32, (1, entry_len), 1) // BLOCK

    def live_of(entry):
        live = jnp.zeros((1, entry_len), jnp.float32)
        for b in range(mask_cols):
            mark = marks_ref[entry * mask_cols + b].astype(jnp.float32)
            live = jnp.where(block_of == b, mark, live)
        return live

    live0 = live_of(seg * NBRS)
    live1 = live_of(seg * NBRS + 1)
    open0 = live0 > 0
    open1 = live1 > 0
    nt = (((1,), (1,)), ((), ()))
    for h in range(head_cols // HD):
        cols = slice(h * HD, (h + 1) * HD)
        vcols = slice(head_cols + h * HD, head_cols + (h + 1) * HD)
        qh = q_ref[:, cols]
        s0 = lax.dot_general(qh, kv0_ref[0, :, cols], nt, preferred_element_type=jnp.float32) * factor
        s1 = lax.dot_general(qh, kv1_ref[0, :, cols], nt, preferred_element_type=jnp.float32) * factor
        s0 = jnp.where(open0, s0, -1e30)
        s1 = jnp.where(open1, s1, -1e30)
        row_max = jnp.maximum(jnp.max(s0, axis=-1, keepdims=True), jnp.max(s1, axis=-1, keepdims=True))
        w0 = jnp.exp(s0 - row_max) * live0
        w1 = jnp.exp(s1 - row_max) * live1
        total = jnp.sum(w0, axis=-1, keepdims=True) + jnp.sum(w1, axis=-1, keepdims=True)
        p0 = (w0 / total).astype(jnp.bfloat16)
        p1 = (w1 / total).astype(jnp.bfloat16)
        att = jnp.dot(p0, kv0_ref[0, :, vcols], preferred_element_type=jnp.float32)
        att = att + jnp.dot(p1, kv1_ref[0, :, vcols], preferred_element_type=jnp.float32)
        o_ref[:, cols] = att.astype(o_ref.dtype)


def attend(flat_idx, marks, queries, slots):
    tok_rows, head_cols = queries.shape
    segment_count = flat_idx.shape[0] // NBRS
    seg_rows = tok_rows // segment_count
    entry_len, kv_cols = slots.shape[1], slots.shape[2]
    grid_spec = pltpu.PrefetchScalarGridSpec(
        num_scalar_prefetch=2,
        grid=(segment_count,),
        in_specs=[
            pl.BlockSpec((seg_rows, head_cols), lambda s, f, m: (s, 0)),
            pl.BlockSpec((1, entry_len, kv_cols), lambda s, f, m: (f[s * NBRS], 0, 0)),
            pl.BlockSpec((1, entry_len, kv_cols), lambda s, f, m: (f[s * NBRS + 1], 0, 0)),
        ],
        out_specs=pl.BlockSpec((seg_rows, head_cols), lambda s, f, m: (s, 0)),
    )
    return pl.pallas_call(
        attend_kernel,
        out_shape=jax.ShapeDtypeStruct((tok_rows, head_cols), jnp.bfloat16),
        grid_spec=grid_spec,
    )(flat_idx, marks, queries, slots, slots)


def local(hidden_in, norm_gain, nbr_table, encodings, enc_mask, w_query, w_key, w_value, w_out):
    segment_count = nbr_table.shape[0]
    nb_dev, entry_len, enc_width = encodings.shape
    mask_cols = enc_mask.shape[1]
    head_cols = w_key.shape[1]
    wanted = nbr_table.reshape(-1)
    need_count = wanted.shape[0]

    info = jnp.concatenate([wanted, enc_mask.reshape(-1)]).astype(jnp.float32)
    all_info = lax.all_gather(info, "retr", axis=0, tiled=False).astype(jnp.int32)
    retr_count = all_info.shape[0]
    all_wanted = all_info[:, :need_count]
    all_marks = all_info[:, need_count:].reshape(retr_count * nb_dev, mask_cols)

    gathered = lax.all_gather(hidden_in, "tensor", axis=1, tiled=True)

    w_both = jnp.concatenate([w_key, w_value], axis=1)
    own_kv = jnp.dot(
        encodings.reshape(nb_dev * entry_len, enc_width), w_both, preferred_element_type=jnp.float32
    ).astype(jnp.bfloat16).reshape(nb_dev, entry_len, 2 * head_cols)

    me = lax.axis_index("retr")
    mine = (all_wanted // nb_dev) == me
    rank = jnp.cumsum(mine.astype(jnp.int32), axis=1) - 1
    slot_ids = jnp.arange(CAP, dtype=jnp.int32)
    chosen = mine[:, None, :] & (rank[:, None, :] == slot_ids[None, :, None])
    local_idx = jnp.sum(jnp.where(chosen, all_wanted[:, None, :] % nb_dev, 0), axis=2)
    send = jnp.take(own_kv, local_idx.reshape(-1), axis=0)
    send = send.reshape(retr_count, CAP * entry_len, 2 * head_cols)
    recv = lax.all_to_all(send, "retr", 0, 0, tiled=True)
    slots = recv.reshape(retr_count * CAP, entry_len, 2 * head_cols)

    owner = wanted // nb_dev
    same = owner[:, None] == owner[None, :]
    earlier = jnp.arange(need_count)[None, :] < jnp.arange(need_count)[:, None]
    my_rank = jnp.sum((same & earlier).astype(jnp.int32), axis=1)
    flat_idx = owner * CAP + my_rank
    picked_marks = jnp.take(all_marks, wanted, axis=0).reshape(-1)

    widened = gathered.astype(jnp.float32)
    mean_sq = jnp.mean(widened * widened, axis=-1, keepdims=True)
    normed = (widened * lax.rsqrt(mean_sq + 1e-05) * norm_gain).astype(jnp.bfloat16)
    queries = jnp.dot(normed, w_query, preferred_element_type=jnp.float32).astype(jnp.bfloat16)

    attended = attend(flat_idx, picked_marks, queries, slots)
    partial_value = jnp.dot(attended, w_out, preferred_element_type=jnp.float32)
    summed = lax.psum_scatter(
        partial_value.astype(jnp.bfloat16), "tensor", scatter_dimension=1, tiled=True
    )
    return (hidden_in.astype(jnp.float32) + summed.astype(jnp.float32)).astype(jnp.bfloat16)


def solution(mesh):
    in_specs = (
        P(("dp", "retr"), "tensor"),
        P(),
        P(("dp", "retr"), None),
        P("retr", None, None),
        P("retr", None),
        P(None, "tensor"),
        P(None, "tensor"),
        P(None, "tensor"),
        P("tensor", None),
    )
    out_specs = P(("dp", "retr"), "tensor")
    return jax.shard_map(local, mesh=mesh, in_specs=in_specs, out_specs=out_specs, check_vma=False)
```

time: 318 us -> 272 us (0.86)
  local copies, waits for them, and re-layouts: 70 us -> 8.54 us
  Pallas kernels: 0 us -> 14.5 us
  blocking collectives: 10.8 us -> 21 us
  matrix products: 21.7 us -> 14.8 us
  other arithmetic: 10.5 us -> 13.9 us
    gather x7 -> x2, local copies, waits for them, and re-layouts: 27.3 us -> 5.53 us  [the longest x1 4.96 us: local(): send = jnp.take(own_kv, local_idx.reshape(-1), axis=0)]
    all_gather x0 -> x1, blocking collectives: none -> 21 us  [local(): lax.all_gather(info, 'retr', axis=0, tiled=False).astype(jnp.int32)]
    convert_element_type x3 -> x0, local copies, waits for them, and re-layouts: 17.3 us -> none  [the longest x1 16.4 us: local(): send = jnp.einsum('qjn,nf->qjf', pick, own_kv, preferred_element_type=jnp...]
    reshape x6 -> x1, local copies, waits for them, and re-layouts: 16.3 us -> 0.09 us  [local(): send = jnp.take(own_kv, local_idx.reshape(-1), axis=0)]
    pallas_call x0 -> x1, Pallas kernels: none -> 14.5 us  [attend(): pl.pallas_call(attend_kernel, out_shape=jax.ShapeDtypeStruct((tok_rows, h...]
    unnamed x1 -> x0, blocking collectives: 10.8 us -> none
    dot_general x2 -> x0, matrix products: 5.6 us -> none  [the longest x1 2.97 us: local(): jnp.einsum('qjn,nf->qjf', pick, own_kv, preferred_element_type=jnp.float32)]
    unnamed x20 -> x10, local copies, waits for them, and re-layouts: 6.5 us -> 0.98 us
  transfers between devices with their start and end apart: 3 -> 3, of which waited for: 3 -> 3; matrix products, arithmetic and copies ran while one was open for 11% -> 10% of each run, Pallas kernels for 0% -> 0%
where the time goes in v2:
time: 272 us
  waiting for transfers between devices  181 us (67%)
  blocking collectives  21 us (8%)
  matrix products  14.8 us (5%)
  Pallas kernels  14.5 us (5%)
  other arithmetic  13.9 us (5%)
  between operations  13.5 us (5%)
  local copies, waits for them, and re-layouts  8.54 us (3%)
  starting transfers between devices  4.71 us (2%)
    all_to_all x1, waiting for transfers between devices, local(): recv = lax.all_to_all(send, 'retr', 0, 0, tiled=True)  105 us
    reduce_scatter x1, waiting for transfers between devices, local(): lax.psum_scatter(partial_value.astype(jnp.bfloat16), 'tensor', scatter_di...  60.4 us
    all_gather x1, blocking collectives, local(): lax.all_gather(info, 'retr', axis=0, tiled=False).astype(jnp.int32)  21 us
    all_gather x1, waiting for transfers between devices, local(): gathered = lax.all_gather(hidden_in, 'tensor', axis=1, tiled=True)  14.6 us
    pallas_call x1, Pallas kernels, attend(): pl.pallas_call(attend_kernel, out_shape=jax.ShapeDtypeStruct((tok_rows, h...  14.5 us
    select_n x2, other arithmetic, local(): send = jnp.take(own_kv, local_idx.reshape(-1), axis=0)  7.37 us
    dot_general x1, matrix products, local(): partial_value = jnp.dot(attended, w_out, preferred_element_type=jnp.float32)  6.63 us
  transfers between devices with their start and end apart: 3, of which 3 were waited for; matrix products, arithmetic and copies ran while one was open for 10% of the time, Pallas kernels for 0%

profile of v2, /device:TPU:1, one launch (start us, length us, event | category | flops | bytes accessed | tf_op | source)
XLA Modules:
  0.0 271.5 jit_solution(9412325272633968669)
XLA Ops:
  6.5 0.0 copy-start
  6.5 0.0 all-gather.3.cloned.1.call-start
  6.5 0.7 all-gather.3.cloned.1.call-update
  7.3 0.8 copy.22
  8.0 0.1 concatenate.17
  8.1 0.8 concatenate.18
  8.9 0.1 fusion.24
  8.9 21.0 %all-gather = f32[16,1,32]{2,1,0:T(1,128)S(1)} all-gather(f32[1,1,32]{2,1,0:T(1,128)S(1)} %fusion.24), channel_id=1, replica_groups=mesh['dp'=2,'retr'=16,'tensor'=8] {'retr'}, dimensions={0}, use_global_device_ids=true | all-gather | bytes 2176 | tf_op jit(solution)/shard_map/all_gather | solution.py:86
  30.0 0.2 reduce_window_sum.11
  30.1 0.1 add_select_fusion
  30.2 0.1 select_reduce_fusion
  30.3 0.1 copy.27
  30.4 0.1 reshape.213
  30.5 0.1 copy.26
  30.6 0.1 broadcast_in_dim.50
  30.7 0.0 copy-done
  30.8 2.8 %fusion.11 = bf16[1024,512]{0,1:T(8,128)(2,1)S(1)} fusion(bf16[512,1024]{1,0:T(8,128)(2,1)S(1)} %bitcast.25, bf16[1024,512]{1,0:T(8,128)(2,1)} %param.16, bf16[1024,512]{1,0:T(8,128)(2,1)} %param.15), kind=kOutput, calls=%fused_computation.16 | convolution fusion | flops 1078460416 | bytes 4194304 | tf_op jit(solution)/shard_map/dot_general | solution.py:94
  33.6 5.0 %gather_fusion.1 = bf16[32,128,1024]{2,1,0:T(8,128)(2,1)} fusion(bf16[4,128,1024]{2,1,0:T(8,128)(2,1)S(1)} %bitcast.26, s32[1024]{0:T(1024)S(1)} %pad_clamp_fusion), kind=kCustom, calls=%fused_computation.1 | custom fusion | bytes 16777344 | tf_op jit(solution)/shard_map/jit(_take)/gather | solution.py:104
  38.5 7.4 %bitcast_select_fusion = bf16[16,256,1024]{2,1,0:T(8,128)(2,1)} fusion(pred[16,256]{1,0:T(8,128)(4,1)S(1)} %bitcast.30, bf16[16,256,1024]{2,1,0:T(8,128)(2,1)} %bitcast.27), kind=kLoop, calls=%fused_computation.7 | loop fusion | flops 4194304 | bytes 16781312 | tf_op jit(solution)/shard_map/jit(_take)/select_n | solution.py:104
  45.9 4.7 %all-to-all-start = ((bf16[16,256,1024]{2,1,0:T(8,128)(2,1)}), bf16[16,256,1024]{2,1,0:T(8,128)(2,1)}, u32[]{:S(2)}, u32[]{:S(2)}) async-start(bf16[16,256,1024]{2,1,0:T(8,128)(2,1)} %bitcast_select_fusion), calls=%async_computation | async-start | bytes 16777216 | tf_op jit(solution)/shard_map/all_to_all | solution.py:106
  50.6 0.0 copy-start.3
  50.6 0.0 reduce-scatter.2.cloned.1.call-start
  50.6 0.1 reshape.210
  50.7 0.1 reshape.208
  50.8 0.1 reshape.209
  50.9 0.6 gather_fusion
  51.5 0.1 broadcast_select_fusion
  51.6 0.6 select_n.79.marks_ref
  52.2 0.2 convert_reduce_fusion
  52.4 0.6 multiply_add_fusion.flat_ref
  52.9 14.6 %all-gather.3.cloned.1.call-done = bf16[512,4096]{1,0:T(8,128)(2,1)} async-done(((bf16[512,512]{1,0:T(8,128)(2,1)}), bf16[512,4096]{1,0:T(8,128)(2,1)}) %all-gather.3.cloned.1.call-update) | async-done | bytes 4194320 | tf_op jit(solution)/shard_map/all_gather | solution.py:91
  67.5 0.0 copy-start.1
  67.5 3.2 %fusion = f32[512]{0:T(512)S(1)} fusion(bf16[512,4096]{1,0:T(8,128)(2,1)} %all-gather.3.cloned.1.call-done), kind=kLoop, calls=%fused_computation.4 | loop fusion | flops 6290944 | bytes 4196352 | tf_op jit(solution)/shard_map/reduce_sum | solution.py:117
  70.8 0.0 copy-done.3
  70.8 0.2 copy-done.1
  71.0 5.4 %fusion.14.q_ref = bf16[512,512]{1,0:T(8,128)(2,1)} fusion(bf16[4096,512]{1,0:T(8,128)(2,1)} %param.14, bf16[512,4096]{1,0:T(8,128)(2,1)S(1)} %copy-done.1, f32[4096]{0:T(1024)S(1)} %copy-done.3, f32[512]{0:T(512)S(1)} %add_rsqrt_fusion), kind=kOutput, calls=%fused_computation.17 | convolution fusion | flops 2156134400 | bytes 8931328 | tf_op jit(solution)/shard_map/dot_general | solution.py:119
  76.3 104.8 %all-to-all-done = bf16[16,256,1024]{2,1,0:T(8,128)(2,1)} async-done(((bf16[16,256,1024]{2,1,0:T(8,128)(2,1)}), bf16[16,256,1024]{2,1,0:T(8,128)(2,1)}, u32[]{:S(2)}, u32[]{:S(2)}) %all-to-all-start) | async-done | bytes 8388640 | tf_op jit(solution)/shard_map/all_to_all | solution.py:106
  181.1 14.5 %shard_map.91 = bf16[512,512]{1,0:T(8,128)(2,1)} custom-call(s32[16]{0:T(128)} %multiply_add_fusion.flat_ref, s32[64]{0:T(128)} %select_n.79.marks_ref, bf16[512,512]{1,0:T(8,128)(2,1)} %fusion.14.q_ref, bf16[32,128,1024]{2,1,0:T(8,128)(2,1)} %bitcast.9.kv0_ref.kv1_ref, bf16[32,128,1024]{2,1,0:T(8,128)(2,1)} %bitcast.9.kv0_ref.kv1_ref), custom_call_target="tpu_custom_call" | custom-call | tf_op jit(solution)/shard_map/pallas_call | solution.py:70
  195.6 6.6 %convolution_convert_fusion = bf16[512,4096]{1,0:T(8,128)(2,1)} fusion(bf16[512,512]{1,0:T(8,128)(2,1)} %shard_map.91, bf16[512,4096]{1,0:T(8,128)(2,1)} %param.17), kind=kOutput, calls=%fused_computation.8 | convolution fusion | flops 2149580800 | bytes 8912896 | tf_op jit(solution)/shard_map/dot_general | solution.py:122
  202.2 0.0 copy-start.2
  202.2 0.0 reduce-scatter.2.cloned.1.call-update
  202.3 60.4 %reduce-scatter.2.cloned.1.call-done = bf16[512,512]{1,0:T(8,128)(2,1)} async-done(((bf16[512,4096]{1,0:T(8,128)(2,1)}), bf16[512,512]{1,0:T(8,128)(2,1)}) %reduce-scatter.2.cloned.1.call-update) | async-done | bytes 524304 | tf_op jit(solution)/shard_map/reduce_scatter | solution.py:123
  262.7 0.0 copy-done.2
  262.7 2.0 add_convert_fusion
  (11 shorter events, 0.1 us)
Async XLA Ops:
  6.5 24.2 %copy-start = (bf16[4,128,1024]{2,1,0:T(8,128)(2,1)S(1)}, bf16[4,128,1024]{2,1,0:T(8,128)(2,1)}, u32[]{:S(2)}) copy-start(bf16[4,128,1024]{2,1,0:T(8,128)(2,1)} %param.12) | copy-start | bytes 3145732
  6.5 61.0 %all-gather.3.cloned.1.call-start = ((), (), s32[]{:S(2)}) async-start(), calls=%async_computation.2 | async-start | bytes 4718592 | tf_op jit(solution)/shard_map/all_gather | solution.py:91
  45.9 135.2 %all-to-all-start = ((bf16[16,256,1024]{2,1,0:T(8,128)(2,1)}), bf16[16,256,1024]{2,1,0:T(8,128)(2,1)}, u32[]{:S(2)}, u32[]{:S(2)}) async-start(bf16[16,256,1024]{2,1,0:T(8,128)(2,1)} %bitcast_select_fusion), calls=%async_computation | async-start | bytes 16777216 | tf_op jit(solution)/shard_map/all_to_all | solution.py:106
  50.6 20.2 %copy-start.3 = (f32[4096]{0:T(1024)S(1)}, f32[4096]{0:T(1024)}, u32[]{:S(2)}) copy-start(f32[4096]{0:T(1024)} %param.10) | copy-start | bytes 49156
  50.6 212.1 %reduce-scatter.2.cloned.1.call-start = ((), (), s32[]{:S(2)}) async-start(), calls=%async_computation.3 | async-start | bytes 4718592 | tf_op jit(solution)/shard_map/reduce_scatter | solution.py:123
  67.5 3.4 %copy-start.1 = (bf16[512,4096]{1,0:T(8,128)(2,1)S(1)}, bf16[512,4096]{1,0:T(8,128)(2,1)}, u32[]{:S(2)}) copy-start(bf16[512,4096]{1,0:T(8,128)(2,1)} %all-gather.3.cloned.1.call-done) | copy-start | bytes 12582916
  202.2 60.5 %copy-start.2 = (bf16[512,512]{1,0:T(8,128)(2,1)S(1)}, bf16[512,512]{1,0:T(8,128)(2,1)}, u32[]{:S(2)}) copy-start(bf16[512,512]{1,0:T(8,128)(2,1)} %param.9) | copy-start | bytes 1572868
Sparse Core Ops, SparseCore 0:
  9.1 58.3 all-gather.2
  202.4 60.2 reduce-scatter.1

commit v3 on v2

v3 whole, which is shorter than its diff:
```python
import functools
import math

import jax
import jax.numpy as jnp
from jax import lax
from jax.experimental import pallas as pl
from jax.experimental.pallas import tpu as pltpu
from jax.sharding import PartitionSpec as P

HD = 128
NBRS = 2
BLOCK = 32
CAP = 2


def attend_kernel(flat_ref, q_ref, kv0_ref, kv1_ref, o_ref, *, entry_len):
    head_cols = q_ref.shape[1]
    factor = 1.0 / math.sqrt(HD)
    live0 = kv0_ref[0, entry_len:entry_len + 1, :entry_len].astype(jnp.float32)
    live1 = kv1_ref[0, entry_len:entry_len + 1, :entry_len].astype(jnp.float32)
    open0 = live0 > 0
    open1 = live1 > 0
    nt = (((1,), (1,)), ((), ()))
    for h in range(head_cols // HD):
        cols = slice(h * HD, (h + 1) * HD)
        vcols = slice(head_cols + h * HD, head_cols + (h + 1) * HD)
        qh = q_ref[:, cols]
        s0 = lax.dot_general(qh, kv0_ref[0, :entry_len, cols], nt, preferred_element_type=jnp.float32) * factor
        s1 = lax.dot_general(qh, kv1_ref[0, :entry_len, cols], nt, preferred_element_type=jnp.float32) * factor
        s0 = jnp.where(open0, s0, -1e30)
        s1 = jnp.where(open1, s1, -1e30)
        row_max = jnp.maximum(jnp.max(s0, axis=-1, keepdims=True), jnp.max(s1, axis=-1, keepdims=True))
        w0 = jnp.exp(s0 - row_max) * live0
        w1 = jnp.exp(s1 - row_max) * live1
        total = jnp.sum(w0, axis=-1, keepdims=True) + jnp.sum(w1, axis=-1, keepdims=True)
        p0 = (w0 / total).astype(jnp.bfloat16)
        p1 = (w1 / total).astype(jnp.bfloat16)
        att = jnp.dot(p0, kv0_ref[0, :entry_len, vcols], preferred_element_type=jnp.float32)
        att = att + jnp.dot(p1, kv1_ref[0, :entry_len, vcols], preferred_element_type=jnp.float32)
        o_ref[:, cols] = att.astype(o_ref.dtype)


def attend(flat_idx, queries, slots, entry_len):
    tok_rows, head_cols = queries.shape
    segment_count = flat_idx.shape[0] // NBRS
    seg_rows = tok_rows // segment_count
    slot_rows, kv_cols = slots.shape[1], slots.shape[2]
    grid_spec = pltpu.PrefetchScalarGridSpec(
        num_scalar_prefetch=1,
        grid=(segment_count,),
        in_specs=[
            pl.BlockSpec((seg_rows, head_cols), lambda s, f: (s, 0)),
            pl.BlockSpec((1, slot_rows, kv_cols), lambda s, f: (f[s * NBRS], 0, 0)),
            pl.BlockSpec((1, slot_rows, kv_cols), lambda s, f: (f[s * NBRS + 1], 0, 0)),
        ],
        out_specs=pl.BlockSpec((seg_rows, head_cols), lambda s, f: (s, 0)),
    )
    return pl.pallas_call(
        functools.partial(attend_kernel, entry_len=entry_len),
        out_shape=jax.ShapeDtypeStruct((tok_rows, head_cols), jnp.bfloat16),
        grid_spec=grid_spec,
    )(flat_idx, queries, slots, slots)


def local(hidden_in, norm_gain, nbr_table, encodings, enc_mask, w_query, w_key, w_value, w_out):
    segment_count = nbr_table.shape[0]
    nb_dev, entry_len, enc_width = encodings.shape
    mask_cols = enc_mask.shape[1]
    head_cols = w_key.shape[1]
    wanted = nbr_table.reshape(-1)
    need_count = wanted.shape[0]

    gathered = lax.all_gather(hidden_in, "tensor", axis=1, tiled=True)

    w_both = jnp.concatenate([w_key, w_value], axis=1)
    own_kv = jnp.dot(
        encodings.reshape(nb_dev * entry_len, enc_width), w_both, preferred_element_type=jnp.float32
    ).astype(jnp.bfloat16).reshape(nb_dev, entry_len, 2 * head_cols)
    key_live = jnp.repeat(enc_mask, BLOCK, axis=1).astype(jnp.bfloat16)
    mask_rows = jnp.zeros((nb_dev, 8, 2 * head_cols), jnp.bfloat16)
    mask_rows = mask_rows.at[:, 0, :entry_len].set(key_live)
    own = jnp.concatenate([own_kv, mask_rows], axis=1)
    slots = lax.all_gather(own, "retr", axis=0, tiled=True)

    widened = gathered.astype(jnp.float32)
    mean_sq = jnp.mean(widened * widened, axis=-1, keepdims=True)
    normed = (widened * lax.rsqrt(mean_sq + 1e-05) * norm_gain).astype(jnp.bfloat16)
    queries = jnp.dot(normed, w_query, preferred_element_type=jnp.float32).astype(jnp.bfloat16)

    attended = attend(wanted, queries, slots, entry_len)
    partial_value = jnp.dot(attended, w_out, preferred_element_type=jnp.float32)
    summed = lax.psum_scatter(
        partial_value.astype(jnp.bfloat16), "tensor", scatter_dimension=1, tiled=True
    )
    return (hidden_in.astype(jnp.float32) + summed.astype(jnp.float32)).astype(jnp.bfloat16)


def solution(mesh):
    in_specs = (
        P(("dp", "retr"), "tensor"),
        P(),
        P(("dp", "retr"), None),
        P("retr", None, None),
        P("retr", None),
        P(None, "tensor"),
        P(None, "tensor"),
        P(None, "tensor"),
        P("tensor", None),
    )
    out_specs = P(("dp", "retr"), "tensor")
    return jax.shard_map(local, mesh=mesh, in_specs=in_specs, out_specs=out_specs, check_vma=False)
```

time: 272 us -> 253 us (0.930)
  blocking collectives: 21 us -> 0 us
  waiting for transfers between devices: 181 us -> 202 us
  local copies, waits for them, and re-layouts: 8.54 us -> 1.08 us
  other arithmetic: 13.9 us -> 6.99 us
  starting transfers between devices: 4.71 us -> 0.08 us
    all_to_all x1 -> x0, waiting for transfers between devices: 105 us -> none  [local(): recv = lax.all_to_all(send, 'retr', 0, 0, tiled=True)]
    all_gather x0 -> x1, waiting for transfers between devices: none -> 91.3 us  [local(): slots = lax.all_gather(own, 'retr', axis=0, tiled=True)]
    all_gather x1, waiting for transfers between devices: 14.6 us -> 54.7 us  [local(): gathered = lax.all_gather(hidden_in, 'tensor', axis=1, tiled=True)]
    all_gather x1 -> x0, blocking collectives: 21 us -> none  [local(): lax.all_gather(info, 'retr', axis=0, tiled=False).astype(jnp.int32)]
    select_n x6 -> x0, other arithmetic: 7.53 us -> none  [the longest x2 7.37 us: local(): send = jnp.take(own_kv, local_idx.reshape(-1), axis=0)]
    gather x2 -> x0, local copies, waits for them, and re-layouts: 5.53 us -> none  [the longest x1 4.96 us: local(): send = jnp.take(own_kv, local_idx.reshape(-1), axis=0)]
    all_to_all x1 -> x0, starting transfers between devices: 4.67 us -> none  [local(): recv = lax.all_to_all(send, 'retr', 0, 0, tiled=True)]
    reduce_scatter x1, waiting for transfers between devices: 60.4 us -> 55.8 us  [local(): lax.psum_scatter(partial_value.astype(jnp.bfloat16), 'tensor', scatter_di...]
  transfers between devices with their start and end apart: 3 -> 3, of which waited for: 3 -> 3; matrix products, arithmetic and copies ran while one was open for 10% -> 6% of each run, Pallas kernels for 0% -> 0%
where the time goes in v3:
time: 253 us
  waiting for transfers between devices  202 us (80%)
  matrix products  14.8 us (6%)
  Pallas kernels  14.5 us (6%)
  between operations  13.1 us (5%)
  other arithmetic  6.99 us (3%)
    all_gather x1, waiting for transfers between devices, local(): slots = lax.all_gather(own, 'retr', axis=0, tiled=True)  91.3 us
    reduce_scatter x1, waiting for transfers between devices, local(): lax.psum_scatter(partial_value.astype(jnp.bfloat16), 'tensor', scatter_di...  55.8 us
    all_gather x1, waiting for transfers between devices, local(): gathered = lax.all_gather(hidden_in, 'tensor', axis=1, tiled=True)  54.7 us
    pallas_call x1, Pallas kernels, attend(): pl.pallas_call(functools.partial(attend_kernel, entry_len=entry_len), out...  14.5 us
    dot_general x1, matrix products, local(): partial_value = jnp.dot(attended, w_out, preferred_element_type=jnp.float32)  6.64 us
    dot_general x1, matrix products, local(): jnp.dot(normed, w_query, preferred_element_type=jnp.float32)  5.37 us
  transfers between devices with their start and end apart: 3, of which 3 were waited for; matrix products, arithmetic and copies ran while one was open for 6% of the time, Pallas kernels for 0%

profile of v3, /device:TPU:1, one launch (start us, length us, event | category | flops | bytes accessed | tf_op | source)
XLA Modules:
  0.0 253.1 jit_solution(7929435940787369756)
XLA Ops:
  6.5 0.0 copy-start
  6.5 0.0 all-gather.3.cloned.1.call-start
  6.5 0.7 all-gather.3.cloned.1.call-update
  7.3 0.0 all-gather.5.cloned.1.call-start
  7.3 0.7 convert_element_type.45
  8.0 0.1 broadcast_in_dim.2
  8.1 0.1 convert_element_type.50
  8.2 0.0 copy-done
  8.2 0.0 copy-start.3
  8.2 2.8 %fusion.12 = bf16[1024,512]{0,1:T(8,128)(2,1)S(1)} fusion(bf16[512,1024]{1,0:T(8,128)(2,1)S(1)} %bitcast.8, bf16[1024,512]{1,0:T(8,128)(2,1)} %param.18, bf16[1024,512]{1,0:T(8,128)(2,1)} %param.17), kind=kOutput, calls=%fused_computation.15 | convolution fusion | flops 1078460416 | bytes 4194304 | tf_op jit(solution)/shard_map/dot_general | solution.py:77
  11.0 0.0 copy-start.4
  11.0 1.1 fusion.18
  12.1 0.0 all-gather.5.cloned.1.call-update
  12.1 0.0 reduce-scatter.2.cloned.1.call-start
  12.1 0.0 copy-done.3
  12.2 0.1 copy.13
  12.2 0.6 reshape.63.flat_ref
  12.9 54.7 %all-gather.3.cloned.1.call-done = bf16[512,4096]{1,0:T(8,128)(2,1)} async-done(((bf16[512,512]{1,0:T(8,128)(2,1)}), bf16[512,4096]{1,0:T(8,128)(2,1)}) %all-gather.3.cloned.1.call-update) | async-done | bytes 4194320 | tf_op jit(solution)/shard_map/all_gather | solution.py:74
  67.5 0.0 copy-start.1
  67.5 3.2 %fusion = f32[512]{0:T(512)S(1)} fusion(bf16[512,4096]{1,0:T(8,128)(2,1)} %all-gather.3.cloned.1.call-done), kind=kLoop, calls=%fused_computation.2 | loop fusion | flops 6290944 | bytes 4196352 | tf_op jit(solution)/shard_map/reduce_sum | solution.py:87
  70.8 0.0 copy-done.4
  70.8 0.2 copy-done.1
  71.0 5.4 %fusion.15.q_ref = bf16[512,512]{1,0:T(8,128)(2,1)} fusion(bf16[4096,512]{1,0:T(8,128)(2,1)} %param.16, bf16[512,4096]{1,0:T(8,128)(2,1)S(1)} %copy-done.1, f32[4096]{0:T(1024)S(1)} %copy-done.4, f32[512]{0:T(512)S(1)} %add_rsqrt_fusion), kind=kOutput, calls=%fused_computation.16 | convolution fusion | flops 2156134400 | bytes 8931328 | tf_op jit(solution)/shard_map/dot_general | solution.py:89
  76.4 91.3 %all-gather.5.cloned.1.call-done.kv0_ref.kv1_ref = bf16[64,136,1024]{2,1,0:T(8,128)(2,1)} async-done(((bf16[4,136,1024]{2,1,0:T(8,128)(2,1)}), bf16[64,136,1024]{2,1,0:T(8,128)(2,1)}) %all-gather.5.cloned.1.call-update) | async-done | bytes 17825808 | tf_op jit(solution)/shard_map/all_gather | solution.py:84
  167.6 14.5 %shard_map.91 = bf16[512,512]{1,0:T(8,128)(2,1)} custom-call(s32[16]{0:T(128)} %reshape.63.flat_ref, bf16[512,512]{1,0:T(8,128)(2,1)} %fusion.15.q_ref, bf16[64,136,1024]{2,1,0:T(8,128)(2,1)} %all-gather.5.cloned.1.call-done.kv0_ref.kv1_ref, bf16[64,136,1024]{2,1,0:T(8,128)(2,1)} %all-gather.5.cloned.1.call-done.kv0_ref.kv1_ref), custom_call_target="tpu_custom_call" | custom-call | tf_op jit(solution)/shard_map/pallas_call | solution.py:59
  182.1 6.6 %convolution_convert_fusion = bf16[512,4096]{1,0:T(8,128)(2,1)} fusion(bf16[512,512]{1,0:T(8,128)(2,1)} %shard_map.91, bf16[512,4096]{1,0:T(8,128)(2,1)} %param.19), kind=kOutput, calls=%fused_computation.5 | convolution fusion | flops 2149580800 | bytes 8912896 | tf_op jit(solution)/shard_map/dot_general | solution.py:92
  188.8 0.0 copy-start.2
  188.8 0.0 reduce-scatter.2.cloned.1.call-update
  188.8 55.8 %reduce-scatter.2.cloned.1.call-done = bf16[512,512]{1,0:T(8,128)(2,1)} async-done(((bf16[512,4096]{1,0:T(8,128)(2,1)}), bf16[512,512]{1,0:T(8,128)(2,1)}) %reduce-scatter.2.cloned.1.call-update) | async-done | bytes 524304 | tf_op jit(solution)/shard_map/reduce_scatter | solution.py:93
  244.6 0.0 copy-done.2
  244.6 2.0 add_convert_fusion
  (1 shorter events, 0.0 us)
Async XLA Ops:
  6.5 1.6 copy-start
  6.5 61.0 %all-gather.3.cloned.1.call-start = ((), (), s32[]{:S(2)}) async-start(), calls=%async_computation.1 | async-start | bytes 4718592 | tf_op jit(solution)/shard_map/all_gather | solution.py:74
  7.3 160.4 %all-gather.5.cloned.1.call-start = ((), (), s32[]{:S(2)}) async-start(), calls=%async_computation.2 | async-start | bytes 18939904 | tf_op jit(solution)/shard_map/all_gather | solution.py:84
  8.2 4.0 %copy-start.3 = (s32[8,2]{0,1:T(2,128)S(1)}, s32[8,2]{0,1:T(2,128)}, u32[]{:S(2)}) copy-start(s32[8,2]{0,1:T(2,128)} %param.13) | copy-start | bytes 196
  11.0 59.8 %copy-start.4 = (f32[4096]{0:T(1024)S(1)}, f32[4096]{0:T(1024)}, u32[]{:S(2)}) copy-start(f32[4096]{0:T(1024)} %param.12) | copy-start | bytes 49156
  12.1 232.5 %reduce-scatter.2.cloned.1.call-start = ((), (), s32[]{:S(2)}) async-start(), calls=%async_computation.3 | async-start | bytes 4718592 | tf_op jit(solution)/shard_map/reduce_scatter | solution.py:93
  67.5 3.4 %copy-start.1 = (bf16[512,4096]{1,0:T(8,128)(2,1)S(1)}, bf16[512,4096]{1,0:T(8,128)(2,1)}, u32[]{:S(2)}) copy-start(bf16[512,4096]{1,0:T(8,128)(2,1)} %all-gather.3.cloned.1.call-done) | copy-start | bytes 12582916
  188.8 55.8 %copy-start.2 = (bf16[512,512]{1,0:T(8,128)(2,1)S(1)}, bf16[512,512]{1,0:T(8,128)(2,1)}, u32[]{:S(2)}) copy-start(bf16[512,512]{1,0:T(8,128)(2,1)} %param.11) | copy-start | bytes 1572868
Sparse Core Ops, SparseCore 0:
  9.1 58.3 all-gather.2
  69.4 98.1 all-gather.4
  188.9 55.6 reduce-scatter.1

commit v4 on v3

--- a/solution.py
+++ b/solution.py
@@ -71,7 +71,13 @@
     wanted = nbr_table.reshape(-1)
     need_count = wanted.shape[0]
 
-    gathered = lax.all_gather(hidden_in, "tensor", axis=1, tiled=True)
+    tensor_count = w_out.shape[1] // hidden_in.shape[1]
+    feat = hidden_in.shape[1]
+    t = lax.axis_index("tensor")
+    pieces = [hidden_in]
+    for k in range(1, tensor_count):
+        perm = [(i, (i + k) % tensor_count) for i in range(tensor_count)]
+        pieces.append(lax.ppermute(hidden_in, "tensor", perm))
 
     w_both = jnp.concatenate([w_key, w_value], axis=1)
     own_kv = jnp.dot(
@@ -83,10 +89,18 @@
     own = jnp.concatenate([own_kv, mask_rows], axis=1)
     slots = lax.all_gather(own, "retr", axis=0, tiled=True)
 
-    widened = gathered.astype(jnp.float32)
-    mean_sq = jnp.mean(widened * widened, axis=-1, keepdims=True)
-    normed = (widened * lax.rsqrt(mean_sq + 1e-05) * norm_gain).astype(jnp.bfloat16)
-    queries = jnp.dot(normed, w_query, preferred_element_type=jnp.float32).astype(jnp.bfloat16)
+    widened = [p.astype(jnp.float32) for p in pieces]
+    sum_sq = sum(jnp.sum(w * w, axis=-1, keepdims=True) for w in widened)
+    inv = lax.rsqrt(sum_sq / (feat * tensor_count) + 1e-05)
+    acc = None
+    for k, w in enumerate(widened):
+        src_block = (t - k) % tensor_count
+        gain = lax.dynamic_slice_in_dim(norm_gain, src_block * feat, feat)
+        normed = (w * inv * gain).astype(jnp.bfloat16)
+        w_rows = lax.dynamic_slice_in_dim(w_query, src_block * feat, feat, axis=0)
+        part = jnp.dot(normed, w_rows, preferred_element_type=jnp.float32)
+        acc = part if acc is None else acc + part
+    queries = acc.astype(jnp.bfloat16)
 
     attended = attend(wanted, queries, slots, entry_len)
     partial_value = jnp.dot(attended, w_out, preferred_element_type=jnp.float32)

time: 253 us -> 207 us (0.82)
  waiting for transfers between devices: 202 us -> 126 us
  starting transfers between devices: 0.08 us -> 27.5 us
    all_gather x1, waiting for transfers between devices: 91.3 us -> 0.01 us  [local(): slots = lax.all_gather(own, 'retr', axis=0, tiled=True)]
    ppermute x0 -> x7, waiting for transfers between devices: none -> 69.5 us  [local(): pieces.append(lax.ppermute(hidden_in, 'tensor', perm))]
    all_gather x1 -> x0, waiting for transfers between devices: 54.7 us -> none  [local(): gathered = lax.all_gather(hidden_in, 'tensor', axis=1, tiled=True)]
    ppermute x0 -> x7, starting transfers between devices: none -> 27.5 us  [local(): pieces.append(lax.ppermute(hidden_in, 'tensor', perm))]
    dot_general x1 -> x8, matrix products: 5.37 us -> 6.91 us  [local(): part = jnp.dot(normed, w_rows, preferred_element_type=jnp.float32)]
  transfers between devices with their start and end apart: 3 -> 9, of which waited for: 3 -> 7; matrix products, arithmetic and copies ran while one was open for 6% -> 5% of each run, Pallas kernels for 0% -> 0%
where the time goes in v4:
time: 207 us; the launch traced here: 206 us
  waiting for transfers between devices  126 us (61%)
  starting transfers between devices  27.5 us (13%)
  matrix products  16.4 us (8%)
  Pallas kernels  14.5 us (7%)
  between operations  13.5 us (7%)
  other arithmetic  7.38 us (4%)
    ppermute x7, waiting for transfers between devices, local(): pieces.append(lax.ppermute(hidden_in, 'tensor', perm))  69.5 us
    reduce_scatter x1, waiting for transfers between devices, local(): lax.psum_scatter(partial_value.astype(jnp.bfloat16), 'tensor', scatter_di...  56.2 us
    ppermute x7, starting transfers between devices, local(): pieces.append(lax.ppermute(hidden_in, 'tensor', perm))  27.5 us
    pallas_call x1, Pallas kernels, attend(): pl.pallas_call(functools.partial(attend_kernel, entry_len=entry_len), out...  14.5 us
    dot_general x8, matrix products, local(): part = jnp.dot(normed, w_rows, preferred_element_type=jnp.float32)  6.91 us
    dot_general x1, matrix products, local(): partial_value = jnp.dot(attended, w_out, preferred_element_type=jnp.float32)  6.63 us
  transfers between devices with their start and end apart: 9, of which 7 were waited for; matrix products, arithmetic and copies ran while one was open for 5% of the time, Pallas kernels for 0%

profile of v4, /device:TPU:1, one launch (start us, length us, event | category | flops | bytes accessed | tf_op | source)
XLA Modules:
  0.0 206.5 jit_solution(18094427141580174104)
XLA Ops:
  6.5 0.8 convert_element_type.98
  7.3 0.1 broadcast_in_dim.2
  7.4 0.1 convert_element_type.103
  7.5 0.3 copy-done
  7.8 2.8 %fusion.5 = bf16[1024,512]{0,1:T(8,128)(2,1)S(1)} fusion(bf16[512,1024]{1,0:T(8,128)(2,1)S(1)} %bitcast.7, bf16[1024,512]{1,0:T(8,128)(2,1)} %param.18, bf16[1024,512]{1,0:T(8,128)(2,1)} %param.17), kind=kOutput, calls=%fused_computation.10 | convolution fusion | flops 1078460416 | bytes 4194304 | tf_op jit(solution)/shard_map/dot_general | solution.py:83
  10.6 1.1 fusion.9
  11.8 0.0 all-gather.2.cloned.1.call-update
  11.8 0.0 reduce-scatter.2.cloned.1.call-start
  11.9 0.0 copy-done.1
  11.9 2.5 %collective-permute-start = (bf16[512,512]{1,0:T(8,128)(2,1)S(1)}, bf16[512,512]{1,0:T(8,128)(2,1)}, u32[]{:S(2)}, u32[]{:S(2)}) collective-permute-start(bf16[512,512]{1,0:T(8,128)(2,1)S(1)} %copy-done.1), channel_id=1, source_target_pairs={{0,1},{1,2},{2,3},{3,4},{4,5},{5,6},{6,7},{7,0},{8,9},{9,10},{10,1... | collective-permute-start | bytes 1572872 | tf_op jit(solution)/shard_map/ppermute | solution.py:80
  14.4 3.0 %collective-permute-start.1 = (bf16[512,512]{1,0:T(8,128)(2,1)S(1)}, bf16[512,512]{1,0:T(8,128)(2,1)}, u32[]{:S(2)}, u32[]{:S(2)}) collective-permute-start(bf16[512,512]{1,0:T(8,128)(2,1)S(1)} %copy-done.1), channel_id=1, source_target_pairs={{0,2},{1,3},{2,4},{3,5},{4,6},{5,7},{6,0},{7,1},{8,10},{9,11},{10,... | collective-permute-start | bytes 1572872 | tf_op jit(solution)/shard_map/ppermute | solution.py:80
  17.4 3.8 %collective-permute-start.2 = (bf16[512,512]{1,0:T(8,128)(2,1)S(1)}, bf16[512,512]{1,0:T(8,128)(2,1)S(1)}, u32[]{:S(2)}, u32[]{:S(2)}) collective-permute-start(bf16[512,512]{1,0:T(8,128)(2,1)S(1)} %copy-done.1), channel_id=1, source_target_pairs={{0,3},{1,4},{2,5},{3,6},{4,7},{5,0},{6,1},{7,2},{8,11},{9,12},{10,... | collective-permute-start | bytes 1572872 | tf_op jit(solution)/shard_map/ppermute | solution.py:80
  21.1 0.5 collective-permute-start.3
  21.6 4.5 %collective-permute-start.4 = (bf16[512,512]{1,0:T(8,128)(2,1)S(1)}, bf16[512,512]{1,0:T(8,128)(2,1)S(1)}, u32[]{:S(2)}, u32[]{:S(2)}) collective-permute-start(bf16[512,512]{1,0:T(8,128)(2,1)S(1)} %copy-done.1), channel_id=1, source_target_pairs={{0,5},{1,6},{2,7},{3,0},{4,1},{5,2},{6,3},{7,4},{8,13},{9,14},{10,... | collective-permute-start | bytes 1572872 | tf_op jit(solution)/shard_map/ppermute | solution.py:80
  26.1 0.0 copy-done.4
  26.1 0.1 copy.13
  26.2 0.7 reshape.98.flat_ref
  26.8 0.2 fusion.31
  27.0 0.1 fusion.77
  27.1 3.0 %collective-permute-done = bf16[512,512]{1,0:T(8,128)(2,1)} collective-permute-done((bf16[512,512]{1,0:T(8,128)(2,1)S(1)}, bf16[512,512]{1,0:T(8,128)(2,1)}, u32[]{:S(2)}, u32[]{:S(2)}) %collective-permute-start) | collective-permute-done | bytes 524320 | tf_op jit(solution)/shard_map/ppermute | solution.py:80
  30.1 1.6 collective-permute-start.5
  31.7 1.2 fusion.10
  32.9 10.4 %collective-permute-done.1 = bf16[512,512]{1,0:T(8,128)(2,1)} collective-permute-done((bf16[512,512]{1,0:T(8,128)(2,1)S(1)}, bf16[512,512]{1,0:T(8,128)(2,1)}, u32[]{:S(2)}, u32[]{:S(2)}) %collective-permute-start.1) | collective-permute-done | bytes 524320 | tf_op jit(solution)/shard_map/ppermute | solution.py:80
  43.3 11.7 %collective-permute-start.6 = (bf16[512,512]{1,0:T(8,128)(2,1)S(1)}, bf16[512,512]{1,0:T(8,128)(2,1)S(1)}, u32[]{:S(2)}, u32[]{:S(2)}) collective-permute-start(bf16[512,512]{1,0:T(8,128)(2,1)S(1)} %copy-done.1), channel_id=1, source_target_pairs={{0,7},{1,0},{2,1},{3,2},{4,3},{5,4},{6,5},{7,6},{8,15},{9,8},{10,9... | collective-permute-start | bytes 1572872 | tf_op jit(solution)/shard_map/ppermute | solution.py:80
  55.0 1.2 fusion.13
  56.2 29.5 %collective-permute-done.2 = bf16[512,512]{1,0:T(8,128)(2,1)S(1)} collective-permute-done((bf16[512,512]{1,0:T(8,128)(2,1)S(1)}, bf16[512,512]{1,0:T(8,128)(2,1)S(1)}, u32[]{:S(2)}, u32[]{:S(2)}) %collective-permute-start.2) | collective-permute-done | bytes 524320 | tf_op jit(solution)/shard_map/ppermute | solution.py:80
  85.7 0.2 fusion.16
  85.8 11.4 %collective-permute-done.3 = bf16[512,512]{1,0:T(8,128)(2,1)S(1)} collective-permute-done((bf16[512,512]{1,0:T(8,128)(2,1)S(1)}, bf16[512,512]{1,0:T(8,128)(2,1)S(1)}, u32[]{:S(2)}, u32[]{:S(2)}) %collective-permute-start.3) | collective-permute-done | bytes 524320 | tf_op jit(solution)/shard_map/ppermute | solution.py:80
  97.3 0.2 fusion.19
  97.4 0.0 collective-permute-done.4
  97.4 0.2 fusion.22
  97.6 7.5 %collective-permute-done.5 = bf16[512,512]{1,0:T(8,128)(2,1)S(1)} collective-permute-done((bf16[512,512]{1,0:T(8,128)(2,1)S(1)}, bf16[512,512]{1,0:T(8,128)(2,1)S(1)}, u32[]{:S(2)}, u32[]{:S(2)}) %collective-permute-start.5) | collective-permute-done | bytes 524320 | tf_op jit(solution)/shard_map/ppermute | solution.py:80
  105.1 0.2 fusion.25
  105.3 7.8 %collective-permute-done.6 = bf16[512,512]{1,0:T(8,128)(2,1)S(1)} collective-permute-done((bf16[512,512]{1,0:T(8,128)(2,1)S(1)}, bf16[512,512]{1,0:T(8,128)(2,1)S(1)}, u32[]{:S(2)}, u32[]{:S(2)}) %collective-permute-start.6) | collective-permute-done | bytes 524320 | tf_op jit(solution)/shard_map/ppermute | solution.py:80
  113.1 0.2 fusion.28
  113.3 0.5 fusion.35
  113.8 1.6 convolution_add_fusion.6
  115.4 1.6 convolution_add_fusion.5
  116.9 0.5 convolution_add_fusion.4
  117.4 0.5 convolution_add_fusion.3
  117.9 0.5 convolution_add_fusion.2
  118.5 0.5 convolution_add_fusion.1
  119.0 1.3 fusion.8.q_ref
  120.3 14.5 %shard_map.91 = bf16[512,512]{1,0:T(8,128)(2,1)} custom-call(s32[16]{0:T(128)} %reshape.98.flat_ref, bf16[512,512]{1,0:T(8,128)(2,1)} %fusion.8.q_ref, bf16[64,136,1024]{2,1,0:T(8,128)(2,1)} %all-gather.2.cloned.1.call-done.kv0_ref.kv1_ref, bf16[64,136,1024]{2,1,0:T(8,128)(2,1)} %all-gather.2.cloned.1.call-done.kv0_ref.kv1_ref), custom_call_target="tpu_custom_call" | custom-call | tf_op jit(solution)/shard_map/pallas_call | solution.py:59
  134.8 6.6 %convolution_convert_fusion = bf16[512,4096]{1,0:T(8,128)(2,1)} fusion(bf16[512,512]{1,0:T(8,128)(2,1)} %shard_map.91, bf16[512,4096]{1,0:T(8,128)(2,1)} %param.19), kind=kOutput, calls=%fused_computation | convolution fusion | flops 2149580800 | bytes 8912896 | tf_op jit(solution)/shard_map/dot_general | solution.py:106
  141.4 0.0 reduce-scatter.2.cloned.1.call-update
  141.4 56.2 %reduce-scatter.2.cloned.1.call-done = bf16[512,512]{1,0:T(8,128)(2,1)} async-done(((bf16[512,4096]{1,0:T(8,128)(2,1)}), bf16[512,512]{1,0:T(8,128)(2,1)}) %reduce-scatter.2.cloned.1.call-update) | async-done | bytes 524304 | tf_op jit(solution)/shard_map/reduce_scatter | solution.py:107
  197.7 2.0 fusion.34
  (10 shorter events, 0.0 us)
Async XLA Ops:
  6.5 1.2 copy-start
  6.5 113.7 %all-gather.2.cloned.1.call-start = ((), (), s32[]{:S(2)}) async-start(), calls=%async_computation.1 | async-start | bytes 18939904 | tf_op jit(solution)/shard_map/all_gather | solution.py:90
  7.8 4.1 %copy-start.1 = (bf16[512,512]{1,0:T(8,128)(2,1)S(1)}, bf16[512,512]{1,0:T(8,128)(2,1)}, u32[]{:S(2)}) copy-start(bf16[512,512]{1,0:T(8,128)(2,1)} %param.11) | copy-start | bytes 1572868
  7.8 18.3 %copy-start.4 = (s32[8,2]{0,1:T(2,128)S(1)}, s32[8,2]{0,1:T(2,128)}, u32[]{:S(2)}) copy-start(s32[8,2]{0,1:T(2,128)} %param.13) | copy-start | bytes 196
  7.8 19.2 %copy-start.3 = (f32[4096]{0:T(1024)S(1)}, f32[4096]{0:T(1024)}, u32[]{:S(2)}) copy-start(f32[4096]{0:T(1024)} %param.12) | copy-start | bytes 49156
  11.8 185.9 %reduce-scatter.2.cloned.1.call-start = ((), (), s32[]{:S(2)}) async-start(), calls=%async_computation.2 | async-start | bytes 4718592 | tf_op jit(solution)/shard_map/reduce_scatter | solution.py:107
  11.9 18.2 %collective-permute-start = (bf16[512,512]{1,0:T(8,128)(2,1)S(1)}, bf16[512,512]{1,0:T(8,128)(2,1)}, u32[]{:S(2)}, u32[]{:S(2)}) collective-permute-start(bf16[512,512]{1,0:T(8,128)(2,1)S(1)} %copy-done.1), channel_id=1, source_target_pairs={{0,1},{1,2},{2,3},{3,4},{4,5},{5,6},{6,7},{7,0},{8,9},{9,10},{10,1... | collective-permute-start | bytes 1572872 | tf_op jit(solution)/shard_map/ppermute | solution.py:80
  14.4 28.9 %collective-permute-start.1 = (bf16[512,512]{1,0:T(8,128)(2,1)S(1)}, bf16[512,512]{1,0:T(8,128)(2,1)}, u32[]{:S(2)}, u32[]{:S(2)}) collective-permute-start(bf16[512,512]{1,0:T(8,128)(2,1)S(1)} %copy-done.1), channel_id=1, source_target_pairs={{0,2},{1,3},{2,4},{3,5},{4,6},{5,7},{6,0},{7,1},{8,10},{9,11},{10,... | collective-permute-start | bytes 1572872 | tf_op jit(solution)/shard_map/ppermute | solution.py:80
  17.4 68.3 %collective-permute-start.2 = (bf16[512,512]{1,0:T(8,128)(2,1)S(1)}, bf16[512,512]{1,0:T(8,128)(2,1)S(1)}, u32[]{:S(2)}, u32[]{:S(2)}) collective-permute-start(bf16[512,512]{1,0:T(8,128)(2,1)S(1)} %copy-done.1), channel_id=1, source_target_pairs={{0,3},{1,4},{2,5},{3,6},{4,7},{5,0},{6,1},{7,2},{8,11},{9,12},{10,... | collective-permute-start | bytes 1572872 | tf_op jit(solution)/shard_map/ppermute | solution.py:80
  21.1 76.1 %collective-permute-start.3 = (bf16[512,512]{1,0:T(8,128)(2,1)S(1)}, bf16[512,512]{1,0:T(8,128)(2,1)S(1)}, u32[]{:S(2)}, u32[]{:S(2)}) collective-permute-start(bf16[512,512]{1,0:T(8,128)(2,1)S(1)} %copy-done.1), channel_id=1, source_target_pairs={{0,4},{1,5},{2,6},{3,7},{4,0},{5,1},{6,2},{7,3},{8,12},{9,13},{10,... | collective-permute-start | bytes 1572872 | tf_op jit(solution)/shard_map/ppermute | solution.py:80
  21.6 75.8 %collective-permute-start.4 = (bf16[512,512]{1,0:T(8,128)(2,1)S(1)}, bf16[512,512]{1,0:T(8,128)(2,1)S(1)}, u32[]{:S(2)}, u32[]{:S(2)}) collective-permute-start(bf16[512,512]{1,0:T(8,128)(2,1)S(1)} %copy-done.1), channel_id=1, source_target_pairs={{0,5},{1,6},{2,7},{3,0},{4,1},{5,2},{6,3},{7,4},{8,13},{9,14},{10,... | collective-permute-start | bytes 1572872 | tf_op jit(solution)/shard_map/ppermute | solution.py:80
  26.8 86.5 %copy-start.2 = (bf16[4096,512]{1,0:T(8,128)(2,1)S(1)}, bf16[4096,512]{1,0:T(8,128)(2,1)}, u32[]{:S(2)}) copy-start(bf16[4096,512]{1,0:T(8,128)(2,1)} %param.16) | copy-start | bytes 12582916
  30.1 75.0 %collective-permute-start.5 = (bf16[512,512]{1,0:T(8,128)(2,1)S(1)}, bf16[512,512]{1,0:T(8,128)(2,1)S(1)}, u32[]{:S(2)}, u32[]{:S(2)}) collective-permute-start(bf16[512,512]{1,0:T(8,128)(2,1)S(1)} %copy-done.1), channel_id=1, source_target_pairs={{0,6},{1,7},{2,0},{3,1},{4,2},{5,3},{6,4},{7,5},{8,14},{9,15},{10,... | collective-permute-start | bytes 1572872 | tf_op jit(solution)/shard_map/ppermute | solution.py:80
  43.3 69.8 %collective-permute-start.6 = (bf16[512,512]{1,0:T(8,128)(2,1)S(1)}, bf16[512,512]{1,0:T(8,128)(2,1)S(1)}, u32[]{:S(2)}, u32[]{:S(2)}) collective-permute-start(bf16[512,512]{1,0:T(8,128)(2,1)S(1)} %copy-done.1), channel_id=1, source_target_pairs={{0,7},{1,0},{2,1},{3,2},{4,3},{5,4},{6,5},{7,6},{8,15},{9,8},{10,9... | collective-permute-start | bytes 1572872 | tf_op jit(solution)/shard_map/ppermute | solution.py:80
Sparse Core Ops, SparseCore 0:
  11.9 103.2 all-gather.1
  141.5 56.0 reduce-scatter.1

commit v5 on v4

--- a/solution.py
+++ b/solution.py
@@ -63,7 +63,7 @@
     )(flat_idx, queries, slots, slots)
 
 
-def local(hidden_in, norm_gain, nbr_table, encodings, enc_mask, w_query, w_key, w_value, w_out):
+def local(dp_count, retr_count, tensor_count, hidden_in, norm_gain, nbr_table, encodings, enc_mask, w_query, w_key, w_value, w_out):
     segment_count = nbr_table.shape[0]
     nb_dev, entry_len, enc_width = encodings.shape
     mask_cols = enc_mask.shape[1]
@@ -71,29 +71,44 @@
     wanted = nbr_table.reshape(-1)
     need_count = wanted.shape[0]
 
-    tensor_count = w_out.shape[1] // hidden_in.shape[1]
     feat = hidden_in.shape[1]
     t = lax.axis_index("tensor")
-    pieces = [hidden_in]
-    for k in range(1, tensor_count):
-        perm = [(i, (i + k) % tensor_count) for i in range(tensor_count)]
-        pieces.append(lax.ppermute(hidden_in, "tensor", perm))
+    fwd = [(i, (i + 1) % tensor_count) for i in range(tensor_count)]
+    bwd = [(i, (i - 1) % tensor_count) for i in range(tensor_count)]
+    pieces = [(0, hidden_in)]
+    up = down = hidden_in
+    half_ring = tensor_count // 2
+    for k in range(1, half_ring):
+        up = lax.ppermute(up, "tensor", fwd)
+        down = lax.ppermute(down, "tensor", bwd)
+        pieces.append((k, up))
+        pieces.append((tensor_count - k, down))
+    half_rows = hidden_in.shape[0] // 2
+    top = lax.ppermute(up[:half_rows], "tensor", fwd)
+    bottom = lax.ppermute(down[half_rows:], "tensor", bwd)
+    pieces.append((half_ring, jnp.concatenate([top, bottom], axis=0)))
 
+    per_dev = nb_dev // dp_count
+    dp_idx = lax.axis_index("dp")
+    enc_half = lax.dynamic_slice_in_dim(encodings, dp_idx * per_dev, per_dev, axis=0)
+    mask_half = lax.dynamic_slice_in_dim(enc_mask, dp_idx * per_dev, per_dev, axis=0)
     w_both = jnp.concatenate([w_key, w_value], axis=1)
     own_kv = jnp.dot(
-        encodings.reshape(nb_dev * entry_len, enc_width), w_both, preferred_element_type=jnp.float32
-    ).astype(jnp.bfloat16).reshape(nb_dev, entry_len, 2 * head_cols)
-    key_live = jnp.repeat(enc_mask, BLOCK, axis=1).astype(jnp.bfloat16)
-    mask_rows = jnp.zeros((nb_dev, 8, 2 * head_cols), jnp.bfloat16)
+        enc_half.reshape(per_dev * entry_len, enc_width), w_both, preferred_element_type=jnp.float32
+    ).astype(jnp.bfloat16).reshape(per_dev, entry_len, 2 * head_cols)
+    key_live = jnp.repeat(mask_half, BLOCK, axis=1).astype(jnp.bfloat16)
+    mask_rows = jnp.zeros((per_dev, 8, 2 * head_cols), jnp.bfloat16)
     mask_rows = mask_rows.at[:, 0, :entry_len].set(key_live)
     own = jnp.concatenate([own_kv, mask_rows], axis=1)
-    slots = lax.all_gather(own, "retr", axis=0, tiled=True)
+    slots = lax.all_gather(own, ("dp", "retr"), axis=0, tiled=True)
+    in_dev = wanted % nb_dev
+    slot_of = ((in_dev // per_dev) * retr_count + wanted // nb_dev) * per_dev + in_dev % per_dev
 
-    widened = [p.astype(jnp.float32) for p in pieces]
+    widened = [p.astype(jnp.float32) for _, p in pieces]
     sum_sq = sum(jnp.sum(w * w, axis=-1, keepdims=True) for w in widened)
     inv = lax.rsqrt(sum_sq / (feat * tensor_count) + 1e-05)
     acc = None
-    for k, w in enumerate(widened):
+    for (k, _), w in zip(pieces, widened):
         src_block = (t - k) % tensor_count
         gain = lax.dynamic_slice_in_dim(norm_gain, src_block * feat, feat)
         normed = (w * inv * gain).astype(jnp.bfloat16)
@@ -102,7 +117,7 @@
         acc = part if acc is None else acc + part
     queries = acc.astype(jnp.bfloat16)
 
-    attended = attend(wanted, queries, slots, entry_len)
+    attended = attend(slot_of, queries, slots, entry_len)
     partial_value = jnp.dot(attended, w_out, preferred_element_type=jnp.float32)
     summed = lax.psum_scatter(
         partial_value.astype(jnp.bfloat16), "tensor", scatter_dimension=1, tiled=True
@@ -123,4 +138,5 @@
         P("tensor", None),
     )
     out_specs = P(("dp", "retr"), "tensor")
-    return jax.shard_map(local, mesh=mesh, in_specs=in_specs, out_specs=out_specs, check_vma=False)
+    body = functools.partial(local, mesh.shape["dp"], mesh.shape["retr"], mesh.shape["tensor"])
+    return jax.shard_map(body, mesh=mesh, in_specs=in_specs, out_specs=out_specs, check_vma=False)

time: 207 us -> 207 us (level)
  waiting for transfers between devices: 126 us -> 141 us
  starting transfers between devices: 27.5 us -> 15 us
    all_gather x1, waiting for transfers between devices: 0.01 us -> 52.4 us  [local(): slots = lax.all_gather(own, ('dp', 'retr'), axis=0, tiled=True)]
    ppermute x7 -> x8, waiting for transfers between devices: 69.5 us -> 32.6 us  [the longest x3 29.5 us: local(): up = lax.ppermute(up, 'tensor', fwd)]
    ppermute x7 -> x8, starting transfers between devices: 27.5 us -> 14.9 us  [the longest x3 9.38 us: local(): down = lax.ppermute(down, 'tensor', bwd)]
  transfers between devices with their start and end apart: 9 -> 10, of which waited for: 7 -> 6; matrix products, arithmetic and copies ran while one was open for 5% -> 4% of each run, Pallas kernels for 0% -> 0%
where the time goes in v5:
time: 207 us
  waiting for transfers between devices  141 us (68%)
  starting transfers between devices  15 us (7%)
  matrix products  14.7 us (7%)
  Pallas kernels  14.5 us (7%)
  between operations  13.6 us (7%)
  other arithmetic  6.5 us (3%)
    reduce_scatter x1, waiting for transfers between devices, local(): lax.psum_scatter(partial_value.astype(jnp.bfloat16), 'tensor', scatter_di...  55.9 us
    all_gather x1, waiting for transfers between devices, local(): slots = lax.all_gather(own, ('dp', 'retr'), axis=0, tiled=True)  52.4 us
    ppermute x3, waiting for transfers between devices, local(): up = lax.ppermute(up, 'tensor', fwd)  29.5 us
    pallas_call x1, Pallas kernels, attend(): pl.pallas_call(functools.partial(attend_kernel, entry_len=entry_len), out...  14.5 us
    ppermute x3, starting transfers between devices, local(): down = lax.ppermute(down, 'tensor', bwd)  9.38 us
    dot_general x1, matrix products, local(): partial_value = jnp.dot(attended, w_out, preferred_element_type=jnp.float32)  6.63 us
    dot_general x8, matrix products, local(): part = jnp.dot(normed, w_rows, preferred_element_type=jnp.float32)  5.86 us
  transfers between devices with their start and end apart: 10, of which 6 were waited for; matrix products, arithmetic and copies ran while one was open for 4% of the time, Pallas kernels for 0%

profile of v5, /device:TPU:1, one launch (start us, length us, event | category | flops | bytes accessed | tf_op | source)
XLA Modules:
  0.0 206.9 jit_solution(13940554789747902113)
XLA Ops:
  6.5 0.0 all-gather.2.cloned.1.call-start
  6.6 1.2 copy-done
  7.8 0.7 fusion.76
  8.5 0.1 broadcast_in_dim.2
  8.6 0.1 convert_element_type.99
  8.7 2.2 %fusion.4 = bf16[256,1024]{1,0:T(8,128)(2,1)S(1)} fusion(bf16[256,1024]{1,0:T(8,128)(2,1)S(1)} %bitcast.6, bf16[1024,512]{1,0:T(8,128)(2,1)} %param.18, bf16[1024,512]{1,0:T(8,128)(2,1)} %param.17), kind=kOutput, calls=%fused_computation.29 | convolution fusion | flops 541327360 | bytes 3145728 | tf_op jit(solution)/shard_map/dot_general | solution.py:96
  10.9 0.9 fusion.34
  11.8 0.0 all-gather.2.cloned.1.call-update
  11.8 0.0 reduce-scatter.2.cloned.1.call-start
  11.9 2.5 %collective-permute-start = (bf16[512,512]{1,0:T(8,128)(2,1)S(1)}, bf16[512,512]{1,0:T(8,128)(2,1)S(1)}, u32[]{:S(2)}, u32[]{:S(2)}) collective-permute-start(bf16[512,512]{1,0:T(8,128)(2,1)S(1)} %copy-done.1), channel_id=1, source_target_pairs={{0,1},{1,2},{2,3},{3,4},{4,5},{5,6},{6,7},{7,0},{8,9},{9,10},{10,1... | collective-permute-start | bytes 1572872 | tf_op jit(solution)/shard_map/ppermute | solution.py:82
  14.4 4.0 %collective-permute-start.1 = (bf16[512,512]{1,0:T(8,128)(2,1)S(1)}, bf16[512,512]{1,0:T(8,128)(2,1)S(1)}, u32[]{:S(2)}, u32[]{:S(2)}) collective-permute-start(bf16[512,512]{1,0:T(8,128)(2,1)S(1)} %copy-done.1), channel_id=1, source_target_pairs={{0,7},{1,0},{2,1},{3,2},{4,3},{5,4},{6,5},{7,6},{8,15},{9,8},{10,9... | collective-permute-start | bytes 1572872 | tf_op jit(solution)/shard_map/ppermute | solution.py:83
  18.4 11.5 %collective-permute-done = bf16[512,512]{1,0:T(8,128)(2,1)S(1)} collective-permute-done((bf16[512,512]{1,0:T(8,128)(2,1)S(1)}, bf16[512,512]{1,0:T(8,128)(2,1)S(1)}, u32[]{:S(2)}, u32[]{:S(2)}) %collective-permute-start) | collective-permute-done | bytes 524320 | tf_op jit(solution)/shard_map/ppermute | solution.py:82
  30.0 0.0 collective-permute-start.2
  30.0 2.7 %collective-permute-start.3 = (bf16[512,512]{1,0:T(8,128)(2,1)S(1)}, bf16[512,512]{1,0:T(8,128)(2,1)}, u32[]{:S(2)}, u32[]{:S(2)}) collective-permute-start(bf16[512,512]{1,0:T(8,128)(2,1)S(1)} %collective-permute-done.1), channel_id=1, source_target_pairs={{0,7},{1,0},{2,1},{3,2},{4,3},{5,4},{6,5},{7,6},{8,15},{9,8},{10,9... | collective-permute-start | bytes 1572872 | tf_op jit(solution)/shard_map/ppermute | solution.py:83
  32.6 0.1 copy.13
  32.7 0.1 reshape.98
  32.8 0.1 fusion.80
  32.9 0.2 fusion.30
  33.1 0.5 fusion.77.flat_ref
  33.6 9.8 %collective-permute-done.2 = bf16[512,512]{1,0:T(8,128)(2,1)S(1)} collective-permute-done((bf16[512,512]{1,0:T(8,128)(2,1)S(1)}, bf16[512,512]{1,0:T(8,128)(2,1)S(1)}, u32[]{:S(2)}, u32[]{:S(2)}) %collective-permute-start.2) | collective-permute-done | bytes 524320 | tf_op jit(solution)/shard_map/ppermute | solution.py:82
  43.4 0.0 collective-permute-start.4
  43.4 0.0 collective-permute-done.3
  43.4 2.7 %collective-permute-start.5 = (bf16[512,512]{1,0:T(8,128)(2,1)}, bf16[512,512]{1,0:T(8,128)(2,1)S(1)}, u32[]{:S(2)}, u32[]{:S(2)}) collective-permute-start(bf16[512,512]{1,0:T(8,128)(2,1)} %collective-permute-done.3), channel_id=1, source_target_pairs={{0,7},{1,0},{2,1},{3,2},{4,3},{5,4},{6,5},{7,6},{8,15},{9,8},{10,9... | collective-permute-start | bytes 1572872 | tf_op jit(solution)/shard_map/ppermute | solution.py:83
  46.1 0.2 fusion.12
  46.3 0.2 fusion.9
  46.4 0.2 fusion.15
  46.6 1.2 fusion.18
  47.8 8.1 %collective-permute-done.4 = bf16[512,512]{1,0:T(8,128)(2,1)S(1)} collective-permute-done((bf16[512,512]{1,0:T(8,128)(2,1)S(1)}, bf16[512,512]{1,0:T(8,128)(2,1)S(1)}, u32[]{:S(2)}, u32[]{:S(2)}) %collective-permute-start.4) | collective-permute-done | bytes 524320 | tf_op jit(solution)/shard_map/ppermute | solution.py:82
  56.0 0.1 collective-permute-start.6
  56.1 2.9 %collective-permute-start.7 = (bf16[256,512]{1,0:T(8,128)(2,1)S(1)}, bf16[256,512]{1,0:T(8,128)(2,1)S(1)}, u32[]{:S(2)}, u32[]{:S(2)}) collective-permute-start(bf16[256,512]{1,0:T(8,128)(2,1)S(1)} %slice.32), channel_id=1, source_target_pairs={{0,7},{1,0},{2,1},{3,2},{4,3},{5,4},{6,5},{7,6},{8,15},{9,8},{10,9... | collective-permute-start | bytes 786440 | tf_op jit(solution)/shard_map/ppermute | solution.py:88
  59.0 0.2 fusion.21
  59.2 0.2 fusion.24
  59.4 3.1 %collective-permute-done.6 = bf16[256,512]{1,0:T(8,128)(2,1)S(1)} collective-permute-done((bf16[256,512]{1,0:T(8,128)(2,1)S(1)}, bf16[256,512]{1,0:T(8,128)(2,1)S(1)}, u32[]{:S(2)}, u32[]{:S(2)}) %collective-permute-start.6) | collective-permute-done | bytes 262176 | tf_op jit(solution)/shard_map/ppermute | solution.py:87
  62.5 0.2 fusion.27
  62.7 0.5 fusion.35
  63.2 0.5 convolution_add_fusion.6
  63.7 0.5 convolution_add_fusion.5
  64.3 0.5 convolution_add_fusion.4
  64.8 1.6 convolution_add_fusion.3
  66.3 0.5 convolution_add_fusion.2
  66.8 0.5 convolution_add_fusion.1
  67.3 1.3 fusion.7.q_ref
  68.6 52.4 %all-gather.2.cloned.1.call-done.kv0_ref.kv1_ref = bf16[64,136,1024]{2,1,0:T(8,128)(2,1)} async-done(((bf16[2,136,1024]{2,1,0:T(8,128)(2,1)}), bf16[64,136,1024]{2,1,0:T(8,128)(2,1)}) %all-gather.2.cloned.1.call-update) | async-done | bytes 17825808 | tf_op jit(solution)/shard_map/all_gather | solution.py:103
  121.0 14.5 %shard_map.91 = bf16[512,512]{1,0:T(8,128)(2,1)} custom-call(s32[16]{0:T(128)} %fusion.77.flat_ref, bf16[512,512]{1,0:T(8,128)(2,1)} %fusion.7.q_ref, bf16[64,136,1024]{2,1,0:T(8,128)(2,1)} %all-gather.2.cloned.1.call-done.kv0_ref.kv1_ref, bf16[64,136,1024]{2,1,0:T(8,128)(2,1)} %all-gather.2.cloned.1.call-done.kv0_ref.kv1_ref), custom_call_target="tpu_custom_call" | custom-call | tf_op jit(solution)/shard_map/pallas_call | solution.py:59
  135.5 6.6 %convolution_convert_fusion = bf16[512,4096]{1,0:T(8,128)(2,1)} fusion(bf16[512,512]{1,0:T(8,128)(2,1)} %shard_map.91, bf16[512,4096]{1,0:T(8,128)(2,1)} %param.19), kind=kOutput, calls=%fused_computation | convolution fusion | flops 2149580800 | bytes 8912896 | tf_op jit(solution)/shard_map/dot_general | solution.py:121
  142.2 0.0 reduce-scatter.2.cloned.1.call-update
  142.2 55.9 %reduce-scatter.2.cloned.1.call-done = bf16[512,512]{1,0:T(8,128)(2,1)} async-done(((bf16[512,4096]{1,0:T(8,128)(2,1)}), bf16[512,512]{1,0:T(8,128)(2,1)}) %reduce-scatter.2.cloned.1.call-update) | async-done | bytes 524304 | tf_op jit(solution)/shard_map/reduce_scatter | solution.py:122
  198.1 2.0 fusion.33
  (16 shorter events, 0.1 us)
Async XLA Ops:
  6.5 1.2 copy-start
  6.5 5.3 %copy-start.1 = (bf16[512,512]{1,0:T(8,128)(2,1)S(1)}, bf16[512,512]{1,0:T(8,128)(2,1)}, u32[]{:S(2)}) copy-start(bf16[512,512]{1,0:T(8,128)(2,1)} %param.11) | copy-start | bytes 1572868
  6.5 26.1 %copy-start.4 = (s32[8,2]{0,1:T(2,128)S(1)}, s32[8,2]{0,1:T(2,128)}, u32[]{:S(2)}) copy-start(s32[8,2]{0,1:T(2,128)} %param.13) | copy-start | bytes 196
  6.5 26.3 %copy-start.3 = (f32[4096]{0:T(1024)S(1)}, f32[4096]{0:T(1024)}, u32[]{:S(2)}) copy-start(f32[4096]{0:T(1024)} %param.12) | copy-start | bytes 49156
  6.5 114.5 %all-gather.2.cloned.1.call-start = ((), (), s32[]{:S(2)}) async-start(), calls=%async_computation.1 | async-start | bytes 18382848 | tf_op jit(solution)/shard_map/all_gather | solution.py:103
  11.8 186.3 %reduce-scatter.2.cloned.1.call-start = ((), (), s32[]{:S(2)}) async-start(), calls=%async_computation.2 | async-start | bytes 4718592 | tf_op jit(solution)/shard_map/reduce_scatter | solution.py:122
  11.9 18.1 %collective-permute-start = (bf16[512,512]{1,0:T(8,128)(2,1)S(1)}, bf16[512,512]{1,0:T(8,128)(2,1)S(1)}, u32[]{:S(2)}, u32[]{:S(2)}) collective-permute-start(bf16[512,512]{1,0:T(8,128)(2,1)S(1)} %copy-done.1), channel_id=1, source_target_pairs={{0,1},{1,2},{2,3},{3,4},{4,5},{5,6},{6,7},{7,0},{8,9},{9,10},{10,1... | collective-permute-start | bytes 1572872 | tf_op jit(solution)/shard_map/ppermute | solution.py:82
  14.4 15.6 %collective-permute-start.1 = (bf16[512,512]{1,0:T(8,128)(2,1)S(1)}, bf16[512,512]{1,0:T(8,128)(2,1)S(1)}, u32[]{:S(2)}, u32[]{:S(2)}) collective-permute-start(bf16[512,512]{1,0:T(8,128)(2,1)S(1)} %copy-done.1), channel_id=1, source_target_pairs={{0,7},{1,0},{2,1},{3,2},{4,3},{5,4},{6,5},{7,6},{8,15},{9,8},{10,9... | collective-permute-start | bytes 1572872 | tf_op jit(solution)/shard_map/ppermute | solution.py:83
  30.0 13.4 %collective-permute-start.2 = (bf16[512,512]{1,0:T(8,128)(2,1)S(1)}, bf16[512,512]{1,0:T(8,128)(2,1)S(1)}, u32[]{:S(2)}, u32[]{:S(2)}) collective-permute-start(bf16[512,512]{1,0:T(8,128)(2,1)S(1)} %collective-permute-done), channel_id=1, source_target_pairs={{0,1},{1,2},{2,3},{3,4},{4,5},{5,6},{6,7},{7,0},{8,9},{9,10},{10,1... | collective-permute-start | bytes 1572872 | tf_op jit(solution)/shard_map/ppermute | solution.py:82
  30.0 13.4 %collective-permute-start.3 = (bf16[512,512]{1,0:T(8,128)(2,1)S(1)}, bf16[512,512]{1,0:T(8,128)(2,1)}, u32[]{:S(2)}, u32[]{:S(2)}) collective-permute-start(bf16[512,512]{1,0:T(8,128)(2,1)S(1)} %collective-permute-done.1), channel_id=1, source_target_pairs={{0,7},{1,0},{2,1},{3,2},{4,3},{5,4},{6,5},{7,6},{8,15},{9,8},{10,9... | collective-permute-start | bytes 1572872 | tf_op jit(solution)/shard_map/ppermute | solution.py:83
  32.8 29.9 %copy-start.2 = (bf16[4096,512]{1,0:T(8,128)(2,1)S(1)}, bf16[4096,512]{1,0:T(8,128)(2,1)}, u32[]{:S(2)}) copy-start(bf16[4096,512]{1,0:T(8,128)(2,1)} %param.16) | copy-start | bytes 12582916
  43.4 12.6 %collective-permute-start.4 = (bf16[512,512]{1,0:T(8,128)(2,1)S(1)}, bf16[512,512]{1,0:T(8,128)(2,1)S(1)}, u32[]{:S(2)}, u32[]{:S(2)}) collective-permute-start(bf16[512,512]{1,0:T(8,128)(2,1)S(1)} %collective-permute-done.2), channel_id=1, source_target_pairs={{0,1},{1,2},{2,3},{3,4},{4,5},{5,6},{6,7},{7,0},{8,9},{9,10},{10,1... | collective-permute-start | bytes 1572872 | tf_op jit(solution)/shard_map/ppermute | solution.py:82
  43.4 12.7 %collective-permute-start.5 = (bf16[512,512]{1,0:T(8,128)(2,1)}, bf16[512,512]{1,0:T(8,128)(2,1)S(1)}, u32[]{:S(2)}, u32[]{:S(2)}) collective-permute-start(bf16[512,512]{1,0:T(8,128)(2,1)} %collective-permute-done.3), channel_id=1, source_target_pairs={{0,7},{1,0},{2,1},{3,2},{4,3},{5,4},{6,5},{7,6},{8,15},{9,8},{10,9... | collective-permute-start | bytes 1572872 | tf_op jit(solution)/shard_map/ppermute | solution.py:83
  56.0 6.5 %collective-permute-start.6 = (bf16[256,512]{1,0:T(8,128)(2,1)S(1)}, bf16[256,512]{1,0:T(8,128)(2,1)S(1)}, u32[]{:S(2)}, u32[]{:S(2)}) collective-permute-start(bf16[256,512]{1,0:T(8,128)(2,1)S(1)} %slice.31), channel_id=1, source_target_pairs={{0,1},{1,2},{2,3},{3,4},{4,5},{5,6},{6,7},{7,0},{8,9},{9,10},{10,1... | collective-permute-start | bytes 786440 | tf_op jit(solution)/shard_map/ppermute | solution.py:87
  56.1 6.4 %collective-permute-start.7 = (bf16[256,512]{1,0:T(8,128)(2,1)S(1)}, bf16[256,512]{1,0:T(8,128)(2,1)S(1)}, u32[]{:S(2)}, u32[]{:S(2)}) collective-permute-start(bf16[256,512]{1,0:T(8,128)(2,1)S(1)} %slice.32), channel_id=1, source_target_pairs={{0,7},{1,0},{2,1},{3,2},{4,3},{5,4},{6,5},{7,6},{8,15},{9,8},{10,9... | collective-permute-start | bytes 786440 | tf_op jit(solution)/shard_map/ppermute | solution.py:88
Sparse Core Ops, SparseCore 0:
  11.9 109.0 all-gather.1
  142.3 55.7 reduce-scatter.1

commit v6 on v5

--- a/solution.py
+++ b/solution.py
@@ -88,21 +88,35 @@
     bottom = lax.ppermute(down[half_rows:], "tensor", bwd)
     pieces.append((half_ring, jnp.concatenate([top, bottom], axis=0)))
 
-    per_dev = nb_dev // dp_count
-    dp_idx = lax.axis_index("dp")
-    enc_half = lax.dynamic_slice_in_dim(encodings, dp_idx * per_dev, per_dev, axis=0)
-    mask_half = lax.dynamic_slice_in_dim(enc_mask, dp_idx * per_dev, per_dev, axis=0)
+    half = t % 2
+    half_len = entry_len // 2
+    enc_rows = lax.dynamic_slice_in_dim(encodings, half * half_len, half_len, axis=1)
+    key_live = jnp.repeat(enc_mask, BLOCK, axis=1).astype(jnp.bfloat16)
+    mask_rows = jnp.zeros((nb_dev, 8, enc_width), jnp.bfloat16)
+    mask_rows = mask_rows.at[:, 0, :entry_len].set(key_live)
+    payload = jnp.concatenate([enc_rows, mask_rows], axis=1)
+    all_enc = lax.all_gather(payload, "retr", axis=0, tiled=True)
+    mine = jnp.take(all_enc, wanted, axis=0)
+    mine_rows = mine[:, :half_len]
+    pair = [(i, i ^ 1) for i in range(tensor_count)]
+    other_rows = lax.ppermute(mine_rows, "tensor", pair)
+
     w_both = jnp.concatenate([w_key, w_value], axis=1)
-    own_kv = jnp.dot(
-        enc_half.reshape(per_dev * entry_len, enc_width), w_both, preferred_element_type=jnp.float32
-    ).astype(jnp.bfloat16).reshape(per_dev, entry_len, 2 * head_cols)
-    key_live = jnp.repeat(mask_half, BLOCK, axis=1).astype(jnp.bfloat16)
-    mask_rows = jnp.zeros((per_dev, 8, 2 * head_cols), jnp.bfloat16)
-    mask_rows = mask_rows.at[:, 0, :entry_len].set(key_live)
-    own = jnp.concatenate([own_kv, mask_rows], axis=1)
-    slots = lax.all_gather(own, ("dp", "retr"), axis=0, tiled=True)
-    in_dev = wanted % nb_dev
-    slot_of = ((in_dev // per_dev) * retr_count + wanted // nb_dev) * per_dev + in_dev % per_dev
+
+    def project(rows):
+        out = jnp.dot(
+            rows.reshape(need_count * half_len, enc_width), w_both,
+            preferred_element_type=jnp.float32,
+        )
+        return out.astype(jnp.bfloat16).reshape(need_count, half_len, 2 * head_cols)
+
+    kv_mine = project(mine_rows)
+    kv_other = project(other_rows)
+    live_row = jnp.roll(mine[:, half_len, :entry_len], -half * half_len, axis=-1)
+    live_rows = jnp.zeros((need_count, 8, 2 * head_cols), jnp.bfloat16)
+    live_rows = live_rows.at[:, 0, :entry_len].set(live_row)
+    slots = jnp.concatenate([kv_mine, kv_other, live_rows], axis=1)
+    slot_of = jnp.arange(need_count, dtype=jnp.int32)
 
     widened = [p.astype(jnp.float32) for _, p in pieces]
     sum_sq = sum(jnp.sum(w * w, axis=-1, keepdims=True) for w in widened)

time: 207 us -> 218 us (1.053)
  waiting for transfers between devices: 141 us -> 129 us
  local copies, waits for them, and re-layouts: 1.69 us -> 13.3 us
  matrix products: 14.7 us -> 21.4 us
  other arithmetic: 6.5 us -> 8.81 us
    all_gather x1, waiting for transfers between devices: 52.4 us -> 6.76 us  [local(): all_enc = lax.all_gather(payload, 'retr', axis=0, tiled=True)]
    ppermute x0 -> x1, waiting for transfers between devices: none -> 38.2 us  [local(): other_rows = lax.ppermute(mine_rows, 'tensor', pair)]
    ppermute x3, waiting for transfers between devices: 29.5 us -> 24 us  [local(): up = lax.ppermute(up, 'tensor', fwd)]
    gather x0 -> x1, local copies, waits for them, and re-layouts: none -> 4.38 us  [local(): mine = jnp.take(all_enc, wanted, axis=0)]
    dot_general x8, matrix products: 5.86 us -> 10.1 us  [local(): part = jnp.dot(normed, w_rows, preferred_element_type=jnp.float32)]
    unnamed x11 -> x35, local copies, waits for them, and re-layouts: 1.27 us -> 4.48 us
    dot_general x1 -> x2, matrix products: 2.24 us -> 4.69 us  [project(): jnp.dot(rows.reshape(need_count * half_len, enc_width), w_both, preferred...]
    concatenate x0 -> x1, local copies, waits for them, and re-layouts: none -> 2.39 us  [local(): w_both = jnp.concatenate([w_key, w_value], axis=1)]
  transfers between devices with their start and end apart: 10 -> 11, of which waited for: 6 -> 7; matrix products, arithmetic and copies ran while one was open for 4% -> 10% of each run, Pallas kernels for 0% -> 0%
where the time goes in v6:
time: 218 us; the launch traced here: 217 us
  waiting for transfers between devices  129 us (59%)
  matrix products  21.4 us (10%)
  starting transfers between devices  16.3 us (7%)
  Pallas kernels  14.5 us (7%)
  between operations  13.7 us (6%)
  local copies, waits for them, and re-layouts  13.3 us (6%)
  other arithmetic  8.81 us (4%)
    reduce_scatter x1, waiting for transfers between devices, local(): lax.psum_scatter(partial_value.astype(jnp.bfloat16), 'tensor', scatter_di...  56.8 us
    ppermute x1, waiting for transfers between devices, local(): other_rows = lax.ppermute(mine_rows, 'tensor', pair)  38.2 us
    ppermute x3, waiting for transfers between devices, local(): up = lax.ppermute(up, 'tensor', fwd)  24 us
    pallas_call x1, Pallas kernels, attend(): pl.pallas_call(functools.partial(attend_kernel, entry_len=entry_len), out...  14.5 us
    dot_general x8, matrix products, local(): part = jnp.dot(normed, w_rows, preferred_element_type=jnp.float32)  10.1 us
    ppermute x3, starting transfers between devices, local(): down = lax.ppermute(down, 'tensor', bwd)  9.37 us
    all_gather x1, waiting for transfers between devices, local(): all_enc = lax.all_gather(payload, 'retr', axis=0, tiled=True)  6.76 us
    dot_general x1, matrix products, local(): partial_value = jnp.dot(attended, w_out, preferred_element_type=jnp.float32)  6.64 us
  transfers between devices with their start and end apart: 11, of which 7 were waited for; matrix products, arithmetic and copies ran while one was open for 10% of the time, Pallas kernels for 0%

profile of v6, /device:TPU:1, one launch (start us, length us, event | category | flops | bytes accessed | tf_op | source)
XLA Modules:
  0.0 217.0 jit_solution(17992437283784747503)
XLA Ops:
  6.5 0.8 convert_element_type.96
  7.5 0.3 copy-done
  7.8 0.9 fusion.29
  8.8 2.5 %collective-permute-start = (bf16[512,512]{1,0:T(8,128)(2,1)}, bf16[512,512]{1,0:T(8,128)(2,1)S(1)}, u32[]{:S(2)}, u32[]{:S(2)}) collective-permute-start(bf16[512,512]{1,0:T(8,128)(2,1)} %param.13), channel_id=1, source_target_pairs={{0,1},{1,2},{2,3},{3,4},{4,5},{5,6},{6,7},{7,0},{8,9},{9,10},{10,1... | collective-permute-start | bytes 1572872 | tf_op jit(solution)/shard_map/ppermute | solution.py:82
  11.3 4.0 %collective-permute-start.1 = (bf16[512,512]{1,0:T(8,128)(2,1)}, bf16[512,512]{1,0:T(8,128)(2,1)S(1)}, u32[]{:S(2)}, u32[]{:S(2)}) collective-permute-start(bf16[512,512]{1,0:T(8,128)(2,1)} %param.13), channel_id=1, source_target_pairs={{0,7},{1,0},{2,1},{3,2},{4,3},{5,4},{6,5},{7,6},{8,15},{9,8},{10,9... | collective-permute-start | bytes 1572872 | tf_op jit(solution)/shard_map/ppermute | solution.py:83
  15.4 0.8 copy.20
  16.2 0.9 fusion.75
  17.1 2.3 %constant_dynamic-update-slice_fusion.1 = bf16[1024,1024]{1,0:T(8,128)(2,1)} fusion(bf16[1024,512]{1,0:T(8,128)(2,1)} %param.19), kind=kLoop, calls=%fused_computation.93 | loop fusion | bytes 2097152
  19.4 7.7 %collective-permute-done = bf16[512,512]{1,0:T(8,128)(2,1)S(1)} collective-permute-done((bf16[512,512]{1,0:T(8,128)(2,1)}, bf16[512,512]{1,0:T(8,128)(2,1)S(1)}, u32[]{:S(2)}, u32[]{:S(2)}) %collective-permute-start) | collective-permute-done | bytes 524320 | tf_op jit(solution)/shard_map/ppermute | solution.py:82
  27.1 2.7 %collective-permute-start.3 = (bf16[512,512]{1,0:T(8,128)(2,1)S(1)}, bf16[512,512]{1,0:T(8,128)(2,1)}, u32[]{:S(2)}, u32[]{:S(2)}) collective-permute-start(bf16[512,512]{1,0:T(8,128)(2,1)S(1)} %collective-permute-done.1), channel_id=1, source_target_pairs={{0,7},{1,0},{2,1},{3,2},{4,3},{5,4},{6,5},{7,6},{8,15},{9,8},{10,9... | collective-permute-start | bytes 1572872 | tf_op jit(solution)/shard_map/ppermute | solution.py:83
  29.9 2.4 %constant_dynamic-update-slice_fusion = bf16[1024,1024]{1,0:T(8,128)(2,1)} fusion(bf16[1024,1024]{1,0:T(8,128)(2,1)} %constant_dynamic-update-slice_fusion.1, bf16[1024,512]{1,0:T(8,128)(2,1)} %param.20), kind=kLoop, calls=%fused_computation.92 | loop fusion | bytes 2097152 | tf_op jit(solution)/shard_map/concatenate | solution.py:104
  32.3 0.2 fusion.25
  32.4 8.1 %collective-permute-done.2 = bf16[512,512]{1,0:T(8,128)(2,1)S(1)} collective-permute-done((bf16[512,512]{1,0:T(8,128)(2,1)S(1)}, bf16[512,512]{1,0:T(8,128)(2,1)S(1)}, u32[]{:S(2)}, u32[]{:S(2)}) %collective-permute-start.2) | collective-permute-done | bytes 524320 | tf_op jit(solution)/shard_map/ppermute | solution.py:82
  40.6 2.7 %collective-permute-start.5 = (bf16[512,512]{1,0:T(8,128)(2,1)}, bf16[512,512]{1,0:T(8,128)(2,1)S(1)}, u32[]{:S(2)}, u32[]{:S(2)}) collective-permute-start(bf16[512,512]{1,0:T(8,128)(2,1)} %collective-permute-done.3), channel_id=1, source_target_pairs={{0,7},{1,0},{2,1},{3,2},{4,3},{5,4},{6,5},{7,6},{8,15},{9,8},{10,9... | collective-permute-start | bytes 1572872 | tf_op jit(solution)/shard_map/ppermute | solution.py:83
  43.2 0.2 fusion.4
  43.4 0.2 fusion.7
  43.6 0.2 fusion.10
  43.8 1.2 fusion.13
  45.0 8.2 %collective-permute-done.4 = bf16[512,512]{1,0:T(8,128)(2,1)S(1)} collective-permute-done((bf16[512,512]{1,0:T(8,128)(2,1)S(1)}, bf16[512,512]{1,0:T(8,128)(2,1)S(1)}, u32[]{:S(2)}, u32[]{:S(2)}) %collective-permute-start.4) | collective-permute-done | bytes 524320 | tf_op jit(solution)/shard_map/ppermute | solution.py:82
  53.3 2.7 %collective-permute-start.7 = (bf16[256,512]{1,0:T(8,128)(2,1)S(1)}, bf16[256,512]{1,0:T(8,128)(2,1)S(1)}, u32[]{:S(2)}, u32[]{:S(2)}) collective-permute-start(bf16[256,512]{1,0:T(8,128)(2,1)S(1)} %slice.65), channel_id=1, source_target_pairs={{0,7},{1,0},{2,1},{3,2},{4,3},{5,4},{6,5},{7,6},{8,15},{9,8},{10,9... | collective-permute-start | bytes 786440 | tf_op jit(solution)/shard_map/ppermute | solution.py:88
  56.0 0.2 fusion.16
  56.2 0.2 fusion.19
  56.4 3.3 %collective-permute-done.6 = bf16[256,512]{1,0:T(8,128)(2,1)S(1)} collective-permute-done((bf16[256,512]{1,0:T(8,128)(2,1)S(1)}, bf16[256,512]{1,0:T(8,128)(2,1)S(1)}, u32[]{:S(2)}, u32[]{:S(2)}) %collective-permute-start.6) | collective-permute-done | bytes 262176 | tf_op jit(solution)/shard_map/ppermute | solution.py:87
  59.7 0.2 fusion.22
  59.9 0.5 copy-done.12
  60.5 1.5 fusion.30
  62.0 1.6 convolution_add_fusion.6
  63.6 2.6 %convolution_add_fusion.5 = f32[512,512]{1,0:T(8,128)} fusion(f32[512,512]{1,0:T(8,128)S(1)} %convolution_add_fusion.6, bf16[512,512]{1,0:T(8,128)(2,1)S(1)} %collective-permute-done.1, bf16[4096,512]{1,0:T(8,128)(2,1)} %param.18, s32[]{:T(128)S(6)} %select_n.111, f32[512]{0:T(512)S(1)} %get-tuple-element.33, f32[512]{0:T(512)S(1)} %add_rsqrt_fusion), kind=kOutput, calls=%fused_computation.16 | convolution fusion | flops 269746176 | bytes 3149828 | tf_op jit(solution)/shard_map/dot_general | solution.py:130
  66.2 6.8 %all-gather.2.cloned.1.call-done = bf16[64,72,1024]{2,1,0:T(8,128)(2,1)} async-done(((bf16[4,72,1024]{2,1,0:T(8,128)(2,1)}), bf16[64,72,1024]{2,1,0:T(8,128)(2,1)}) %all-gather.2.cloned.1.call-update) | async-done | bytes 9437200 | tf_op jit(solution)/shard_map/all_gather | solution.py:98
  72.9 4.4 %gather_fusion = bf16[16,72,1024]{2,1,0:T(8,128)(2,1)S(1)} fusion(bf16[64,72,1024]{2,1,0:T(8,128)(2,1)} %all-gather.2.cloned.1.call-done, s32[1024]{0:T(1024)S(1)} %pad_clamp_fusion), kind=kCustom, calls=%fused_computation | custom fusion | bytes 4718656 | tf_op jit(solution)/shard_map/jit(_take)/gather | solution.py:99
  77.4 0.3 broadcast_select_fusion
  77.7 0.2 slice.66
  77.9 1.5 collective-permute-start.8
  79.4 0.4 copy-done.8
  79.9 0.5 convolution_add_fusion.4
  80.4 1.6 convolution_add_fusion.3
  82.1 0.5 convolution_add_fusion.2
  82.6 0.5 convolution_add_fusion.1
  83.1 1.3 fusion.2.q_ref
  84.6 2.3 %convolution_convert_fusion.2 = bf16[1024,1024]{1,0:T(8,128)(2,1)S(1)} fusion(bf16[1024,1024]{1,0:T(8,128)(2,1)S(1)} %bitcast.19, bf16[1024,1024]{1,0:T(8,128)(2,1)S(1)} %copy-done.11), kind=kOutput, calls=%fused_computation.7 | convolution fusion | flops 2148532224 | bytes 6291456 | tf_op jit(solution)/shard_map/dot_general | solution.py:107
  86.9 38.2 %collective-permute-done.8 = bf16[16,64,1024]{2,1,0:T(8,128)(2,1)S(1)} collective-permute-done((bf16[16,64,1024]{2,1,0:T(8,128)(2,1)S(1)}, bf16[16,64,1024]{2,1,0:T(8,128)(2,1)S(1)}, u32[]{:S(2)}, u32[]{:S(2)}) %collective-permute-start.8) | collective-permute-done | bytes 2097184 | tf_op jit(solution)/shard_map/ppermute | solution.py:102
  125.1 2.4 %convolution_convert_fusion.1 = bf16[1024,1024]{1,0:T(8,128)(2,1)S(1)} fusion(bf16[1024,1024]{1,0:T(8,128)(2,1)S(1)} %bitcast.21, bf16[1024,1024]{1,0:T(8,128)(2,1)S(1)} %copy-done.11), kind=kOutput, calls=%fused_computation.6 | convolution fusion | flops 2148532224 | bytes 6291456 | tf_op jit(solution)/shard_map/dot_general | solution.py:107
  127.5 2.3 %fusion.1.kv0_ref.kv1_ref = bf16[16,136,1024]{2,1,0:T(8,128)(2,1)} fusion(bf16[16,1,128]{2,1,0:T(2,128)(2,1)S(1)} %copy.23, bf16[16,64,1024]{2,1,0:T(8,128)(2,1)S(1)} %bitcast.18, bf16[16,64,1024]{2,1,0:T(8,128)(2,1)S(1)} %bitcast.17), kind=kLoop, calls=%fused_computation.4 | loop fusion | flops 17825792 | bytes 8654848 | tf_op jit(solution)/shard_map/concatenate | solution.py:118
  129.7 0.6 iota.3.flat_ref
  130.3 14.5 %shard_map.91 = bf16[512,512]{1,0:T(8,128)(2,1)} custom-call(s32[16]{0:T(128)} %iota.3.flat_ref, bf16[512,512]{1,0:T(8,128)(2,1)} %fusion.2.q_ref, bf16[16,136,1024]{2,1,0:T(8,128)(2,1)} %fusion.1.kv0_ref.kv1_ref, bf16[16,136,1024]{2,1,0:T(8,128)(2,1)} %fusion.1.kv0_ref.kv1_ref), custom_call_target="tpu_custom_call" | custom-call | tf_op jit(solution)/shard_map/pallas_call | solution.py:59
  144.8 6.6 %convolution_convert_fusion = bf16[512,4096]{1,0:T(8,128)(2,1)} fusion(bf16[512,512]{1,0:T(8,128)(2,1)} %shard_map.91, bf16[512,4096]{1,0:T(8,128)(2,1)} %param.21), kind=kOutput, calls=%fused_computation.3 | convolution fusion | flops 2149580800 | bytes 8912896 | tf_op jit(solution)/shard_map/dot_general | solution.py:135
  151.5 56.8 %reduce-scatter.2.cloned.1.call-done = bf16[512,512]{1,0:T(8,128)(2,1)} async-done(((bf16[512,4096]{1,0:T(8,128)(2,1)}), bf16[512,512]{1,0:T(8,128)(2,1)}) %reduce-scatter.2.cloned.1.call-update) | async-done | bytes 524304 | tf_op jit(solution)/shard_map/reduce_scatter | solution.py:136
  208.2 2.0 fusion.28
  (55 shorter events, 1.0 us)
Async XLA Ops:
  6.5 1.2 copy-start
  6.5 25.7 %copy-start.1 = (bf16[512,512]{1,0:T(8,128)(2,1)S(1)}, bf16[512,512]{1,0:T(8,128)(2,1)}, u32[]{:S(2)}) copy-start(bf16[512,512]{1,0:T(8,128)(2,1)} %param.13) | copy-start | bytes 1572868
  6.5 66.4 %all-gather.2.cloned.1.call-start = ((), (), s32[]{:S(2)}) async-start(), calls=%async_computation.1 | async-start | bytes 10027008 | tf_op jit(solution)/shard_map/all_gather | solution.py:98
  8.7 199.5 %reduce-scatter.2.cloned.1.call-start = ((), (), s32[]{:S(2)}) async-start(), calls=%async_computation.2 | async-start | bytes 4718592 | tf_op jit(solution)/shard_map/reduce_scatter | solution.py:136
  8.8 18.3 %collective-permute-start = (bf16[512,512]{1,0:T(8,128)(2,1)}, bf16[512,512]{1,0:T(8,128)(2,1)S(1)}, u32[]{:S(2)}, u32[]{:S(2)}) collective-permute-start(bf16[512,512]{1,0:T(8,128)(2,1)} %param.13), channel_id=1, source_target_pairs={{0,1},{1,2},{2,3},{3,4},{4,5},{5,6},{6,7},{7,0},{8,9},{9,10},{10,1... | collective-permute-start | bytes 1572872 | tf_op jit(solution)/shard_map/ppermute | solution.py:82
  11.3 15.8 %collective-permute-start.1 = (bf16[512,512]{1,0:T(8,128)(2,1)}, bf16[512,512]{1,0:T(8,128)(2,1)S(1)}, u32[]{:S(2)}, u32[]{:S(2)}) collective-permute-start(bf16[512,512]{1,0:T(8,128)(2,1)} %param.13), channel_id=1, source_target_pairs={{0,7},{1,0},{2,1},{3,2},{4,3},{5,4},{6,5},{7,6},{8,15},{9,8},{10,9... | collective-permute-start | bytes 1572872 | tf_op jit(solution)/shard_map/ppermute | solution.py:83
  27.1 13.4 %collective-permute-start.2 = (bf16[512,512]{1,0:T(8,128)(2,1)S(1)}, bf16[512,512]{1,0:T(8,128)(2,1)S(1)}, u32[]{:S(2)}, u32[]{:S(2)}) collective-permute-start(bf16[512,512]{1,0:T(8,128)(2,1)S(1)} %collective-permute-done), channel_id=1, source_target_pairs={{0,1},{1,2},{2,3},{3,4},{4,5},{5,6},{6,7},{7,0},{8,9},{9,10},{10,1... | collective-permute-start | bytes 1572872 | tf_op jit(solution)/shard_map/ppermute | solution.py:82
  27.1 13.4 %collective-permute-start.3 = (bf16[512,512]{1,0:T(8,128)(2,1)S(1)}, bf16[512,512]{1,0:T(8,128)(2,1)}, u32[]{:S(2)}, u32[]{:S(2)}) collective-permute-start(bf16[512,512]{1,0:T(8,128)(2,1)S(1)} %collective-permute-done.1), channel_id=1, source_target_pairs={{0,7},{1,0},{2,1},{3,2},{4,3},{5,4},{6,5},{7,6},{8,15},{9,8},{10,9... | collective-permute-start | bytes 1572872 | tf_op jit(solution)/shard_map/ppermute | solution.py:83
  40.5 23.1 %copy-start.9 = (bf16[512,512]{1,0:T(8,128)(2,1)}, bf16[512,512]{1,0:T(8,128)(2,1)S(1)}, u32[]{:S(2)}) copy-start(bf16[512,512]{1,0:T(8,128)(2,1)S(1)} %collective-permute-done.2) | copy-start | bytes 1572868
  40.5 12.6 %collective-permute-start.4 = (bf16[512,512]{1,0:T(8,128)(2,1)S(1)}, bf16[512,512]{1,0:T(8,128)(2,1)S(1)}, u32[]{:S(2)}, u32[]{:S(2)}) collective-permute-start(bf16[512,512]{1,0:T(8,128)(2,1)S(1)} %collective-permute-done.2), channel_id=1, source_target_pairs={{0,1},{1,2},{2,3},{3,4},{4,5},{5,6},{6,7},{7,0},{8,9},{9,10},{10,1... | collective-permute-start | bytes 1572872 | tf_op jit(solution)/shard_map/ppermute | solution.py:82
  40.6 12.7 %collective-permute-start.5 = (bf16[512,512]{1,0:T(8,128)(2,1)}, bf16[512,512]{1,0:T(8,128)(2,1)S(1)}, u32[]{:S(2)}, u32[]{:S(2)}) collective-permute-start(bf16[512,512]{1,0:T(8,128)(2,1)} %collective-permute-done.3), channel_id=1, source_target_pairs={{0,7},{1,0},{2,1},{3,2},{4,3},{5,4},{6,5},{7,6},{8,15},{9,8},{10,9... | collective-permute-start | bytes 1572872 | tf_op jit(solution)/shard_map/ppermute | solution.py:83
  53.1 6.7 %copy-start.4 = (bf16[512,512]{1,0:T(8,128)(2,1)}, bf16[512,512]{1,0:T(8,128)(2,1)S(1)}, u32[]{:S(2)}) copy-start(bf16[512,512]{1,0:T(8,128)(2,1)S(1)} %collective-permute-done.4) | copy-start | bytes 1572868
  53.2 6.5 %collective-permute-start.6 = (bf16[256,512]{1,0:T(8,128)(2,1)S(1)}, bf16[256,512]{1,0:T(8,128)(2,1)S(1)}, u32[]{:S(2)}, u32[]{:S(2)}) collective-permute-start(bf16[256,512]{1,0:T(8,128)(2,1)S(1)} %slice.64), channel_id=1, source_target_pairs={{0,1},{1,2},{2,3},{3,4},{4,5},{5,6},{6,7},{7,0},{8,9},{9,10},{10,1... | collective-permute-start | bytes 786440 | tf_op jit(solution)/shard_map/ppermute | solution.py:87
  53.3 6.6 %copy-start.6 = (bf16[512,512]{1,0:T(8,128)(2,1)}, bf16[512,512]{1,0:T(8,128)(2,1)S(1)}, u32[]{:S(2)}) copy-start(bf16[512,512]{1,0:T(8,128)(2,1)S(1)} %collective-permute-done.5) | copy-start | bytes 1572868
  53.3 6.4 %collective-permute-start.7 = (bf16[256,512]{1,0:T(8,128)(2,1)S(1)}, bf16[256,512]{1,0:T(8,128)(2,1)S(1)}, u32[]{:S(2)}, u32[]{:S(2)}) collective-permute-start(bf16[256,512]{1,0:T(8,128)(2,1)S(1)} %slice.65), channel_id=1, source_target_pairs={{0,7},{1,0},{2,1},{3,2},{4,3},{5,4},{6,5},{7,6},{8,15},{9,8},{10,9... | collective-permute-start | bytes 786440 | tf_op jit(solution)/shard_map/ppermute | solution.py:88
  59.7 0.7 copy-start.12
  59.7 0.8 copy-start.14
  77.3 2.1 copy-start.3
  77.3 2.5 %copy-start.8 = (bf16[4096,512]{1,0:T(8,128)(2,1)S(1)}, bf16[4096,512]{1,0:T(8,128)(2,1)}, u32[]{:S(2)}) copy-start(bf16[4096,512]{1,0:T(8,128)(2,1)} %param.18) | copy-start | bytes 12582916
  77.3 2.6 %copy-start.10 = (bf16[512,512]{1,0:T(8,128)(2,1)S(1)}, bf16[512,512]{1,0:T(8,128)(2,1)}, u32[]{:S(2)}) copy-start(bf16[512,512]{1,0:T(8,128)(2,1)} %copy-done.9) | copy-start | bytes 1572868
  77.9 4.2 %copy-start.5 = (bf16[512,512]{1,0:T(8,128)(2,1)S(1)}, bf16[512,512]{1,0:T(8,128)(2,1)}, u32[]{:S(2)}) copy-start(bf16[512,512]{1,0:T(8,128)(2,1)} %copy-done.4) | copy-start | bytes 1572868
  77.9 47.2 %collective-permute-start.8 = (bf16[16,64,1024]{2,1,0:T(8,128)(2,1)S(1)}, bf16[16,64,1024]{2,1,0:T(8,128)(2,1)S(1)}, u32[]{:S(2)}, u32[]{:S(2)}) collective-permute-start(bf16[16,64,1024]{2,1,0:T(8,128)(2,1)S(1)} %slice.66), channel_id=1, source_target_pairs={{0,1},{1,0},{2,3},{3,2},{4,5},{5,4},{6,7},{7,6},{8,9},{9,8},{10,11... | collective-permute-start | bytes 6291464 | tf_op jit(solution)/shard_map/ppermute | solution.py:102
  79.9 2.7 %copy-start.7 = (bf16[512,512]{1,0:T(8,128)(2,1)S(1)}, bf16[512,512]{1,0:T(8,128)(2,1)}, u32[]{:S(2)}) copy-start(bf16[512,512]{1,0:T(8,128)(2,1)} %copy-done.6) | copy-start | bytes 1572868
  80.4 2.7 %copy-start.13 = (bf16[256,512]{1,0:T(8,128)(2,1)S(1)}, bf16[256,512]{1,0:T(8,128)(2,1)}, u32[]{:S(2)}) copy-start(bf16[256,512]{1,0:T(8,128)(2,1)} %copy-done.12) | copy-start | bytes 786436
  80.4 2.7 %copy-start.15 = (bf16[256,512]{1,0:T(8,128)(2,1)S(1)}, bf16[256,512]{1,0:T(8,128)(2,1)}, u32[]{:S(2)}) copy-start(bf16[256,512]{1,0:T(8,128)(2,1)} %copy-done.14) | copy-start | bytes 786436
  82.1 2.5 %copy-start.11 = (bf16[1024,1024]{1,0:T(8,128)(2,1)S(1)}, bf16[1024,1024]{1,0:T(8,128)(2,1)}, u32[]{:S(2)}) copy-start(bf16[1024,1024]{1,0:T(8,128)(2,1)} %constant_dynamic-update-slice_fusion) | copy-start | bytes 6291460
  151.4 56.8 %copy-start.2 = (bf16[512,512]{1,0:T(8,128)(2,1)S(1)}, bf16[512,512]{1,0:T(8,128)(2,1)}, u32[]{:S(2)}) copy-start(bf16[512,512]{1,0:T(8,128)(2,1)} %param.13) | copy-start | bytes 1572868
Sparse Core Ops, SparseCore 0:
  9.2 63.7 all-gather.1
  151.6 56.5 reduce-scatter.1

commit v7 on v6

v7 whole, which is shorter than its diff:
```python
import functools
import math

import jax
import jax.numpy as jnp
from jax import lax
from jax.experimental import pallas as pl
from jax.experimental.pallas import tpu as pltpu
from jax.sharding import PartitionSpec as P

HD = 128
NBRS = 2
BLOCK = 32
CAP = 2
PAIR_CHUNKS = 4


def attend_kernel(q_ref, a_ref, b_ref, l_ref, o_ref):
    head_cols = q_ref.shape[1]
    half_len = a_ref.shape[1]
    factor = 1.0 / math.sqrt(HD)
    nt = (((1,), (1,)), ((), ()))
    lives = [l_ref[e, 0:1, :].astype(jnp.float32) for e in range(NBRS)]
    opens = [live > 0 for live in lives]
    for h in range(head_cols // HD):
        cols = slice(h * HD, (h + 1) * HD)
        vcols = slice(head_cols + h * HD, head_cols + (h + 1) * HD)
        qh = q_ref[:, cols]
        scores = []
        for e in range(NBRS):
            keys = jnp.concatenate([a_ref[e, :, cols], b_ref[e, :, cols]], axis=0)
            s = lax.dot_general(qh, keys, nt, preferred_element_type=jnp.float32) * factor
            scores.append(jnp.where(opens[e], s, -1e30))
        row_max = scores[0].max(axis=-1, keepdims=True)
        for s in scores[1:]:
            row_max = jnp.maximum(row_max, s.max(axis=-1, keepdims=True))
        weights = [jnp.exp(s - row_max) * live for s, live in zip(scores, lives)]
        total = sum(jnp.sum(w, axis=-1, keepdims=True) for w in weights)
        att = None
        for e, w in enumerate(weights):
            probs = (w / total).astype(jnp.bfloat16)
            values = jnp.concatenate([a_ref[e, :, vcols], b_ref[e, :, vcols]], axis=0)
            part = jnp.dot(probs, values, preferred_element_type=jnp.float32)
            att = part if att is None else att + part
        o_ref[:, cols] = att.astype(o_ref.dtype)


def attend(queries, kv_a, kv_b, live):
    tok_rows, head_cols = queries.shape
    segment_count = kv_a.shape[0] // NBRS
    seg_rows = tok_rows // segment_count
    half_len, kv_cols = kv_a.shape[1], kv_a.shape[2]
    live_rows, key_count = live.shape[1], live.shape[2]
    return pl.pallas_call(
        attend_kernel,
        out_shape=jax.ShapeDtypeStruct((tok_rows, head_cols), jnp.bfloat16),
        grid=(segment_count,),
        in_specs=[
            pl.BlockSpec((seg_rows, head_cols), lambda s: (s, 0)),
            pl.BlockSpec((NBRS, half_len, kv_cols), lambda s: (s, 0, 0)),
            pl.BlockSpec((NBRS, half_len, kv_cols), lambda s: (s, 0, 0)),
            pl.BlockSpec((NBRS, live_rows, key_count), lambda s: (s, 0, 0)),
        ],
        out_specs=pl.BlockSpec((seg_rows, head_cols), lambda s: (s, 0)),
    )(queries, kv_a, kv_b, live)


def local(dp_count, retr_count, tensor_count, hidden_in, norm_gain, nbr_table, encodings, enc_mask, w_query, w_key, w_value, w_out):
    segment_count = nbr_table.shape[0]
    nb_dev, entry_len, enc_width = encodings.shape
    mask_cols = enc_mask.shape[1]
    head_cols = w_key.shape[1]
    wanted = nbr_table.reshape(-1)
    need_count = wanted.shape[0]

    feat = hidden_in.shape[1]
    t = lax.axis_index("tensor")
    fwd = [(i, (i + 1) % tensor_count) for i in range(tensor_count)]
    bwd = [(i, (i - 1) % tensor_count) for i in range(tensor_count)]
    pieces = [(0, hidden_in)]
    up = down = hidden_in
    half_ring = tensor_count // 2
    for k in range(1, half_ring):
        up = lax.ppermute(up, "tensor", fwd)
        down = lax.ppermute(down, "tensor", bwd)
        pieces.append((k, up))
        pieces.append((tensor_count - k, down))
    half_rows = hidden_in.shape[0] // 2
    top = lax.ppermute(up[:half_rows], "tensor", fwd)
    bottom = lax.ppermute(down[half_rows:], "tensor", bwd)
    pieces.append((half_ring, jnp.concatenate([top, bottom], axis=0)))

    half = t % 2
    half_len = entry_len // 2
    enc_rows = lax.dynamic_slice_in_dim(encodings, half * half_len, half_len, axis=1)
    key_live = jnp.repeat(enc_mask, BLOCK, axis=1).astype(jnp.bfloat16)
    mask_rows = jnp.zeros((nb_dev, 8, enc_width), jnp.bfloat16)
    mask_rows = mask_rows.at[:, 0, :entry_len].set(key_live)
    payload = jnp.concatenate([enc_rows, mask_rows], axis=1)
    all_enc = lax.all_gather(payload, "retr", axis=0, tiled=True)
    mine = jnp.take(all_enc, wanted, axis=0)
    mine_rows = mine[:, :half_len]
    pair = [(i, i ^ 1) for i in range(tensor_count)]
    chunk = need_count // PAIR_CHUNKS
    other_chunks = [
        lax.ppermute(mine_rows[c * chunk:(c + 1) * chunk], "tensor", pair)
        for c in range(PAIR_CHUNKS)
    ]

    w_both = jnp.concatenate([w_key, w_value], axis=1)

    def project(rows):
        count = rows.shape[0]
        out = jnp.dot(
            rows.reshape(count * half_len, enc_width), w_both,
            preferred_element_type=jnp.float32,
        )
        return out.astype(jnp.bfloat16).reshape(count, half_len, 2 * head_cols)

    kv_mine = project(mine_rows)
    kv_other = jnp.concatenate([project(c) for c in other_chunks], axis=0)
    live_row = jnp.roll(mine[:, half_len:half_len + 8, :entry_len], -half * half_len, axis=-1)

    widened = [p.astype(jnp.float32) for _, p in pieces]
    sum_sq = sum(jnp.sum(w * w, axis=-1, keepdims=True) for w in widened)
    inv = lax.rsqrt(sum_sq / (feat * tensor_count) + 1e-05)
    acc = None
    for (k, _), w in zip(pieces, widened):
        src_block = (t - k) % tensor_count
        gain = lax.dynamic_slice_in_dim(norm_gain, src_block * feat, feat)
        normed = (w * inv * gain).astype(jnp.bfloat16)
        w_rows = lax.dynamic_slice_in_dim(w_query, src_block * feat, feat, axis=0)
        part = jnp.dot(normed, w_rows, preferred_element_type=jnp.float32)
        acc = part if acc is None else acc + part
    queries = acc.astype(jnp.bfloat16)

    attended = attend(queries, kv_mine, kv_other, live_row)
    partial_value = jnp.dot(attended, w_out, preferred_element_type=jnp.float32)
    summed = lax.psum_scatter(
        partial_value.astype(jnp.bfloat16), "tensor", scatter_dimension=1, tiled=True
    )
    return (hidden_in.astype(jnp.float32) + summed.astype(jnp.float32)).astype(jnp.bfloat16)


def solution(mesh):
    in_specs = (
        P(("dp", "retr"), "tensor"),
        P(),
        P(("dp", "retr"), None),
        P("retr", None, None),
        P("retr", None),
        P(None, "tensor"),
        P(None, "tensor"),
        P(None, "tensor"),
        P("tensor", None),
    )
    out_specs = P(("dp", "retr"), "tensor")
    body = functools.partial(local, mesh.shape["dp"], mesh.shape["retr"], mesh.shape["tensor"])
    return jax.shard_map(body, mesh=mesh, in_specs=in_specs, out_specs=out_specs, check_vma=False)
```

time: 218 us -> 214 us (0.982)
  local copies, waits for them, and re-layouts: 13.3 us -> 10.3 us
  matrix products: 21.4 us -> 19.1 us
    dot_general x8, matrix products: 10.1 us -> 5.89 us  [local(): part = jnp.dot(normed, w_rows, preferred_element_type=jnp.float32)]
    unnamed x35 -> x16, local copies, waits for them, and re-layouts: 4.48 us -> 2.62 us
    dot_general x2 -> x5, matrix products: 4.69 us -> 6.55 us  [project(): jnp.dot(rows.reshape(count * half_len, enc_width), w_both, preferred_elem...]
    ppermute x1 -> x4, waiting for transfers between devices: 38.2 us -> 37.4 us  [local(): lax.ppermute(mine_rows[c * chunk:(c + 1) * chunk], 'tensor', pair)]
  transfers between devices with their start and end apart: 11 -> 14, of which waited for: 7 -> 10; matrix products, arithmetic and copies ran while one was open for 10% -> 9% of each run, Pallas kernels for 0% -> 0%
where the time goes in v7:
time: 214 us
  waiting for transfers between devices  130 us (61%)
  matrix products  19.1 us (9%)
  starting transfers between devices  18 us (8%)
  Pallas kernels  13.8 us (6%)
  between operations  13.6 us (6%)
  local copies, waits for them, and re-layouts  10.3 us (5%)
  other arithmetic  8.84 us (4%)
    reduce_scatter x1, waiting for transfers between devices, local(): lax.psum_scatter(partial_value.astype(jnp.bfloat16), 'tensor', scatter_di...  56.8 us
    ppermute x4, waiting for transfers between devices, local(): lax.ppermute(mine_rows[c * chunk:(c + 1) * chunk], 'tensor', pair)  37.4 us
    ppermute x3, waiting for transfers between devices, local(): up = lax.ppermute(up, 'tensor', fwd)  25.1 us
    pallas_call x1, Pallas kernels, attend(): pl.pallas_call(attend_kernel, out_shape=jax.ShapeDtypeStruct((tok_rows, h...  13.8 us
    ppermute x3, starting transfers between devices, local(): down = lax.ppermute(down, 'tensor', bwd)  9.38 us
    all_gather x1, waiting for transfers between devices, local(): all_enc = lax.all_gather(payload, 'retr', axis=0, tiled=True)  7.37 us
    dot_general x1, matrix products, local(): partial_value = jnp.dot(attended, w_out, preferred_element_type=jnp.float32)  6.64 us
    dot_general x5, matrix products, project(): jnp.dot(rows.reshape(count * half_len, enc_width), w_both, preferred_elem...  6.55 us
  transfers between devices with their start and end apart: 14, of which 10 were waited for; matrix products, arithmetic and copies ran while one was open for 9% of the time, Pallas kernels for 0%

profile of v7, /device:TPU:1, one launch (start us, length us, event | category | flops | bytes accessed | tf_op | source)
XLA Modules:
  0.0 213.6 jit_solution(15157669640392503560)
XLA Ops:
  6.6 0.8 convert_element_type.105
  7.6 0.2 copy-done
  7.8 0.9 fusion.27
  8.8 2.5 %collective-permute-start = (bf16[512,512]{1,0:T(8,128)(2,1)S(1)}, bf16[512,512]{1,0:T(8,128)(2,1)S(1)}, u32[]{:S(2)}, u32[]{:S(2)}) collective-permute-start(bf16[512,512]{1,0:T(8,128)(2,1)S(1)} %copy-done.1), channel_id=1, source_target_pairs={{0,1},{1,2},{2,3},{3,4},{4,5},{5,6},{6,7},{7,0},{8,9},{9,10},{10,1... | collective-permute-start | bytes 1572872 | tf_op jit(solution)/shard_map/ppermute | solution.py:84
  11.3 4.0 %collective-permute-start.1 = (bf16[512,512]{1,0:T(8,128)(2,1)S(1)}, bf16[512,512]{1,0:T(8,128)(2,1)S(1)}, u32[]{:S(2)}, u32[]{:S(2)}) collective-permute-start(bf16[512,512]{1,0:T(8,128)(2,1)S(1)} %copy-done.1), channel_id=1, source_target_pairs={{0,7},{1,0},{2,1},{3,2},{4,3},{5,4},{6,5},{7,6},{8,15},{9,8},{10,9... | collective-permute-start | bytes 1572872 | tf_op jit(solution)/shard_map/ppermute | solution.py:85
  15.6 2.3 %constant_dynamic-update-slice_fusion.1 = bf16[1024,1024]{1,0:T(8,128)(2,1)} fusion(bf16[1024,512]{1,0:T(8,128)(2,1)} %param.17), kind=kLoop, calls=%fused_computation.93 | loop fusion | bytes 2097152
  17.9 9.0 %collective-permute-done = bf16[512,512]{1,0:T(8,128)(2,1)S(1)} collective-permute-done((bf16[512,512]{1,0:T(8,128)(2,1)S(1)}, bf16[512,512]{1,0:T(8,128)(2,1)S(1)}, u32[]{:S(2)}, u32[]{:S(2)}) %collective-permute-start) | collective-permute-done | bytes 524320 | tf_op jit(solution)/shard_map/ppermute | solution.py:84
  26.9 2.7 %collective-permute-start.3 = (bf16[512,512]{1,0:T(8,128)(2,1)S(1)}, bf16[512,512]{1,0:T(8,128)(2,1)}, u32[]{:S(2)}, u32[]{:S(2)}) collective-permute-start(bf16[512,512]{1,0:T(8,128)(2,1)S(1)} %collective-permute-done.1), channel_id=1, source_target_pairs={{0,7},{1,0},{2,1},{3,2},{4,3},{5,4},{6,5},{7,6},{8,15},{9,8},{10,9... | collective-permute-start | bytes 1572872 | tf_op jit(solution)/shard_map/ppermute | solution.py:85
  29.6 2.3 %constant_dynamic-update-slice_fusion = bf16[1024,1024]{1,0:T(8,128)(2,1)} fusion(bf16[1024,1024]{1,0:T(8,128)(2,1)} %constant_dynamic-update-slice_fusion.1, bf16[1024,512]{1,0:T(8,128)(2,1)} %param.18), kind=kLoop, calls=%fused_computation.92 | loop fusion | bytes 2097152 | tf_op jit(solution)/shard_map/concatenate | solution.py:110
  32.1 8.2 %collective-permute-done.2 = bf16[512,512]{1,0:T(8,128)(2,1)S(1)} collective-permute-done((bf16[512,512]{1,0:T(8,128)(2,1)S(1)}, bf16[512,512]{1,0:T(8,128)(2,1)S(1)}, u32[]{:S(2)}, u32[]{:S(2)}) %collective-permute-start.2) | collective-permute-done | bytes 524320 | tf_op jit(solution)/shard_map/ppermute | solution.py:84
  40.3 2.7 %collective-permute-start.5 = (bf16[512,512]{1,0:T(8,128)(2,1)}, bf16[512,512]{1,0:T(8,128)(2,1)S(1)}, u32[]{:S(2)}, u32[]{:S(2)}) collective-permute-start(bf16[512,512]{1,0:T(8,128)(2,1)} %collective-permute-done.3), channel_id=1, source_target_pairs={{0,7},{1,0},{2,1},{3,2},{4,3},{5,4},{6,5},{7,6},{8,15},{9,8},{10,9... | collective-permute-start | bytes 1572872 | tf_op jit(solution)/shard_map/ppermute | solution.py:85
  43.2 0.2 fusion.5
  43.4 1.4 fusion.11
  44.9 8.0 %collective-permute-done.4 = bf16[512,512]{1,0:T(8,128)(2,1)S(1)} collective-permute-done((bf16[512,512]{1,0:T(8,128)(2,1)S(1)}, bf16[512,512]{1,0:T(8,128)(2,1)S(1)}, u32[]{:S(2)}, u32[]{:S(2)}) %collective-permute-start.4) | collective-permute-done | bytes 524320 | tf_op jit(solution)/shard_map/ppermute | solution.py:84
  53.0 2.7 %collective-permute-start.7 = (bf16[256,512]{1,0:T(8,128)(2,1)S(1)}, bf16[256,512]{1,0:T(8,128)(2,1)S(1)}, u32[]{:S(2)}, u32[]{:S(2)}) collective-permute-start(bf16[256,512]{1,0:T(8,128)(2,1)S(1)} %slice.62), channel_id=1, source_target_pairs={{0,7},{1,0},{2,1},{3,2},{4,3},{5,4},{6,5},{7,6},{8,15},{9,8},{10,9... | collective-permute-start | bytes 786440 | tf_op jit(solution)/shard_map/ppermute | solution.py:90
  56.1 3.3 %collective-permute-done.6 = bf16[256,512]{1,0:T(8,128)(2,1)S(1)} collective-permute-done((bf16[256,512]{1,0:T(8,128)(2,1)S(1)}, bf16[256,512]{1,0:T(8,128)(2,1)S(1)}, u32[]{:S(2)}, u32[]{:S(2)}) %collective-permute-start.6) | collective-permute-done | bytes 262176 | tf_op jit(solution)/shard_map/ppermute | solution.py:89
  59.6 0.5 fusion.28
  60.1 0.5 convolution_add_fusion.6
  60.6 0.5 convolution_add_fusion.5
  61.1 0.5 convolution_add_fusion.4
  61.7 1.6 convolution_add_fusion.3
  63.3 0.5 convolution_add_fusion.2
  63.8 0.5 convolution_add_fusion.1
  64.3 1.3 fusion.q_ref
  65.6 7.4 %all-gather.2.cloned.1.call-done = bf16[64,72,1024]{2,1,0:T(8,128)(2,1)} async-done(((bf16[4,72,1024]{2,1,0:T(8,128)(2,1)}), bf16[64,72,1024]{2,1,0:T(8,128)(2,1)}) %all-gather.2.cloned.1.call-update) | async-done | bytes 9437200 | tf_op jit(solution)/shard_map/all_gather | solution.py:100
  72.9 4.4 %gather_fusion = bf16[16,72,1024]{2,1,0:T(8,128)(2,1)S(1)} fusion(bf16[64,72,1024]{2,1,0:T(8,128)(2,1)} %all-gather.2.cloned.1.call-done, s32[1024]{0:T(1024)S(1)} %pad_clamp_fusion), kind=kCustom, calls=%fused_computation | custom fusion | bytes 4718656 | tf_op jit(solution)/shard_map/jit(_take)/gather | solution.py:101
  77.3 0.3 broadcast_select_fusion
  77.6 0.2 fusion.72
  77.9 0.2 slice.63
  78.1 1.5 collective-permute-start.11
  79.6 0.2 collective-permute-start.8
  79.8 1.3 collective-permute-start.9
  81.1 0.2 collective-permute-start.10
  81.3 3.7 %convolution_convert_fusion.1 = bf16[1024,1024]{1,0:T(8,128)(2,1)} fusion(bf16[1024,1024]{1,0:T(8,128)(2,1)S(1)} %bitcast.25, bf16[1024,1024]{1,0:T(8,128)(2,1)S(1)} %copy-done.4), kind=kOutput, calls=%fused_computation.4 | convolution fusion | flops 2148532224 | bytes 6291456 | tf_op jit(solution)/shard_map/dot_general | solution.py:114
  85.0 0.7 fusion.61.l_ref
  85.7 5.9 %collective-permute-done.11 = bf16[4,64,1024]{2,1,0:T(8,128)(2,1)S(1)} collective-permute-done((bf16[4,64,1024]{2,1,0:T(8,128)(2,1)S(1)}, bf16[4,64,1024]{2,1,0:T(8,128)(2,1)S(1)}, u32[]{:S(2)}, u32[]{:S(2)}) %collective-permute-start.11) | collective-permute-done | bytes 524320 | tf_op jit(solution)/shard_map/ppermute | solution.py:106
  91.6 0.7 convolution_convert_fusion.2
  92.3 10.5 %collective-permute-done.8 = bf16[4,64,1024]{2,1,0:T(8,128)(2,1)S(1)} collective-permute-done((bf16[4,64,1024]{2,1,0:T(8,128)(2,1)S(1)}, bf16[4,64,1024]{2,1,0:T(8,128)(2,1)S(1)}, u32[]{:S(2)}, u32[]{:S(2)}) %collective-permute-start.8) | collective-permute-done | bytes 524320 | tf_op jit(solution)/shard_map/ppermute | solution.py:106
  102.8 0.7 convolution_convert_fusion.5
  103.5 10.5 %collective-permute-done.9 = bf16[4,64,1024]{2,1,0:T(8,128)(2,1)S(1)} collective-permute-done((bf16[4,64,1024]{2,1,0:T(8,128)(2,1)S(1)}, bf16[4,64,1024]{2,1,0:T(8,128)(2,1)S(1)}, u32[]{:S(2)}, u32[]{:S(2)}) %collective-permute-start.9) | collective-permute-done | bytes 524320 | tf_op jit(solution)/shard_map/ppermute | solution.py:106
  114.1 0.7 convolution_convert_fusion.4
  114.8 10.5 %collective-permute-done.10 = bf16[4,64,1024]{2,1,0:T(8,128)(2,1)S(1)} collective-permute-done((bf16[4,64,1024]{2,1,0:T(8,128)(2,1)S(1)}, bf16[4,64,1024]{2,1,0:T(8,128)(2,1)S(1)}, u32[]{:S(2)}, u32[]{:S(2)}) %collective-permute-start.10) | collective-permute-done | bytes 524320 | tf_op jit(solution)/shard_map/ppermute | solution.py:106
  125.3 0.7 convolution_convert_fusion.3
  126.0 1.6 pad_maximum_fusion.b_ref
  127.6 13.8 %shard_map.91 = bf16[512,512]{1,0:T(8,128)(2,1)} custom-call(bf16[512,512]{1,0:T(8,128)(2,1)} %fusion.q_ref, bf16[16,64,1024]{2,1,0:T(8,128)(2,1)} %bitcast.24, bf16[16,64,1024]{2,1,0:T(8,128)(2,1)} %pad_maximum_fusion.b_ref, bf16[16,8,128]{2,1,0:T(8,128)(2,1)} %fusion.61.l_ref), custom_call_target="tpu_custom_call" | custom-call | tf_op jit(solution)/shard_map/pallas_call | solution.py:54
  141.4 6.6 %convolution_convert_fusion = bf16[512,4096]{1,0:T(8,128)(2,1)} fusion(bf16[512,512]{1,0:T(8,128)(2,1)} %shard_map.91, bf16[512,4096]{1,0:T(8,128)(2,1)} %param.19), kind=kOutput, calls=%fused_computation.1 | convolution fusion | flops 2149580800 | bytes 8912896 | tf_op jit(solution)/shard_map/dot_general | solution.py:138
  148.1 56.8 %reduce-scatter.2.cloned.1.call-done = bf16[512,512]{1,0:T(8,128)(2,1)} async-done(((bf16[512,4096]{1,0:T(8,128)(2,1)}), bf16[512,512]{1,0:T(8,128)(2,1)}) %reduce-scatter.2.cloned.1.call-update) | async-done | bytes 524304 | tf_op jit(solution)/shard_map/reduce_scatter | solution.py:139
  204.8 2.0 fusion.26
  (44 shorter events, 1.9 us)
Async XLA Ops:
  6.5 1.2 copy-start
  6.5 2.2 %copy-start.1 = (bf16[512,512]{1,0:T(8,128)(2,1)S(1)}, bf16[512,512]{1,0:T(8,128)(2,1)}, u32[]{:S(2)}) copy-start(bf16[512,512]{1,0:T(8,128)(2,1)} %param.11) | copy-start | bytes 1572868
  6.5 8.8 %copy-start.6 = (s32[8,2]{0,1:T(2,128)S(1)}, s32[8,2]{0,1:T(2,128)}, u32[]{:S(2)}) copy-start(s32[8,2]{0,1:T(2,128)} %param.13) | copy-start | bytes 196
  6.5 9.0 %copy-start.5 = (f32[4096]{0:T(1024)S(1)}, f32[4096]{0:T(1024)}, u32[]{:S(2)}) copy-start(f32[4096]{0:T(1024)} %param.12) | copy-start | bytes 49156
  6.5 66.4 %all-gather.2.cloned.1.call-start = ((), (), s32[]{:S(2)}) async-start(), calls=%async_computation.1 | async-start | bytes 10027008 | tf_op jit(solution)/shard_map/all_gather | solution.py:100
  8.7 196.1 %reduce-scatter.2.cloned.1.call-start = ((), (), s32[]{:S(2)}) async-start(), calls=%async_computation.2 | async-start | bytes 4718592 | tf_op jit(solution)/shard_map/reduce_scatter | solution.py:139
  8.8 18.1 %collective-permute-start = (bf16[512,512]{1,0:T(8,128)(2,1)S(1)}, bf16[512,512]{1,0:T(8,128)(2,1)S(1)}, u32[]{:S(2)}, u32[]{:S(2)}) collective-permute-start(bf16[512,512]{1,0:T(8,128)(2,1)S(1)} %copy-done.1), channel_id=1, source_target_pairs={{0,1},{1,2},{2,3},{3,4},{4,5},{5,6},{6,7},{7,0},{8,9},{9,10},{10,1... | collective-permute-start | bytes 1572872 | tf_op jit(solution)/shard_map/ppermute | solution.py:84
  11.3 15.6 %collective-permute-start.1 = (bf16[512,512]{1,0:T(8,128)(2,1)S(1)}, bf16[512,512]{1,0:T(8,128)(2,1)S(1)}, u32[]{:S(2)}, u32[]{:S(2)}) collective-permute-start(bf16[512,512]{1,0:T(8,128)(2,1)S(1)} %copy-done.1), channel_id=1, source_target_pairs={{0,7},{1,0},{2,1},{3,2},{4,3},{5,4},{6,5},{7,6},{8,15},{9,8},{10,9... | collective-permute-start | bytes 1572872 | tf_op jit(solution)/shard_map/ppermute | solution.py:85
  26.9 13.4 %collective-permute-start.2 = (bf16[512,512]{1,0:T(8,128)(2,1)S(1)}, bf16[512,512]{1,0:T(8,128)(2,1)S(1)}, u32[]{:S(2)}, u32[]{:S(2)}) collective-permute-start(bf16[512,512]{1,0:T(8,128)(2,1)S(1)} %collective-permute-done), channel_id=1, source_target_pairs={{0,1},{1,2},{2,3},{3,4},{4,5},{5,6},{6,7},{7,0},{8,9},{9,10},{10,1... | collective-permute-start | bytes 1572872 | tf_op jit(solution)/shard_map/ppermute | solution.py:84
  26.9 13.4 %collective-permute-start.3 = (bf16[512,512]{1,0:T(8,128)(2,1)S(1)}, bf16[512,512]{1,0:T(8,128)(2,1)}, u32[]{:S(2)}, u32[]{:S(2)}) collective-permute-start(bf16[512,512]{1,0:T(8,128)(2,1)S(1)} %collective-permute-done.1), channel_id=1, source_target_pairs={{0,7},{1,0},{2,1},{3,2},{4,3},{5,4},{6,5},{7,6},{8,15},{9,8},{10,9... | collective-permute-start | bytes 1572872 | tf_op jit(solution)/shard_map/ppermute | solution.py:85
  40.3 12.6 %collective-permute-start.4 = (bf16[512,512]{1,0:T(8,128)(2,1)S(1)}, bf16[512,512]{1,0:T(8,128)(2,1)S(1)}, u32[]{:S(2)}, u32[]{:S(2)}) collective-permute-start(bf16[512,512]{1,0:T(8,128)(2,1)S(1)} %collective-permute-done.2), channel_id=1, source_target_pairs={{0,1},{1,2},{2,3},{3,4},{4,5},{5,6},{6,7},{7,0},{8,9},{9,10},{10,1... | collective-permute-start | bytes 1572872 | tf_op jit(solution)/shard_map/ppermute | solution.py:84
  40.3 12.7 %collective-permute-start.5 = (bf16[512,512]{1,0:T(8,128)(2,1)}, bf16[512,512]{1,0:T(8,128)(2,1)S(1)}, u32[]{:S(2)}, u32[]{:S(2)}) collective-permute-start(bf16[512,512]{1,0:T(8,128)(2,1)} %collective-permute-done.3), channel_id=1, source_target_pairs={{0,7},{1,0},{2,1},{3,2},{4,3},{5,4},{6,5},{7,6},{8,15},{9,8},{10,9... | collective-permute-start | bytes 1572872 | tf_op jit(solution)/shard_map/ppermute | solution.py:85
  43.2 16.5 %copy-start.3 = (bf16[4096,512]{1,0:T(8,128)(2,1)S(1)}, bf16[4096,512]{1,0:T(8,128)(2,1)}, u32[]{:S(2)}) copy-start(bf16[4096,512]{1,0:T(8,128)(2,1)} %param.16) | copy-start | bytes 12582916
  52.9 6.5 %collective-permute-start.6 = (bf16[256,512]{1,0:T(8,128)(2,1)S(1)}, bf16[256,512]{1,0:T(8,128)(2,1)S(1)}, u32[]{:S(2)}, u32[]{:S(2)}) collective-permute-start(bf16[256,512]{1,0:T(8,128)(2,1)S(1)} %slice.61), channel_id=1, source_target_pairs={{0,1},{1,2},{2,3},{3,4},{4,5},{5,6},{6,7},{7,0},{8,9},{9,10},{10,1... | collective-permute-start | bytes 786440 | tf_op jit(solution)/shard_map/ppermute | solution.py:89
  53.0 6.4 %collective-permute-start.7 = (bf16[256,512]{1,0:T(8,128)(2,1)S(1)}, bf16[256,512]{1,0:T(8,128)(2,1)S(1)}, u32[]{:S(2)}, u32[]{:S(2)}) collective-permute-start(bf16[256,512]{1,0:T(8,128)(2,1)S(1)} %slice.62), channel_id=1, source_target_pairs={{0,7},{1,0},{2,1},{3,2},{4,3},{5,4},{6,5},{7,6},{8,15},{9,8},{10,9... | collective-permute-start | bytes 786440 | tf_op jit(solution)/shard_map/ppermute | solution.py:90
  77.9 3.5 %copy-start.4 = (bf16[1024,1024]{1,0:T(8,128)(2,1)S(1)}, bf16[1024,1024]{1,0:T(8,128)(2,1)}, u32[]{:S(2)}) copy-start(bf16[1024,1024]{1,0:T(8,128)(2,1)} %constant_dynamic-update-slice_fusion) | copy-start | bytes 6291460
  78.1 13.5 %collective-permute-start.11 = (bf16[4,64,1024]{2,1,0:T(8,128)(2,1)S(1)}, bf16[4,64,1024]{2,1,0:T(8,128)(2,1)S(1)}, u32[]{:S(2)}, u32[]{:S(2)}) collective-permute-start(bf16[4,64,1024]{2,1,0:T(8,128)(2,1)S(1)} %get-tuple-element.18), channel_id=1, source_target_pairs={{0,1},{1,0},{2,3},{3,2},{4,5},{5,4},{6,7},{7,6},{8,9},{9,8},{10,11... | collective-permute-start | bytes 1572872 | tf_op jit(solution)/shard_map/ppermute | solution.py:106
  79.6 23.2 %collective-permute-start.8 = (bf16[4,64,1024]{2,1,0:T(8,128)(2,1)S(1)}, bf16[4,64,1024]{2,1,0:T(8,128)(2,1)S(1)}, u32[]{:S(2)}, u32[]{:S(2)}) collective-permute-start(bf16[4,64,1024]{2,1,0:T(8,128)(2,1)S(1)} %get-tuple-element.17), channel_id=1, source_target_pairs={{0,1},{1,0},{2,3},{3,2},{4,5},{5,4},{6,7},{7,6},{8,9},{9,8},{10,11... | collective-permute-start | bytes 1572872 | tf_op jit(solution)/shard_map/ppermute | solution.py:106
  79.8 34.2 %collective-permute-start.9 = (bf16[4,64,1024]{2,1,0:T(8,128)(2,1)S(1)}, bf16[4,64,1024]{2,1,0:T(8,128)(2,1)S(1)}, u32[]{:S(2)}, u32[]{:S(2)}) collective-permute-start(bf16[4,64,1024]{2,1,0:T(8,128)(2,1)S(1)} %get-tuple-element.20), channel_id=1, source_target_pairs={{0,1},{1,0},{2,3},{3,2},{4,5},{5,4},{6,7},{7,6},{8,9},{9,8},{10,11... | collective-permute-start | bytes 1572872 | tf_op jit(solution)/shard_map/ppermute | solution.py:106
  81.1 44.2 %collective-permute-start.10 = (bf16[4,64,1024]{2,1,0:T(8,128)(2,1)S(1)}, bf16[4,64,1024]{2,1,0:T(8,128)(2,1)S(1)}, u32[]{:S(2)}, u32[]{:S(2)}) collective-permute-start(bf16[4,64,1024]{2,1,0:T(8,128)(2,1)S(1)} %get-tuple-element.19), channel_id=1, source_target_pairs={{0,1},{1,0},{2,3},{3,2},{4,5},{5,4},{6,7},{7,6},{8,9},{9,8},{10,11... | collective-permute-start | bytes 1572872 | tf_op jit(solution)/shard_map/ppermute | solution.py:106
  148.1 56.8 %copy-start.2 = (bf16[512,512]{1,0:T(8,128)(2,1)S(1)}, bf16[512,512]{1,0:T(8,128)(2,1)}, u32[]{:S(2)}) copy-start(bf16[512,512]{1,0:T(8,128)(2,1)} %param.11) | copy-start | bytes 1572868
Sparse Core Ops, SparseCore 0:
  9.2 63.7 all-gather.1
  148.2 56.5 reduce-scatter.1

commit v8 on v7

--- a/solution.py
+++ b/solution.py
@@ -12,7 +12,6 @@
 NBRS = 2
 BLOCK = 32
 CAP = 2
-PAIR_CHUNKS = 4
 
 
 def attend_kernel(q_ref, a_ref, b_ref, l_ref, o_ref):
@@ -92,20 +91,28 @@
 
     half = t % 2
     half_len = entry_len // 2
-    enc_rows = lax.dynamic_slice_in_dim(encodings, half * half_len, half_len, axis=1)
+    part_len = half_len // 2
     key_live = jnp.repeat(enc_mask, BLOCK, axis=1).astype(jnp.bfloat16)
     mask_rows = jnp.zeros((nb_dev, 8, enc_width), jnp.bfloat16)
     mask_rows = mask_rows.at[:, 0, :entry_len].set(key_live)
-    payload = jnp.concatenate([enc_rows, mask_rows], axis=1)
-    all_enc = lax.all_gather(payload, "retr", axis=0, tiled=True)
-    mine = jnp.take(all_enc, wanted, axis=0)
-    mine_rows = mine[:, :half_len]
     pair = [(i, i ^ 1) for i in range(tensor_count)]
-    chunk = need_count // PAIR_CHUNKS
-    other_chunks = [
-        lax.ppermute(mine_rows[c * chunk:(c + 1) * chunk], "tensor", pair)
-        for c in range(PAIR_CHUNKS)
-    ]
+    own_parts, other_parts = [], []
+    live_row = None
+    for p in range(2):
+        rows = lax.dynamic_slice_in_dim(
+            encodings, half * half_len + p * part_len, part_len, axis=1
+        )
+        if p == 0:
+            rows = jnp.concatenate([rows, mask_rows], axis=1)
+        gathered_rows = lax.all_gather(rows, "retr", axis=0, tiled=True)
+        mine = jnp.take(gathered_rows, wanted, axis=0)
+        if p == 0:
+            live_row = jnp.roll(
+                mine[:, part_len:part_len + 8, :entry_len], -half * half_len, axis=-1
+            )
+        mine_rows = mine[:, :part_len]
+        own_parts.append(mine_rows)
+        other_parts.append(lax.ppermute(mine_rows, "tensor", pair))
 
     w_both = jnp.concatenate([w_key, w_value], axis=1)
 
@@ -117,9 +124,8 @@
         )
         return out.astype(jnp.bfloat16).reshape(count, half_len, 2 * head_cols)
 
-    kv_mine = project(mine_rows)
-    kv_other = jnp.concatenate([project(c) for c in other_chunks], axis=0)
-    live_row = jnp.roll(mine[:, half_len:half_len + 8, :entry_len], -half * half_len, axis=-1)
+    kv_mine = project(jnp.concatenate(own_parts, axis=1))
+    kv_other = project(jnp.concatenate(other_parts, axis=1))
 
     widened = [p.astype(jnp.float32) for _, p in pieces]
     sum_sq = sum(jnp.sum(w * w, axis=-1, keepdims=True) for w in widened)

time: 214 us -> 216 us (level)
  local copies, waits for them, and re-layouts: 10.3 us -> 13.2 us
    ppermute x3, waiting for transfers between devices: 25.1 us -> 0.01 us  [local(): up = lax.ppermute(up, 'tensor', fwd)]
    ppermute x3, waiting for transfers between devices: 0.01 us -> 24.5 us  [local(): down = lax.ppermute(down, 'tensor', bwd)]
    ppermute x4 -> x2, waiting for transfers between devices: 37.4 us -> 14.7 us  [local(): other_parts.append(lax.ppermute(mine_rows, 'tensor', pair))]
    all_gather x1 -> x2, waiting for transfers between devices: 7.37 us -> 26.2 us  [local(): gathered_rows = lax.all_gather(rows, 'retr', axis=0, tiled=True)]
    ppermute x3, starting transfers between devices: 9.38 us -> 13.3 us  [local(): down = lax.ppermute(down, 'tensor', bwd)]
    ppermute x1, waiting for transfers between devices: 0.01 us -> 2.84 us  [local(): bottom = lax.ppermute(down[half_rows:], 'tensor', bwd)]
    ppermute x3, starting transfers between devices: 2.54 us -> 0.01 us  [local(): up = lax.ppermute(up, 'tensor', fwd)]
    gather x1 -> x2, local copies, waits for them, and re-layouts: 4.38 us -> 5.92 us  [local(): mine = jnp.take(gathered_rows, wanted, axis=0)]
  transfers between devices with their start and end apart: 14 -> 13, of which waited for: 10 -> 8; matrix products, arithmetic and copies ran while one was open for 9% -> 11% of each run, Pallas kernels for 0% -> 0%
where the time goes in v8:
time: 216 us; the launch traced here: 215 us
  waiting for transfers between devices  128 us (59%)
  matrix products  20.8 us (10%)
  starting transfers between devices  18.7 us (9%)
  Pallas kernels  13.8 us (6%)
  between operations  13.4 us (6%)
  local copies, waits for them, and re-layouts  13.2 us (6%)
  other arithmetic  7.57 us (4%)
    reduce_scatter x1, waiting for transfers between devices, local(): lax.psum_scatter(partial_value.astype(jnp.bfloat16), 'tensor', scatter_di...  56.2 us
    all_gather x2, waiting for transfers between devices, local(): gathered_rows = lax.all_gather(rows, 'retr', axis=0, tiled=True)  26.2 us
    ppermute x3, waiting for transfers between devices, local(): down = lax.ppermute(down, 'tensor', bwd)  24.5 us
    ppermute x2, waiting for transfers between devices, local(): other_parts.append(lax.ppermute(mine_rows, 'tensor', pair))  14.7 us
    pallas_call x1, Pallas kernels, attend(): pl.pallas_call(attend_kernel, out_shape=jax.ShapeDtypeStruct((tok_rows, h...  13.8 us
    ppermute x3, starting transfers between devices, local(): down = lax.ppermute(down, 'tensor', bwd)  13.3 us
    dot_general x2, matrix products, project(): jnp.dot(rows.reshape(count * half_len, enc_width), w_both, preferred_elem...  7.33 us
    dot_general x8, matrix products, local(): part = jnp.dot(normed, w_rows, preferred_element_type=jnp.float32)  6.81 us
  transfers between devices with their start and end apart: 13, of which 8 were waited for; matrix products, arithmetic and copies ran while one was open for 11% of the time, Pallas kernels for 0%

profile of v8, /device:TPU:1, one launch (start us, length us, event | category | flops | bytes accessed | tf_op | source)
XLA Modules:
  0.0 215.2 jit_solution(12431344434361530515)
XLA Ops:
  6.6 1.9 constant_dynamic-slice_fusion.1
  8.6 0.7 convert_element_type.96
  9.4 0.8 fusion.60
  10.3 6.5 %collective-permute-start.1 = (bf16[512,512]{1,0:T(8,128)(2,1)S(1)}, bf16[512,512]{1,0:T(8,128)(2,1)S(1)}, u32[]{:S(2)}, u32[]{:S(2)}) collective-permute-start(bf16[512,512]{1,0:T(8,128)(2,1)S(1)} %copy-done), channel_id=1, source_target_pairs={{0,7},{1,0},{2,1},{3,2},{4,3},{5,4},{6,5},{7,6},{8,15},{9,8},{10,9... | collective-permute-start | bytes 1572872 | tf_op jit(solution)/shard_map/ppermute | solution.py:84
  16.9 0.1 fusion.72
  17.0 1.1 constant_dynamic-update-slice_fusion.1
  18.1 9.2 %collective-permute-done.1 = bf16[512,512]{1,0:T(8,128)(2,1)S(1)} collective-permute-done((bf16[512,512]{1,0:T(8,128)(2,1)S(1)}, bf16[512,512]{1,0:T(8,128)(2,1)S(1)}, u32[]{:S(2)}, u32[]{:S(2)}) %collective-permute-start.1) | collective-permute-done | bytes 524320 | tf_op jit(solution)/shard_map/ppermute | solution.py:84
  27.4 3.4 %collective-permute-start.3 = (bf16[512,512]{1,0:T(8,128)(2,1)S(1)}, bf16[512,512]{1,0:T(8,128)(2,1)S(1)}, u32[]{:S(2)}, u32[]{:S(2)}) collective-permute-start(bf16[512,512]{1,0:T(8,128)(2,1)S(1)} %collective-permute-done.1), channel_id=1, source_target_pairs={{0,7},{1,0},{2,1},{3,2},{4,3},{5,4},{6,5},{7,6},{8,15},{9,8},{10,9... | collective-permute-start | bytes 1572872 | tf_op jit(solution)/shard_map/ppermute | solution.py:84
  30.9 2.3 %constant_dynamic-update-slice_fusion = bf16[1024,1024]{1,0:T(8,128)(2,1)} fusion(bf16[1024,1024]{1,0:T(8,128)(2,1)} %constant_dynamic-update-slice_fusion.1, bf16[1024,512]{1,0:T(8,128)(2,1)} %param.18), kind=kLoop, calls=%fused_computation.92 | loop fusion | bytes 2097152 | tf_op jit(solution)/shard_map/concatenate | solution.py:117
  33.2 0.2 fusion.22
  33.4 7.1 %collective-permute-done.3 = bf16[512,512]{1,0:T(8,128)(2,1)S(1)} collective-permute-done((bf16[512,512]{1,0:T(8,128)(2,1)S(1)}, bf16[512,512]{1,0:T(8,128)(2,1)S(1)}, u32[]{:S(2)}, u32[]{:S(2)}) %collective-permute-start.3) | collective-permute-done | bytes 524320 | tf_op jit(solution)/shard_map/ppermute | solution.py:84
  40.5 3.4 %collective-permute-start.5 = (bf16[512,512]{1,0:T(8,128)(2,1)S(1)}, bf16[512,512]{1,0:T(8,128)(2,1)S(1)}, u32[]{:S(2)}, u32[]{:S(2)}) collective-permute-start(bf16[512,512]{1,0:T(8,128)(2,1)S(1)} %collective-permute-done.3), channel_id=1, source_target_pairs={{0,7},{1,0},{2,1},{3,2},{4,3},{5,4},{6,5},{7,6},{8,15},{9,8},{10,9... | collective-permute-start | bytes 1572872 | tf_op jit(solution)/shard_map/ppermute | solution.py:84
  43.9 0.2 fusion.4
  44.1 0.2 fusion.1
  44.3 0.2 fusion.10
  44.5 0.2 fusion.7
  44.7 8.2 %collective-permute-done.5 = bf16[512,512]{1,0:T(8,128)(2,1)S(1)} collective-permute-done((bf16[512,512]{1,0:T(8,128)(2,1)S(1)}, bf16[512,512]{1,0:T(8,128)(2,1)S(1)}, u32[]{:S(2)}, u32[]{:S(2)}) %collective-permute-start.5) | collective-permute-done | bytes 524320 | tf_op jit(solution)/shard_map/ppermute | solution.py:84
  52.9 3.5 %collective-permute-start.7 = (bf16[256,512]{1,0:T(8,128)(2,1)S(1)}, bf16[256,512]{1,0:T(8,128)(2,1)S(1)}, u32[]{:S(2)}, u32[]{:S(2)}) collective-permute-start(bf16[256,512]{1,0:T(8,128)(2,1)S(1)} %slice.44), channel_id=1, source_target_pairs={{0,7},{1,0},{2,1},{3,2},{4,3},{5,4},{6,5},{7,6},{8,15},{9,8},{10,9... | collective-permute-start | bytes 786440 | tf_op jit(solution)/shard_map/ppermute | solution.py:89
  56.5 0.2 fusion.16
  56.6 0.2 fusion.13
  56.8 2.8 %collective-permute-done.7 = bf16[256,512]{1,0:T(8,128)(2,1)S(1)} collective-permute-done((bf16[256,512]{1,0:T(8,128)(2,1)S(1)}, bf16[256,512]{1,0:T(8,128)(2,1)S(1)}, u32[]{:S(2)}, u32[]{:S(2)}) %collective-permute-start.7) | collective-permute-done | bytes 262176 | tf_op jit(solution)/shard_map/ppermute | solution.py:89
  59.7 3.2 %collective-permute-done.6 = bf16[256,512]{1,0:T(8,128)(2,1)S(1)} collective-permute-done((bf16[256,512]{1,0:T(8,128)(2,1)S(1)}, bf16[256,512]{1,0:T(8,128)(2,1)S(1)}, u32[]{:S(2)}, u32[]{:S(2)}) %collective-permute-start.6) | collective-permute-done | bytes 262176 | tf_op jit(solution)/shard_map/ppermute | solution.py:88
  62.9 0.2 fusion.19
  63.1 0.5 fusion.27
  63.6 0.5 convolution_add_fusion.6
  64.1 0.5 convolution_add_fusion.5
  64.6 0.5 convolution_add_fusion.4
  65.1 0.5 convolution_add_fusion.3
  65.6 0.5 convolution_add_fusion.2
  66.1 1.5 convolution_add_fusion.1
  67.6 2.8 %gather_fusion.1 = bf16[16,32,1024]{2,1,0:T(8,128)(2,1)S(1)} fusion(bf16[64,32,1024]{2,1,0:T(8,128)(2,1)} %all-gather.5.cloned.1.call-done, s32[1024]{0:T(1024)S(1)} %pad_clamp_fusion), kind=kCustom, calls=%fused_computation.1 | custom fusion | bytes 2097216 | tf_op jit(solution)/shard_map/jit(_take)/gather | solution.py:108
  70.4 0.2 broadcast_select_fusion.1
  70.7 26.2 %all-gather.3.cloned.1.call-done = bf16[64,40,1024]{2,1,0:T(8,128)(2,1)} async-done(((bf16[4,40,1024]{2,1,0:T(8,128)(2,1)}), bf16[64,40,1024]{2,1,0:T(8,128)(2,1)}) %all-gather.3.cloned.1.call-update) | async-done | bytes 5242896 | tf_op jit(solution)/shard_map/all_gather | solution.py:107
  96.8 3.1 %gather_fusion = bf16[16,40,1024]{2,1,0:T(8,128)(2,1)S(1)} fusion(bf16[64,40,1024]{2,1,0:T(8,128)(2,1)} %all-gather.3.cloned.1.call-done, s32[1024]{0:T(1024)S(1)} %pad_clamp_fusion), kind=kCustom, calls=%fused_computation | custom fusion | bytes 2621504 | tf_op jit(solution)/shard_map/jit(_take)/gather | solution.py:108
  100.0 0.2 broadcast_select_fusion
  100.2 1.6 collective-permute-start.8
  101.8 2.3 %fusion.q_ref = bf16[512,512]{1,0:T(8,128)(2,1)} fusion(f32[512,512]{1,0:T(8,128)S(1)} %copy-done.3, bf16[4096,512]{1,0:T(8,128)(2,1)} %param.16, s32[]{:T(128)S(6)} %select_n.130, f32[512]{0:T(512)S(1)} %get-tuple-element.19, f32[512]{0:T(512)S(1)} %add_rsqrt_fusion, bf16[256,512]{1,0:T(8,128)(2,1)S(1)} %collective-permute-done.7, ...), kind=kOutput, calls=%fused_computation.32 | convolution fusion | flops 270794752 | bytes 2625540 | tf_op jit(solution)/shard_map/dot_general | solution.py:139
  104.2 0.7 fusion.61.l_ref
  104.9 0.2 pad_maximum_fusion
  105.1 1.4 copy-done.4
  106.5 3.7 %convolution_convert_fusion.2 = bf16[1024,1024]{1,0:T(8,128)(2,1)} fusion(bf16[1024,1024]{1,0:T(8,128)(2,1)S(1)} %bitcast.15, bf16[1024,1024]{1,0:T(8,128)(2,1)S(1)} %copy-done.4), kind=kOutput, calls=%fused_computation.6 | convolution fusion | flops 2148532224 | bytes 6291456 | tf_op jit(solution)/shard_map/dot_general | solution.py:121
  110.2 14.7 %collective-permute-done.8 = bf16[16,32,1024]{2,1,0:T(8,128)(2,1)S(1)} collective-permute-done((bf16[16,32,1024]{2,1,0:T(8,128)(2,1)S(1)}, bf16[16,32,1024]{2,1,0:T(8,128)(2,1)S(1)}, u32[]{:S(2)}, u32[]{:S(2)}) %collective-permute-start.8) | collective-permute-done | bytes 1048608 | tf_op jit(solution)/shard_map/ppermute | solution.py:115
  124.9 1.4 pad_maximum_fusion.1
  126.4 3.6 %convolution_convert_fusion.1 = bf16[1024,1024]{1,0:T(8,128)(2,1)} fusion(bf16[1024,1024]{1,0:T(8,128)(2,1)S(1)} %bitcast.14, bf16[1024,1024]{1,0:T(8,128)(2,1)S(1)} %copy-done.4), kind=kOutput, calls=%fused_computation.5 | convolution fusion | flops 2148532224 | bytes 6291456 | tf_op jit(solution)/shard_map/dot_general | solution.py:121
  130.0 13.8 %shard_map.91 = bf16[512,512]{1,0:T(8,128)(2,1)} custom-call(bf16[512,512]{1,0:T(8,128)(2,1)} %fusion.q_ref, bf16[16,64,1024]{2,1,0:T(8,128)(2,1)} %bitcast.12, bf16[16,64,1024]{2,1,0:T(8,128)(2,1)} %bitcast.13, bf16[16,8,128]{2,1,0:T(8,128)(2,1)} %fusion.61.l_ref), custom_call_target="tpu_custom_call" | custom-call | tf_op jit(solution)/shard_map/pallas_call | solution.py:53
  143.8 6.6 %convolution_convert_fusion = bf16[512,4096]{1,0:T(8,128)(2,1)} fusion(bf16[512,512]{1,0:T(8,128)(2,1)} %shard_map.91, bf16[512,4096]{1,0:T(8,128)(2,1)} %param.19), kind=kOutput, calls=%fused_computation.2 | convolution fusion | flops 2149580800 | bytes 8912896 | tf_op jit(solution)/shard_map/dot_general | solution.py:144
  150.5 56.2 %reduce-scatter.2.cloned.1.call-done = bf16[512,512]{1,0:T(8,128)(2,1)} async-done(((bf16[512,4096]{1,0:T(8,128)(2,1)}), bf16[512,512]{1,0:T(8,128)(2,1)}) %reduce-scatter.2.cloned.1.call-update) | async-done | bytes 524304 | tf_op jit(solution)/shard_map/reduce_scatter | solution.py:145
  206.7 2.0 fusion.25
  (42 shorter events, 0.9 us)
Async XLA Ops:
  6.5 3.7 %copy-start = (bf16[512,512]{1,0:T(8,128)(2,1)S(1)}, bf16[512,512]{1,0:T(8,128)(2,1)}, u32[]{:S(2)}) copy-start(bf16[512,512]{1,0:T(8,128)(2,1)} %param.11) | copy-start | bytes 1572868
  6.5 10.2 %copy-start.6 = (s32[8,2]{0,1:T(2,128)S(1)}, s32[8,2]{0,1:T(2,128)}, u32[]{:S(2)}) copy-start(s32[8,2]{0,1:T(2,128)} %param.13) | copy-start | bytes 196
  6.5 10.4 %copy-start.5 = (f32[4096]{0:T(1024)S(1)}, f32[4096]{0:T(1024)}, u32[]{:S(2)}) copy-start(f32[4096]{0:T(1024)} %param.12) | copy-start | bytes 49156
  6.5 10.5 %copy-start.2 = (bf16[1024,512]{1,0:T(8,128)(2,1)S(1)}, bf16[1024,512]{1,0:T(8,128)(2,1)}, u32[]{:S(2)}) copy-start(bf16[1024,512]{1,0:T(8,128)(2,1)} %param.17) | copy-start | bytes 3145732
  6.5 61.0 %all-gather.5.cloned.1.call-start = ((), (), s32[]{:S(2)}) async-start(), calls=%async_computation.2 | async-start | bytes 4456448 | tf_op jit(solution)/shard_map/all_gather | solution.py:107
  8.5 88.3 %all-gather.3.cloned.1.call-start = ((), (), s32[]{:S(2)}) async-start(), calls=%async_computation.1 | async-start | bytes 5570560 | tf_op jit(solution)/shard_map/all_gather | solution.py:107
  10.2 196.5 %reduce-scatter.2.cloned.1.call-start = ((), (), s32[]{:S(2)}) async-start(), calls=%async_computation.3 | async-start | bytes 4718592 | tf_op jit(solution)/shard_map/reduce_scatter | solution.py:145
  10.3 17.1 %collective-permute-start.1 = (bf16[512,512]{1,0:T(8,128)(2,1)S(1)}, bf16[512,512]{1,0:T(8,128)(2,1)S(1)}, u32[]{:S(2)}, u32[]{:S(2)}) collective-permute-start(bf16[512,512]{1,0:T(8,128)(2,1)S(1)} %copy-done), channel_id=1, source_target_pairs={{0,7},{1,0},{2,1},{3,2},{4,3},{5,4},{6,5},{7,6},{8,15},{9,8},{10,9... | collective-permute-start | bytes 1572872 | tf_op jit(solution)/shard_map/ppermute | solution.py:84
  16.7 14.0 %collective-permute-start = (bf16[512,512]{1,0:T(8,128)(2,1)S(1)}, bf16[512,512]{1,0:T(8,128)(2,1)S(1)}, u32[]{:S(2)}, u32[]{:S(2)}) collective-permute-start(bf16[512,512]{1,0:T(8,128)(2,1)S(1)} %copy-done), channel_id=1, source_target_pairs={{0,1},{1,2},{2,3},{3,4},{4,5},{5,6},{6,7},{7,0},{8,9},{9,10},{10,1... | collective-permute-start | bytes 1572872 | tf_op jit(solution)/shard_map/ppermute | solution.py:83
  27.4 13.2 %collective-permute-start.3 = (bf16[512,512]{1,0:T(8,128)(2,1)S(1)}, bf16[512,512]{1,0:T(8,128)(2,1)S(1)}, u32[]{:S(2)}, u32[]{:S(2)}) collective-permute-start(bf16[512,512]{1,0:T(8,128)(2,1)S(1)} %collective-permute-done.1), channel_id=1, source_target_pairs={{0,7},{1,0},{2,1},{3,2},{4,3},{5,4},{6,5},{7,6},{8,15},{9,8},{10,9... | collective-permute-start | bytes 1572872 | tf_op jit(solution)/shard_map/ppermute | solution.py:84
  30.8 13.2 %collective-permute-start.2 = (bf16[512,512]{1,0:T(8,128)(2,1)S(1)}, bf16[512,512]{1,0:T(8,128)(2,1)S(1)}, u32[]{:S(2)}, u32[]{:S(2)}) collective-permute-start(bf16[512,512]{1,0:T(8,128)(2,1)S(1)} %collective-permute-done), channel_id=1, source_target_pairs={{0,1},{1,2},{2,3},{3,4},{4,5},{5,6},{6,7},{7,0},{8,9},{9,10},{10,1... | collective-permute-start | bytes 1572872 | tf_op jit(solution)/shard_map/ppermute | solution.py:83
  40.5 12.3 %collective-permute-start.5 = (bf16[512,512]{1,0:T(8,128)(2,1)S(1)}, bf16[512,512]{1,0:T(8,128)(2,1)S(1)}, u32[]{:S(2)}, u32[]{:S(2)}) collective-permute-start(bf16[512,512]{1,0:T(8,128)(2,1)S(1)} %collective-permute-done.3), channel_id=1, source_target_pairs={{0,7},{1,0},{2,1},{3,2},{4,3},{5,4},{6,5},{7,6},{8,15},{9,8},{10,9... | collective-permute-start | bytes 1572872 | tf_op jit(solution)/shard_map/ppermute | solution.py:84
  43.9 12.4 %collective-permute-start.4 = (bf16[512,512]{1,0:T(8,128)(2,1)S(1)}, bf16[512,512]{1,0:T(8,128)(2,1)S(1)}, u32[]{:S(2)}, u32[]{:S(2)}) collective-permute-start(bf16[512,512]{1,0:T(8,128)(2,1)S(1)} %collective-permute-done.2), channel_id=1, source_target_pairs={{0,1},{1,2},{2,3},{3,4},{4,5},{5,6},{6,7},{7,0},{8,9},{9,10},{10,1... | collective-permute-start | bytes 1572872 | tf_op jit(solution)/shard_map/ppermute | solution.py:83
  44.1 19.0 %copy-start.1 = (bf16[4096,512]{1,0:T(8,128)(2,1)S(1)}, bf16[4096,512]{1,0:T(8,128)(2,1)}, u32[]{:S(2)}) copy-start(bf16[4096,512]{1,0:T(8,128)(2,1)} %param.16) | copy-start | bytes 12582916
  52.9 6.8 %collective-permute-start.7 = (bf16[256,512]{1,0:T(8,128)(2,1)S(1)}, bf16[256,512]{1,0:T(8,128)(2,1)S(1)}, u32[]{:S(2)}, u32[]{:S(2)}) collective-permute-start(bf16[256,512]{1,0:T(8,128)(2,1)S(1)} %slice.44), channel_id=1, source_target_pairs={{0,7},{1,0},{2,1},{3,2},{4,3},{5,4},{6,5},{7,6},{8,15},{9,8},{10,9... | collective-permute-start | bytes 786440 | tf_op jit(solution)/shard_map/ppermute | solution.py:89
  56.4 6.5 %collective-permute-start.6 = (bf16[256,512]{1,0:T(8,128)(2,1)S(1)}, bf16[256,512]{1,0:T(8,128)(2,1)S(1)}, u32[]{:S(2)}, u32[]{:S(2)}) collective-permute-start(bf16[256,512]{1,0:T(8,128)(2,1)S(1)} %slice.43), channel_id=1, source_target_pairs={{0,1},{1,2},{2,3},{3,4},{4,5},{5,6},{6,7},{7,0},{8,9},{9,10},{10,1... | collective-permute-start | bytes 786440 | tf_op jit(solution)/shard_map/ppermute | solution.py:88
  70.6 39.6 %collective-permute-start.9 = (bf16[16,32,1024]{2,1,0:T(8,128)(2,1)S(1)}, bf16[16,32,1024]{2,1,0:T(8,128)(2,1)}, u32[]{:S(2)}, u32[]{:S(2)}) collective-permute-start(bf16[16,32,1024]{2,1,0:T(8,128)(2,1)S(1)} %broadcast_select_fusion.1), channel_id=1, source_target_pairs={{0,1},{1,0},{2,3},{3,2},{4,5},{5,4},{6,7},{7,6},{8,9},{9,8},{10,11... | collective-permute-start | bytes 3145736 | tf_op jit(solution)/shard_map/ppermute | solution.py:115
  99.9 1.9 copy-start.3
  100.2 24.7 %collective-permute-start.8 = (bf16[16,32,1024]{2,1,0:T(8,128)(2,1)S(1)}, bf16[16,32,1024]{2,1,0:T(8,128)(2,1)S(1)}, u32[]{:S(2)}, u32[]{:S(2)}) collective-permute-start(bf16[16,32,1024]{2,1,0:T(8,128)(2,1)S(1)} %slice.45), channel_id=1, source_target_pairs={{0,1},{1,0},{2,3},{3,2},{4,5},{5,4},{6,7},{7,6},{8,9},{9,8},{10,11... | collective-permute-start | bytes 3145736 | tf_op jit(solution)/shard_map/ppermute | solution.py:115
  104.9 1.6 copy-start.4
Sparse Core Ops, SparseCore 0:
  9.2 43.9 all-gather.4
  55.1 41.7 all-gather.2
  150.6 55.9 reduce-scatter.1

commit v9 on v5

--- a/solution.py
+++ b/solution.py
@@ -12,6 +12,7 @@
 NBRS = 2
 BLOCK = 32
 CAP = 2
+OUT_CHUNKS = 2
 
 
 def attend_kernel(flat_ref, q_ref, kv0_ref, kv1_ref, o_ref, *, entry_len):
@@ -117,12 +118,20 @@
         acc = part if acc is None else acc + part
     queries = acc.astype(jnp.bfloat16)
 
-    attended = attend(slot_of, queries, slots, entry_len)
-    partial_value = jnp.dot(attended, w_out, preferred_element_type=jnp.float32)
-    summed = lax.psum_scatter(
-        partial_value.astype(jnp.bfloat16), "tensor", scatter_dimension=1, tiled=True
-    )
-    return (hidden_in.astype(jnp.float32) + summed.astype(jnp.float32)).astype(jnp.bfloat16)
+    tok_rows = queries.shape[0]
+    outs = []
+    for c in range(OUT_CHUNKS):
+        rows = slice(c * tok_rows // OUT_CHUNKS, (c + 1) * tok_rows // OUT_CHUNKS)
+        ids = slice(c * need_count // OUT_CHUNKS, (c + 1) * need_count // OUT_CHUNKS)
+        attended = attend(slot_of[ids], queries[rows], slots, entry_len)
+        partial_value = jnp.dot(attended, w_out, preferred_element_type=jnp.float32)
+        summed = lax.psum_scatter(
+            partial_value.astype(jnp.bfloat16), "tensor", scatter_dimension=1, tiled=True
+        )
+        outs.append(
+            (hidden_in[rows].astype(jnp.float32) + summed.astype(jnp.float32)).astype(jnp.bfloat16)
+        )
+    return jnp.concatenate(outs, axis=0)
 
 
 def solution(mesh):

time: 207 us -> 230 us (1.11); the launches traced: 207 us -> 225 us
  waiting for transfers between devices: 141 us -> 156 us
  Pallas kernels: 14.5 us -> 16.9 us
  other arithmetic: 6.5 us -> 4.16 us
  local copies, waits for them, and re-layouts: 1.69 us -> 3.99 us
    reduce_scatter x1 -> x2, waiting for transfers between devices: 55.9 us -> 69 us  [local(): lax.psum_scatter(partial_value.astype(jnp.bfloat16), 'tensor', scatter_di...]
    dot_general x1 -> x2, matrix products: 6.63 us -> 9.78 us  [local(): partial_value = jnp.dot(attended, w_out, preferred_element_type=jnp.float32)]
    pallas_call x1 -> x2, Pallas kernels: 14.5 us -> 16.9 us  [attend(): pl.pallas_call(functools.partial(attend_kernel, entry_len=entry_len), out...]
  transfers between devices with their start and end apart: 10 -> 11, of which waited for: 6 -> 7; matrix products, arithmetic and copies ran while one was open for 4% -> 5% of each run, Pallas kernels for 0% -> 4%
where the time goes in v9:
time: 230 us; the launch traced here: 225 us
  waiting for transfers between devices  156 us (68%)
  Pallas kernels  16.9 us (7%)
  matrix products  16 us (7%)
  starting transfers between devices  15 us (7%)
  between operations  13.3 us (6%)
  other arithmetic  4.16 us (2%)
  local copies, waits for them, and re-layouts  3.99 us (2%)
    reduce_scatter x2, waiting for transfers between devices, local(): lax.psum_scatter(partial_value.astype(jnp.bfloat16), 'tensor', scatter_di...  69 us
    all_gather x1, waiting for transfers between devices, local(): slots = lax.all_gather(own, ('dp', 'retr'), axis=0, tiled=True)  53.4 us
    ppermute x3, waiting for transfers between devices, local(): up = lax.ppermute(up, 'tensor', fwd)  30.4 us
    pallas_call x2, Pallas kernels, attend(): pl.pallas_call(functools.partial(attend_kernel, entry_len=entry_len), out...  16.9 us
    dot_general x2, matrix products, local(): partial_value = jnp.dot(attended, w_out, preferred_element_type=jnp.float32)  9.78 us
    ppermute x3, starting transfers between devices, local(): down = lax.ppermute(down, 'tensor', bwd)  9.37 us
  transfers between devices with their start and end apart: 11, of which 7 were waited for; matrix products, arithmetic and copies ran while one was open for 5% of the time, Pallas kernels for 4%

profile of v9, /device:TPU:1, one launch (start us, length us, event | category | flops | bytes accessed | tf_op | source)
XLA Modules:
  0.0 225.2 jit_solution(17636705074937045938)
XLA Ops:
  6.6 1.2 copy-done
  7.8 0.7 fusion.75
  8.5 0.1 broadcast_in_dim.2
  8.6 0.1 convert_element_type.118
  8.7 2.2 fusion.4
  10.9 0.9 fusion.33
  11.8 0.0 reduce-scatter.5.cloned.1.call-start
  11.9 2.5 %collective-permute-start = (bf16[512,512]{1,0:T(8,128)(2,1)S(1)}, bf16[512,512]{1,0:T(8,128)(2,1)S(1)}, u32[]{:S(2)}, u32[]{:S(2)}) collective-permute-start(bf16[512,512]{1,0:T(8,128)(2,1)S(1)} %copy-done.1), channel_id=1, source_target_pairs={{0,1},{1,2},{2,3},{3,4},{4,5},{5,6},{6,7},{7,0},{8,9},{9,10},{10,1... | collective-permute-start | bytes 1572872 | tf_op jit(solution)/shard_map/ppermute | solution.py:83
  14.4 4.0 %collective-permute-start.1 = (bf16[512,512]{1,0:T(8,128)(2,1)S(1)}, bf16[512,512]{1,0:T(8,128)(2,1)S(1)}, u32[]{:S(2)}, u32[]{:S(2)}) collective-permute-start(bf16[512,512]{1,0:T(8,128)(2,1)S(1)} %copy-done.1), channel_id=1, source_target_pairs={{0,7},{1,0},{2,1},{3,2},{4,3},{5,4},{6,5},{7,6},{8,15},{9,8},{10,9... | collective-permute-start | bytes 1572872 | tf_op jit(solution)/shard_map/ppermute | solution.py:84
  18.4 0.1 copy.13
  18.5 0.1 reshape.98
  18.6 0.2 fusion.9
  18.8 11.2 %collective-permute-done = bf16[512,512]{1,0:T(8,128)(2,1)S(1)} collective-permute-done((bf16[512,512]{1,0:T(8,128)(2,1)S(1)}, bf16[512,512]{1,0:T(8,128)(2,1)S(1)}, u32[]{:S(2)}, u32[]{:S(2)}) %collective-permute-start) | collective-permute-done | bytes 524320 | tf_op jit(solution)/shard_map/ppermute | solution.py:83
  30.0 2.7 %collective-permute-start.3 = (bf16[512,512]{1,0:T(8,128)(2,1)S(1)}, bf16[512,512]{1,0:T(8,128)(2,1)S(1)}, u32[]{:S(2)}, u32[]{:S(2)}) collective-permute-start(bf16[512,512]{1,0:T(8,128)(2,1)S(1)} %collective-permute-done.1), channel_id=1, source_target_pairs={{0,7},{1,0},{2,1},{3,2},{4,3},{5,4},{6,5},{7,6},{8,15},{9,8},{10,9... | collective-permute-start | bytes 1572872 | tf_op jit(solution)/shard_map/ppermute | solution.py:84
  32.6 0.1 fusion.80
  32.8 0.7 fusion.81
  33.4 10.0 %collective-permute-done.2 = bf16[512,512]{1,0:T(8,128)(2,1)S(1)} collective-permute-done((bf16[512,512]{1,0:T(8,128)(2,1)S(1)}, bf16[512,512]{1,0:T(8,128)(2,1)S(1)}, u32[]{:S(2)}, u32[]{:S(2)}) %collective-permute-start.2) | collective-permute-done | bytes 524320 | tf_op jit(solution)/shard_map/ppermute | solution.py:83
  43.4 2.7 %collective-permute-start.5 = (bf16[512,512]{1,0:T(8,128)(2,1)S(1)}, bf16[512,512]{1,0:T(8,128)(2,1)S(1)}, u32[]{:S(2)}, u32[]{:S(2)}) collective-permute-start(bf16[512,512]{1,0:T(8,128)(2,1)S(1)} %collective-permute-done.3), channel_id=1, source_target_pairs={{0,7},{1,0},{2,1},{3,2},{4,3},{5,4},{6,5},{7,6},{8,15},{9,8},{10,9... | collective-permute-start | bytes 1572872 | tf_op jit(solution)/shard_map/ppermute | solution.py:84
  46.1 0.2 fusion.12
  46.3 0.2 fusion.15
  46.4 0.2 fusion.18
  46.6 0.2 fusion.21
  46.8 9.2 %collective-permute-done.4 = bf16[512,512]{1,0:T(8,128)(2,1)S(1)} collective-permute-done((bf16[512,512]{1,0:T(8,128)(2,1)S(1)}, bf16[512,512]{1,0:T(8,128)(2,1)S(1)}, u32[]{:S(2)}, u32[]{:S(2)}) %collective-permute-start.4) | collective-permute-done | bytes 524320 | tf_op jit(solution)/shard_map/ppermute | solution.py:83
  56.0 0.1 collective-permute-start.6
  56.1 2.9 %collective-permute-start.7 = (bf16[256,512]{1,0:T(8,128)(2,1)S(1)}, bf16[256,512]{1,0:T(8,128)(2,1)S(1)}, u32[]{:S(2)}, u32[]{:S(2)}) collective-permute-start(bf16[256,512]{1,0:T(8,128)(2,1)S(1)} %slice.56), channel_id=1, source_target_pairs={{0,7},{1,0},{2,1},{3,2},{4,3},{5,4},{6,5},{7,6},{8,15},{9,8},{10,9... | collective-permute-start | bytes 786440 | tf_op jit(solution)/shard_map/ppermute | solution.py:89
  59.0 0.2 fusion.24
  59.2 0.2 fusion.27
  59.4 3.1 %collective-permute-done.6 = bf16[256,512]{1,0:T(8,128)(2,1)S(1)} collective-permute-done((bf16[256,512]{1,0:T(8,128)(2,1)S(1)}, bf16[256,512]{1,0:T(8,128)(2,1)S(1)}, u32[]{:S(2)}, u32[]{:S(2)}) %collective-permute-start.6) | collective-permute-done | bytes 262176 | tf_op jit(solution)/shard_map/ppermute | solution.py:88
  62.5 0.2 fusion.30
  62.7 0.5 fusion.41
  63.2 0.5 convolution_add_fusion.6
  63.7 0.5 convolution_add_fusion.5
  64.3 0.5 convolution_add_fusion.4
  64.8 0.5 convolution_add_fusion.3
  65.3 0.5 convolution_add_fusion.2
  65.8 0.5 convolution_add_fusion.1
  66.3 0.5 fusion.7
  66.8 0.8 fusion.79
  67.6 53.4 %all-gather.2.cloned.1.call-done.kv0_ref.kv1_ref = bf16[64,136,1024]{2,1,0:T(8,128)(2,1)} async-done(((bf16[2,136,1024]{2,1,0:T(8,128)(2,1)}), bf16[64,136,1024]{2,1,0:T(8,128)(2,1)}) %all-gather.2.cloned.1.call-update) | async-done | bytes 17825808 | tf_op jit(solution)/shard_map/all_gather | solution.py:104
  121.0 8.4 %shard_map.92 = bf16[256,512]{1,0:T(8,128)(2,1)} custom-call(s32[8]{0:T(128)} %get-tuple-element.30.flat_ref, bf16[256,512]{1,0:T(8,128)(2,1)} %get-tuple-element.20.q_ref, bf16[64,136,1024]{2,1,0:T(8,128)(2,1)} %all-gather.2.cloned.1.call-done.kv0_ref.kv1_ref, bf16[64,136,1024]{2,1,0:T(8,128)(2,1)} %all-gather.2.cloned.1.call-done.kv0_ref.kv1_ref), custom_call_target="tpu_custom_call" | custom-call | tf_op jit(solution)/shard_map/pallas_call | solution.py:60
  129.5 4.9 %convolution_convert_fusion = bf16[256,4096]{1,0:T(8,128)(2,1)} fusion(bf16[256,512]{1,0:T(8,128)(2,1)} %shard_map.92, bf16[512,4096]{1,0:T(8,128)(2,1)} %param.19), kind=kOutput, calls=%fused_computation | convolution fusion | flops 1074790400 | bytes 6553600 | tf_op jit(solution)/shard_map/dot_general | solution.py:127
  134.4 0.0 reduce-scatter.3.cloned.1.call-start
  134.4 8.4 %shard_map.91 = bf16[256,512]{1,0:T(8,128)(2,1)} custom-call(s32[8]{0:T(128)} %get-tuple-element.29.flat_ref, bf16[256,512]{1,0:T(8,128)(2,1)} %get-tuple-element.19.q_ref, bf16[64,136,1024]{2,1,0:T(8,128)(2,1)} %all-gather.2.cloned.1.call-done.kv0_ref.kv1_ref, bf16[64,136,1024]{2,1,0:T(8,128)(2,1)} %all-gather.2.cloned.1.call-done.kv0_ref.kv1_ref), custom_call_target="tpu_custom_call" | custom-call | tf_op jit(solution)/shard_map/pallas_call | solution.py:60
  142.9 4.9 %convolution_convert_fusion.1 = bf16[256,4096]{1,0:T(8,128)(2,1)} fusion(bf16[256,512]{1,0:T(8,128)(2,1)} %shard_map.91, bf16[512,4096]{1,0:T(8,128)(2,1)} %param.19), kind=kOutput, calls=%fused_computation.1 | convolution fusion | flops 1074790400 | bytes 6553600 | tf_op jit(solution)/shard_map/dot_general | solution.py:127
  147.8 25.4 %reduce-scatter.5.cloned.1.call-done = bf16[256,512]{1,0:T(8,128)(2,1)} async-done(((bf16[256,4096]{1,0:T(8,128)(2,1)}), bf16[256,512]{1,0:T(8,128)(2,1)}) %reduce-scatter.5.cloned.1.call-update) | async-done | bytes 262160 | tf_op jit(solution)/shard_map/reduce_scatter | solution.py:128
  173.2 43.5 %reduce-scatter.3.cloned.1.call-done = bf16[256,512]{1,0:T(8,128)(2,1)} async-done(((bf16[256,4096]{1,0:T(8,128)(2,1)}), bf16[256,512]{1,0:T(8,128)(2,1)}) %reduce-scatter.3.cloned.1.call-update) | async-done | bytes 262160 | tf_op jit(solution)/shard_map/reduce_scatter | solution.py:128
  216.7 1.2 add_convert_fusion.1
  217.9 0.8 copy-done.5
  (26 shorter events, 0.2 us)
Async XLA Ops:
  6.5 1.2 copy-start
  6.5 5.3 %copy-start.1 = (bf16[512,512]{1,0:T(8,128)(2,1)S(1)}, bf16[512,512]{1,0:T(8,128)(2,1)}, u32[]{:S(2)}) copy-start(bf16[512,512]{1,0:T(8,128)(2,1)} %param.11) | copy-start | bytes 1572868
  6.5 11.9 %copy-start.4 = (s32[8,2]{0,1:T(2,128)S(1)}, s32[8,2]{0,1:T(2,128)}, u32[]{:S(2)}) copy-start(s32[8,2]{0,1:T(2,128)} %param.13) | copy-start | bytes 196
  6.5 114.5 %all-gather.2.cloned.1.call-start = ((), (), s32[]{:S(2)}) async-start(), calls=%async_computation.2 | async-start | bytes 18382848 | tf_op jit(solution)/shard_map/all_gather | solution.py:104
  7.8 24.9 %copy-start.3 = (f32[4096]{0:T(1024)S(1)}, f32[4096]{0:T(1024)}, u32[]{:S(2)}) copy-start(f32[4096]{0:T(1024)} %param.12) | copy-start | bytes 49156
  11.8 161.4 %reduce-scatter.5.cloned.1.call-start = ((), (), s32[]{:S(2)}) async-start(), calls=%async_computation.4 | async-start | bytes 2359296 | tf_op jit(solution)/shard_map/reduce_scatter | solution.py:128
  11.9 18.1 %collective-permute-start = (bf16[512,512]{1,0:T(8,128)(2,1)S(1)}, bf16[512,512]{1,0:T(8,128)(2,1)S(1)}, u32[]{:S(2)}, u32[]{:S(2)}) collective-permute-start(bf16[512,512]{1,0:T(8,128)(2,1)S(1)} %copy-done.1), channel_id=1, source_target_pairs={{0,1},{1,2},{2,3},{3,4},{4,5},{5,6},{6,7},{7,0},{8,9},{9,10},{10,1... | collective-permute-start | bytes 1572872 | tf_op jit(solution)/shard_map/ppermute | solution.py:83
  14.4 15.6 %collective-permute-start.1 = (bf16[512,512]{1,0:T(8,128)(2,1)S(1)}, bf16[512,512]{1,0:T(8,128)(2,1)S(1)}, u32[]{:S(2)}, u32[]{:S(2)}) collective-permute-start(bf16[512,512]{1,0:T(8,128)(2,1)S(1)} %copy-done.1), channel_id=1, source_target_pairs={{0,7},{1,0},{2,1},{3,2},{4,3},{5,4},{6,5},{7,6},{8,15},{9,8},{10,9... | collective-permute-start | bytes 1572872 | tf_op jit(solution)/shard_map/ppermute | solution.py:84
  18.6 44.1 %copy-start.2 = (bf16[4096,512]{1,0:T(8,128)(2,1)S(1)}, bf16[4096,512]{1,0:T(8,128)(2,1)}, u32[]{:S(2)}) copy-start(bf16[4096,512]{1,0:T(8,128)(2,1)} %param.16) | copy-start | bytes 12582916
  30.0 13.4 %collective-permute-start.2 = (bf16[512,512]{1,0:T(8,128)(2,1)S(1)}, bf16[512,512]{1,0:T(8,128)(2,1)S(1)}, u32[]{:S(2)}, u32[]{:S(2)}) collective-permute-start(bf16[512,512]{1,0:T(8,128)(2,1)S(1)} %collective-permute-done), channel_id=1, source_target_pairs={{0,1},{1,2},{2,3},{3,4},{4,5},{5,6},{6,7},{7,0},{8,9},{9,10},{10,1... | collective-permute-start | bytes 1572872 | tf_op jit(solution)/shard_map/ppermute | solution.py:83
  30.0 13.4 %collective-permute-start.3 = (bf16[512,512]{1,0:T(8,128)(2,1)S(1)}, bf16[512,512]{1,0:T(8,128)(2,1)S(1)}, u32[]{:S(2)}, u32[]{:S(2)}) collective-permute-start(bf16[512,512]{1,0:T(8,128)(2,1)S(1)} %collective-permute-done.1), channel_id=1, source_target_pairs={{0,7},{1,0},{2,1},{3,2},{4,3},{5,4},{6,5},{7,6},{8,15},{9,8},{10,9... | collective-permute-start | bytes 1572872 | tf_op jit(solution)/shard_map/ppermute | solution.py:84
  43.4 12.6 %collective-permute-start.4 = (bf16[512,512]{1,0:T(8,128)(2,1)S(1)}, bf16[512,512]{1,0:T(8,128)(2,1)S(1)}, u32[]{:S(2)}, u32[]{:S(2)}) collective-permute-start(bf16[512,512]{1,0:T(8,128)(2,1)S(1)} %collective-permute-done.2), channel_id=1, source_target_pairs={{0,1},{1,2},{2,3},{3,4},{4,5},{5,6},{6,7},{7,0},{8,9},{9,10},{10,1... | collective-permute-start | bytes 1572872 | tf_op jit(solution)/shard_map/ppermute | solution.py:83
  43.4 12.7 %collective-permute-start.5 = (bf16[512,512]{1,0:T(8,128)(2,1)S(1)}, bf16[512,512]{1,0:T(8,128)(2,1)S(1)}, u32[]{:S(2)}, u32[]{:S(2)}) collective-permute-start(bf16[512,512]{1,0:T(8,128)(2,1)S(1)} %collective-permute-done.3), channel_id=1, source_target_pairs={{0,7},{1,0},{2,1},{3,2},{4,3},{5,4},{6,5},{7,6},{8,15},{9,8},{10,9... | collective-permute-start | bytes 1572872 | tf_op jit(solution)/shard_map/ppermute | solution.py:84
  56.0 6.5 %collective-permute-start.6 = (bf16[256,512]{1,0:T(8,128)(2,1)S(1)}, bf16[256,512]{1,0:T(8,128)(2,1)S(1)}, u32[]{:S(2)}, u32[]{:S(2)}) collective-permute-start(bf16[256,512]{1,0:T(8,128)(2,1)S(1)} %slice.55), channel_id=1, source_target_pairs={{0,1},{1,2},{2,3},{3,4},{4,5},{5,6},{6,7},{7,0},{8,9},{9,10},{10,1... | collective-permute-start | bytes 786440 | tf_op jit(solution)/shard_map/ppermute | solution.py:88
  56.1 6.4 %collective-permute-start.7 = (bf16[256,512]{1,0:T(8,128)(2,1)S(1)}, bf16[256,512]{1,0:T(8,128)(2,1)S(1)}, u32[]{:S(2)}, u32[]{:S(2)}) collective-permute-start(bf16[256,512]{1,0:T(8,128)(2,1)S(1)} %slice.56), channel_id=1, source_target_pairs={{0,7},{1,0},{2,1},{3,2},{4,3},{5,4},{6,5},{7,6},{8,15},{9,8},{10,9... | collective-permute-start | bytes 786440 | tf_op jit(solution)/shard_map/ppermute | solution.py:89
  134.4 82.4 %reduce-scatter.3.cloned.1.call-start = ((), (), s32[]{:S(2)}) async-start(), calls=%async_computation.3 | async-start | bytes 2359296 | tf_op jit(solution)/shard_map/reduce_scatter | solution.py:128
  217.9 0.8 copy-start.5
Sparse Core Ops, SparseCore 0:
  11.9 109.0 all-gather.1
  134.5 38.6 reduce-scatter.4
  175.8 40.9 reduce-scatter.2

commit v10 on v5

--- a/solution.py
+++ b/solution.py
@@ -17,27 +17,28 @@
 def attend_kernel(flat_ref, q_ref, kv0_ref, kv1_ref, o_ref, *, entry_len):
     head_cols = q_ref.shape[1]
     factor = 1.0 / math.sqrt(HD)
-    live0 = kv0_ref[0, entry_len:entry_len + 1, :entry_len].astype(jnp.float32)
-    live1 = kv1_ref[0, entry_len:entry_len + 1, :entry_len].astype(jnp.float32)
-    open0 = live0 > 0
-    open1 = live1 > 0
+    live = jnp.concatenate(
+        [
+            kv0_ref[0, entry_len:entry_len + 1, :entry_len],
+            kv1_ref[0, entry_len:entry_len + 1, :entry_len],
+        ],
+        axis=1,
+    ).astype(jnp.float32)
+    key_open = live > 0
     nt = (((1,), (1,)), ((), ()))
     for h in range(head_cols // HD):
         cols = slice(h * HD, (h + 1) * HD)
         vcols = slice(head_cols + h * HD, head_cols + (h + 1) * HD)
-        qh = q_ref[:, cols]
-        s0 = lax.dot_general(qh, kv0_ref[0, :entry_len, cols], nt, preferred_element_type=jnp.float32) * factor
-        s1 = lax.dot_general(qh, kv1_ref[0, :entry_len, cols], nt, preferred_element_type=jnp.float32) * factor
-        s0 = jnp.where(open0, s0, -1e30)
-        s1 = jnp.where(open1, s1, -1e30)
-        row_max = jnp.maximum(jnp.max(s0, axis=-1, keepdims=True), jnp.max(s1, axis=-1, keepdims=True))
-        w0 = jnp.exp(s0 - row_max) * live0
-        w1 = jnp.exp(s1 - row_max) * live1
-        total = jnp.sum(w0, axis=-1, keepdims=True) + jnp.sum(w1, axis=-1, keepdims=True)
-        p0 = (w0 / total).astype(jnp.bfloat16)
-        p1 = (w1 / total).astype(jnp.bfloat16)
-        att = jnp.dot(p0, kv0_ref[0, :entry_len, vcols], preferred_element_type=jnp.float32)
-        att = att + jnp.dot(p1, kv1_ref[0, :entry_len, vcols], preferred_element_type=jnp.float32)
+        keys = jnp.concatenate([kv0_ref[0, :entry_len, cols], kv1_ref[0, :entry_len, cols]], axis=0)
+        values = jnp.concatenate(
+            [kv0_ref[0, :entry_len, vcols], kv1_ref[0, :entry_len, vcols]], axis=0
+        )
+        scores = lax.dot_general(q_ref[:, cols], keys, nt, preferred_element_type=jnp.float32) * factor
+        scores = jnp.where(key_open, scores, -1e30)
+        row_max = jnp.max(scores, axis=-1, keepdims=True)
+        weights = jnp.exp(scores - row_max) * live
+        probs = (weights / jnp.sum(weights, axis=-1, keepdims=True)).astype(jnp.bfloat16)
+        att = jnp.dot(probs, values, preferred_element_type=jnp.float32)
         o_ref[:, cols] = att.astype(o_ref.dtype)
 
 

time: 207 us -> 207 us (level)
  no operation moved by 1% of the time
where the time goes in v10:
time: 207 us; the launch traced here: 206 us
  waiting for transfers between devices  141 us (68%)
  starting transfers between devices  15 us (7%)
  matrix products  14.7 us (7%)
  Pallas kernels  14 us (7%)
  between operations  13.6 us (7%)
  other arithmetic  6.5 us (3%)
    reduce_scatter x1, waiting for transfers between devices, local(): lax.psum_scatter(partial_value.astype(jnp.bfloat16), 'tensor', scatter_di...  55.9 us
    all_gather x1, waiting for transfers between devices, local(): slots = lax.all_gather(own, ('dp', 'retr'), axis=0, tiled=True)  52.4 us
    ppermute x3, waiting for transfers between devices, local(): up = lax.ppermute(up, 'tensor', fwd)  29.5 us
    pallas_call x1, Pallas kernels, attend(): pl.pallas_call(functools.partial(attend_kernel, entry_len=entry_len), out...  14 us
    ppermute x3, starting transfers between devices, local(): down = lax.ppermute(down, 'tensor', bwd)  9.38 us
    dot_general x1, matrix products, local(): partial_value = jnp.dot(attended, w_out, preferred_element_type=jnp.float32)  6.63 us
    dot_general x8, matrix products, local(): part = jnp.dot(normed, w_rows, preferred_element_type=jnp.float32)  5.86 us
  transfers between devices with their start and end apart: 10, of which 6 were waited for; matrix products, arithmetic and copies ran while one was open for 4% of the time, Pallas kernels for 0%

profile of v10, /device:TPU:1, one launch (start us, length us, event | category | flops | bytes accessed | tf_op | source)
XLA Modules:
  0.0 206.4 jit_solution(15025638968179694658)
XLA Ops:
  6.5 0.0 all-gather.2.cloned.1.call-start
  6.6 1.2 copy-done
  7.8 0.7 fusion.76
  8.5 0.1 broadcast_in_dim.2
  8.6 0.1 convert_element_type.99
  8.7 2.2 %fusion.4 = bf16[256,1024]{1,0:T(8,128)(2,1)S(1)} fusion(bf16[256,1024]{1,0:T(8,128)(2,1)S(1)} %bitcast.6, bf16[1024,512]{1,0:T(8,128)(2,1)} %param.18, bf16[1024,512]{1,0:T(8,128)(2,1)} %param.17), kind=kOutput, calls=%fused_computation.29 | convolution fusion | flops 541327360 | bytes 3145728 | tf_op jit(solution)/shard_map/dot_general | solution.py:97
  10.9 0.9 fusion.34
  11.8 0.0 all-gather.2.cloned.1.call-update
  11.8 0.0 reduce-scatter.2.cloned.1.call-start
  11.9 2.5 %collective-permute-start = (bf16[512,512]{1,0:T(8,128)(2,1)S(1)}, bf16[512,512]{1,0:T(8,128)(2,1)S(1)}, u32[]{:S(2)}, u32[]{:S(2)}) collective-permute-start(bf16[512,512]{1,0:T(8,128)(2,1)S(1)} %copy-done.1), channel_id=1, source_target_pairs={{0,1},{1,2},{2,3},{3,4},{4,5},{5,6},{6,7},{7,0},{8,9},{9,10},{10,1... | collective-permute-start | bytes 1572872 | tf_op jit(solution)/shard_map/ppermute | solution.py:83
  14.4 4.0 %collective-permute-start.1 = (bf16[512,512]{1,0:T(8,128)(2,1)S(1)}, bf16[512,512]{1,0:T(8,128)(2,1)S(1)}, u32[]{:S(2)}, u32[]{:S(2)}) collective-permute-start(bf16[512,512]{1,0:T(8,128)(2,1)S(1)} %copy-done.1), channel_id=1, source_target_pairs={{0,7},{1,0},{2,1},{3,2},{4,3},{5,4},{6,5},{7,6},{8,15},{9,8},{10,9... | collective-permute-start | bytes 1572872 | tf_op jit(solution)/shard_map/ppermute | solution.py:84
  18.4 11.5 %collective-permute-done = bf16[512,512]{1,0:T(8,128)(2,1)S(1)} collective-permute-done((bf16[512,512]{1,0:T(8,128)(2,1)S(1)}, bf16[512,512]{1,0:T(8,128)(2,1)S(1)}, u32[]{:S(2)}, u32[]{:S(2)}) %collective-permute-start) | collective-permute-done | bytes 524320 | tf_op jit(solution)/shard_map/ppermute | solution.py:83
  30.0 0.0 collective-permute-start.2
  30.0 2.7 %collective-permute-start.3 = (bf16[512,512]{1,0:T(8,128)(2,1)S(1)}, bf16[512,512]{1,0:T(8,128)(2,1)}, u32[]{:S(2)}, u32[]{:S(2)}) collective-permute-start(bf16[512,512]{1,0:T(8,128)(2,1)S(1)} %collective-permute-done.1), channel_id=1, source_target_pairs={{0,7},{1,0},{2,1},{3,2},{4,3},{5,4},{6,5},{7,6},{8,15},{9,8},{10,9... | collective-permute-start | bytes 1572872 | tf_op jit(solution)/shard_map/ppermute | solution.py:84
  32.6 0.1 copy.13
  32.7 0.1 reshape.98
  32.8 0.1 fusion.80
  32.9 0.2 fusion.30
  33.1 0.5 fusion.77.flat_ref
  33.6 9.8 %collective-permute-done.2 = bf16[512,512]{1,0:T(8,128)(2,1)S(1)} collective-permute-done((bf16[512,512]{1,0:T(8,128)(2,1)S(1)}, bf16[512,512]{1,0:T(8,128)(2,1)S(1)}, u32[]{:S(2)}, u32[]{:S(2)}) %collective-permute-start.2) | collective-permute-done | bytes 524320 | tf_op jit(solution)/shard_map/ppermute | solution.py:83
  43.4 0.0 collective-permute-start.4
  43.4 0.0 collective-permute-done.3
  43.4 2.7 %collective-permute-start.5 = (bf16[512,512]{1,0:T(8,128)(2,1)}, bf16[512,512]{1,0:T(8,128)(2,1)S(1)}, u32[]{:S(2)}, u32[]{:S(2)}) collective-permute-start(bf16[512,512]{1,0:T(8,128)(2,1)} %collective-permute-done.3), channel_id=1, source_target_pairs={{0,7},{1,0},{2,1},{3,2},{4,3},{5,4},{6,5},{7,6},{8,15},{9,8},{10,9... | collective-permute-start | bytes 1572872 | tf_op jit(solution)/shard_map/ppermute | solution.py:84
  46.1 0.2 fusion.12
  46.3 0.2 fusion.9
  46.4 0.2 fusion.15
  46.6 1.2 fusion.18
  47.8 8.1 %collective-permute-done.4 = bf16[512,512]{1,0:T(8,128)(2,1)S(1)} collective-permute-done((bf16[512,512]{1,0:T(8,128)(2,1)S(1)}, bf16[512,512]{1,0:T(8,128)(2,1)S(1)}, u32[]{:S(2)}, u32[]{:S(2)}) %collective-permute-start.4) | collective-permute-done | bytes 524320 | tf_op jit(solution)/shard_map/ppermute | solution.py:83
  56.0 0.1 collective-permute-start.6
  56.1 2.9 %collective-permute-start.7 = (bf16[256,512]{1,0:T(8,128)(2,1)S(1)}, bf16[256,512]{1,0:T(8,128)(2,1)S(1)}, u32[]{:S(2)}, u32[]{:S(2)}) collective-permute-start(bf16[256,512]{1,0:T(8,128)(2,1)S(1)} %slice.32), channel_id=1, source_target_pairs={{0,7},{1,0},{2,1},{3,2},{4,3},{5,4},{6,5},{7,6},{8,15},{9,8},{10,9... | collective-permute-start | bytes 786440 | tf_op jit(solution)/shard_map/ppermute | solution.py:89
  59.0 0.2 fusion.21
  59.2 0.2 fusion.24
  59.4 3.1 %collective-permute-done.6 = bf16[256,512]{1,0:T(8,128)(2,1)S(1)} collective-permute-done((bf16[256,512]{1,0:T(8,128)(2,1)S(1)}, bf16[256,512]{1,0:T(8,128)(2,1)S(1)}, u32[]{:S(2)}, u32[]{:S(2)}) %collective-permute-start.6) | collective-permute-done | bytes 262176 | tf_op jit(solution)/shard_map/ppermute | solution.py:88
  62.5 0.2 fusion.27
  62.7 0.5 fusion.35
  63.2 0.5 convolution_add_fusion.6
  63.7 0.5 convolution_add_fusion.5
  64.3 0.5 convolution_add_fusion.4
  64.8 1.6 convolution_add_fusion.3
  66.3 0.5 convolution_add_fusion.2
  66.8 0.5 convolution_add_fusion.1
  67.3 1.3 fusion.7.q_ref
  68.6 52.4 %all-gather.2.cloned.1.call-done.kv0_ref.kv1_ref = bf16[64,136,1024]{2,1,0:T(8,128)(2,1)} async-done(((bf16[2,136,1024]{2,1,0:T(8,128)(2,1)}), bf16[64,136,1024]{2,1,0:T(8,128)(2,1)}) %all-gather.2.cloned.1.call-update) | async-done | bytes 17825808 | tf_op jit(solution)/shard_map/all_gather | solution.py:104
  121.0 14.0 %shard_map.91 = bf16[512,512]{1,0:T(8,128)(2,1)} custom-call(s32[16]{0:T(128)} %fusion.77.flat_ref, bf16[512,512]{1,0:T(8,128)(2,1)} %fusion.7.q_ref, bf16[64,136,1024]{2,1,0:T(8,128)(2,1)} %all-gather.2.cloned.1.call-done.kv0_ref.kv1_ref, bf16[64,136,1024]{2,1,0:T(8,128)(2,1)} %all-gather.2.cloned.1.call-done.kv0_ref.kv1_ref), custom_call_target="tpu_custom_call" | custom-call | tf_op jit(solution)/shard_map/pallas_call | solution.py:60
  135.0 6.6 %convolution_convert_fusion = bf16[512,4096]{1,0:T(8,128)(2,1)} fusion(bf16[512,512]{1,0:T(8,128)(2,1)} %shard_map.91, bf16[512,4096]{1,0:T(8,128)(2,1)} %param.19), kind=kOutput, calls=%fused_computation | convolution fusion | flops 2149580800 | bytes 8912896 | tf_op jit(solution)/shard_map/dot_general | solution.py:122
  141.7 0.0 reduce-scatter.2.cloned.1.call-update
  141.7 55.9 %reduce-scatter.2.cloned.1.call-done = bf16[512,512]{1,0:T(8,128)(2,1)} async-done(((bf16[512,4096]{1,0:T(8,128)(2,1)}), bf16[512,512]{1,0:T(8,128)(2,1)}) %reduce-scatter.2.cloned.1.call-update) | async-done | bytes 524304 | tf_op jit(solution)/shard_map/reduce_scatter | solution.py:123
  197.6 2.0 fusion.33
  (16 shorter events, 0.1 us)
Async XLA Ops:
  6.5 1.2 copy-start
  6.5 5.3 %copy-start.1 = (bf16[512,512]{1,0:T(8,128)(2,1)S(1)}, bf16[512,512]{1,0:T(8,128)(2,1)}, u32[]{:S(2)}) copy-start(bf16[512,512]{1,0:T(8,128)(2,1)} %param.11) | copy-start | bytes 1572868
  6.5 26.1 %copy-start.4 = (s32[8,2]{0,1:T(2,128)S(1)}, s32[8,2]{0,1:T(2,128)}, u32[]{:S(2)}) copy-start(s32[8,2]{0,1:T(2,128)} %param.13) | copy-start | bytes 196
  6.5 26.3 %copy-start.3 = (f32[4096]{0:T(1024)S(1)}, f32[4096]{0:T(1024)}, u32[]{:S(2)}) copy-start(f32[4096]{0:T(1024)} %param.12) | copy-start | bytes 49156
  6.5 114.5 %all-gather.2.cloned.1.call-start = ((), (), s32[]{:S(2)}) async-start(), calls=%async_computation.1 | async-start | bytes 18382848 | tf_op jit(solution)/shard_map/all_gather | solution.py:104
  11.8 185.8 %reduce-scatter.2.cloned.1.call-start = ((), (), s32[]{:S(2)}) async-start(), calls=%async_computation.2 | async-start | bytes 4718592 | tf_op jit(solution)/shard_map/reduce_scatter | solution.py:123
  11.9 18.1 %collective-permute-start = (bf16[512,512]{1,0:T(8,128)(2,1)S(1)}, bf16[512,512]{1,0:T(8,128)(2,1)S(1)}, u32[]{:S(2)}, u32[]{:S(2)}) collective-permute-start(bf16[512,512]{1,0:T(8,128)(2,1)S(1)} %copy-done.1), channel_id=1, source_target_pairs={{0,1},{1,2},{2,3},{3,4},{4,5},{5,6},{6,7},{7,0},{8,9},{9,10},{10,1... | collective-permute-start | bytes 1572872 | tf_op jit(solution)/shard_map/ppermute | solution.py:83
  14.4 15.6 %collective-permute-start.1 = (bf16[512,512]{1,0:T(8,128)(2,1)S(1)}, bf16[512,512]{1,0:T(8,128)(2,1)S(1)}, u32[]{:S(2)}, u32[]{:S(2)}) collective-permute-start(bf16[512,512]{1,0:T(8,128)(2,1)S(1)} %copy-done.1), channel_id=1, source_target_pairs={{0,7},{1,0},{2,1},{3,2},{4,3},{5,4},{6,5},{7,6},{8,15},{9,8},{10,9... | collective-permute-start | bytes 1572872 | tf_op jit(solution)/shard_map/ppermute | solution.py:84
  30.0 13.4 %collective-permute-start.2 = (bf16[512,512]{1,0:T(8,128)(2,1)S(1)}, bf16[512,512]{1,0:T(8,128)(2,1)S(1)}, u32[]{:S(2)}, u32[]{:S(2)}) collective-permute-start(bf16[512,512]{1,0:T(8,128)(2,1)S(1)} %collective-permute-done), channel_id=1, source_target_pairs={{0,1},{1,2},{2,3},{3,4},{4,5},{5,6},{6,7},{7,0},{8,9},{9,10},{10,1... | collective-permute-start | bytes 1572872 | tf_op jit(solution)/shard_map/ppermute | solution.py:83
  30.0 13.4 %collective-permute-start.3 = (bf16[512,512]{1,0:T(8,128)(2,1)S(1)}, bf16[512,512]{1,0:T(8,128)(2,1)}, u32[]{:S(2)}, u32[]{:S(2)}) collective-permute-start(bf16[512,512]{1,0:T(8,128)(2,1)S(1)} %collective-permute-done.1), channel_id=1, source_target_pairs={{0,7},{1,0},{2,1},{3,2},{4,3},{5,4},{6,5},{7,6},{8,15},{9,8},{10,9... | collective-permute-start | bytes 1572872 | tf_op jit(solution)/shard_map/ppermute | solution.py:84
  32.8 29.9 %copy-start.2 = (bf16[4096,512]{1,0:T(8,128)(2,1)S(1)}, bf16[4096,512]{1,0:T(8,128)(2,1)}, u32[]{:S(2)}) copy-start(bf16[4096,512]{1,0:T(8,128)(2,1)} %param.16) | copy-start | bytes 12582916
  43.4 12.6 %collective-permute-start.4 = (bf16[512,512]{1,0:T(8,128)(2,1)S(1)}, bf16[512,512]{1,0:T(8,128)(2,1)S(1)}, u32[]{:S(2)}, u32[]{:S(2)}) collective-permute-start(bf16[512,512]{1,0:T(8,128)(2,1)S(1)} %collective-permute-done.2), channel_id=1, source_target_pairs={{0,1},{1,2},{2,3},{3,4},{4,5},{5,6},{6,7},{7,0},{8,9},{9,10},{10,1... | collective-permute-start | bytes 1572872 | tf_op jit(solution)/shard_map/ppermute | solution.py:83
  43.4 12.7 %collective-permute-start.5 = (bf16[512,512]{1,0:T(8,128)(2,1)}, bf16[512,512]{1,0:T(8,128)(2,1)S(1)}, u32[]{:S(2)}, u32[]{:S(2)}) collective-permute-start(bf16[512,512]{1,0:T(8,128)(2,1)} %collective-permute-done.3), channel_id=1, source_target_pairs={{0,7},{1,0},{2,1},{3,2},{4,3},{5,4},{6,5},{7,6},{8,15},{9,8},{10,9... | collective-permute-start | bytes 1572872 | tf_op jit(solution)/shard_map/ppermute | solution.py:84
  56.0 6.5 %collective-permute-start.6 = (bf16[256,512]{1,0:T(8,128)(2,1)S(1)}, bf16[256,512]{1,0:T(8,128)(2,1)S(1)}, u32[]{:S(2)}, u32[]{:S(2)}) collective-permute-start(bf16[256,512]{1,0:T(8,128)(2,1)S(1)} %slice.31), channel_id=1, source_target_pairs={{0,1},{1,2},{2,3},{3,4},{4,5},{5,6},{6,7},{7,0},{8,9},{9,10},{10,1... | collective-permute-start | bytes 786440 | tf_op jit(solution)/shard_map/ppermute | solution.py:88
  56.1 6.4 %collective-permute-start.7 = (bf16[256,512]{1,0:T(8,128)(2,1)S(1)}, bf16[256,512]{1,0:T(8,128)(2,1)S(1)}, u32[]{:S(2)}, u32[]{:S(2)}) collective-permute-start(bf16[256,512]{1,0:T(8,128)(2,1)S(1)} %slice.32), channel_id=1, source_target_pairs={{0,7},{1,0},{2,1},{3,2},{4,3},{5,4},{6,5},{7,6},{8,15},{9,8},{10,9... | collective-permute-start | bytes 786440 | tf_op jit(solution)/shard_map/ppermute | solution.py:89
Sparse Core Ops, SparseCore 0:
  11.9 109.0 all-gather.1
  141.8 55.7 reduce-scatter.1

commit v11 on v10

--- a/solution.py
+++ b/solution.py
@@ -25,15 +25,15 @@
         axis=1,
     ).astype(jnp.float32)
     key_open = live > 0
-    nt = (((1,), (1,)), ((), ()))
     for h in range(head_cols // HD):
         cols = slice(h * HD, (h + 1) * HD)
         vcols = slice(head_cols + h * HD, head_cols + (h + 1) * HD)
-        keys = jnp.concatenate([kv0_ref[0, :entry_len, cols], kv1_ref[0, :entry_len, cols]], axis=0)
+        kcols = slice(h * entry_len, (h + 1) * entry_len)
+        keys_t = jnp.concatenate([kv0_ref[0, :HD, kcols], kv1_ref[0, :HD, kcols]], axis=1)
         values = jnp.concatenate(
             [kv0_ref[0, :entry_len, vcols], kv1_ref[0, :entry_len, vcols]], axis=0
         )
-        scores = lax.dot_general(q_ref[:, cols], keys, nt, preferred_element_type=jnp.float32) * factor
+        scores = jnp.dot(q_ref[:, cols], keys_t, preferred_element_type=jnp.float32) * factor
         scores = jnp.where(key_open, scores, -1e30)
         row_max = jnp.max(scores, axis=-1, keepdims=True)
         weights = jnp.exp(scores - row_max) * live
@@ -97,6 +97,10 @@
     own_kv = jnp.dot(
         enc_half.reshape(per_dev * entry_len, enc_width), w_both, preferred_element_type=jnp.float32
     ).astype(jnp.bfloat16).reshape(per_dev, entry_len, 2 * head_cols)
+    head_count = head_cols // HD
+    keys_t = own_kv[:, :, :head_cols].reshape(per_dev, entry_len, head_count, HD)
+    keys_t = keys_t.transpose(0, 3, 2, 1).reshape(per_dev, HD, head_count * entry_len)
+    own_kv = jnp.concatenate([keys_t, own_kv[:, :, head_cols:]], axis=2)
     key_live = jnp.repeat(mask_half, BLOCK, axis=1).astype(jnp.bfloat16)
     mask_rows = jnp.zeros((per_dev, 8, 2 * head_cols), jnp.bfloat16)
     mask_rows = mask_rows.at[:, 0, :entry_len].set(key_live)

time: 207 us -> 201 us (0.971)
  Pallas kernels: 14 us -> 8.49 us
    pallas_call x1, Pallas kernels: 14 us -> 8.49 us  [attend(): pl.pallas_call(functools.partial(attend_kernel, entry_len=entry_len), out...]
  transfers between devices with their start and end apart: 10 -> 10, of which waited for: 6 -> 6; matrix products, arithmetic and copies ran while one was open for 4% -> 5% of each run, Pallas kernels for 0% -> 0%
where the time goes in v11:
time: 201 us
  waiting for transfers between devices  141 us (70%)
  starting transfers between devices  14.9 us (7%)
  matrix products  14.8 us (7%)
  between operations  13.6 us (7%)
  Pallas kernels  8.49 us (4%)
  other arithmetic  5.84 us (3%)
  local copies, waits for them, and re-layouts  2.16 us (1%)
    reduce_scatter x1, waiting for transfers between devices, local(): lax.psum_scatter(partial_value.astype(jnp.bfloat16), 'tensor', scatter_di...  55.9 us
    all_gather x1, waiting for transfers between devices, local(): slots = lax.all_gather(own, ('dp', 'retr'), axis=0, tiled=True)  52.4 us
    ppermute x3, waiting for transfers between devices, local(): up = lax.ppermute(up, 'tensor', fwd)  29.4 us
    ppermute x3, starting transfers between devices, local(): down = lax.ppermute(down, 'tensor', bwd)  9.37 us
    pallas_call x1, Pallas kernels, attend(): pl.pallas_call(functools.partial(attend_kernel, entry_len=entry_len), out...  8.49 us
    dot_general x1, matrix products, local(): partial_value = jnp.dot(attended, w_out, preferred_element_type=jnp.float32)  6.63 us
    dot_general x8, matrix products, local(): part = jnp.dot(normed, w_rows, preferred_element_type=jnp.float32)  5.86 us
  transfers between devices with their start and end apart: 10, of which 6 were waited for; matrix products, arithmetic and copies ran while one was open for 5% of the time, Pallas kernels for 0%

profile of v11, /device:TPU:1, one launch (start us, length us, event | category | flops | bytes accessed | tf_op | source)
XLA Modules:
  0.0 200.8 jit_solution(5173930342124557010)
XLA Ops:
  6.5 1.2 copy-done
  7.8 0.0 copy-start.1
  7.8 0.0 copy-start.4
  7.8 2.3 %fusion.4 = bf16[256,1024]{1,0:T(8,128)(2,1)S(1)} fusion(bf16[256,1024]{1,0:T(8,128)(2,1)S(1)} %bitcast.8, bf16[1024,512]{1,0:T(8,128)(2,1)} %param.18, bf16[1024,512]{1,0:T(8,128)(2,1)} %param.17), kind=kOutput, calls=%fused_computation.29 | convolution fusion | flops 541327360 | bytes 3145728 | tf_op jit(solution)/shard_map/dot_general | solution.py:97
  10.2 0.1 reshape.107
  10.3 0.2 copy.16
  10.5 0.1 reshape.108
  10.6 0.1 broadcast_in_dim.2
  10.7 0.1 convert_element_type.99
  10.8 0.9 fusion.34
  11.7 0.0 all-gather.2.cloned.1.call-update
  11.7 0.0 reduce-scatter.2.cloned.1.call-start
  11.8 2.5 %collective-permute-start = (bf16[512,512]{1,0:T(8,128)(2,1)S(1)}, bf16[512,512]{1,0:T(8,128)(2,1)S(1)}, u32[]{:S(2)}, u32[]{:S(2)}) collective-permute-start(bf16[512,512]{1,0:T(8,128)(2,1)S(1)} %copy-done.1), channel_id=1, source_target_pairs={{0,1},{1,2},{2,3},{3,4},{4,5},{5,6},{6,7},{7,0},{8,9},{9,10},{10,1... | collective-permute-start | bytes 1572872 | tf_op jit(solution)/shard_map/ppermute | solution.py:83
  14.3 4.0 %collective-permute-start.1 = (bf16[512,512]{1,0:T(8,128)(2,1)S(1)}, bf16[512,512]{1,0:T(8,128)(2,1)S(1)}, u32[]{:S(2)}, u32[]{:S(2)}) collective-permute-start(bf16[512,512]{1,0:T(8,128)(2,1)S(1)} %copy-done.1), channel_id=1, source_target_pairs={{0,7},{1,0},{2,1},{3,2},{4,3},{5,4},{6,5},{7,6},{8,15},{9,8},{10,9... | collective-permute-start | bytes 1572872 | tf_op jit(solution)/shard_map/ppermute | solution.py:84
  18.3 11.5 %collective-permute-done = bf16[512,512]{1,0:T(8,128)(2,1)S(1)} collective-permute-done((bf16[512,512]{1,0:T(8,128)(2,1)S(1)}, bf16[512,512]{1,0:T(8,128)(2,1)S(1)}, u32[]{:S(2)}, u32[]{:S(2)}) %collective-permute-start) | collective-permute-done | bytes 524320 | tf_op jit(solution)/shard_map/ppermute | solution.py:83
  29.9 2.7 %collective-permute-start.3 = (bf16[512,512]{1,0:T(8,128)(2,1)S(1)}, bf16[512,512]{1,0:T(8,128)(2,1)}, u32[]{:S(2)}, u32[]{:S(2)}) collective-permute-start(bf16[512,512]{1,0:T(8,128)(2,1)S(1)} %collective-permute-done.1), channel_id=1, source_target_pairs={{0,7},{1,0},{2,1},{3,2},{4,3},{5,4},{6,5},{7,6},{8,15},{9,8},{10,9... | collective-permute-start | bytes 1572872 | tf_op jit(solution)/shard_map/ppermute | solution.py:84
  32.5 0.1 copy.15
  32.6 0.1 reshape.104
  32.7 0.1 fusion.81
  32.8 0.2 fusion.30
  33.0 0.5 fusion.77.flat_ref
  33.5 9.8 %collective-permute-done.2 = bf16[512,512]{1,0:T(8,128)(2,1)S(1)} collective-permute-done((bf16[512,512]{1,0:T(8,128)(2,1)S(1)}, bf16[512,512]{1,0:T(8,128)(2,1)S(1)}, u32[]{:S(2)}, u32[]{:S(2)}) %collective-permute-start.2) | collective-permute-done | bytes 524320 | tf_op jit(solution)/shard_map/ppermute | solution.py:83
  43.3 2.7 %collective-permute-start.5 = (bf16[512,512]{1,0:T(8,128)(2,1)}, bf16[512,512]{1,0:T(8,128)(2,1)S(1)}, u32[]{:S(2)}, u32[]{:S(2)}) collective-permute-start(bf16[512,512]{1,0:T(8,128)(2,1)} %collective-permute-done.3), channel_id=1, source_target_pairs={{0,7},{1,0},{2,1},{3,2},{4,3},{5,4},{6,5},{7,6},{8,15},{9,8},{10,9... | collective-permute-start | bytes 1572872 | tf_op jit(solution)/shard_map/ppermute | solution.py:84
  46.0 0.2 fusion.12
  46.1 0.2 fusion.9
  46.3 0.2 fusion.15
  46.5 1.2 fusion.18
  47.7 8.1 %collective-permute-done.4 = bf16[512,512]{1,0:T(8,128)(2,1)S(1)} collective-permute-done((bf16[512,512]{1,0:T(8,128)(2,1)S(1)}, bf16[512,512]{1,0:T(8,128)(2,1)S(1)}, u32[]{:S(2)}, u32[]{:S(2)}) %collective-permute-start.4) | collective-permute-done | bytes 524320 | tf_op jit(solution)/shard_map/ppermute | solution.py:83
  55.9 0.1 collective-permute-start.6
  56.0 2.9 %collective-permute-start.7 = (bf16[256,512]{1,0:T(8,128)(2,1)S(1)}, bf16[256,512]{1,0:T(8,128)(2,1)S(1)}, u32[]{:S(2)}, u32[]{:S(2)}) collective-permute-start(bf16[256,512]{1,0:T(8,128)(2,1)S(1)} %slice.40), channel_id=1, source_target_pairs={{0,7},{1,0},{2,1},{3,2},{4,3},{5,4},{6,5},{7,6},{8,15},{9,8},{10,9... | collective-permute-start | bytes 786440 | tf_op jit(solution)/shard_map/ppermute | solution.py:89
  58.9 0.2 fusion.21
  59.1 0.2 fusion.24
  59.3 3.1 %collective-permute-done.6 = bf16[256,512]{1,0:T(8,128)(2,1)S(1)} collective-permute-done((bf16[256,512]{1,0:T(8,128)(2,1)S(1)}, bf16[256,512]{1,0:T(8,128)(2,1)S(1)}, u32[]{:S(2)}, u32[]{:S(2)}) %collective-permute-start.6) | collective-permute-done | bytes 262176 | tf_op jit(solution)/shard_map/ppermute | solution.py:88
  62.4 0.2 fusion.27
  62.6 0.5 fusion.35
  63.1 0.5 convolution_add_fusion.6
  63.6 0.5 convolution_add_fusion.5
  64.1 0.5 convolution_add_fusion.4
  64.6 1.5 convolution_add_fusion.3
  66.2 0.5 convolution_add_fusion.2
  66.7 0.5 convolution_add_fusion.1
  67.2 1.3 fusion.7.q_ref
  68.5 52.4 %all-gather.2.cloned.1.call-done.kv0_ref.kv1_ref = bf16[64,136,1024]{2,1,0:T(8,128)(2,1)} async-done(((bf16[2,136,1024]{2,1,0:T(8,128)(2,1)}), bf16[64,136,1024]{2,1,0:T(8,128)(2,1)}) %all-gather.2.cloned.1.call-update) | async-done | bytes 17825808 | tf_op jit(solution)/shard_map/all_gather | solution.py:108
  121.0 8.5 %shard_map.91 = bf16[512,512]{1,0:T(8,128)(2,1)} custom-call(s32[16]{0:T(128)} %fusion.77.flat_ref, bf16[512,512]{1,0:T(8,128)(2,1)} %fusion.7.q_ref, bf16[64,136,1024]{2,1,0:T(8,128)(2,1)} %all-gather.2.cloned.1.call-done.kv0_ref.kv1_ref, bf16[64,136,1024]{2,1,0:T(8,128)(2,1)} %all-gather.2.cloned.1.call-done.kv0_ref.kv1_ref), custom_call_target="tpu_custom_call" | custom-call | tf_op jit(solution)/shard_map/pallas_call | solution.py:60
  129.4 6.6 %convolution_convert_fusion = bf16[512,4096]{1,0:T(8,128)(2,1)} fusion(bf16[512,512]{1,0:T(8,128)(2,1)} %shard_map.91, bf16[512,4096]{1,0:T(8,128)(2,1)} %param.19), kind=kOutput, calls=%fused_computation | convolution fusion | flops 2149580800 | bytes 8912896 | tf_op jit(solution)/shard_map/dot_general | solution.py:126
  136.1 0.0 reduce-scatter.2.cloned.1.call-update
  136.1 55.9 %reduce-scatter.2.cloned.1.call-done = bf16[512,512]{1,0:T(8,128)(2,1)} async-done(((bf16[512,4096]{1,0:T(8,128)(2,1)}), bf16[512,512]{1,0:T(8,128)(2,1)}) %reduce-scatter.2.cloned.1.call-update) | async-done | bytes 524304 | tf_op jit(solution)/shard_map/reduce_scatter | solution.py:127
  192.0 2.0 fusion.33
  (22 shorter events, 0.2 us)
Async XLA Ops:
  6.5 1.2 copy-start
  6.5 114.4 %all-gather.2.cloned.1.call-start = ((), (), s32[]{:S(2)}) async-start(), calls=%async_computation.1 | async-start | bytes 18382848 | tf_op jit(solution)/shard_map/all_gather | solution.py:108
  7.8 2.8 %copy-start.5 = (s32[4,4]{1,0:T(4,128)S(1)}, s32[4,4]{1,0:T(4,128)}, u32[]{:S(2)}) copy-start(s32[4,4]{1,0:T(4,128)} %param.15) | copy-start | bytes 196
  7.8 4.0 %copy-start.1 = (bf16[512,512]{1,0:T(8,128)(2,1)S(1)}, bf16[512,512]{1,0:T(8,128)(2,1)}, u32[]{:S(2)}) copy-start(bf16[512,512]{1,0:T(8,128)(2,1)} %param.11) | copy-start | bytes 1572868
  7.8 24.7 %copy-start.4 = (s32[8,2]{0,1:T(2,128)S(1)}, s32[8,2]{0,1:T(2,128)}, u32[]{:S(2)}) copy-start(s32[8,2]{0,1:T(2,128)} %param.13) | copy-start | bytes 196
  7.8 24.9 %copy-start.3 = (f32[4096]{0:T(1024)S(1)}, f32[4096]{0:T(1024)}, u32[]{:S(2)}) copy-start(f32[4096]{0:T(1024)} %param.12) | copy-start | bytes 49156
  11.7 180.3 %reduce-scatter.2.cloned.1.call-start = ((), (), s32[]{:S(2)}) async-start(), calls=%async_computation.2 | async-start | bytes 4718592 | tf_op jit(solution)/shard_map/reduce_scatter | solution.py:127
  11.8 18.1 %collective-permute-start = (bf16[512,512]{1,0:T(8,128)(2,1)S(1)}, bf16[512,512]{1,0:T(8,128)(2,1)S(1)}, u32[]{:S(2)}, u32[]{:S(2)}) collective-permute-start(bf16[512,512]{1,0:T(8,128)(2,1)S(1)} %copy-done.1), channel_id=1, source_target_pairs={{0,1},{1,2},{2,3},{3,4},{4,5},{5,6},{6,7},{7,0},{8,9},{9,10},{10,1... | collective-permute-start | bytes 1572872 | tf_op jit(solution)/shard_map/ppermute | solution.py:83
  14.3 15.6 %collective-permute-start.1 = (bf16[512,512]{1,0:T(8,128)(2,1)S(1)}, bf16[512,512]{1,0:T(8,128)(2,1)S(1)}, u32[]{:S(2)}, u32[]{:S(2)}) collective-permute-start(bf16[512,512]{1,0:T(8,128)(2,1)S(1)} %copy-done.1), channel_id=1, source_target_pairs={{0,7},{1,0},{2,1},{3,2},{4,3},{5,4},{6,5},{7,6},{8,15},{9,8},{10,9... | collective-permute-start | bytes 1572872 | tf_op jit(solution)/shard_map/ppermute | solution.py:84
  29.8 13.4 %collective-permute-start.2 = (bf16[512,512]{1,0:T(8,128)(2,1)S(1)}, bf16[512,512]{1,0:T(8,128)(2,1)S(1)}, u32[]{:S(2)}, u32[]{:S(2)}) collective-permute-start(bf16[512,512]{1,0:T(8,128)(2,1)S(1)} %collective-permute-done), channel_id=1, source_target_pairs={{0,1},{1,2},{2,3},{3,4},{4,5},{5,6},{6,7},{7,0},{8,9},{9,10},{10,1... | collective-permute-start | bytes 1572872 | tf_op jit(solution)/shard_map/ppermute | solution.py:83
  29.9 13.4 %collective-permute-start.3 = (bf16[512,512]{1,0:T(8,128)(2,1)S(1)}, bf16[512,512]{1,0:T(8,128)(2,1)}, u32[]{:S(2)}, u32[]{:S(2)}) collective-permute-start(bf16[512,512]{1,0:T(8,128)(2,1)S(1)} %collective-permute-done.1), channel_id=1, source_target_pairs={{0,7},{1,0},{2,1},{3,2},{4,3},{5,4},{6,5},{7,6},{8,15},{9,8},{10,9... | collective-permute-start | bytes 1572872 | tf_op jit(solution)/shard_map/ppermute | solution.py:84
  32.7 29.9 %copy-start.2 = (bf16[4096,512]{1,0:T(8,128)(2,1)S(1)}, bf16[4096,512]{1,0:T(8,128)(2,1)}, u32[]{:S(2)}) copy-start(bf16[4096,512]{1,0:T(8,128)(2,1)} %param.16) | copy-start | bytes 12582916
  43.3 12.6 %collective-permute-start.4 = (bf16[512,512]{1,0:T(8,128)(2,1)S(1)}, bf16[512,512]{1,0:T(8,128)(2,1)S(1)}, u32[]{:S(2)}, u32[]{:S(2)}) collective-permute-start(bf16[512,512]{1,0:T(8,128)(2,1)S(1)} %collective-permute-done.2), channel_id=1, source_target_pairs={{0,1},{1,2},{2,3},{3,4},{4,5},{5,6},{6,7},{7,0},{8,9},{9,10},{10,1... | collective-permute-start | bytes 1572872 | tf_op jit(solution)/shard_map/ppermute | solution.py:83
  43.3 12.7 %collective-permute-start.5 = (bf16[512,512]{1,0:T(8,128)(2,1)}, bf16[512,512]{1,0:T(8,128)(2,1)S(1)}, u32[]{:S(2)}, u32[]{:S(2)}) collective-permute-start(bf16[512,512]{1,0:T(8,128)(2,1)} %collective-permute-done.3), channel_id=1, source_target_pairs={{0,7},{1,0},{2,1},{3,2},{4,3},{5,4},{6,5},{7,6},{8,15},{9,8},{10,9... | collective-permute-start | bytes 1572872 | tf_op jit(solution)/shard_map/ppermute | solution.py:84
  55.9 6.5 %collective-permute-start.6 = (bf16[256,512]{1,0:T(8,128)(2,1)S(1)}, bf16[256,512]{1,0:T(8,128)(2,1)S(1)}, u32[]{:S(2)}, u32[]{:S(2)}) collective-permute-start(bf16[256,512]{1,0:T(8,128)(2,1)S(1)} %slice.39), channel_id=1, source_target_pairs={{0,1},{1,2},{2,3},{3,4},{4,5},{5,6},{6,7},{7,0},{8,9},{9,10},{10,1... | collective-permute-start | bytes 786440 | tf_op jit(solution)/shard_map/ppermute | solution.py:88
  56.0 6.4 %collective-permute-start.7 = (bf16[256,512]{1,0:T(8,128)(2,1)S(1)}, bf16[256,512]{1,0:T(8,128)(2,1)S(1)}, u32[]{:S(2)}, u32[]{:S(2)}) collective-permute-start(bf16[256,512]{1,0:T(8,128)(2,1)S(1)} %slice.40), channel_id=1, source_target_pairs={{0,7},{1,0},{2,1},{3,2},{4,3},{5,4},{6,5},{7,6},{8,15},{9,8},{10,9... | collective-permute-start | bytes 786440 | tf_op jit(solution)/shard_map/ppermute | solution.py:89
Sparse Core Ops, SparseCore 0:
  11.8 109.0 all-gather.1
  136.2 55.7 reduce-scatter.1

commit v12 on v11

--- a/solution.py
+++ b/solution.py
@@ -89,10 +89,9 @@
     bottom = lax.ppermute(down[half_rows:], "tensor", bwd)
     pieces.append((half_ring, jnp.concatenate([top, bottom], axis=0)))
 
-    per_dev = nb_dev // dp_count
-    dp_idx = lax.axis_index("dp")
-    enc_half = lax.dynamic_slice_in_dim(encodings, dp_idx * per_dev, per_dev, axis=0)
-    mask_half = lax.dynamic_slice_in_dim(enc_mask, dp_idx * per_dev, per_dev, axis=0)
+    per_dev = nb_dev
+    enc_half = encodings
+    mask_half = enc_mask
     w_both = jnp.concatenate([w_key, w_value], axis=1)
     own_kv = jnp.dot(
         enc_half.reshape(per_dev * entry_len, enc_width), w_both, preferred_element_type=jnp.float32
@@ -105,9 +104,8 @@
     mask_rows = jnp.zeros((per_dev, 8, 2 * head_cols), jnp.bfloat16)
     mask_rows = mask_rows.at[:, 0, :entry_len].set(key_live)
     own = jnp.concatenate([own_kv, mask_rows], axis=1)
-    slots = lax.all_gather(own, ("dp", "retr"), axis=0, tiled=True)
-    in_dev = wanted % nb_dev
-    slot_of = ((in_dev // per_dev) * retr_count + wanted // nb_dev) * per_dev + in_dev % per_dev
+    slots = lax.all_gather(own, "retr", axis=0, tiled=True)
+    slot_of = wanted
 
     widened = [p.astype(jnp.float32) for _, p in pieces]
     sum_sq = sum(jnp.sum(w * w, axis=-1, keepdims=True) for w in widened)

time: 201 us -> 197 us (0.980)
  waiting for transfers between devices: 141 us -> 135 us
    all_gather x1, waiting for transfers between devices: 52.4 us -> 46.6 us  [local(): slots = lax.all_gather(own, 'retr', axis=0, tiled=True)]
where the time goes in v12:
time: 197 us; the launch traced here: 196 us
  waiting for transfers between devices  135 us (69%)
  matrix products  15.3 us (8%)
  starting transfers between devices  14.9 us (8%)
  between operations  13.6 us (7%)
  Pallas kernels  8.49 us (4%)
  other arithmetic  5.63 us (3%)
  local copies, waits for them, and re-layouts  3.19 us (2%)
    reduce_scatter x1, waiting for transfers between devices, local(): lax.psum_scatter(partial_value.astype(jnp.bfloat16), 'tensor', scatter_di...  55.8 us
    all_gather x1, waiting for transfers between devices, local(): slots = lax.all_gather(own, 'retr', axis=0, tiled=True)  46.6 us
    ppermute x3, waiting for transfers between devices, local(): up = lax.ppermute(up, 'tensor', fwd)  29.4 us
    ppermute x3, starting transfers between devices, local(): down = lax.ppermute(down, 'tensor', bwd)  9.38 us
    pallas_call x1, Pallas kernels, attend(): pl.pallas_call(functools.partial(attend_kernel, entry_len=entry_len), out...  8.49 us
    dot_general x1, matrix products, local(): partial_value = jnp.dot(attended, w_out, preferred_element_type=jnp.float32)  6.63 us
    dot_general x8, matrix products, local(): part = jnp.dot(normed, w_rows, preferred_element_type=jnp.float32)  5.83 us
  transfers between devices with their start and end apart: 10, of which 6 were waited for; matrix products, arithmetic and copies ran while one was open for 5% of the time, Pallas kernels for 0%

profile of v12, /device:TPU:1, one launch (start us, length us, event | category | flops | bytes accessed | tf_op | source)
XLA Modules:
  0.0 196.1 jit_solution(6323660615950735875)
XLA Ops:
  6.5 1.2 copy-done
  7.8 2.8 %fusion.5 = bf16[1024,512]{0,1:T(8,128)(2,1)S(1)} fusion(bf16[512,1024]{1,0:T(8,128)(2,1)S(1)} %bitcast.8, bf16[1024,512]{1,0:T(8,128)(2,1)} %param.18, bf16[1024,512]{1,0:T(8,128)(2,1)} %param.17), kind=kOutput, calls=%fused_computation.10 | convolution fusion | flops 1078460416 | bytes 4194304 | tf_op jit(solution)/shard_map/dot_general | solution.py:96
  10.6 0.0 copy-start.4
  10.6 0.0 copy-start.1
  10.6 0.1 fusion.78
  10.7 0.1 reshape.107
  10.8 0.5 copy.16
  11.3 0.2 reshape.108
  11.5 0.1 broadcast_in_dim.2
  11.6 0.1 convert_element_type.103
  11.7 1.2 fusion.9
  12.9 0.0 all-gather.2.cloned.1.call-update
  12.9 0.0 reduce-scatter.2.cloned.1.call-start
  13.0 2.5 %collective-permute-start = (bf16[512,512]{1,0:T(8,128)(2,1)S(1)}, bf16[512,512]{1,0:T(8,128)(2,1)S(1)}, u32[]{:S(2)}, u32[]{:S(2)}) collective-permute-start(bf16[512,512]{1,0:T(8,128)(2,1)S(1)} %copy-done.1), channel_id=1, source_target_pairs={{0,1},{1,2},{2,3},{3,4},{4,5},{5,6},{6,7},{7,0},{8,9},{9,10},{10,1... | collective-permute-start | bytes 1572872 | tf_op jit(solution)/shard_map/ppermute | solution.py:83
  15.5 4.0 %collective-permute-start.1 = (bf16[512,512]{1,0:T(8,128)(2,1)S(1)}, bf16[512,512]{1,0:T(8,128)(2,1)S(1)}, u32[]{:S(2)}, u32[]{:S(2)}) collective-permute-start(bf16[512,512]{1,0:T(8,128)(2,1)S(1)} %copy-done.1), channel_id=1, source_target_pairs={{0,7},{1,0},{2,1},{3,2},{4,3},{5,4},{6,5},{7,6},{8,15},{9,8},{10,9... | collective-permute-start | bytes 1572872 | tf_op jit(solution)/shard_map/ppermute | solution.py:84
  19.5 11.5 %collective-permute-done = bf16[512,512]{1,0:T(8,128)(2,1)S(1)} collective-permute-done((bf16[512,512]{1,0:T(8,128)(2,1)S(1)}, bf16[512,512]{1,0:T(8,128)(2,1)S(1)}, u32[]{:S(2)}, u32[]{:S(2)}) %collective-permute-start) | collective-permute-done | bytes 524320 | tf_op jit(solution)/shard_map/ppermute | solution.py:83
  31.1 2.7 %collective-permute-start.3 = (bf16[512,512]{1,0:T(8,128)(2,1)S(1)}, bf16[512,512]{1,0:T(8,128)(2,1)}, u32[]{:S(2)}, u32[]{:S(2)}) collective-permute-start(bf16[512,512]{1,0:T(8,128)(2,1)S(1)} %collective-permute-done.1), channel_id=1, source_target_pairs={{0,7},{1,0},{2,1},{3,2},{4,3},{5,4},{6,5},{7,6},{8,15},{9,8},{10,9... | collective-permute-start | bytes 1572872 | tf_op jit(solution)/shard_map/ppermute | solution.py:84
  33.8 0.1 copy.15
  33.8 0.7 reshape.104.flat_ref
  34.5 0.1 fusion.79
  34.6 0.2 fusion.31
  34.8 9.7 %collective-permute-done.2 = bf16[512,512]{1,0:T(8,128)(2,1)S(1)} collective-permute-done((bf16[512,512]{1,0:T(8,128)(2,1)S(1)}, bf16[512,512]{1,0:T(8,128)(2,1)S(1)}, u32[]{:S(2)}, u32[]{:S(2)}) %collective-permute-start.2) | collective-permute-done | bytes 524320 | tf_op jit(solution)/shard_map/ppermute | solution.py:83
  44.5 2.7 %collective-permute-start.5 = (bf16[512,512]{1,0:T(8,128)(2,1)}, bf16[512,512]{1,0:T(8,128)(2,1)S(1)}, u32[]{:S(2)}, u32[]{:S(2)}) collective-permute-start(bf16[512,512]{1,0:T(8,128)(2,1)} %collective-permute-done.3), channel_id=1, source_target_pairs={{0,7},{1,0},{2,1},{3,2},{4,3},{5,4},{6,5},{7,6},{8,15},{9,8},{10,9... | collective-permute-start | bytes 1572872 | tf_op jit(solution)/shard_map/ppermute | solution.py:84
  47.2 0.2 fusion.10
  47.4 0.2 fusion.13
  47.6 0.2 fusion.16
  47.7 1.2 fusion.19
  49.0 8.2 %collective-permute-done.4 = bf16[512,512]{1,0:T(8,128)(2,1)S(1)} collective-permute-done((bf16[512,512]{1,0:T(8,128)(2,1)S(1)}, bf16[512,512]{1,0:T(8,128)(2,1)S(1)}, u32[]{:S(2)}, u32[]{:S(2)}) %collective-permute-start.4) | collective-permute-done | bytes 524320 | tf_op jit(solution)/shard_map/ppermute | solution.py:83
  57.1 0.1 collective-permute-start.6
  57.3 2.9 %collective-permute-start.7 = (bf16[256,512]{1,0:T(8,128)(2,1)S(1)}, bf16[256,512]{1,0:T(8,128)(2,1)S(1)}, u32[]{:S(2)}, u32[]{:S(2)}) collective-permute-start(bf16[256,512]{1,0:T(8,128)(2,1)S(1)} %slice.40), channel_id=1, source_target_pairs={{0,7},{1,0},{2,1},{3,2},{4,3},{5,4},{6,5},{7,6},{8,15},{9,8},{10,9... | collective-permute-start | bytes 786440 | tf_op jit(solution)/shard_map/ppermute | solution.py:89
  60.2 0.2 fusion.22
  60.3 0.2 fusion.25
  60.5 3.1 %collective-permute-done.6 = bf16[256,512]{1,0:T(8,128)(2,1)S(1)} collective-permute-done((bf16[256,512]{1,0:T(8,128)(2,1)S(1)}, bf16[256,512]{1,0:T(8,128)(2,1)S(1)}, u32[]{:S(2)}, u32[]{:S(2)}) %collective-permute-start.6) | collective-permute-done | bytes 262176 | tf_op jit(solution)/shard_map/ppermute | solution.py:88
  63.6 0.2 fusion.28
  63.9 0.5 fusion.35
  64.4 0.5 convolution_add_fusion.6
  64.9 0.5 convolution_add_fusion.5
  65.4 0.5 convolution_add_fusion.4
  65.9 1.5 convolution_add_fusion.3
  67.4 0.5 convolution_add_fusion.2
  67.9 0.5 convolution_add_fusion.1
  68.4 1.3 fusion.8.q_ref
  69.7 46.6 %all-gather.2.cloned.1.call-done.kv0_ref.kv1_ref = bf16[64,136,1024]{2,1,0:T(8,128)(2,1)} async-done(((bf16[4,136,1024]{2,1,0:T(8,128)(2,1)}), bf16[64,136,1024]{2,1,0:T(8,128)(2,1)}) %all-gather.2.cloned.1.call-update) | async-done | bytes 17825808 | tf_op jit(solution)/shard_map/all_gather | solution.py:107
  116.3 8.5 %shard_map.91 = bf16[512,512]{1,0:T(8,128)(2,1)} custom-call(s32[16]{0:T(128)} %reshape.104.flat_ref, bf16[512,512]{1,0:T(8,128)(2,1)} %fusion.8.q_ref, bf16[64,136,1024]{2,1,0:T(8,128)(2,1)} %all-gather.2.cloned.1.call-done.kv0_ref.kv1_ref, bf16[64,136,1024]{2,1,0:T(8,128)(2,1)} %all-gather.2.cloned.1.call-done.kv0_ref.kv1_ref), custom_call_target="tpu_custom_call" | custom-call | tf_op jit(solution)/shard_map/pallas_call | solution.py:60
  124.8 6.6 %convolution_convert_fusion = bf16[512,4096]{1,0:T(8,128)(2,1)} fusion(bf16[512,512]{1,0:T(8,128)(2,1)} %shard_map.91, bf16[512,4096]{1,0:T(8,128)(2,1)} %param.19), kind=kOutput, calls=%fused_computation | convolution fusion | flops 2149580800 | bytes 8912896 | tf_op jit(solution)/shard_map/dot_general | solution.py:124
  131.4 0.0 reduce-scatter.2.cloned.1.call-update
  131.5 55.8 %reduce-scatter.2.cloned.1.call-done = bf16[512,512]{1,0:T(8,128)(2,1)} async-done(((bf16[512,4096]{1,0:T(8,128)(2,1)}), bf16[512,512]{1,0:T(8,128)(2,1)}) %reduce-scatter.2.cloned.1.call-update) | async-done | bytes 524304 | tf_op jit(solution)/shard_map/reduce_scatter | solution.py:125
  187.3 2.0 %fusion.34 = bf16[512,512]{1,0:T(8,128)(2,1)} fusion(bf16[512,512]{1,0:T(8,128)(2,1)S(1)} %copy-done.1, bf16[512,512]{1,0:T(8,128)(2,1)} %reduce-scatter.2.cloned.1.call-done), kind=kLoop, calls=%fused_computation.58 | loop fusion | flops 1048576 | bytes 1572864 | tf_op jit(solution)/shard_map/convert_element_type | solution.py:128
  (20 shorter events, 0.1 us)
Async XLA Ops:
  6.5 1.2 copy-start
  6.5 109.8 %all-gather.2.cloned.1.call-start = ((), (), s32[]{:S(2)}) async-start(), calls=%async_computation.1 | async-start | bytes 18939904 | tf_op jit(solution)/shard_map/all_gather | solution.py:107
  10.6 1.0 copy-start.4
  10.6 2.4 %copy-start.1 = (bf16[512,512]{1,0:T(8,128)(2,1)S(1)}, bf16[512,512]{1,0:T(8,128)(2,1)}, u32[]{:S(2)}) copy-start(bf16[512,512]{1,0:T(8,128)(2,1)} %param.11) | copy-start | bytes 1572868
  10.6 23.2 %copy-start.5 = (s32[8,2]{0,1:T(2,128)S(1)}, s32[8,2]{0,1:T(2,128)}, u32[]{:S(2)}) copy-start(s32[8,2]{0,1:T(2,128)} %param.13) | copy-start | bytes 196
  10.6 23.9 %copy-start.3 = (f32[4096]{0:T(1024)S(1)}, f32[4096]{0:T(1024)}, u32[]{:S(2)}) copy-start(f32[4096]{0:T(1024)} %param.12) | copy-start | bytes 49156
  12.9 174.3 %reduce-scatter.2.cloned.1.call-start = ((), (), s32[]{:S(2)}) async-start(), calls=%async_computation.2 | async-start | bytes 4718592 | tf_op jit(solution)/shard_map/reduce_scatter | solution.py:125
  13.0 18.1 %collective-permute-start = (bf16[512,512]{1,0:T(8,128)(2,1)S(1)}, bf16[512,512]{1,0:T(8,128)(2,1)S(1)}, u32[]{:S(2)}, u32[]{:S(2)}) collective-permute-start(bf16[512,512]{1,0:T(8,128)(2,1)S(1)} %copy-done.1), channel_id=1, source_target_pairs={{0,1},{1,2},{2,3},{3,4},{4,5},{5,6},{6,7},{7,0},{8,9},{9,10},{10,1... | collective-permute-start | bytes 1572872 | tf_op jit(solution)/shard_map/ppermute | solution.py:83
  15.5 15.6 %collective-permute-start.1 = (bf16[512,512]{1,0:T(8,128)(2,1)S(1)}, bf16[512,512]{1,0:T(8,128)(2,1)S(1)}, u32[]{:S(2)}, u32[]{:S(2)}) collective-permute-start(bf16[512,512]{1,0:T(8,128)(2,1)S(1)} %copy-done.1), channel_id=1, source_target_pairs={{0,7},{1,0},{2,1},{3,2},{4,3},{5,4},{6,5},{7,6},{8,15},{9,8},{10,9... | collective-permute-start | bytes 1572872 | tf_op jit(solution)/shard_map/ppermute | solution.py:84
  31.1 13.4 %collective-permute-start.2 = (bf16[512,512]{1,0:T(8,128)(2,1)S(1)}, bf16[512,512]{1,0:T(8,128)(2,1)S(1)}, u32[]{:S(2)}, u32[]{:S(2)}) collective-permute-start(bf16[512,512]{1,0:T(8,128)(2,1)S(1)} %collective-permute-done), channel_id=1, source_target_pairs={{0,1},{1,2},{2,3},{3,4},{4,5},{5,6},{6,7},{7,0},{8,9},{9,10},{10,1... | collective-permute-start | bytes 1572872 | tf_op jit(solution)/shard_map/ppermute | solution.py:83
  31.1 13.4 %collective-permute-start.3 = (bf16[512,512]{1,0:T(8,128)(2,1)S(1)}, bf16[512,512]{1,0:T(8,128)(2,1)}, u32[]{:S(2)}, u32[]{:S(2)}) collective-permute-start(bf16[512,512]{1,0:T(8,128)(2,1)S(1)} %collective-permute-done.1), channel_id=1, source_target_pairs={{0,7},{1,0},{2,1},{3,2},{4,3},{5,4},{6,5},{7,6},{8,15},{9,8},{10,9... | collective-permute-start | bytes 1572872 | tf_op jit(solution)/shard_map/ppermute | solution.py:84
  34.5 29.3 %copy-start.2 = (bf16[4096,512]{1,0:T(8,128)(2,1)S(1)}, bf16[4096,512]{1,0:T(8,128)(2,1)}, u32[]{:S(2)}) copy-start(bf16[4096,512]{1,0:T(8,128)(2,1)} %param.16) | copy-start | bytes 12582916
  44.5 12.6 %collective-permute-start.4 = (bf16[512,512]{1,0:T(8,128)(2,1)S(1)}, bf16[512,512]{1,0:T(8,128)(2,1)S(1)}, u32[]{:S(2)}, u32[]{:S(2)}) collective-permute-start(bf16[512,512]{1,0:T(8,128)(2,1)S(1)} %collective-permute-done.2), channel_id=1, source_target_pairs={{0,1},{1,2},{2,3},{3,4},{4,5},{5,6},{6,7},{7,0},{8,9},{9,10},{10,1... | collective-permute-start | bytes 1572872 | tf_op jit(solution)/shard_map/ppermute | solution.py:83
  44.5 12.7 %collective-permute-start.5 = (bf16[512,512]{1,0:T(8,128)(2,1)}, bf16[512,512]{1,0:T(8,128)(2,1)S(1)}, u32[]{:S(2)}, u32[]{:S(2)}) collective-permute-start(bf16[512,512]{1,0:T(8,128)(2,1)} %collective-permute-done.3), channel_id=1, source_target_pairs={{0,7},{1,0},{2,1},{3,2},{4,3},{5,4},{6,5},{7,6},{8,15},{9,8},{10,9... | collective-permute-start | bytes 1572872 | tf_op jit(solution)/shard_map/ppermute | solution.py:84
  57.1 6.5 %collective-permute-start.6 = (bf16[256,512]{1,0:T(8,128)(2,1)S(1)}, bf16[256,512]{1,0:T(8,128)(2,1)S(1)}, u32[]{:S(2)}, u32[]{:S(2)}) collective-permute-start(bf16[256,512]{1,0:T(8,128)(2,1)S(1)} %slice.39), channel_id=1, source_target_pairs={{0,1},{1,2},{2,3},{3,4},{4,5},{5,6},{6,7},{7,0},{8,9},{9,10},{10,1... | collective-permute-start | bytes 786440 | tf_op jit(solution)/shard_map/ppermute | solution.py:88
  57.3 6.4 %collective-permute-start.7 = (bf16[256,512]{1,0:T(8,128)(2,1)S(1)}, bf16[256,512]{1,0:T(8,128)(2,1)S(1)}, u32[]{:S(2)}, u32[]{:S(2)}) collective-permute-start(bf16[256,512]{1,0:T(8,128)(2,1)S(1)} %slice.40), channel_id=1, source_target_pairs={{0,7},{1,0},{2,1},{3,2},{4,3},{5,4},{6,5},{7,6},{8,15},{9,8},{10,9... | collective-permute-start | bytes 786440 | tf_op jit(solution)/shard_map/ppermute | solution.py:89
Sparse Core Ops, SparseCore 0:
  13.0 103.2 all-gather.1
  131.6 55.6 reduce-scatter.1

commit v13 on v12

--- a/solution.py
+++ b/solution.py
@@ -14,16 +14,10 @@
 CAP = 2
 
 
-def attend_kernel(flat_ref, q_ref, kv0_ref, kv1_ref, o_ref, *, entry_len):
+def attend_kernel(flat_ref, q_ref, kv0_ref, kv1_ref, live_ref, o_ref, *, entry_len):
     head_cols = q_ref.shape[1]
     factor = 1.0 / math.sqrt(HD)
-    live = jnp.concatenate(
-        [
-            kv0_ref[0, entry_len:entry_len + 1, :entry_len],
-            kv1_ref[0, entry_len:entry_len + 1, :entry_len],
-        ],
-        axis=1,
-    ).astype(jnp.float32)
+    live = live_ref[0]
     key_open = live > 0
     for h in range(head_cols // HD):
         cols = slice(h * HD, (h + 1) * HD)
@@ -42,7 +36,7 @@
         o_ref[:, cols] = att.astype(o_ref.dtype)
 
 
-def attend(flat_idx, queries, slots, entry_len):
+def attend(flat_idx, queries, slots, live, entry_len):
     tok_rows, head_cols = queries.shape
     segment_count = flat_idx.shape[0] // NBRS
     seg_rows = tok_rows // segment_count
@@ -54,6 +48,7 @@
             pl.BlockSpec((seg_rows, head_cols), lambda s, f: (s, 0)),
             pl.BlockSpec((1, slot_rows, kv_cols), lambda s, f: (f[s * NBRS], 0, 0)),
             pl.BlockSpec((1, slot_rows, kv_cols), lambda s, f: (f[s * NBRS + 1], 0, 0)),
+            pl.BlockSpec((1, 1, live.shape[2]), lambda s, f: (s, 0, 0)),
         ],
         out_specs=pl.BlockSpec((seg_rows, head_cols), lambda s, f: (s, 0)),
     )
@@ -61,7 +56,7 @@
         functools.partial(attend_kernel, entry_len=entry_len),
         out_shape=jax.ShapeDtypeStruct((tok_rows, head_cols), jnp.bfloat16),
         grid_spec=grid_spec,
-    )(flat_idx, queries, slots, slots)
+    )(flat_idx, queries, slots, slots, live)
 
 
 def local(dp_count, retr_count, tensor_count, hidden_in, norm_gain, nbr_table, encodings, enc_mask, w_query, w_key, w_value, w_out):
@@ -100,12 +95,13 @@
     keys_t = own_kv[:, :, :head_cols].reshape(per_dev, entry_len, head_count, HD)
     keys_t = keys_t.transpose(0, 3, 2, 1).reshape(per_dev, HD, head_count * entry_len)
     own_kv = jnp.concatenate([keys_t, own_kv[:, :, head_cols:]], axis=2)
-    key_live = jnp.repeat(mask_half, BLOCK, axis=1).astype(jnp.bfloat16)
-    mask_rows = jnp.zeros((per_dev, 8, 2 * head_cols), jnp.bfloat16)
-    mask_rows = mask_rows.at[:, 0, :entry_len].set(key_live)
-    own = jnp.concatenate([own_kv, mask_rows], axis=1)
-    slots = lax.all_gather(own, "retr", axis=0, tiled=True)
+    slots = lax.all_gather(own_kv, "retr", axis=0, tiled=True)
     slot_of = wanted
+    mask_copies = jnp.broadcast_to(mask_half[None], (retr_count,) + mask_half.shape)
+    all_marks = lax.all_to_all(mask_copies, "retr", 0, 0, tiled=True)
+    all_marks = all_marks.reshape(retr_count * nb_dev, mask_cols)
+    key_live = jnp.repeat(jnp.take(all_marks, wanted, axis=0), BLOCK, axis=1)
+    key_live = key_live.astype(jnp.float32).reshape(segment_count, 1, NBRS * entry_len)
 
     widened = [p.astype(jnp.float32) for _, p in pieces]
     sum_sq = sum(jnp.sum(w * w, axis=-1, keepdims=True) for w in widened)
@@ -120,7 +116,7 @@
         acc = part if acc is None else acc + part
     queries = acc.astype(jnp.bfloat16)
 
-    attended = attend(slot_of, queries, slots, entry_len)
+    attended = attend(slot_of, queries, slots, key_live, entry_len)
     partial_value = jnp.dot(attended, w_out, preferred_element_type=jnp.float32)
     summed = lax.psum_scatter(
         partial_value.astype(jnp.bfloat16), "tensor", scatter_dimension=1, tiled=True

time: 197 us -> 191 us (0.970)
  waiting for transfers between devices: 135 us -> 120 us
  starting transfers between devices: 14.9 us -> 23.4 us
    ppermute x3, waiting for transfers between devices: 29.4 us -> 0.01 us  [local(): up = lax.ppermute(up, 'tensor', fwd)]
    ppermute x3, waiting for transfers between devices: 0.01 us -> 18.4 us  [local(): down = lax.ppermute(down, 'tensor', bwd)]
    all_gather x1, waiting for transfers between devices: 46.6 us -> 39.6 us  [local(): slots = lax.all_gather(own_kv, 'retr', axis=0, tiled=True)]
    all_to_all x0 -> x1, starting transfers between devices: none -> 6.28 us  [local(): all_marks = lax.all_to_all(mask_copies, 'retr', 0, 0, tiled=True)]
    ppermute x3, starting transfers between devices: 9.38 us -> 13.3 us  [local(): down = lax.ppermute(down, 'tensor', bwd)]
    ppermute x1, waiting for transfers between devices: 0.01 us -> 2.66 us  [local(): bottom = lax.ppermute(down[half_rows:], 'tensor', bwd)]
    ppermute x3, starting transfers between devices: 2.54 us -> 0.01 us  [local(): up = lax.ppermute(up, 'tensor', fwd)]
  transfers between devices with their start and end apart: 10 -> 11, of which waited for: 6 -> 7; matrix products, arithmetic and copies ran while one was open for 5% -> 6% of each run, Pallas kernels for 0% -> 0%
where the time goes in v13:
time: 191 us
  waiting for transfers between devices  120 us (63%)
  starting transfers between devices  23.4 us (12%)
  matrix products  15.4 us (8%)
  between operations  13.8 us (7%)
  Pallas kernels  8.46 us (4%)
  other arithmetic  5.64 us (3%)
  local copies, waits for them, and re-layouts  4.46 us (2%)
    reduce_scatter x1, waiting for transfers between devices, local(): lax.psum_scatter(partial_value.astype(jnp.bfloat16), 'tensor', scatter_di...  55.6 us
    all_gather x1, waiting for transfers between devices, local(): slots = lax.all_gather(own_kv, 'retr', axis=0, tiled=True)  39.6 us
    ppermute x3, waiting for transfers between devices, local(): down = lax.ppermute(down, 'tensor', bwd)  18.4 us
    ppermute x3, starting transfers between devices, local(): down = lax.ppermute(down, 'tensor', bwd)  13.3 us
    pallas_call x1, Pallas kernels, attend(): pl.pallas_call(functools.partial(attend_kernel, entry_len=entry_len), out...  8.46 us
    dot_general x1, matrix products, local(): partial_value = jnp.dot(attended, w_out, preferred_element_type=jnp.float32)  6.63 us
    all_to_all x1, starting transfers between devices, local(): all_marks = lax.all_to_all(mask_copies, 'retr', 0, 0, tiled=True)  6.28 us
    dot_general x8, matrix products, local(): part = jnp.dot(normed, w_rows, preferred_element_type=jnp.float32)  5.95 us
  transfers between devices with their start and end apart: 11, of which 7 were waited for; matrix products, arithmetic and copies ran while one was open for 6% of the time, Pallas kernels for 0%

profile of v13, /device:TPU:1, one launch (start us, length us, event | category | flops | bytes accessed | tf_op | source)
XLA Modules:
  0.0 190.8 jit_solution(3262488231904856718)
XLA Ops:
  6.5 1.2 copy-done
  7.8 2.8 %fusion.4 = bf16[1024,512]{0,1:T(8,128)(2,1)S(1)} fusion(bf16[512,1024]{1,0:T(8,128)(2,1)S(1)} %bitcast.11, bf16[1024,512]{1,0:T(8,128)(2,1)} %param.16, bf16[1024,512]{1,0:T(8,128)(2,1)} %param.15), kind=kOutput, calls=%fused_computation.9 | convolution fusion | flops 1078460416 | bytes 4194304 | tf_op jit(solution)/shard_map/dot_general | solution.py:91
  10.6 0.1 fusion.77
  10.7 0.1 reshape.115
  10.8 0.5 copy.17
  11.3 0.2 reshape.116
  11.5 1.1 pad_maximum_fusion
  12.7 6.5 %collective-permute-start.1 = (bf16[512,512]{1,0:T(8,128)(2,1)S(1)}, bf16[512,512]{1,0:T(8,128)(2,1)S(1)}, u32[]{:S(2)}, u32[]{:S(2)}) collective-permute-start(bf16[512,512]{1,0:T(8,128)(2,1)S(1)} %copy-done.1), channel_id=1, source_target_pairs={{0,7},{1,0},{2,1},{3,2},{4,3},{5,4},{6,5},{7,6},{8,15},{9,8},{10,9... | collective-permute-start | bytes 1572872 | tf_op jit(solution)/shard_map/ppermute | solution.py:79
  19.1 0.6 broadcast_in_dim.15
  19.8 6.3 %all-to-all-start = ((s32[16,4,4]{2,1,0:T(4,128)}), s32[16,4,4]{2,1,0:T(4,128)S(1)}, u32[]{:S(2)}, u32[]{:S(2)}) async-start(s32[16,4,4]{2,1,0:T(4,128)} %broadcast_in_dim.15), calls=%async_computation | async-start | bytes 65536 | tf_op jit(solution)/shard_map/all_to_all | solution.py:101
  26.2 0.1 copy.16
  26.3 0.1 reshape.112.flat_ref
  26.4 0.1 reshape.118
  26.5 0.1 fusion.78
  26.6 0.2 fusion.29
  26.8 3.0 %collective-permute-done.1 = bf16[512,512]{1,0:T(8,128)(2,1)S(1)} collective-permute-done((bf16[512,512]{1,0:T(8,128)(2,1)S(1)}, bf16[512,512]{1,0:T(8,128)(2,1)S(1)}, u32[]{:S(2)}, u32[]{:S(2)}) %collective-permute-start.1) | collective-permute-done | bytes 524320 | tf_op jit(solution)/shard_map/ppermute | solution.py:79
  29.7 3.4 %collective-permute-start.3 = (bf16[512,512]{1,0:T(8,128)(2,1)S(1)}, bf16[512,512]{1,0:T(8,128)(2,1)S(1)}, u32[]{:S(2)}, u32[]{:S(2)}) collective-permute-start(bf16[512,512]{1,0:T(8,128)(2,1)S(1)} %collective-permute-done.1), channel_id=1, source_target_pairs={{0,7},{1,0},{2,1},{3,2},{4,3},{5,4},{6,5},{7,6},{8,15},{9,8},{10,9... | collective-permute-start | bytes 1572872 | tf_op jit(solution)/shard_map/ppermute | solution.py:79
  33.2 0.6 gather_fusion
  33.7 0.1 select_convert_fusion
  33.8 0.1 broadcast_in_dim.17
  33.9 0.7 convert_element_type.101.live_ref
  34.6 8.3 %collective-permute-done.3 = bf16[512,512]{1,0:T(8,128)(2,1)S(1)} collective-permute-done((bf16[512,512]{1,0:T(8,128)(2,1)S(1)}, bf16[512,512]{1,0:T(8,128)(2,1)S(1)}, u32[]{:S(2)}, u32[]{:S(2)}) %collective-permute-start.3) | collective-permute-done | bytes 524320 | tf_op jit(solution)/shard_map/ppermute | solution.py:79
  42.9 3.4 %collective-permute-start.5 = (bf16[512,512]{1,0:T(8,128)(2,1)S(1)}, bf16[512,512]{1,0:T(8,128)(2,1)S(1)}, u32[]{:S(2)}, u32[]{:S(2)}) collective-permute-start(bf16[512,512]{1,0:T(8,128)(2,1)S(1)} %collective-permute-done.3), channel_id=1, source_target_pairs={{0,7},{1,0},{2,1},{3,2},{4,3},{5,4},{6,5},{7,6},{8,15},{9,8},{10,9... | collective-permute-start | bytes 1572872 | tf_op jit(solution)/shard_map/ppermute | solution.py:79
  46.3 0.2 fusion.11
  46.5 0.2 fusion.8
  46.7 0.2 fusion.17
  46.8 1.2 fusion.14
  48.1 7.1 %collective-permute-done.5 = bf16[512,512]{1,0:T(8,128)(2,1)S(1)} collective-permute-done((bf16[512,512]{1,0:T(8,128)(2,1)S(1)}, bf16[512,512]{1,0:T(8,128)(2,1)S(1)}, u32[]{:S(2)}, u32[]{:S(2)}) %collective-permute-start.5) | collective-permute-done | bytes 524320 | tf_op jit(solution)/shard_map/ppermute | solution.py:79
  55.2 3.5 %collective-permute-start.7 = (bf16[256,512]{1,0:T(8,128)(2,1)S(1)}, bf16[256,512]{1,0:T(8,128)(2,1)S(1)}, u32[]{:S(2)}, u32[]{:S(2)}) collective-permute-start(bf16[256,512]{1,0:T(8,128)(2,1)S(1)} %slice.19), channel_id=1, source_target_pairs={{0,7},{1,0},{2,1},{3,2},{4,3},{5,4},{6,5},{7,6},{8,15},{9,8},{10,9... | collective-permute-start | bytes 786440 | tf_op jit(solution)/shard_map/ppermute | solution.py:84
  58.7 0.3 collective-permute-start.6
  59.0 0.2 fusion.23
  59.2 0.2 fusion.20
  59.4 2.7 %collective-permute-done.7 = bf16[256,512]{1,0:T(8,128)(2,1)S(1)} collective-permute-done((bf16[256,512]{1,0:T(8,128)(2,1)S(1)}, bf16[256,512]{1,0:T(8,128)(2,1)S(1)}, u32[]{:S(2)}, u32[]{:S(2)}) %collective-permute-start.7) | collective-permute-done | bytes 262176 | tf_op jit(solution)/shard_map/ppermute | solution.py:84
  62.0 3.4 %collective-permute-done.6 = bf16[256,512]{1,0:T(8,128)(2,1)S(1)} collective-permute-done((bf16[256,512]{1,0:T(8,128)(2,1)S(1)}, bf16[256,512]{1,0:T(8,128)(2,1)S(1)}, u32[]{:S(2)}, u32[]{:S(2)}) %collective-permute-start.6) | collective-permute-done | bytes 262176 | tf_op jit(solution)/shard_map/ppermute | solution.py:83
  65.4 0.2 fusion.26
  65.6 0.5 fusion.33
  66.1 0.5 convolution_add_fusion.6
  66.7 0.5 convolution_add_fusion.5
  67.2 1.6 convolution_add_fusion.4
  68.8 0.5 convolution_add_fusion.3
  69.3 0.5 convolution_add_fusion.2
  69.8 0.5 convolution_add_fusion.1
  70.3 1.3 fusion.7.q_ref
  71.6 39.6 %all-gather.2.cloned.1.call-done.kv0_ref.kv1_ref = bf16[64,128,1024]{2,1,0:T(8,128)(2,1)} async-done(((bf16[4,128,1024]{2,1,0:T(8,128)(2,1)}), bf16[64,128,1024]{2,1,0:T(8,128)(2,1)}) %all-gather.2.cloned.1.call-update) | async-done | bytes 16777232 | tf_op jit(solution)/shard_map/all_gather | solution.py:98
  111.3 8.5 %shard_map.91 = bf16[512,512]{1,0:T(8,128)(2,1)} custom-call(s32[16]{0:T(128)} %copy-done.5, bf16[512,512]{1,0:T(8,128)(2,1)} %fusion.7.q_ref, bf16[64,128,1024]{2,1,0:T(8,128)(2,1)} %all-gather.2.cloned.1.call-done.kv0_ref.kv1_ref, bf16[64,128,1024]{2,1,0:T(8,128)(2,1)} %all-gather.2.cloned.1.call-done.kv0_ref.kv1_ref, ...), custom_call_target="tpu_custom_call" | custom-call | tf_op jit(solution)/shard_map/pallas_call | solution.py:55
  119.7 6.6 %convolution_convert_fusion = bf16[512,4096]{1,0:T(8,128)(2,1)} fusion(bf16[512,512]{1,0:T(8,128)(2,1)} %shard_map.91, bf16[512,4096]{1,0:T(8,128)(2,1)} %param.17), kind=kOutput, calls=%fused_computation.1 | convolution fusion | flops 2149580800 | bytes 8912896 | tf_op jit(solution)/shard_map/dot_general | solution.py:120
  126.4 55.6 %reduce-scatter.2.cloned.1.call-done = bf16[512,512]{1,0:T(8,128)(2,1)} async-done(((bf16[512,4096]{1,0:T(8,128)(2,1)}), bf16[512,512]{1,0:T(8,128)(2,1)}) %reduce-scatter.2.cloned.1.call-update) | async-done | bytes 524304 | tf_op jit(solution)/shard_map/reduce_scatter | solution.py:121
  182.0 2.0 %fusion.32 = bf16[512,512]{1,0:T(8,128)(2,1)} fusion(bf16[512,512]{1,0:T(8,128)(2,1)S(1)} %copy-done.1, bf16[512,512]{1,0:T(8,128)(2,1)} %reduce-scatter.2.cloned.1.call-done), kind=kLoop, calls=%fused_computation.56 | loop fusion | flops 1048576 | bytes 1572864 | tf_op jit(solution)/shard_map/convert_element_type | solution.py:124
  (30 shorter events, 0.2 us)
Async XLA Ops:
  6.5 1.2 copy-start
  6.5 104.7 %all-gather.2.cloned.1.call-start = ((), (), s32[]{:S(2)}) async-start(), calls=%async_computation.2 | async-start | bytes 17825792 | tf_op jit(solution)/shard_map/all_gather | solution.py:98
  10.6 2.1 %copy-start.1 = (bf16[512,512]{1,0:T(8,128)(2,1)S(1)}, bf16[512,512]{1,0:T(8,128)(2,1)}, u32[]{:S(2)}) copy-start(bf16[512,512]{1,0:T(8,128)(2,1)} %param.9) | copy-start | bytes 1572868
  10.6 8.6 %copy-start.4 = (s32[4,4]{1,0:T(4,128)S(1)}, s32[4,4]{1,0:T(4,128)}, u32[]{:S(2)}) copy-start(s32[4,4]{1,0:T(4,128)} %param.13) | copy-start | bytes 196
  10.6 15.6 %copy-start.6 = (s32[8,2]{0,1:T(2,128)S(1)}, s32[8,2]{0,1:T(2,128)}, u32[]{:S(2)}) copy-start(s32[8,2]{0,1:T(2,128)} %param.11) | copy-start | bytes 196
  10.6 15.9 %copy-start.3 = (f32[4096]{0:T(1024)S(1)}, f32[4096]{0:T(1024)}, u32[]{:S(2)}) copy-start(f32[4096]{0:T(1024)} %param.10) | copy-start | bytes 49156
  12.7 17.1 %collective-permute-start.1 = (bf16[512,512]{1,0:T(8,128)(2,1)S(1)}, bf16[512,512]{1,0:T(8,128)(2,1)S(1)}, u32[]{:S(2)}, u32[]{:S(2)}) collective-permute-start(bf16[512,512]{1,0:T(8,128)(2,1)S(1)} %copy-done.1), channel_id=1, source_target_pairs={{0,7},{1,0},{2,1},{3,2},{4,3},{5,4},{6,5},{7,6},{8,15},{9,8},{10,9... | collective-permute-start | bytes 1572872 | tf_op jit(solution)/shard_map/ppermute | solution.py:79
  19.1 14.0 %collective-permute-start = (bf16[512,512]{1,0:T(8,128)(2,1)S(1)}, bf16[512,512]{1,0:T(8,128)(2,1)S(1)}, u32[]{:S(2)}, u32[]{:S(2)}) collective-permute-start(bf16[512,512]{1,0:T(8,128)(2,1)S(1)} %copy-done.1), channel_id=1, source_target_pairs={{0,1},{1,2},{2,3},{3,4},{4,5},{5,6},{6,7},{7,0},{8,9},{9,10},{10,1... | collective-permute-start | bytes 1572872 | tf_op jit(solution)/shard_map/ppermute | solution.py:78
  19.8 13.4 %all-to-all-start = ((s32[16,4,4]{2,1,0:T(4,128)}), s32[16,4,4]{2,1,0:T(4,128)S(1)}, u32[]{:S(2)}, u32[]{:S(2)}) async-start(s32[16,4,4]{2,1,0:T(4,128)} %broadcast_in_dim.15), calls=%async_computation | async-start | bytes 65536 | tf_op jit(solution)/shard_map/all_to_all | solution.py:101
  26.0 156.0 %reduce-scatter.2.cloned.1.call-start = ((), (), s32[]{:S(2)}) async-start(), calls=%async_computation.3 | async-start | bytes 4718592 | tf_op jit(solution)/shard_map/reduce_scatter | solution.py:121
  26.4 40.3 %copy-start.5 = (s32[16]{0:T(128)}, s32[16]{0:T(128)S(1)}, u32[]{:S(2)}) copy-start(s32[16]{0:T(128)S(1)} %reshape.112.flat_ref) | copy-start | bytes 196
  29.7 13.2 %collective-permute-start.3 = (bf16[512,512]{1,0:T(8,128)(2,1)S(1)}, bf16[512,512]{1,0:T(8,128)(2,1)S(1)}, u32[]{:S(2)}, u32[]{:S(2)}) collective-permute-start(bf16[512,512]{1,0:T(8,128)(2,1)S(1)} %collective-permute-done.1), channel_id=1, source_target_pairs={{0,7},{1,0},{2,1},{3,2},{4,3},{5,4},{6,5},{7,6},{8,15},{9,8},{10,9... | collective-permute-start | bytes 1572872 | tf_op jit(solution)/shard_map/ppermute | solution.py:79
  33.1 13.2 %collective-permute-start.2 = (bf16[512,512]{1,0:T(8,128)(2,1)S(1)}, bf16[512,512]{1,0:T(8,128)(2,1)}, u32[]{:S(2)}, u32[]{:S(2)}) collective-permute-start(bf16[512,512]{1,0:T(8,128)(2,1)S(1)} %collective-permute-done), channel_id=1, source_target_pairs={{0,1},{1,2},{2,3},{3,4},{4,5},{5,6},{6,7},{7,0},{8,9},{9,10},{10,1... | collective-permute-start | bytes 1572872 | tf_op jit(solution)/shard_map/ppermute | solution.py:78
  34.6 31.0 %copy-start.2 = (bf16[4096,512]{1,0:T(8,128)(2,1)S(1)}, bf16[4096,512]{1,0:T(8,128)(2,1)}, u32[]{:S(2)}) copy-start(bf16[4096,512]{1,0:T(8,128)(2,1)} %param.14) | copy-start | bytes 12582916
  42.9 12.3 %collective-permute-start.5 = (bf16[512,512]{1,0:T(8,128)(2,1)S(1)}, bf16[512,512]{1,0:T(8,128)(2,1)S(1)}, u32[]{:S(2)}, u32[]{:S(2)}) collective-permute-start(bf16[512,512]{1,0:T(8,128)(2,1)S(1)} %collective-permute-done.3), channel_id=1, source_target_pairs={{0,7},{1,0},{2,1},{3,2},{4,3},{5,4},{6,5},{7,6},{8,15},{9,8},{10,9... | collective-permute-start | bytes 1572872 | tf_op jit(solution)/shard_map/ppermute | solution.py:79
  46.3 12.4 %collective-permute-start.4 = (bf16[512,512]{1,0:T(8,128)(2,1)}, bf16[512,512]{1,0:T(8,128)(2,1)S(1)}, u32[]{:S(2)}, u32[]{:S(2)}) collective-permute-start(bf16[512,512]{1,0:T(8,128)(2,1)} %collective-permute-done.2), channel_id=1, source_target_pairs={{0,1},{1,2},{2,3},{3,4},{4,5},{5,6},{6,7},{7,0},{8,9},{9,10},{10,1... | collective-permute-start | bytes 1572872 | tf_op jit(solution)/shard_map/ppermute | solution.py:78
  55.2 6.8 %collective-permute-start.7 = (bf16[256,512]{1,0:T(8,128)(2,1)S(1)}, bf16[256,512]{1,0:T(8,128)(2,1)S(1)}, u32[]{:S(2)}, u32[]{:S(2)}) collective-permute-start(bf16[256,512]{1,0:T(8,128)(2,1)S(1)} %slice.19), channel_id=1, source_target_pairs={{0,7},{1,0},{2,1},{3,2},{4,3},{5,4},{6,5},{7,6},{8,15},{9,8},{10,9... | collective-permute-start | bytes 786440 | tf_op jit(solution)/shard_map/ppermute | solution.py:84
  58.7 6.7 %collective-permute-start.6 = (bf16[256,512]{1,0:T(8,128)(2,1)S(1)}, bf16[256,512]{1,0:T(8,128)(2,1)S(1)}, u32[]{:S(2)}, u32[]{:S(2)}) collective-permute-start(bf16[256,512]{1,0:T(8,128)(2,1)S(1)} %slice.18), channel_id=1, source_target_pairs={{0,1},{1,2},{2,3},{3,4},{4,5},{5,6},{6,7},{7,0},{8,9},{9,10},{10,1... | collective-permute-start | bytes 786440 | tf_op jit(solution)/shard_map/ppermute | solution.py:83
Sparse Core Ops, SparseCore 0:
  12.8 98.4 all-gather.1
  126.5 55.4 reduce-scatter.1

commit v14 on v13

--- a/solution.py
+++ b/solution.py
@@ -12,28 +12,34 @@
 NBRS = 2
 BLOCK = 32
 CAP = 2
+SEGS_PER_STEP = 2
 
 
-def attend_kernel(flat_ref, q_ref, kv0_ref, kv1_ref, live_ref, o_ref, *, entry_len):
+def attend_kernel(flat_ref, q_ref, *refs, entry_len):
+    kv_refs, live_ref, o_ref = refs[:-2], refs[-2], refs[-1]
     head_cols = q_ref.shape[1]
+    seg_rows = q_ref.shape[0] // SEGS_PER_STEP
     factor = 1.0 / math.sqrt(HD)
-    live = live_ref[0]
-    key_open = live > 0
-    for h in range(head_cols // HD):
-        cols = slice(h * HD, (h + 1) * HD)
-        vcols = slice(head_cols + h * HD, head_cols + (h + 1) * HD)
-        kcols = slice(h * entry_len, (h + 1) * entry_len)
-        keys_t = jnp.concatenate([kv0_ref[0, :HD, kcols], kv1_ref[0, :HD, kcols]], axis=1)
-        values = jnp.concatenate(
-            [kv0_ref[0, :entry_len, vcols], kv1_ref[0, :entry_len, vcols]], axis=0
-        )
-        scores = jnp.dot(q_ref[:, cols], keys_t, preferred_element_type=jnp.float32) * factor
-        scores = jnp.where(key_open, scores, -1e30)
-        row_max = jnp.max(scores, axis=-1, keepdims=True)
-        weights = jnp.exp(scores - row_max) * live
-        probs = (weights / jnp.sum(weights, axis=-1, keepdims=True)).astype(jnp.bfloat16)
-        att = jnp.dot(probs, values, preferred_element_type=jnp.float32)
-        o_ref[:, cols] = att.astype(o_ref.dtype)
+    for g in range(SEGS_PER_STEP):
+        kv0_ref, kv1_ref = kv_refs[g * NBRS], kv_refs[g * NBRS + 1]
+        rows = slice(g * seg_rows, (g + 1) * seg_rows)
+        live = live_ref[g]
+        key_open = live > 0
+        for h in range(head_cols // HD):
+            cols = slice(h * HD, (h + 1) * HD)
+            vcols = slice(head_cols + h * HD, head_cols + (h + 1) * HD)
+            kcols = slice(h * entry_len, (h + 1) * entry_len)
+            keys_t = jnp.concatenate([kv0_ref[0, :HD, kcols], kv1_ref[0, :HD, kcols]], axis=1)
+            values = jnp.concatenate(
+                [kv0_ref[0, :entry_len, vcols], kv1_ref[0, :entry_len, vcols]], axis=0
+            )
+            scores = jnp.dot(q_ref[rows, cols], keys_t, preferred_element_type=jnp.float32) * factor
+            scores = jnp.where(key_open, scores, -1e30)
+            row_max = jnp.max(scores, axis=-1, keepdims=True)
+            weights = jnp.exp(scores - row_max) * live
+            probs = (weights / jnp.sum(weights, axis=-1, keepdims=True)).astype(jnp.bfloat16)
+            att = jnp.dot(probs, values, preferred_element_type=jnp.float32)
+            o_ref[rows, cols] = att.astype(o_ref.dtype)
 
 
 def attend(flat_idx, queries, slots, live, entry_len):
@@ -41,22 +47,24 @@
     segment_count = flat_idx.shape[0] // NBRS
     seg_rows = tok_rows // segment_count
     slot_rows, kv_cols = slots.shape[1], slots.shape[2]
+    per_step = NBRS * SEGS_PER_STEP
+
+    def kv_spec(j):
+        return pl.BlockSpec((1, slot_rows, kv_cols), lambda s, f: (f[s * per_step + j], 0, 0))
+
     grid_spec = pltpu.PrefetchScalarGridSpec(
         num_scalar_prefetch=1,
-        grid=(segment_count,),
-        in_specs=[
-            pl.BlockSpec((seg_rows, head_cols), lambda s, f: (s, 0)),
-            pl.BlockSpec((1, slot_rows, kv_cols), lambda s, f: (f[s * NBRS], 0, 0)),
-            pl.BlockSpec((1, slot_rows, kv_cols), lambda s, f: (f[s * NBRS + 1], 0, 0)),
-            pl.BlockSpec((1, 1, live.shape[2]), lambda s, f: (s, 0, 0)),
-        ],
-        out_specs=pl.BlockSpec((seg_rows, head_cols), lambda s, f: (s, 0)),
+        grid=(segment_count // SEGS_PER_STEP,),
+        in_specs=[pl.BlockSpec((seg_rows * SEGS_PER_STEP, head_cols), lambda s, f: (s, 0))]
+        + [kv_spec(j) for j in range(per_step)]
+        + [pl.BlockSpec((SEGS_PER_STEP, 1, live.shape[2]), lambda s, f: (s, 0, 0))],
+        out_specs=pl.BlockSpec((seg_rows * SEGS_PER_STEP, head_cols), lambda s, f: (s, 0)),
     )
     return pl.pallas_call(
         functools.partial(attend_kernel, entry_len=entry_len),
         out_shape=jax.ShapeDtypeStruct((tok_rows, head_cols), jnp.bfloat16),
         grid_spec=grid_spec,
-    )(flat_idx, queries, slots, slots, live)
+    )(flat_idx, queries, *([slots] * per_step), live)
 
 
 def local(dp_count, retr_count, tensor_count, hidden_in, norm_gain, nbr_table, encodings, enc_mask, w_query, w_key, w_value, w_out):

time: 191 us -> 189 us (0.990)
  Pallas kernels: 8.46 us -> 5.97 us
    pallas_call x1, Pallas kernels: 8.46 us -> 5.97 us  [attend(): pl.pallas_call(functools.partial(attend_kernel, entry_len=entry_len), out...]
where the time goes in v14:
time: 189 us; the launch traced here: 188 us
  waiting for transfers between devices  120 us (63%)
  starting transfers between devices  23.4 us (12%)
  matrix products  15.4 us (8%)
  between operations  13.8 us (7%)
  Pallas kernels  5.97 us (3%)
  other arithmetic  5.64 us (3%)
  local copies, waits for them, and re-layouts  4.46 us (2%)
    reduce_scatter x1, waiting for transfers between devices, local(): lax.psum_scatter(partial_value.astype(jnp.bfloat16), 'tensor', scatter_di...  55.6 us
    all_gather x1, waiting for transfers between devices, local(): slots = lax.all_gather(own_kv, 'retr', axis=0, tiled=True)  39.6 us
    ppermute x3, waiting for transfers between devices, local(): down = lax.ppermute(down, 'tensor', bwd)  18.4 us
    ppermute x3, starting transfers between devices, local(): down = lax.ppermute(down, 'tensor', bwd)  13.3 us
    dot_general x1, matrix products, local(): partial_value = jnp.dot(attended, w_out, preferred_element_type=jnp.float32)  6.63 us
    all_to_all x1, starting transfers between devices, local(): all_marks = lax.all_to_all(mask_copies, 'retr', 0, 0, tiled=True)  6.28 us
    pallas_call x1, Pallas kernels, attend(): pl.pallas_call(functools.partial(attend_kernel, entry_len=entry_len), out...  5.97 us
    dot_general x8, matrix products, local(): part = jnp.dot(normed, w_rows, preferred_element_type=jnp.float32)  5.95 us
  transfers between devices with their start and end apart: 11, of which 7 were waited for; matrix products, arithmetic and copies ran while one was open for 6% of the time, Pallas kernels for 0%

profile of v14, /device:TPU:1, one launch (start us, length us, event | category | flops | bytes accessed | tf_op | source)
XLA Modules:
  0.0 188.3 jit_solution(3141645725846251901)
XLA Ops:
  6.5 1.2 copy-done
  7.8 2.8 %fusion.4 = bf16[1024,512]{0,1:T(8,128)(2,1)S(1)} fusion(bf16[512,1024]{1,0:T(8,128)(2,1)S(1)} %bitcast.11, bf16[1024,512]{1,0:T(8,128)(2,1)} %param.16, bf16[1024,512]{1,0:T(8,128)(2,1)} %param.15), kind=kOutput, calls=%fused_computation.9 | convolution fusion | flops 1078460416 | bytes 4194304 | tf_op jit(solution)/shard_map/dot_general | solution.py:99
  10.6 0.1 fusion.77
  10.7 0.1 reshape.115
  10.8 0.5 copy.17
  11.3 0.2 reshape.116
  11.5 1.1 pad_maximum_fusion
  12.7 6.5 %collective-permute-start.1 = (bf16[512,512]{1,0:T(8,128)(2,1)S(1)}, bf16[512,512]{1,0:T(8,128)(2,1)S(1)}, u32[]{:S(2)}, u32[]{:S(2)}) collective-permute-start(bf16[512,512]{1,0:T(8,128)(2,1)S(1)} %copy-done.1), channel_id=1, source_target_pairs={{0,7},{1,0},{2,1},{3,2},{4,3},{5,4},{6,5},{7,6},{8,15},{9,8},{10,9... | collective-permute-start | bytes 1572872 | tf_op jit(solution)/shard_map/ppermute | solution.py:87
  19.1 0.6 broadcast_in_dim.15
  19.8 6.3 %all-to-all-start = ((s32[16,4,4]{2,1,0:T(4,128)}), s32[16,4,4]{2,1,0:T(4,128)S(1)}, u32[]{:S(2)}, u32[]{:S(2)}) async-start(s32[16,4,4]{2,1,0:T(4,128)} %broadcast_in_dim.15), calls=%async_computation | async-start | bytes 65536 | tf_op jit(solution)/shard_map/all_to_all | solution.py:109
  26.2 0.1 copy.16
  26.3 0.1 reshape.112.flat_ref
  26.4 0.1 reshape.118
  26.5 0.1 fusion.78
  26.6 0.2 fusion.29
  26.8 3.0 %collective-permute-done.1 = bf16[512,512]{1,0:T(8,128)(2,1)S(1)} collective-permute-done((bf16[512,512]{1,0:T(8,128)(2,1)S(1)}, bf16[512,512]{1,0:T(8,128)(2,1)S(1)}, u32[]{:S(2)}, u32[]{:S(2)}) %collective-permute-start.1) | collective-permute-done | bytes 524320 | tf_op jit(solution)/shard_map/ppermute | solution.py:87
  29.7 3.4 %collective-permute-start.3 = (bf16[512,512]{1,0:T(8,128)(2,1)S(1)}, bf16[512,512]{1,0:T(8,128)(2,1)S(1)}, u32[]{:S(2)}, u32[]{:S(2)}) collective-permute-start(bf16[512,512]{1,0:T(8,128)(2,1)S(1)} %collective-permute-done.1), channel_id=1, source_target_pairs={{0,7},{1,0},{2,1},{3,2},{4,3},{5,4},{6,5},{7,6},{8,15},{9,8},{10,9... | collective-permute-start | bytes 1572872 | tf_op jit(solution)/shard_map/ppermute | solution.py:87
  33.2 0.6 gather_fusion
  33.7 0.1 select_convert_fusion
  33.8 0.1 broadcast_in_dim.17
  33.9 0.7 convert_element_type.101.refs_4_
  34.6 8.3 %collective-permute-done.3 = bf16[512,512]{1,0:T(8,128)(2,1)S(1)} collective-permute-done((bf16[512,512]{1,0:T(8,128)(2,1)S(1)}, bf16[512,512]{1,0:T(8,128)(2,1)S(1)}, u32[]{:S(2)}, u32[]{:S(2)}) %collective-permute-start.3) | collective-permute-done | bytes 524320 | tf_op jit(solution)/shard_map/ppermute | solution.py:87
  42.9 3.4 %collective-permute-start.5 = (bf16[512,512]{1,0:T(8,128)(2,1)S(1)}, bf16[512,512]{1,0:T(8,128)(2,1)S(1)}, u32[]{:S(2)}, u32[]{:S(2)}) collective-permute-start(bf16[512,512]{1,0:T(8,128)(2,1)S(1)} %collective-permute-done.3), channel_id=1, source_target_pairs={{0,7},{1,0},{2,1},{3,2},{4,3},{5,4},{6,5},{7,6},{8,15},{9,8},{10,9... | collective-permute-start | bytes 1572872 | tf_op jit(solution)/shard_map/ppermute | solution.py:87
  46.3 0.2 fusion.11
  46.5 0.2 fusion.8
  46.7 0.2 fusion.17
  46.8 1.2 fusion.14
  48.1 7.1 %collective-permute-done.5 = bf16[512,512]{1,0:T(8,128)(2,1)S(1)} collective-permute-done((bf16[512,512]{1,0:T(8,128)(2,1)S(1)}, bf16[512,512]{1,0:T(8,128)(2,1)S(1)}, u32[]{:S(2)}, u32[]{:S(2)}) %collective-permute-start.5) | collective-permute-done | bytes 524320 | tf_op jit(solution)/shard_map/ppermute | solution.py:87
  55.2 3.5 %collective-permute-start.7 = (bf16[256,512]{1,0:T(8,128)(2,1)S(1)}, bf16[256,512]{1,0:T(8,128)(2,1)S(1)}, u32[]{:S(2)}, u32[]{:S(2)}) collective-permute-start(bf16[256,512]{1,0:T(8,128)(2,1)S(1)} %slice.19), channel_id=1, source_target_pairs={{0,7},{1,0},{2,1},{3,2},{4,3},{5,4},{6,5},{7,6},{8,15},{9,8},{10,9... | collective-permute-start | bytes 786440 | tf_op jit(solution)/shard_map/ppermute | solution.py:92
  58.7 0.3 collective-permute-start.6
  59.0 0.2 fusion.23
  59.2 0.2 fusion.20
  59.4 2.7 %collective-permute-done.7 = bf16[256,512]{1,0:T(8,128)(2,1)S(1)} collective-permute-done((bf16[256,512]{1,0:T(8,128)(2,1)S(1)}, bf16[256,512]{1,0:T(8,128)(2,1)S(1)}, u32[]{:S(2)}, u32[]{:S(2)}) %collective-permute-start.7) | collective-permute-done | bytes 262176 | tf_op jit(solution)/shard_map/ppermute | solution.py:92
  62.0 3.4 %collective-permute-done.6 = bf16[256,512]{1,0:T(8,128)(2,1)S(1)} collective-permute-done((bf16[256,512]{1,0:T(8,128)(2,1)S(1)}, bf16[256,512]{1,0:T(8,128)(2,1)S(1)}, u32[]{:S(2)}, u32[]{:S(2)}) %collective-permute-start.6) | collective-permute-done | bytes 262176 | tf_op jit(solution)/shard_map/ppermute | solution.py:91
  65.4 0.2 fusion.26
  65.6 0.5 fusion.33
  66.1 0.5 convolution_add_fusion.6
  66.7 0.5 convolution_add_fusion.5
  67.2 1.6 convolution_add_fusion.4
  68.8 0.5 convolution_add_fusion.3
  69.3 0.5 convolution_add_fusion.2
  69.8 0.5 convolution_add_fusion.1
  70.3 1.3 fusion.7.q_ref
  71.6 39.6 %all-gather.2.cloned.1.call-done.refs_0_.refs_1_.refs_2_.refs_3_ = bf16[64,128,1024]{2,1,0:T(8,128)(2,1)} async-done(((bf16[4,128,1024]{2,1,0:T(8,128)(2,1)}), bf16[64,128,1024]{2,1,0:T(8,128)(2,1)}) %all-gather.2.cloned.1.call-update) | async-done | bytes 16777232 | tf_op jit(solution)/shard_map/all_gather | solution.py:106
  111.3 6.0 %shard_map.91 = bf16[512,512]{1,0:T(8,128)(2,1)} custom-call(s32[16]{0:T(128)} %copy-done.5, bf16[512,512]{1,0:T(8,128)(2,1)} %fusion.7.q_ref, bf16[64,128,1024]{2,1,0:T(8,128)(2,1)} %all-gather.2.cloned.1.call-done.refs_0_.refs_1_.refs_2_.refs_3_, bf16[64,128,1024]{2,1,0:T(8,128)(2,1)} %all-gather.2.cloned.1.call-done.refs_0_.refs_1_.refs_2_.refs_3_, ...), custom_call_target="tpu_custom_call" | custom-call | tf_op jit(solution)/shard_map/pallas_call | solution.py:63
  117.2 6.6 %convolution_convert_fusion = bf16[512,4096]{1,0:T(8,128)(2,1)} fusion(bf16[512,512]{1,0:T(8,128)(2,1)} %shard_map.91, bf16[512,4096]{1,0:T(8,128)(2,1)} %param.17), kind=kOutput, calls=%fused_computation.1 | convolution fusion | flops 2149580800 | bytes 8912896 | tf_op jit(solution)/shard_map/dot_general | solution.py:128
  123.9 55.6 %reduce-scatter.2.cloned.1.call-done = bf16[512,512]{1,0:T(8,128)(2,1)} async-done(((bf16[512,4096]{1,0:T(8,128)(2,1)}), bf16[512,512]{1,0:T(8,128)(2,1)}) %reduce-scatter.2.cloned.1.call-update) | async-done | bytes 524304 | tf_op jit(solution)/shard_map/reduce_scatter | solution.py:129
  179.5 2.0 %fusion.32 = bf16[512,512]{1,0:T(8,128)(2,1)} fusion(bf16[512,512]{1,0:T(8,128)(2,1)S(1)} %copy-done.1, bf16[512,512]{1,0:T(8,128)(2,1)} %reduce-scatter.2.cloned.1.call-done), kind=kLoop, calls=%fused_computation.56 | loop fusion | flops 1048576 | bytes 1572864 | tf_op jit(solution)/shard_map/convert_element_type | solution.py:132
  (30 shorter events, 0.2 us)
Async XLA Ops:
  6.5 1.2 copy-start
  6.5 104.7 %all-gather.2.cloned.1.call-start = ((), (), s32[]{:S(2)}) async-start(), calls=%async_computation.2 | async-start | bytes 17825792 | tf_op jit(solution)/shard_map/all_gather | solution.py:106
  10.6 2.1 %copy-start.1 = (bf16[512,512]{1,0:T(8,128)(2,1)S(1)}, bf16[512,512]{1,0:T(8,128)(2,1)}, u32[]{:S(2)}) copy-start(bf16[512,512]{1,0:T(8,128)(2,1)} %param.9) | copy-start | bytes 1572868
  10.6 8.6 %copy-start.4 = (s32[4,4]{1,0:T(4,128)S(1)}, s32[4,4]{1,0:T(4,128)}, u32[]{:S(2)}) copy-start(s32[4,4]{1,0:T(4,128)} %param.13) | copy-start | bytes 196
  10.6 15.6 %copy-start.6 = (s32[8,2]{0,1:T(2,128)S(1)}, s32[8,2]{0,1:T(2,128)}, u32[]{:S(2)}) copy-start(s32[8,2]{0,1:T(2,128)} %param.11) | copy-start | bytes 196
  10.6 15.9 %copy-start.3 = (f32[4096]{0:T(1024)S(1)}, f32[4096]{0:T(1024)}, u32[]{:S(2)}) copy-start(f32[4096]{0:T(1024)} %param.10) | copy-start | bytes 49156
  12.7 17.1 %collective-permute-start.1 = (bf16[512,512]{1,0:T(8,128)(2,1)S(1)}, bf16[512,512]{1,0:T(8,128)(2,1)S(1)}, u32[]{:S(2)}, u32[]{:S(2)}) collective-permute-start(bf16[512,512]{1,0:T(8,128)(2,1)S(1)} %copy-done.1), channel_id=1, source_target_pairs={{0,7},{1,0},{2,1},{3,2},{4,3},{5,4},{6,5},{7,6},{8,15},{9,8},{10,9... | collective-permute-start | bytes 1572872 | tf_op jit(solution)/shard_map/ppermute | solution.py:87
  19.1 14.0 %collective-permute-start = (bf16[512,512]{1,0:T(8,128)(2,1)S(1)}, bf16[512,512]{1,0:T(8,128)(2,1)S(1)}, u32[]{:S(2)}, u32[]{:S(2)}) collective-permute-start(bf16[512,512]{1,0:T(8,128)(2,1)S(1)} %copy-done.1), channel_id=1, source_target_pairs={{0,1},{1,2},{2,3},{3,4},{4,5},{5,6},{6,7},{7,0},{8,9},{9,10},{10,1... | collective-permute-start | bytes 1572872 | tf_op jit(solution)/shard_map/ppermute | solution.py:86
  19.8 13.4 %all-to-all-start = ((s32[16,4,4]{2,1,0:T(4,128)}), s32[16,4,4]{2,1,0:T(4,128)S(1)}, u32[]{:S(2)}, u32[]{:S(2)}) async-start(s32[16,4,4]{2,1,0:T(4,128)} %broadcast_in_dim.15), calls=%async_computation | async-start | bytes 65536 | tf_op jit(solution)/shard_map/all_to_all | solution.py:109
  26.0 153.5 %reduce-scatter.2.cloned.1.call-start = ((), (), s32[]{:S(2)}) async-start(), calls=%async_computation.3 | async-start | bytes 4718592 | tf_op jit(solution)/shard_map/reduce_scatter | solution.py:129
  26.4 40.3 %copy-start.5 = (s32[16]{0:T(128)}, s32[16]{0:T(128)S(1)}, u32[]{:S(2)}) copy-start(s32[16]{0:T(128)S(1)} %reshape.112.flat_ref) | copy-start | bytes 196
  29.7 13.2 %collective-permute-start.3 = (bf16[512,512]{1,0:T(8,128)(2,1)S(1)}, bf16[512,512]{1,0:T(8,128)(2,1)S(1)}, u32[]{:S(2)}, u32[]{:S(2)}) collective-permute-start(bf16[512,512]{1,0:T(8,128)(2,1)S(1)} %collective-permute-done.1), channel_id=1, source_target_pairs={{0,7},{1,0},{2,1},{3,2},{4,3},{5,4},{6,5},{7,6},{8,15},{9,8},{10,9... | collective-permute-start | bytes 1572872 | tf_op jit(solution)/shard_map/ppermute | solution.py:87
  33.1 13.2 %collective-permute-start.2 = (bf16[512,512]{1,0:T(8,128)(2,1)S(1)}, bf16[512,512]{1,0:T(8,128)(2,1)}, u32[]{:S(2)}, u32[]{:S(2)}) collective-permute-start(bf16[512,512]{1,0:T(8,128)(2,1)S(1)} %collective-permute-done), channel_id=1, source_target_pairs={{0,1},{1,2},{2,3},{3,4},{4,5},{5,6},{6,7},{7,0},{8,9},{9,10},{10,1... | collective-permute-start | bytes 1572872 | tf_op jit(solution)/shard_map/ppermute | solution.py:86
  34.6 31.0 %copy-start.2 = (bf16[4096,512]{1,0:T(8,128)(2,1)S(1)}, bf16[4096,512]{1,0:T(8,128)(2,1)}, u32[]{:S(2)}) copy-start(bf16[4096,512]{1,0:T(8,128)(2,1)} %param.14) | copy-start | bytes 12582916
  42.9 12.3 %collective-permute-start.5 = (bf16[512,512]{1,0:T(8,128)(2,1)S(1)}, bf16[512,512]{1,0:T(8,128)(2,1)S(1)}, u32[]{:S(2)}, u32[]{:S(2)}) collective-permute-start(bf16[512,512]{1,0:T(8,128)(2,1)S(1)} %collective-permute-done.3), channel_id=1, source_target_pairs={{0,7},{1,0},{2,1},{3,2},{4,3},{5,4},{6,5},{7,6},{8,15},{9,8},{10,9... | collective-permute-start | bytes 1572872 | tf_op jit(solution)/shard_map/ppermute | solution.py:87
  46.3 12.4 %collective-permute-start.4 = (bf16[512,512]{1,0:T(8,128)(2,1)}, bf16[512,512]{1,0:T(8,128)(2,1)S(1)}, u32[]{:S(2)}, u32[]{:S(2)}) collective-permute-start(bf16[512,512]{1,0:T(8,128)(2,1)} %collective-permute-done.2), channel_id=1, source_target_pairs={{0,1},{1,2},{2,3},{3,4},{4,5},{5,6},{6,7},{7,0},{8,9},{9,10},{10,1... | collective-permute-start | bytes 1572872 | tf_op jit(solution)/shard_map/ppermute | solution.py:86
  55.2 6.8 %collective-permute-start.7 = (bf16[256,512]{1,0:T(8,128)(2,1)S(1)}, bf16[256,512]{1,0:T(8,128)(2,1)S(1)}, u32[]{:S(2)}, u32[]{:S(2)}) collective-permute-start(bf16[256,512]{1,0:T(8,128)(2,1)S(1)} %slice.19), channel_id=1, source_target_pairs={{0,7},{1,0},{2,1},{3,2},{4,3},{5,4},{6,5},{7,6},{8,15},{9,8},{10,9... | collective-permute-start | bytes 786440 | tf_op jit(solution)/shard_map/ppermute | solution.py:92
  58.7 6.7 %collective-permute-start.6 = (bf16[256,512]{1,0:T(8,128)(2,1)S(1)}, bf16[256,512]{1,0:T(8,128)(2,1)S(1)}, u32[]{:S(2)}, u32[]{:S(2)}) collective-permute-start(bf16[256,512]{1,0:T(8,128)(2,1)S(1)} %slice.18), channel_id=1, source_target_pairs={{0,1},{1,2},{2,3},{3,4},{4,5},{5,6},{6,7},{7,0},{8,9},{9,10},{10,1... | collective-permute-start | bytes 786440 | tf_op jit(solution)/shard_map/ppermute | solution.py:91
Sparse Core Ops, SparseCore 0:
  12.8 98.4 all-gather.1
  124.0 55.4 reduce-scatter.1

commit v15 on v14

--- a/solution.py
+++ b/solution.py
@@ -12,7 +12,7 @@
 NBRS = 2
 BLOCK = 32
 CAP = 2
-SEGS_PER_STEP = 2
+SEGS_PER_STEP = 4
 
 
 def attend_kernel(flat_ref, q_ref, *refs, entry_len):

time: 189 us -> 188 us (level)
  no operation moved by 1% of the time
where the time goes in v15:
time: 188 us; the launch traced here: 187 us
  waiting for transfers between devices  120 us (64%)
  starting transfers between devices  23.4 us (12%)
  matrix products  15.4 us (8%)
  between operations  13.8 us (7%)
  other arithmetic  5.64 us (3%)
  Pallas kernels  5.04 us (3%)
  local copies, waits for them, and re-layouts  4.46 us (2%)
    reduce_scatter x1, waiting for transfers between devices, local(): lax.psum_scatter(partial_value.astype(jnp.bfloat16), 'tensor', scatter_di...  55.6 us
    all_gather x1, waiting for transfers between devices, local(): slots = lax.all_gather(own_kv, 'retr', axis=0, tiled=True)  39.6 us
    ppermute x3, waiting for transfers between devices, local(): down = lax.ppermute(down, 'tensor', bwd)  18.4 us
    ppermute x3, starting transfers between devices, local(): down = lax.ppermute(down, 'tensor', bwd)  13.3 us
    dot_general x1, matrix products, local(): partial_value = jnp.dot(attended, w_out, preferred_element_type=jnp.float32)  6.63 us
    all_to_all x1, starting transfers between devices, local(): all_marks = lax.all_to_all(mask_copies, 'retr', 0, 0, tiled=True)  6.28 us
    dot_general x8, matrix products, local(): part = jnp.dot(normed, w_rows, preferred_element_type=jnp.float32)  5.95 us
    pallas_call x1, Pallas kernels, attend(): pl.pallas_call(functools.partial(attend_kernel, entry_len=entry_len), out...  5.04 us
  transfers between devices with their start and end apart: 11, of which 7 were waited for; matrix products, arithmetic and copies ran while one was open for 6% of the time, Pallas kernels for 0%

profile of v15, /device:TPU:1, one launch (start us, length us, event | category | flops | bytes accessed | tf_op | source)
XLA Modules:
  0.0 187.4 jit_solution(3726678975615221534)
XLA Ops:
  6.5 1.2 copy-done
  7.8 2.8 %fusion.4 = bf16[1024,512]{0,1:T(8,128)(2,1)S(1)} fusion(bf16[512,1024]{1,0:T(8,128)(2,1)S(1)} %bitcast.11, bf16[1024,512]{1,0:T(8,128)(2,1)} %param.16, bf16[1024,512]{1,0:T(8,128)(2,1)} %param.15), kind=kOutput, calls=%fused_computation.9 | convolution fusion | flops 1078460416 | bytes 4194304 | tf_op jit(solution)/shard_map/dot_general | solution.py:99
  10.6 0.1 fusion.77
  10.7 0.1 reshape.115
  10.8 0.5 copy.17
  11.3 0.2 reshape.116
  11.5 1.1 pad_maximum_fusion
  12.7 6.5 %collective-permute-start.1 = (bf16[512,512]{1,0:T(8,128)(2,1)S(1)}, bf16[512,512]{1,0:T(8,128)(2,1)S(1)}, u32[]{:S(2)}, u32[]{:S(2)}) collective-permute-start(bf16[512,512]{1,0:T(8,128)(2,1)S(1)} %copy-done.1), channel_id=1, source_target_pairs={{0,7},{1,0},{2,1},{3,2},{4,3},{5,4},{6,5},{7,6},{8,15},{9,8},{10,9... | collective-permute-start | bytes 1572872 | tf_op jit(solution)/shard_map/ppermute | solution.py:87
  19.1 0.6 broadcast_in_dim.15
  19.8 6.3 %all-to-all-start = ((s32[16,4,4]{2,1,0:T(4,128)}), s32[16,4,4]{2,1,0:T(4,128)S(1)}, u32[]{:S(2)}, u32[]{:S(2)}) async-start(s32[16,4,4]{2,1,0:T(4,128)} %broadcast_in_dim.15), calls=%async_computation | async-start | bytes 65536 | tf_op jit(solution)/shard_map/all_to_all | solution.py:109
  26.2 0.1 copy.16
  26.3 0.1 reshape.112.flat_ref
  26.4 0.1 reshape.118
  26.5 0.1 fusion.78
  26.6 0.2 fusion.29
  26.8 3.0 %collective-permute-done.1 = bf16[512,512]{1,0:T(8,128)(2,1)S(1)} collective-permute-done((bf16[512,512]{1,0:T(8,128)(2,1)S(1)}, bf16[512,512]{1,0:T(8,128)(2,1)S(1)}, u32[]{:S(2)}, u32[]{:S(2)}) %collective-permute-start.1) | collective-permute-done | bytes 524320 | tf_op jit(solution)/shard_map/ppermute | solution.py:87
  29.7 3.4 %collective-permute-start.3 = (bf16[512,512]{1,0:T(8,128)(2,1)S(1)}, bf16[512,512]{1,0:T(8,128)(2,1)S(1)}, u32[]{:S(2)}, u32[]{:S(2)}) collective-permute-start(bf16[512,512]{1,0:T(8,128)(2,1)S(1)} %collective-permute-done.1), channel_id=1, source_target_pairs={{0,7},{1,0},{2,1},{3,2},{4,3},{5,4},{6,5},{7,6},{8,15},{9,8},{10,9... | collective-permute-start | bytes 1572872 | tf_op jit(solution)/shard_map/ppermute | solution.py:87
  33.2 0.6 gather_fusion
  33.7 0.1 select_convert_fusion
  33.8 0.1 broadcast_in_dim.17
  33.9 0.7 convert_element_type.101.refs_8_
  34.6 8.3 %collective-permute-done.3 = bf16[512,512]{1,0:T(8,128)(2,1)S(1)} collective-permute-done((bf16[512,512]{1,0:T(8,128)(2,1)S(1)}, bf16[512,512]{1,0:T(8,128)(2,1)S(1)}, u32[]{:S(2)}, u32[]{:S(2)}) %collective-permute-start.3) | collective-permute-done | bytes 524320 | tf_op jit(solution)/shard_map/ppermute | solution.py:87
  42.9 3.4 %collective-permute-start.5 = (bf16[512,512]{1,0:T(8,128)(2,1)S(1)}, bf16[512,512]{1,0:T(8,128)(2,1)S(1)}, u32[]{:S(2)}, u32[]{:S(2)}) collective-permute-start(bf16[512,512]{1,0:T(8,128)(2,1)S(1)} %collective-permute-done.3), channel_id=1, source_target_pairs={{0,7},{1,0},{2,1},{3,2},{4,3},{5,4},{6,5},{7,6},{8,15},{9,8},{10,9... | collective-permute-start | bytes 1572872 | tf_op jit(solution)/shard_map/ppermute | solution.py:87
  46.3 0.2 fusion.11
  46.5 0.2 fusion.8
  46.7 0.2 fusion.17
  46.8 1.2 fusion.14
  48.1 7.1 %collective-permute-done.5 = bf16[512,512]{1,0:T(8,128)(2,1)S(1)} collective-permute-done((bf16[512,512]{1,0:T(8,128)(2,1)S(1)}, bf16[512,512]{1,0:T(8,128)(2,1)S(1)}, u32[]{:S(2)}, u32[]{:S(2)}) %collective-permute-start.5) | collective-permute-done | bytes 524320 | tf_op jit(solution)/shard_map/ppermute | solution.py:87
  55.2 3.5 %collective-permute-start.7 = (bf16[256,512]{1,0:T(8,128)(2,1)S(1)}, bf16[256,512]{1,0:T(8,128)(2,1)S(1)}, u32[]{:S(2)}, u32[]{:S(2)}) collective-permute-start(bf16[256,512]{1,0:T(8,128)(2,1)S(1)} %slice.19), channel_id=1, source_target_pairs={{0,7},{1,0},{2,1},{3,2},{4,3},{5,4},{6,5},{7,6},{8,15},{9,8},{10,9... | collective-permute-start | bytes 786440 | tf_op jit(solution)/shard_map/ppermute | solution.py:92
  58.7 0.3 collective-permute-start.6
  59.0 0.2 fusion.23
  59.2 0.2 fusion.20
  59.4 2.7 %collective-permute-done.7 = bf16[256,512]{1,0:T(8,128)(2,1)S(1)} collective-permute-done((bf16[256,512]{1,0:T(8,128)(2,1)S(1)}, bf16[256,512]{1,0:T(8,128)(2,1)S(1)}, u32[]{:S(2)}, u32[]{:S(2)}) %collective-permute-start.7) | collective-permute-done | bytes 262176 | tf_op jit(solution)/shard_map/ppermute | solution.py:92
  62.0 3.4 %collective-permute-done.6 = bf16[256,512]{1,0:T(8,128)(2,1)S(1)} collective-permute-done((bf16[256,512]{1,0:T(8,128)(2,1)S(1)}, bf16[256,512]{1,0:T(8,128)(2,1)S(1)}, u32[]{:S(2)}, u32[]{:S(2)}) %collective-permute-start.6) | collective-permute-done | bytes 262176 | tf_op jit(solution)/shard_map/ppermute | solution.py:91
  65.4 0.2 fusion.26
  65.6 0.5 fusion.33
  66.1 0.5 convolution_add_fusion.6
  66.7 0.5 convolution_add_fusion.5
  67.2 1.6 convolution_add_fusion.4
  68.8 0.5 convolution_add_fusion.3
  69.3 0.5 convolution_add_fusion.2
  69.8 0.5 convolution_add_fusion.1
  70.3 1.3 fusion.7.q_ref
  71.6 39.6 %all-gather.2.cloned.1.call-done.refs_0_.refs_1_.refs_2_.refs_3_.refs_4_.refs_5_.refs_6_.refs_7_ = bf16[64,128,1024]{2,1,0:T(8,128)(2,1)} async-done(((bf16[4,128,1024]{2,1,0:T(8,128)(2,1)}), bf16[64,128,1024]{2,1,0:T(8,128)(2,1)}) %all-gather.2.cloned.1.call-update) | async-done | bytes 16777232 | tf_op jit(solution)/shard_map/all_gather | solution.py:106
  111.3 5.0 %shard_map.91 = bf16[512,512]{1,0:T(8,128)(2,1)} custom-call(s32[16]{0:T(128)} %copy-done.5, bf16[512,512]{1,0:T(8,128)(2,1)} %fusion.7.q_ref, bf16[64,128,1024]{2,1,0:T(8,128)(2,1)} %all-gather.2.cloned.1.call-done.refs_0_.refs_1_.refs_2_.refs_3_.refs_4_.refs_5_.refs_6_.refs_7_, ...), custom_call_target="tpu_custom_call" | custom-call | tf_op jit(solution)/shard_map/pallas_call | solution.py:63
  116.3 6.6 %convolution_convert_fusion = bf16[512,4096]{1,0:T(8,128)(2,1)} fusion(bf16[512,512]{1,0:T(8,128)(2,1)} %shard_map.91, bf16[512,4096]{1,0:T(8,128)(2,1)} %param.17), kind=kOutput, calls=%fused_computation.1 | convolution fusion | flops 2149580800 | bytes 8912896 | tf_op jit(solution)/shard_map/dot_general | solution.py:128
  123.0 55.6 %reduce-scatter.2.cloned.1.call-done = bf16[512,512]{1,0:T(8,128)(2,1)} async-done(((bf16[512,4096]{1,0:T(8,128)(2,1)}), bf16[512,512]{1,0:T(8,128)(2,1)}) %reduce-scatter.2.cloned.1.call-update) | async-done | bytes 524304 | tf_op jit(solution)/shard_map/reduce_scatter | solution.py:129
  178.6 2.0 %fusion.32 = bf16[512,512]{1,0:T(8,128)(2,1)} fusion(bf16[512,512]{1,0:T(8,128)(2,1)S(1)} %copy-done.1, bf16[512,512]{1,0:T(8,128)(2,1)} %reduce-scatter.2.cloned.1.call-done), kind=kLoop, calls=%fused_computation.56 | loop fusion | flops 1048576 | bytes 1572864 | tf_op jit(solution)/shard_map/convert_element_type | solution.py:132
  (30 shorter events, 0.2 us)
Async XLA Ops:
  6.5 1.2 copy-start
  6.5 104.7 %all-gather.2.cloned.1.call-start = ((), (), s32[]{:S(2)}) async-start(), calls=%async_computation.2 | async-start | bytes 17825792 | tf_op jit(solution)/shard_map/all_gather | solution.py:106
  10.6 2.1 %copy-start.1 = (bf16[512,512]{1,0:T(8,128)(2,1)S(1)}, bf16[512,512]{1,0:T(8,128)(2,1)}, u32[]{:S(2)}) copy-start(bf16[512,512]{1,0:T(8,128)(2,1)} %param.9) | copy-start | bytes 1572868
  10.6 8.6 %copy-start.4 = (s32[4,4]{1,0:T(4,128)S(1)}, s32[4,4]{1,0:T(4,128)}, u32[]{:S(2)}) copy-start(s32[4,4]{1,0:T(4,128)} %param.13) | copy-start | bytes 196
  10.6 15.6 %copy-start.6 = (s32[8,2]{0,1:T(2,128)S(1)}, s32[8,2]{0,1:T(2,128)}, u32[]{:S(2)}) copy-start(s32[8,2]{0,1:T(2,128)} %param.11) | copy-start | bytes 196
  10.6 15.9 %copy-start.3 = (f32[4096]{0:T(1024)S(1)}, f32[4096]{0:T(1024)}, u32[]{:S(2)}) copy-start(f32[4096]{0:T(1024)} %param.10) | copy-start | bytes 49156
  12.7 17.1 %collective-permute-start.1 = (bf16[512,512]{1,0:T(8,128)(2,1)S(1)}, bf16[512,512]{1,0:T(8,128)(2,1)S(1)}, u32[]{:S(2)}, u32[]{:S(2)}) collective-permute-start(bf16[512,512]{1,0:T(8,128)(2,1)S(1)} %copy-done.1), channel_id=1, source_target_pairs={{0,7},{1,0},{2,1},{3,2},{4,3},{5,4},{6,5},{7,6},{8,15},{9,8},{10,9... | collective-permute-start | bytes 1572872 | tf_op jit(solution)/shard_map/ppermute | solution.py:87
  19.1 14.0 %collective-permute-start = (bf16[512,512]{1,0:T(8,128)(2,1)S(1)}, bf16[512,512]{1,0:T(8,128)(2,1)S(1)}, u32[]{:S(2)}, u32[]{:S(2)}) collective-permute-start(bf16[512,512]{1,0:T(8,128)(2,1)S(1)} %copy-done.1), channel_id=1, source_target_pairs={{0,1},{1,2},{2,3},{3,4},{4,5},{5,6},{6,7},{7,0},{8,9},{9,10},{10,1... | collective-permute-start | bytes 1572872 | tf_op jit(solution)/shard_map/ppermute | solution.py:86
  19.8 13.4 %all-to-all-start = ((s32[16,4,4]{2,1,0:T(4,128)}), s32[16,4,4]{2,1,0:T(4,128)S(1)}, u32[]{:S(2)}, u32[]{:S(2)}) async-start(s32[16,4,4]{2,1,0:T(4,128)} %broadcast_in_dim.15), calls=%async_computation | async-start | bytes 65536 | tf_op jit(solution)/shard_map/all_to_all | solution.py:109
  26.0 152.6 %reduce-scatter.2.cloned.1.call-start = ((), (), s32[]{:S(2)}) async-start(), calls=%async_computation.3 | async-start | bytes 4718592 | tf_op jit(solution)/shard_map/reduce_scatter | solution.py:129
  26.4 40.3 %copy-start.5 = (s32[16]{0:T(128)}, s32[16]{0:T(128)S(1)}, u32[]{:S(2)}) copy-start(s32[16]{0:T(128)S(1)} %reshape.112.flat_ref) | copy-start | bytes 196
  29.7 13.2 %collective-permute-start.3 = (bf16[512,512]{1,0:T(8,128)(2,1)S(1)}, bf16[512,512]{1,0:T(8,128)(2,1)S(1)}, u32[]{:S(2)}, u32[]{:S(2)}) collective-permute-start(bf16[512,512]{1,0:T(8,128)(2,1)S(1)} %collective-permute-done.1), channel_id=1, source_target_pairs={{0,7},{1,0},{2,1},{3,2},{4,3},{5,4},{6,5},{7,6},{8,15},{9,8},{10,9... | collective-permute-start | bytes 1572872 | tf_op jit(solution)/shard_map/ppermute | solution.py:87
  33.1 13.2 %collective-permute-start.2 = (bf16[512,512]{1,0:T(8,128)(2,1)S(1)}, bf16[512,512]{1,0:T(8,128)(2,1)}, u32[]{:S(2)}, u32[]{:S(2)}) collective-permute-start(bf16[512,512]{1,0:T(8,128)(2,1)S(1)} %collective-permute-done), channel_id=1, source_target_pairs={{0,1},{1,2},{2,3},{3,4},{4,5},{5,6},{6,7},{7,0},{8,9},{9,10},{10,1... | collective-permute-start | bytes 1572872 | tf_op jit(solution)/shard_map/ppermute | solution.py:86
  34.6 31.0 %copy-start.2 = (bf16[4096,512]{1,0:T(8,128)(2,1)S(1)}, bf16[4096,512]{1,0:T(8,128)(2,1)}, u32[]{:S(2)}) copy-start(bf16[4096,512]{1,0:T(8,128)(2,1)} %param.14) | copy-start | bytes 12582916
  42.9 12.3 %collective-permute-start.5 = (bf16[512,512]{1,0:T(8,128)(2,1)S(1)}, bf16[512,512]{1,0:T(8,128)(2,1)S(1)}, u32[]{:S(2)}, u32[]{:S(2)}) collective-permute-start(bf16[512,512]{1,0:T(8,128)(2,1)S(1)} %collective-permute-done.3), channel_id=1, source_target_pairs={{0,7},{1,0},{2,1},{3,2},{4,3},{5,4},{6,5},{7,6},{8,15},{9,8},{10,9... | collective-permute-start | bytes 1572872 | tf_op jit(solution)/shard_map/ppermute | solution.py:87
  46.3 12.4 %collective-permute-start.4 = (bf16[512,512]{1,0:T(8,128)(2,1)}, bf16[512,512]{1,0:T(8,128)(2,1)S(1)}, u32[]{:S(2)}, u32[]{:S(2)}) collective-permute-start(bf16[512,512]{1,0:T(8,128)(2,1)} %collective-permute-done.2), channel_id=1, source_target_pairs={{0,1},{1,2},{2,3},{3,4},{4,5},{5,6},{6,7},{7,0},{8,9},{9,10},{10,1... | collective-permute-start | bytes 1572872 | tf_op jit(solution)/shard_map/ppermute | solution.py:86
  55.2 6.8 %collective-permute-start.7 = (bf16[256,512]{1,0:T(8,128)(2,1)S(1)}, bf16[256,512]{1,0:T(8,128)(2,1)S(1)}, u32[]{:S(2)}, u32[]{:S(2)}) collective-permute-start(bf16[256,512]{1,0:T(8,128)(2,1)S(1)} %slice.19), channel_id=1, source_target_pairs={{0,7},{1,0},{2,1},{3,2},{4,3},{5,4},{6,5},{7,6},{8,15},{9,8},{10,9... | collective-permute-start | bytes 786440 | tf_op jit(solution)/shard_map/ppermute | solution.py:92
  58.7 6.7 %collective-permute-start.6 = (bf16[256,512]{1,0:T(8,128)(2,1)S(1)}, bf16[256,512]{1,0:T(8,128)(2,1)S(1)}, u32[]{:S(2)}, u32[]{:S(2)}) collective-permute-start(bf16[256,512]{1,0:T(8,128)(2,1)S(1)} %slice.18), channel_id=1, source_target_pairs={{0,1},{1,2},{2,3},{3,4},{4,5},{5,6},{6,7},{7,0},{8,9},{9,10},{10,1... | collective-permute-start | bytes 786440 | tf_op jit(solution)/shard_map/ppermute | solution.py:91
Sparse Core Ops, SparseCore 0:
  12.8 98.4 all-gather.1
  123.1 55.4 reduce-scatter.1

commit v16 on v15

--- a/solution.py
+++ b/solution.py
@@ -126,10 +126,13 @@
 
     attended = attend(slot_of, queries, slots, key_live, entry_len)
     partial_value = jnp.dot(attended, w_out, preferred_element_type=jnp.float32)
-    summed = lax.psum_scatter(
+    own_block = lax.dynamic_slice_in_dim(partial_value, t * feat, feat, axis=1)
+    partial_value = lax.dynamic_update_slice_in_dim(
+        partial_value, own_block + hidden_in.astype(jnp.float32), t * feat, axis=1
+    )
+    return lax.psum_scatter(
         partial_value.astype(jnp.bfloat16), "tensor", scatter_dimension=1, tiled=True
     )
-    return (hidden_in.astype(jnp.float32) + summed.astype(jnp.float32)).astype(jnp.bfloat16)
 
 
 def solution(mesh):

time: 188 us -> 187 us (level)
  matrix products: 15.4 us -> 13.4 us
    dot_general x1, matrix products: 6.63 us -> 4.7 us  [local(): partial_value = jnp.dot(attended, w_out, preferred_element_type=jnp.float32)]
where the time goes in v16:
time: 187 us; the launch traced here: 186 us
  waiting for transfers between devices  120 us (64%)
  starting transfers between devices  23.4 us (13%)
  between operations  13.8 us (7%)
  matrix products  13.4 us (7%)
  other arithmetic  6.49 us (3%)
  Pallas kernels  5.04 us (3%)
  local copies, waits for them, and re-layouts  4.49 us (2%)
    reduce_scatter x1, waiting for transfers between devices, local(): lax.psum_scatter(partial_value.astype(jnp.bfloat16), 'tensor', scatter_di...  55.6 us
    all_gather x1, waiting for transfers between devices, local(): slots = lax.all_gather(own_kv, 'retr', axis=0, tiled=True)  39.6 us
    ppermute x3, waiting for transfers between devices, local(): down = lax.ppermute(down, 'tensor', bwd)  18.4 us
    ppermute x3, starting transfers between devices, local(): down = lax.ppermute(down, 'tensor', bwd)  13.3 us
    all_to_all x1, starting transfers between devices, local(): all_marks = lax.all_to_all(mask_copies, 'retr', 0, 0, tiled=True)  6.28 us
    dot_general x8, matrix products, local(): part = jnp.dot(normed, w_rows, preferred_element_type=jnp.float32)  5.93 us
    pallas_call x1, Pallas kernels, attend(): pl.pallas_call(functools.partial(attend_kernel, entry_len=entry_len), out...  5.04 us
    dot_general x1, matrix products, local(): partial_value = jnp.dot(attended, w_out, preferred_element_type=jnp.float32)  4.7 us
  transfers between devices with their start and end apart: 11, of which 7 were waited for; matrix products, arithmetic and copies ran while one was open for 6% of the time, Pallas kernels for 0%

profile of v16, /device:TPU:1, one launch (start us, length us, event | category | flops | bytes accessed | tf_op | source)
XLA Modules:
  0.0 186.4 jit_solution(3968043261229981001)
XLA Ops:
  6.5 1.2 copy-done
  7.8 2.8 %fusion.4 = bf16[1024,512]{0,1:T(8,128)(2,1)S(1)} fusion(bf16[512,1024]{1,0:T(8,128)(2,1)S(1)} %bitcast.11, bf16[1024,512]{1,0:T(8,128)(2,1)} %param.16, bf16[1024,512]{1,0:T(8,128)(2,1)} %param.15), kind=kOutput, calls=%fused_computation.8 | convolution fusion | flops 1078460416 | bytes 4194304 | tf_op jit(solution)/shard_map/dot_general | solution.py:99
  10.6 0.1 fusion.77
  10.7 0.1 reshape.115
  10.8 0.5 copy.17
  11.3 0.2 reshape.116
  11.5 1.1 pad_maximum_fusion
  12.7 6.5 %collective-permute-start.1 = (bf16[512,512]{1,0:T(8,128)(2,1)S(1)}, bf16[512,512]{1,0:T(8,128)(2,1)S(1)}, u32[]{:S(2)}, u32[]{:S(2)}) collective-permute-start(bf16[512,512]{1,0:T(8,128)(2,1)S(1)} %copy-done.1), channel_id=1, source_target_pairs={{0,7},{1,0},{2,1},{3,2},{4,3},{5,4},{6,5},{7,6},{8,15},{9,8},{10,9... | collective-permute-start | bytes 1572872 | tf_op jit(solution)/shard_map/ppermute | solution.py:87
  19.2 0.6 broadcast_in_dim.15
  19.8 6.3 %all-to-all-start = ((s32[16,4,4]{2,1,0:T(4,128)}), s32[16,4,4]{2,1,0:T(4,128)S(1)}, u32[]{:S(2)}, u32[]{:S(2)}) async-start(s32[16,4,4]{2,1,0:T(4,128)} %broadcast_in_dim.15), calls=%async_computation | async-start | bytes 65536 | tf_op jit(solution)/shard_map/all_to_all | solution.py:109
  26.3 0.1 copy.16
  26.4 0.1 reshape.112.flat_ref
  26.4 0.1 reshape.118
  26.5 0.1 fusion.78
  26.6 0.2 fusion.29
  26.8 3.0 %collective-permute-done.1 = bf16[512,512]{1,0:T(8,128)(2,1)S(1)} collective-permute-done((bf16[512,512]{1,0:T(8,128)(2,1)S(1)}, bf16[512,512]{1,0:T(8,128)(2,1)S(1)}, u32[]{:S(2)}, u32[]{:S(2)}) %collective-permute-start.1) | collective-permute-done | bytes 524320 | tf_op jit(solution)/shard_map/ppermute | solution.py:87
  29.8 3.4 %collective-permute-start.3 = (bf16[512,512]{1,0:T(8,128)(2,1)S(1)}, bf16[512,512]{1,0:T(8,128)(2,1)S(1)}, u32[]{:S(2)}, u32[]{:S(2)}) collective-permute-start(bf16[512,512]{1,0:T(8,128)(2,1)S(1)} %collective-permute-done.1), channel_id=1, source_target_pairs={{0,7},{1,0},{2,1},{3,2},{4,3},{5,4},{6,5},{7,6},{8,15},{9,8},{10,9... | collective-permute-start | bytes 1572872 | tf_op jit(solution)/shard_map/ppermute | solution.py:87
  33.2 0.6 gather_fusion
  33.9 0.1 broadcast_in_dim.17
  34.0 0.7 convert_element_type.95.refs_8_
  34.7 8.3 %collective-permute-done.3 = bf16[512,512]{1,0:T(8,128)(2,1)S(1)} collective-permute-done((bf16[512,512]{1,0:T(8,128)(2,1)S(1)}, bf16[512,512]{1,0:T(8,128)(2,1)S(1)}, u32[]{:S(2)}, u32[]{:S(2)}) %collective-permute-start.3) | collective-permute-done | bytes 524320 | tf_op jit(solution)/shard_map/ppermute | solution.py:87
  42.9 3.4 %collective-permute-start.5 = (bf16[512,512]{1,0:T(8,128)(2,1)S(1)}, bf16[512,512]{1,0:T(8,128)(2,1)S(1)}, u32[]{:S(2)}, u32[]{:S(2)}) collective-permute-start(bf16[512,512]{1,0:T(8,128)(2,1)S(1)} %collective-permute-done.3), channel_id=1, source_target_pairs={{0,7},{1,0},{2,1},{3,2},{4,3},{5,4},{6,5},{7,6},{8,15},{9,8},{10,9... | collective-permute-start | bytes 1572872 | tf_op jit(solution)/shard_map/ppermute | solution.py:87
  46.4 0.2 fusion.11
  46.5 0.2 fusion.8
  46.7 0.2 fusion.17
  46.9 1.2 fusion.14
  48.1 7.1 %collective-permute-done.5 = bf16[512,512]{1,0:T(8,128)(2,1)S(1)} collective-permute-done((bf16[512,512]{1,0:T(8,128)(2,1)S(1)}, bf16[512,512]{1,0:T(8,128)(2,1)S(1)}, u32[]{:S(2)}, u32[]{:S(2)}) %collective-permute-start.5) | collective-permute-done | bytes 524320 | tf_op jit(solution)/shard_map/ppermute | solution.py:87
  55.3 3.5 %collective-permute-start.7 = (bf16[256,512]{1,0:T(8,128)(2,1)S(1)}, bf16[256,512]{1,0:T(8,128)(2,1)S(1)}, u32[]{:S(2)}, u32[]{:S(2)}) collective-permute-start(bf16[256,512]{1,0:T(8,128)(2,1)S(1)} %slice.19), channel_id=1, source_target_pairs={{0,7},{1,0},{2,1},{3,2},{4,3},{5,4},{6,5},{7,6},{8,15},{9,8},{10,9... | collective-permute-start | bytes 786440 | tf_op jit(solution)/shard_map/ppermute | solution.py:92
  58.8 0.3 collective-permute-start.6
  59.1 0.2 fusion.23
  59.2 0.2 fusion.20
  59.4 2.7 %collective-permute-done.7 = bf16[256,512]{1,0:T(8,128)(2,1)S(1)} collective-permute-done((bf16[256,512]{1,0:T(8,128)(2,1)S(1)}, bf16[256,512]{1,0:T(8,128)(2,1)S(1)}, u32[]{:S(2)}, u32[]{:S(2)}) %collective-permute-start.7) | collective-permute-done | bytes 262176 | tf_op jit(solution)/shard_map/ppermute | solution.py:92
  62.1 3.4 %collective-permute-done.6 = bf16[256,512]{1,0:T(8,128)(2,1)S(1)} collective-permute-done((bf16[256,512]{1,0:T(8,128)(2,1)S(1)}, bf16[256,512]{1,0:T(8,128)(2,1)S(1)}, u32[]{:S(2)}, u32[]{:S(2)}) %collective-permute-start.6) | collective-permute-done | bytes 262176 | tf_op jit(solution)/shard_map/ppermute | solution.py:91
  65.5 0.2 fusion.26
  65.7 0.5 fusion.33
  66.2 0.5 convolution_add_fusion.6
  66.7 0.5 convolution_add_fusion.5
  67.2 1.6 convolution_add_fusion.4
  68.9 0.5 convolution_add_fusion.3
  69.4 0.5 convolution_add_fusion.2
  69.9 0.5 convolution_add_fusion.1
  70.4 1.3 fusion.7.q_ref
  71.7 39.6 %all-gather.2.cloned.1.call-done.refs_0_.refs_1_.refs_2_.refs_3_.refs_4_.refs_5_.refs_6_.refs_7_ = bf16[64,128,1024]{2,1,0:T(8,128)(2,1)} async-done(((bf16[4,128,1024]{2,1,0:T(8,128)(2,1)}), bf16[64,128,1024]{2,1,0:T(8,128)(2,1)}) %all-gather.2.cloned.1.call-update) | async-done | bytes 16777232 | tf_op jit(solution)/shard_map/all_gather | solution.py:106
  111.3 5.0 %shard_map.91 = bf16[512,512]{1,0:T(8,128)(2,1)} custom-call(s32[16]{0:T(128)} %copy-done.5, bf16[512,512]{1,0:T(8,128)(2,1)} %fusion.7.q_ref, bf16[64,128,1024]{2,1,0:T(8,128)(2,1)} %all-gather.2.cloned.1.call-done.refs_0_.refs_1_.refs_2_.refs_3_.refs_4_.refs_5_.refs_6_.refs_7_, ...), custom_call_target="tpu_custom_call" | custom-call | tf_op jit(solution)/shard_map/pallas_call | solution.py:63
  116.4 4.7 %fusion.79 = f32[512,4096]{1,0:T(8,128)S(1)} fusion(bf16[512,512]{1,0:T(8,128)(2,1)} %shard_map.91, bf16[512,4096]{1,0:T(8,128)(2,1)} %param.17), kind=kOutput, calls=%fused_computation.102 | convolution fusion | flops 2147483648 | bytes 13107200 | tf_op jit(solution)/shard_map/dot_general | solution.py:128
  121.1 0.2 fusion.32
  121.3 2.5 %convert_element_type.96 = bf16[512,4096]{1,0:T(8,128)(2,1)} convert(f32[512,4096]{1,0:T(8,128)S(1)} %fusion.32) | non-fusion elementwise | flops 2097152 | bytes 12582912 | tf_op jit(solution)/shard_map/convert_element_type | solution.py:134
  123.9 55.6 %reduce-scatter.2.cloned.1.call-done = bf16[512,512]{1,0:T(8,128)(2,1)} async-done(((bf16[512,4096]{1,0:T(8,128)(2,1)}), bf16[512,512]{1,0:T(8,128)(2,1)}) %reduce-scatter.2.cloned.1.call-update) | async-done | bytes 524304 | tf_op jit(solution)/shard_map/reduce_scatter | solution.py:133
  (31 shorter events, 0.3 us)
Async XLA Ops:
  6.5 1.2 copy-start
  6.5 104.8 %all-gather.2.cloned.1.call-start = ((), (), s32[]{:S(2)}) async-start(), calls=%async_computation.2 | async-start | bytes 17825792 | tf_op jit(solution)/shard_map/all_gather | solution.py:106
  10.6 2.1 %copy-start.1 = (bf16[512,512]{1,0:T(8,128)(2,1)S(1)}, bf16[512,512]{1,0:T(8,128)(2,1)}, u32[]{:S(2)}) copy-start(bf16[512,512]{1,0:T(8,128)(2,1)} %param.9) | copy-start | bytes 1572868
  10.6 8.6 %copy-start.4 = (s32[4,4]{1,0:T(4,128)S(1)}, s32[4,4]{1,0:T(4,128)}, u32[]{:S(2)}) copy-start(s32[4,4]{1,0:T(4,128)} %param.13) | copy-start | bytes 196
  10.6 15.7 %copy-start.6 = (s32[8,2]{0,1:T(2,128)S(1)}, s32[8,2]{0,1:T(2,128)}, u32[]{:S(2)}) copy-start(s32[8,2]{0,1:T(2,128)} %param.11) | copy-start | bytes 196
  10.6 15.9 %copy-start.3 = (f32[4096]{0:T(1024)S(1)}, f32[4096]{0:T(1024)}, u32[]{:S(2)}) copy-start(f32[4096]{0:T(1024)} %param.10) | copy-start | bytes 49156
  12.7 17.1 %collective-permute-start.1 = (bf16[512,512]{1,0:T(8,128)(2,1)S(1)}, bf16[512,512]{1,0:T(8,128)(2,1)S(1)}, u32[]{:S(2)}, u32[]{:S(2)}) collective-permute-start(bf16[512,512]{1,0:T(8,128)(2,1)S(1)} %copy-done.1), channel_id=1, source_target_pairs={{0,7},{1,0},{2,1},{3,2},{4,3},{5,4},{6,5},{7,6},{8,15},{9,8},{10,9... | collective-permute-start | bytes 1572872 | tf_op jit(solution)/shard_map/ppermute | solution.py:87
  19.2 14.0 %collective-permute-start = (bf16[512,512]{1,0:T(8,128)(2,1)S(1)}, bf16[512,512]{1,0:T(8,128)(2,1)S(1)}, u32[]{:S(2)}, u32[]{:S(2)}) collective-permute-start(bf16[512,512]{1,0:T(8,128)(2,1)S(1)} %copy-done.1), channel_id=1, source_target_pairs={{0,1},{1,2},{2,3},{3,4},{4,5},{5,6},{6,7},{7,0},{8,9},{9,10},{10,1... | collective-permute-start | bytes 1572872 | tf_op jit(solution)/shard_map/ppermute | solution.py:86
  19.8 13.4 %all-to-all-start = ((s32[16,4,4]{2,1,0:T(4,128)}), s32[16,4,4]{2,1,0:T(4,128)S(1)}, u32[]{:S(2)}, u32[]{:S(2)}) async-start(s32[16,4,4]{2,1,0:T(4,128)} %broadcast_in_dim.15), calls=%async_computation | async-start | bytes 65536 | tf_op jit(solution)/shard_map/all_to_all | solution.py:109
  26.1 153.4 %reduce-scatter.2.cloned.1.call-start = ((), (), s32[]{:S(2)}) async-start(), calls=%async_computation.3 | async-start | bytes 4718592 | tf_op jit(solution)/shard_map/reduce_scatter | solution.py:133
  26.4 40.2 %copy-start.5 = (s32[16]{0:T(128)}, s32[16]{0:T(128)S(1)}, u32[]{:S(2)}) copy-start(s32[16]{0:T(128)S(1)} %reshape.112.flat_ref) | copy-start | bytes 196
  29.8 13.2 %collective-permute-start.3 = (bf16[512,512]{1,0:T(8,128)(2,1)S(1)}, bf16[512,512]{1,0:T(8,128)(2,1)S(1)}, u32[]{:S(2)}, u32[]{:S(2)}) collective-permute-start(bf16[512,512]{1,0:T(8,128)(2,1)S(1)} %collective-permute-done.1), channel_id=1, source_target_pairs={{0,7},{1,0},{2,1},{3,2},{4,3},{5,4},{6,5},{7,6},{8,15},{9,8},{10,9... | collective-permute-start | bytes 1572872 | tf_op jit(solution)/shard_map/ppermute | solution.py:87
  33.2 13.2 %collective-permute-start.2 = (bf16[512,512]{1,0:T(8,128)(2,1)S(1)}, bf16[512,512]{1,0:T(8,128)(2,1)}, u32[]{:S(2)}, u32[]{:S(2)}) collective-permute-start(bf16[512,512]{1,0:T(8,128)(2,1)S(1)} %collective-permute-done), channel_id=1, source_target_pairs={{0,1},{1,2},{2,3},{3,4},{4,5},{5,6},{6,7},{7,0},{8,9},{9,10},{10,1... | collective-permute-start | bytes 1572872 | tf_op jit(solution)/shard_map/ppermute | solution.py:86
  34.6 31.0 %copy-start.2 = (bf16[4096,512]{1,0:T(8,128)(2,1)S(1)}, bf16[4096,512]{1,0:T(8,128)(2,1)}, u32[]{:S(2)}) copy-start(bf16[4096,512]{1,0:T(8,128)(2,1)} %param.14) | copy-start | bytes 12582916
  42.9 12.3 %collective-permute-start.5 = (bf16[512,512]{1,0:T(8,128)(2,1)S(1)}, bf16[512,512]{1,0:T(8,128)(2,1)S(1)}, u32[]{:S(2)}, u32[]{:S(2)}) collective-permute-start(bf16[512,512]{1,0:T(8,128)(2,1)S(1)} %collective-permute-done.3), channel_id=1, source_target_pairs={{0,7},{1,0},{2,1},{3,2},{4,3},{5,4},{6,5},{7,6},{8,15},{9,8},{10,9... | collective-permute-start | bytes 1572872 | tf_op jit(solution)/shard_map/ppermute | solution.py:87
  46.4 12.4 %collective-permute-start.4 = (bf16[512,512]{1,0:T(8,128)(2,1)}, bf16[512,512]{1,0:T(8,128)(2,1)S(1)}, u32[]{:S(2)}, u32[]{:S(2)}) collective-permute-start(bf16[512,512]{1,0:T(8,128)(2,1)} %collective-permute-done.2), channel_id=1, source_target_pairs={{0,1},{1,2},{2,3},{3,4},{4,5},{5,6},{6,7},{7,0},{8,9},{9,10},{10,1... | collective-permute-start | bytes 1572872 | tf_op jit(solution)/shard_map/ppermute | solution.py:86
  55.3 6.8 %collective-permute-start.7 = (bf16[256,512]{1,0:T(8,128)(2,1)S(1)}, bf16[256,512]{1,0:T(8,128)(2,1)S(1)}, u32[]{:S(2)}, u32[]{:S(2)}) collective-permute-start(bf16[256,512]{1,0:T(8,128)(2,1)S(1)} %slice.19), channel_id=1, source_target_pairs={{0,7},{1,0},{2,1},{3,2},{4,3},{5,4},{6,5},{7,6},{8,15},{9,8},{10,9... | collective-permute-start | bytes 786440 | tf_op jit(solution)/shard_map/ppermute | solution.py:92
  58.8 6.7 %collective-permute-start.6 = (bf16[256,512]{1,0:T(8,128)(2,1)S(1)}, bf16[256,512]{1,0:T(8,128)(2,1)S(1)}, u32[]{:S(2)}, u32[]{:S(2)}) collective-permute-start(bf16[256,512]{1,0:T(8,128)(2,1)S(1)} %slice.18), channel_id=1, source_target_pairs={{0,1},{1,2},{2,3},{3,4},{4,5},{5,6},{6,7},{7,0},{8,9},{9,10},{10,1... | collective-permute-start | bytes 786440 | tf_op jit(solution)/shard_map/ppermute | solution.py:91
Sparse Core Ops, SparseCore 0:
  12.8 98.4 all-gather.1
  124.0 55.4 reduce-scatter.1

commit v17 on v15

--- a/solution.py
+++ b/solution.py
@@ -95,14 +95,13 @@
     per_dev = nb_dev
     enc_half = encodings
     mask_half = enc_mask
-    w_both = jnp.concatenate([w_key, w_value], axis=1)
-    own_kv = jnp.dot(
-        enc_half.reshape(per_dev * entry_len, enc_width), w_both, preferred_element_type=jnp.float32
-    ).astype(jnp.bfloat16).reshape(per_dev, entry_len, 2 * head_cols)
+    enc_flat = enc_half.reshape(per_dev * entry_len, enc_width)
+    own_k = jnp.dot(enc_flat, w_key, preferred_element_type=jnp.float32).astype(jnp.bfloat16)
+    own_v = jnp.dot(enc_flat, w_value, preferred_element_type=jnp.float32).astype(jnp.bfloat16)
     head_count = head_cols // HD
-    keys_t = own_kv[:, :, :head_cols].reshape(per_dev, entry_len, head_count, HD)
+    keys_t = own_k.reshape(per_dev, entry_len, head_count, HD)
     keys_t = keys_t.transpose(0, 3, 2, 1).reshape(per_dev, HD, head_count * entry_len)
-    own_kv = jnp.concatenate([keys_t, own_kv[:, :, head_cols:]], axis=2)
+    own_kv = jnp.concatenate([keys_t, own_v.reshape(per_dev, entry_len, head_cols)], axis=2)
     slots = lax.all_gather(own_kv, "retr", axis=0, tiled=True)
     slot_of = wanted
     mask_copies = jnp.broadcast_to(mask_half[None], (retr_count,) + mask_half.shape)

time: 188 us -> 189 us (level)
    dot_general x1 -> x2, matrix products: 2.79 us -> 3.91 us  [the longest x1 1.98 us: local(): jnp.dot(enc_flat, w_key, preferred_element_type=jnp.float32)]
where the time goes in v17:
time: 189 us; the launch traced here: 188 us
  waiting for transfers between devices  120 us (63%)
  starting transfers between devices  23.4 us (12%)
  matrix products  16.5 us (9%)
  between operations  13.8 us (7%)
  other arithmetic  5.64 us (3%)
  Pallas kernels  5.04 us (3%)
  local copies, waits for them, and re-layouts  4.39 us (2%)
    reduce_scatter x1, waiting for transfers between devices, local(): lax.psum_scatter(partial_value.astype(jnp.bfloat16), 'tensor', scatter_di...  55.6 us
    all_gather x1, waiting for transfers between devices, local(): slots = lax.all_gather(own_kv, 'retr', axis=0, tiled=True)  39.6 us
    ppermute x3, waiting for transfers between devices, local(): down = lax.ppermute(down, 'tensor', bwd)  18.4 us
    ppermute x3, starting transfers between devices, local(): down = lax.ppermute(down, 'tensor', bwd)  13.3 us
    dot_general x1, matrix products, local(): partial_value = jnp.dot(attended, w_out, preferred_element_type=jnp.float32)  6.63 us
    all_to_all x1, starting transfers between devices, local(): all_marks = lax.all_to_all(mask_copies, 'retr', 0, 0, tiled=True)  6.28 us
    dot_general x8, matrix products, local(): part = jnp.dot(normed, w_rows, preferred_element_type=jnp.float32)  5.95 us
    pallas_call x1, Pallas kernels, attend(): pl.pallas_call(functools.partial(attend_kernel, entry_len=entry_len), out...  5.04 us
  transfers between devices with their start and end apart: 11, of which 7 were waited for; matrix products, arithmetic and copies ran while one was open for 6% of the time, Pallas kernels for 0%

profile of v17, /device:TPU:1, one launch (start us, length us, event | category | flops | bytes accessed | tf_op | source)
XLA Modules:
  0.0 188.5 jit_solution(2389411617660024358)
XLA Ops:
  6.5 1.2 copy-done
  7.8 1.9 %convolution_convert_fusion.1 = bf16[512,512]{1,0:T(8,128)(2,1)S(1)} fusion(bf16[512,1024]{1,0:T(8,128)(2,1)S(1)} %bitcast.13, bf16[1024,512]{1,0:T(8,128)(2,1)} %param.16), kind=kOutput, calls=%fused_computation.27 | convolution fusion | flops 537133056 | bytes 2621440 | tf_op jit(solution)/shard_map/dot_general | solution.py:100
  9.7 2.0 %convolution_convert_fusion.2 = bf16[512,512]{1,0:T(8,128)(2,1)S(1)} fusion(bf16[512,1024]{1,0:T(8,128)(2,1)S(1)} %bitcast.12, bf16[1024,512]{1,0:T(8,128)(2,1)} %param.15), kind=kOutput, calls=%fused_computation.28 | convolution fusion | flops 537133056 | bytes 2621440 | tf_op jit(solution)/shard_map/dot_general | solution.py:99
  11.7 0.1 reshape.114
  11.9 0.5 copy.17
  12.3 0.2 reshape.115
  12.6 1.1 pad_maximum_fusion
  13.7 6.5 %collective-permute-start.1 = (bf16[512,512]{1,0:T(8,128)(2,1)S(1)}, bf16[512,512]{1,0:T(8,128)(2,1)S(1)}, u32[]{:S(2)}, u32[]{:S(2)}) collective-permute-start(bf16[512,512]{1,0:T(8,128)(2,1)S(1)} %copy-done.1), channel_id=1, source_target_pairs={{0,7},{1,0},{2,1},{3,2},{4,3},{5,4},{6,5},{7,6},{8,15},{9,8},{10,9... | collective-permute-start | bytes 1572872 | tf_op jit(solution)/shard_map/ppermute | solution.py:87
  20.2 0.6 broadcast_in_dim.15
  20.8 6.3 %all-to-all-start = ((s32[16,4,4]{2,1,0:T(4,128)}), s32[16,4,4]{2,1,0:T(4,128)S(1)}, u32[]{:S(2)}, u32[]{:S(2)}) async-start(s32[16,4,4]{2,1,0:T(4,128)} %broadcast_in_dim.15), calls=%async_computation | async-start | bytes 65536 | tf_op jit(solution)/shard_map/all_to_all | solution.py:108
  27.3 0.1 copy.16
  27.4 0.1 reshape.112.flat_ref
  27.5 0.1 reshape.118
  27.5 0.1 fusion.69
  27.6 0.2 fusion.22
  27.8 3.0 %collective-permute-done.1 = bf16[512,512]{1,0:T(8,128)(2,1)S(1)} collective-permute-done((bf16[512,512]{1,0:T(8,128)(2,1)S(1)}, bf16[512,512]{1,0:T(8,128)(2,1)S(1)}, u32[]{:S(2)}, u32[]{:S(2)}) %collective-permute-start.1) | collective-permute-done | bytes 524320 | tf_op jit(solution)/shard_map/ppermute | solution.py:87
  30.8 3.4 %collective-permute-start.3 = (bf16[512,512]{1,0:T(8,128)(2,1)S(1)}, bf16[512,512]{1,0:T(8,128)(2,1)S(1)}, u32[]{:S(2)}, u32[]{:S(2)}) collective-permute-start(bf16[512,512]{1,0:T(8,128)(2,1)S(1)} %collective-permute-done.1), channel_id=1, source_target_pairs={{0,7},{1,0},{2,1},{3,2},{4,3},{5,4},{6,5},{7,6},{8,15},{9,8},{10,9... | collective-permute-start | bytes 1572872 | tf_op jit(solution)/shard_map/ppermute | solution.py:87
  34.2 0.6 gather_fusion
  34.8 0.1 select_convert_fusion
  34.9 0.1 broadcast_in_dim.17
  35.0 0.7 convert_element_type.101.refs_8_
  35.7 8.3 %collective-permute-done.3 = bf16[512,512]{1,0:T(8,128)(2,1)S(1)} collective-permute-done((bf16[512,512]{1,0:T(8,128)(2,1)S(1)}, bf16[512,512]{1,0:T(8,128)(2,1)S(1)}, u32[]{:S(2)}, u32[]{:S(2)}) %collective-permute-start.3) | collective-permute-done | bytes 524320 | tf_op jit(solution)/shard_map/ppermute | solution.py:87
  44.0 3.4 %collective-permute-start.5 = (bf16[512,512]{1,0:T(8,128)(2,1)S(1)}, bf16[512,512]{1,0:T(8,128)(2,1)S(1)}, u32[]{:S(2)}, u32[]{:S(2)}) collective-permute-start(bf16[512,512]{1,0:T(8,128)(2,1)S(1)} %collective-permute-done.3), channel_id=1, source_target_pairs={{0,7},{1,0},{2,1},{3,2},{4,3},{5,4},{6,5},{7,6},{8,15},{9,8},{10,9... | collective-permute-start | bytes 1572872 | tf_op jit(solution)/shard_map/ppermute | solution.py:87
  47.4 0.2 fusion.4
  47.5 0.2 fusion.1
  47.7 0.2 fusion.10
  47.9 1.2 fusion.7
  49.1 7.1 %collective-permute-done.5 = bf16[512,512]{1,0:T(8,128)(2,1)S(1)} collective-permute-done((bf16[512,512]{1,0:T(8,128)(2,1)S(1)}, bf16[512,512]{1,0:T(8,128)(2,1)S(1)}, u32[]{:S(2)}, u32[]{:S(2)}) %collective-permute-start.5) | collective-permute-done | bytes 524320 | tf_op jit(solution)/shard_map/ppermute | solution.py:87
  56.3 3.5 %collective-permute-start.7 = (bf16[256,512]{1,0:T(8,128)(2,1)S(1)}, bf16[256,512]{1,0:T(8,128)(2,1)S(1)}, u32[]{:S(2)}, u32[]{:S(2)}) collective-permute-start(bf16[256,512]{1,0:T(8,128)(2,1)S(1)} %slice.11), channel_id=1, source_target_pairs={{0,7},{1,0},{2,1},{3,2},{4,3},{5,4},{6,5},{7,6},{8,15},{9,8},{10,9... | collective-permute-start | bytes 786440 | tf_op jit(solution)/shard_map/ppermute | solution.py:92
  59.8 0.3 collective-permute-start.6
  60.1 0.2 fusion.16
  60.2 0.2 fusion.13
  60.4 2.7 %collective-permute-done.7 = bf16[256,512]{1,0:T(8,128)(2,1)S(1)} collective-permute-done((bf16[256,512]{1,0:T(8,128)(2,1)S(1)}, bf16[256,512]{1,0:T(8,128)(2,1)S(1)}, u32[]{:S(2)}, u32[]{:S(2)}) %collective-permute-start.7) | collective-permute-done | bytes 262176 | tf_op jit(solution)/shard_map/ppermute | solution.py:92
  63.1 3.4 %collective-permute-done.6 = bf16[256,512]{1,0:T(8,128)(2,1)S(1)} collective-permute-done((bf16[256,512]{1,0:T(8,128)(2,1)S(1)}, bf16[256,512]{1,0:T(8,128)(2,1)S(1)}, u32[]{:S(2)}, u32[]{:S(2)}) %collective-permute-start.6) | collective-permute-done | bytes 262176 | tf_op jit(solution)/shard_map/ppermute | solution.py:91
  66.5 0.2 fusion.19
  66.7 0.5 fusion.26
  67.2 0.5 convolution_add_fusion.6
  67.7 0.5 convolution_add_fusion.5
  68.2 1.6 convolution_add_fusion.4
  69.9 0.5 convolution_add_fusion.3
  70.4 0.5 convolution_add_fusion.2
  70.9 0.5 convolution_add_fusion.1
  71.4 1.3 fusion.q_ref
  72.7 39.6 %all-gather.2.cloned.1.call-done.refs_0_.refs_1_.refs_2_.refs_3_.refs_4_.refs_5_.refs_6_.refs_7_ = bf16[64,128,1024]{2,1,0:T(8,128)(2,1)} async-done(((bf16[4,128,1024]{2,1,0:T(8,128)(2,1)}), bf16[64,128,1024]{2,1,0:T(8,128)(2,1)}) %all-gather.2.cloned.1.call-update) | async-done | bytes 16777232 | tf_op jit(solution)/shard_map/all_gather | solution.py:105
  112.3 5.0 %shard_map.91 = bf16[512,512]{1,0:T(8,128)(2,1)} custom-call(s32[16]{0:T(128)} %copy-done.5, bf16[512,512]{1,0:T(8,128)(2,1)} %fusion.q_ref, bf16[64,128,1024]{2,1,0:T(8,128)(2,1)} %all-gather.2.cloned.1.call-done.refs_0_.refs_1_.refs_2_.refs_3_.refs_4_.refs_5_.refs_6_.refs_7_, ...), custom_call_target="tpu_custom_call" | custom-call | tf_op jit(solution)/shard_map/pallas_call | solution.py:63
  117.4 6.6 %convolution_convert_fusion = bf16[512,4096]{1,0:T(8,128)(2,1)} fusion(bf16[512,512]{1,0:T(8,128)(2,1)} %shard_map.91, bf16[512,4096]{1,0:T(8,128)(2,1)} %param.17), kind=kOutput, calls=%fused_computation.1 | convolution fusion | flops 2149580800 | bytes 8912896 | tf_op jit(solution)/shard_map/dot_general | solution.py:127
  124.0 55.6 %reduce-scatter.2.cloned.1.call-done = bf16[512,512]{1,0:T(8,128)(2,1)} async-done(((bf16[512,4096]{1,0:T(8,128)(2,1)}), bf16[512,512]{1,0:T(8,128)(2,1)}) %reduce-scatter.2.cloned.1.call-update) | async-done | bytes 524304 | tf_op jit(solution)/shard_map/reduce_scatter | solution.py:128
  179.7 2.0 %fusion.25 = bf16[512,512]{1,0:T(8,128)(2,1)} fusion(bf16[512,512]{1,0:T(8,128)(2,1)S(1)} %copy-done.1, bf16[512,512]{1,0:T(8,128)(2,1)} %reduce-scatter.2.cloned.1.call-done), kind=kLoop, calls=%fused_computation.53 | loop fusion | flops 1048576 | bytes 1572864 | tf_op jit(solution)/shard_map/convert_element_type | solution.py:131
  (30 shorter events, 0.2 us)
Async XLA Ops:
  6.5 1.2 copy-start
  6.5 105.8 %all-gather.2.cloned.1.call-start = ((), (), s32[]{:S(2)}) async-start(), calls=%async_computation.2 | async-start | bytes 17825792 | tf_op jit(solution)/shard_map/all_gather | solution.py:105
  9.7 4.0 %copy-start.1 = (bf16[512,512]{1,0:T(8,128)(2,1)S(1)}, bf16[512,512]{1,0:T(8,128)(2,1)}, u32[]{:S(2)}) copy-start(bf16[512,512]{1,0:T(8,128)(2,1)} %param.9) | copy-start | bytes 1572868
  9.7 10.5 %copy-start.4 = (s32[4,4]{1,0:T(4,128)S(1)}, s32[4,4]{1,0:T(4,128)}, u32[]{:S(2)}) copy-start(s32[4,4]{1,0:T(4,128)} %param.13) | copy-start | bytes 196
  9.7 17.6 %copy-start.6 = (s32[8,2]{0,1:T(2,128)S(1)}, s32[8,2]{0,1:T(2,128)}, u32[]{:S(2)}) copy-start(s32[8,2]{0,1:T(2,128)} %param.11) | copy-start | bytes 196
  11.7 15.8 %copy-start.3 = (f32[4096]{0:T(1024)S(1)}, f32[4096]{0:T(1024)}, u32[]{:S(2)}) copy-start(f32[4096]{0:T(1024)} %param.10) | copy-start | bytes 49156
  13.7 17.1 %collective-permute-start.1 = (bf16[512,512]{1,0:T(8,128)(2,1)S(1)}, bf16[512,512]{1,0:T(8,128)(2,1)S(1)}, u32[]{:S(2)}, u32[]{:S(2)}) collective-permute-start(bf16[512,512]{1,0:T(8,128)(2,1)S(1)} %copy-done.1), channel_id=1, source_target_pairs={{0,7},{1,0},{2,1},{3,2},{4,3},{5,4},{6,5},{7,6},{8,15},{9,8},{10,9... | collective-permute-start | bytes 1572872 | tf_op jit(solution)/shard_map/ppermute | solution.py:87
  20.2 14.0 %collective-permute-start = (bf16[512,512]{1,0:T(8,128)(2,1)S(1)}, bf16[512,512]{1,0:T(8,128)(2,1)S(1)}, u32[]{:S(2)}, u32[]{:S(2)}) collective-permute-start(bf16[512,512]{1,0:T(8,128)(2,1)S(1)} %copy-done.1), channel_id=1, source_target_pairs={{0,1},{1,2},{2,3},{3,4},{4,5},{5,6},{6,7},{7,0},{8,9},{9,10},{10,1... | collective-permute-start | bytes 1572872 | tf_op jit(solution)/shard_map/ppermute | solution.py:86
  20.8 13.4 %all-to-all-start = ((s32[16,4,4]{2,1,0:T(4,128)}), s32[16,4,4]{2,1,0:T(4,128)S(1)}, u32[]{:S(2)}, u32[]{:S(2)}) async-start(s32[16,4,4]{2,1,0:T(4,128)} %broadcast_in_dim.15), calls=%async_computation | async-start | bytes 65536 | tf_op jit(solution)/shard_map/all_to_all | solution.py:108
  27.1 152.6 %reduce-scatter.2.cloned.1.call-start = ((), (), s32[]{:S(2)}) async-start(), calls=%async_computation.3 | async-start | bytes 4718592 | tf_op jit(solution)/shard_map/reduce_scatter | solution.py:128
  27.5 40.3 %copy-start.5 = (s32[16]{0:T(128)}, s32[16]{0:T(128)S(1)}, u32[]{:S(2)}) copy-start(s32[16]{0:T(128)S(1)} %reshape.112.flat_ref) | copy-start | bytes 196
  30.8 13.2 %collective-permute-start.3 = (bf16[512,512]{1,0:T(8,128)(2,1)S(1)}, bf16[512,512]{1,0:T(8,128)(2,1)S(1)}, u32[]{:S(2)}, u32[]{:S(2)}) collective-permute-start(bf16[512,512]{1,0:T(8,128)(2,1)S(1)} %collective-permute-done.1), channel_id=1, source_target_pairs={{0,7},{1,0},{2,1},{3,2},{4,3},{5,4},{6,5},{7,6},{8,15},{9,8},{10,9... | collective-permute-start | bytes 1572872 | tf_op jit(solution)/shard_map/ppermute | solution.py:87
  34.2 13.2 %collective-permute-start.2 = (bf16[512,512]{1,0:T(8,128)(2,1)S(1)}, bf16[512,512]{1,0:T(8,128)(2,1)}, u32[]{:S(2)}, u32[]{:S(2)}) collective-permute-start(bf16[512,512]{1,0:T(8,128)(2,1)S(1)} %collective-permute-done), channel_id=1, source_target_pairs={{0,1},{1,2},{2,3},{3,4},{4,5},{5,6},{6,7},{7,0},{8,9},{9,10},{10,1... | collective-permute-start | bytes 1572872 | tf_op jit(solution)/shard_map/ppermute | solution.py:86
  35.7 31.0 %copy-start.2 = (bf16[4096,512]{1,0:T(8,128)(2,1)S(1)}, bf16[4096,512]{1,0:T(8,128)(2,1)}, u32[]{:S(2)}) copy-start(bf16[4096,512]{1,0:T(8,128)(2,1)} %param.14) | copy-start | bytes 12582916
  44.0 12.3 %collective-permute-start.5 = (bf16[512,512]{1,0:T(8,128)(2,1)S(1)}, bf16[512,512]{1,0:T(8,128)(2,1)S(1)}, u32[]{:S(2)}, u32[]{:S(2)}) collective-permute-start(bf16[512,512]{1,0:T(8,128)(2,1)S(1)} %collective-permute-done.3), channel_id=1, source_target_pairs={{0,7},{1,0},{2,1},{3,2},{4,3},{5,4},{6,5},{7,6},{8,15},{9,8},{10,9... | collective-permute-start | bytes 1572872 | tf_op jit(solution)/shard_map/ppermute | solution.py:87
  47.4 12.4 %collective-permute-start.4 = (bf16[512,512]{1,0:T(8,128)(2,1)}, bf16[512,512]{1,0:T(8,128)(2,1)S(1)}, u32[]{:S(2)}, u32[]{:S(2)}) collective-permute-start(bf16[512,512]{1,0:T(8,128)(2,1)} %collective-permute-done.2), channel_id=1, source_target_pairs={{0,1},{1,2},{2,3},{3,4},{4,5},{5,6},{6,7},{7,0},{8,9},{9,10},{10,1... | collective-permute-start | bytes 1572872 | tf_op jit(solution)/shard_map/ppermute | solution.py:86
  56.3 6.8 %collective-permute-start.7 = (bf16[256,512]{1,0:T(8,128)(2,1)S(1)}, bf16[256,512]{1,0:T(8,128)(2,1)S(1)}, u32[]{:S(2)}, u32[]{:S(2)}) collective-permute-start(bf16[256,512]{1,0:T(8,128)(2,1)S(1)} %slice.11), channel_id=1, source_target_pairs={{0,7},{1,0},{2,1},{3,2},{4,3},{5,4},{6,5},{7,6},{8,15},{9,8},{10,9... | collective-permute-start | bytes 786440 | tf_op jit(solution)/shard_map/ppermute | solution.py:92
  59.8 6.7 %collective-permute-start.6 = (bf16[256,512]{1,0:T(8,128)(2,1)S(1)}, bf16[256,512]{1,0:T(8,128)(2,1)S(1)}, u32[]{:S(2)}, u32[]{:S(2)}) collective-permute-start(bf16[256,512]{1,0:T(8,128)(2,1)S(1)} %slice.10), channel_id=1, source_target_pairs={{0,1},{1,2},{2,3},{3,4},{4,5},{5,6},{6,7},{7,0},{8,9},{9,10},{10,1... | collective-permute-start | bytes 786440 | tf_op jit(solution)/shard_map/ppermute | solution.py:91
Sparse Core Ops, SparseCore 0:
  13.8 98.4 all-gather.1
  124.1 55.4 reduce-scatter.1
